TPU v7x, 32 devices: a whole 2x2x4 slice. The times are simulated.
32 devices in a mesh: ctx: 16 (over z, x, core), head: 2 (over y).
Axes of the slice: x: 2, y: 2, z: 4, core: 2. Of those that a mesh axis runs over, the one named last changes fastest.
Arguments:
- attn_q: bfloat16 [4096, 8192], P(('ctx', 'head')), may hold values from -8 to 8
- attn_k: bfloat16 [4096, 8192], P(('ctx', 'head')), may hold values from -8 to 8
- attn_v: bfloat16 [4096, 8192], P(('ctx', 'head')), may hold values from -5 to 5
- attn_dout: bfloat16 [4096, 8192], P(('ctx', 'head')), may hold values from -5 to 5
- doc_ids: int32 [4096], replicated, may hold values from 0 to 7, never falling along the last dimension, each value on 1 to 1024 neighbouring positions
Outputs:
- attn_dq: bfloat16 [4096, 8192], P('ctx', 'head')
- attn_dk: bfloat16 [4096, 8192], P('ctx', 'head')
- attn_dv: bfloat16 [4096, 8192], P('ctx', 'head')
Inputs may be any that keep to these rules, and one draw needn't show every extreme that they name: `doc_ids`: document numbers never fall along the window; each document holds 1 to 1024 consecutive tokens, and one holds exactly 1024.
All inputs are finite; a program needn't handle non-finite values.
Results may differ from a plain program's by a relative error of at most 0.0088.
Values may be sent and summed in bfloat16 or wider, within the bound.
No kernel may reach another device: no remote copies, remote signals or barrier semaphores. Data moves between devices by JAX's collectives and lax.ppermute only.
A program may use at most 256 MiB of HBM per device.

v0:
```python
from functools import reduce

import jax
import jax.numpy as jnp
from jax import lax
from jax.sharding import PartitionSpec as P

HEAD_DIM = 128
REACH = 4


masked_value = -1e30


def shifted(value, axis, steps):
    count = lax.axis_size(axis)
    leading, last = (max(0, -steps), min(count, count - steps))
    return lax.ppermute(value, axis, [(source, source + steps) for source in range(leading, last)])


def per_device(attn_q, attn_k, attn_v, attn_dout, doc_ids):
    query, keys, values, dout = (
        lax.all_to_all(attn_q, "head", split_axis=1, concat_axis=0, tiled=True),
        lax.all_to_all(attn_k, "head", split_axis=1, concat_axis=0, tiled=True),
        lax.all_to_all(attn_v, "head", split_axis=1, concat_axis=0, tiled=True),
        lax.all_to_all(attn_dout, "head", split_axis=1, concat_axis=0, tiled=True),
    )
    tok = query.shape[0]
    width = query.shape[1]
    heads_local = width // HEAD_DIM
    ctx_count = lax.axis_size("ctx")
    ctx_pos = lax.axis_index("ctx")
    scale = HEAD_DIM ** (-0.5)

    def head_major(block):
        return jnp.transpose(block.reshape(tok, heads_local, HEAD_DIM), (1, 0, 2))

    q_own = head_major(query)
    k_own = head_major(keys)
    v_own = head_major(values)
    d_own = head_major(dout)
    row_ids = jnp.arange(tok, dtype=jnp.int32)

    def block_info(owner):
        start = jnp.clip(owner * tok, 0, tok * (ctx_count - 1))
        docs = lax.dynamic_slice_in_dim(doc_ids, start, tok)
        return (owner * tok + row_ids, docs, (owner >= 0) & (owner < ctx_count))

    def allowed(q_info, k_info):
        causal = k_info[0][None, :] <= q_info[0][:, None]
        same_doc = k_info[1][None, :] == q_info[1][:, None]
        return causal & same_doc & q_info[2] & k_info[2]

    def scores(q_blk, k_blk, mask):
        raw = jnp.einsum("hqd,hkd->hqk", q_blk, k_blk, preferred_element_type=jnp.float32) * scale
        return jnp.where(mask[None], raw, masked_value)

    own = block_info(ctx_pos)
    key_list = [k_own]
    value_list = [v_own]
    masks = [allowed(own, own)]
    for shift in range(1, REACH + 1):
        far_k, far_v = shifted((k_own, v_own), "ctx", shift)
        key_list.append(far_k)
        value_list.append(far_v)
        masks.append(allowed(own, block_info(ctx_pos - shift)))
    logits = [scores(q_own, key_list[index], masks[index]) for index in range(REACH + 1)]
    top = reduce(jnp.maximum, [jnp.max(item, axis=2) for item in logits])
    denom = reduce(jnp.add, [jnp.sum(jnp.exp(item - top[:, :, None]), axis=2) for item in logits])
    lse = top + jnp.log(denom)
    probs = [
        jnp.where(masks[index][None], jnp.exp(logits[index] - lse[:, :, None]), 0.0)
        for index in range(REACH + 1)
    ]
    attn_out = reduce(
        jnp.add,
        [
            jnp.einsum(
                "hqk,hkd->hqd",
                probs[index].astype(jnp.bfloat16),
                value_list[index],
                preferred_element_type=jnp.float32,
            )
            for index in range(REACH + 1)
        ],
    )
    delta = jnp.sum(d_own.astype(jnp.float32) * attn_out, axis=2)
    shape3 = (heads_local, tok, HEAD_DIM)
    dq_acc = jnp.zeros(shape3, jnp.float32)
    dk_acc = jnp.zeros(shape3, jnp.float32)
    dv_acc = jnp.zeros(shape3, jnp.float32)
    for index in range(REACH + 1):
        k_blk = key_list[index]
        v_blk = value_list[index]
        prob = probs[index]
        prob_bf = prob.astype(jnp.bfloat16)
        dprobs = jnp.einsum("hqd,hkd->hqk", d_own, v_blk, preferred_element_type=jnp.float32)
        dscores = (prob * (dprobs - delta[:, :, None])).astype(jnp.bfloat16)
        dq_acc = dq_acc + jnp.einsum(
            "hqk,hkd->hqd", dscores, k_blk, preferred_element_type=jnp.float32
        )
        if index == 0:
            dk_acc = (
                jnp.einsum("hqk,hqd->hkd", dscores, q_own, preferred_element_type=jnp.float32)
                * scale
            )
            dv_acc = jnp.einsum("hqk,hqd->hkd", prob_bf, d_own, preferred_element_type=jnp.float32)
    for shift in range(1, REACH + 1):
        q_blk, d_blk = shifted((q_own, d_own), "ctx", -shift)
        far_lse, far_delta = shifted((lse, delta), "ctx", -shift)
        mask = allowed(block_info(ctx_pos + shift), own)
        logit = scores(q_blk, k_own, mask)
        prob = jnp.where(mask[None], jnp.exp(logit - far_lse[:, :, None]), 0.0)
        prob_bf = prob.astype(jnp.bfloat16)
        dprobs = jnp.einsum("hqd,hkd->hqk", d_blk, v_own, preferred_element_type=jnp.float32)
        dscores = (prob * (dprobs - far_delta[:, :, None])).astype(jnp.bfloat16)
        dk_acc = (
            dk_acc
            + jnp.einsum("hqk,hqd->hkd", dscores, q_blk, preferred_element_type=jnp.float32) * scale
        )
        dv_acc = dv_acc + jnp.einsum(
            "hqk,hqd->hkd", prob_bf, d_blk, preferred_element_type=jnp.float32
        )

    def token_major(block):
        return jnp.transpose(block, (1, 0, 2)).reshape(tok, width)

    attn_dq = token_major((dq_acc * scale).astype(jnp.bfloat16))
    attn_dk = token_major(dk_acc.astype(jnp.bfloat16))
    attn_dv = token_major(dv_acc.astype(jnp.bfloat16))
    return (attn_dq, attn_dk, attn_dv)


def solution(mesh):
    return jax.shard_map(
        per_device,
        mesh=mesh,
        in_specs=(
            P(("ctx", "head"), None),
            P(("ctx", "head"), None),
            P(("ctx", "head"), None),
            P(("ctx", "head"), None),
            P(),
        ),
        out_specs=(P("ctx", "head"), P("ctx", "head"), P("ctx", "head")),
        check_vma=False,
    )
```

profile of v0, /device:TPU:20, one launch (start us, length us, event | category | flops | bytes accessed | tf_op | source)
XLA Modules:
  0.0 669.0 jit_solution(12698922298471909461)
XLA Ops:
  11.1 20.2 %all-to-all-done.1 = bf16[128,2,4096]{2,0,1:T(8,128)(2,1)S(1)} async-done(((bf16[128,2,4096]{2,0,1:T(8,128)(2,1)}), bf16[128,2,4096]{2,0,1:T(8,128)(2,1)S(1)}, u32[]{:S(2)}, u32[]{:S(2)}) %all-to-all-start.1) | async-done | bytes 2097184 | tf_op jit(solution)/shard_map/all_to_all | solution.py:24
  41.3 19.4 %all-to-all-done = bf16[128,2,4096]{2,0,1:T(8,128)(2,1)S(1)} async-done(((bf16[128,2,4096]{2,0,1:T(8,128)(2,1)}), bf16[128,2,4096]{2,0,1:T(8,128)(2,1)S(1)}, u32[]{:S(2)}, u32[]{:S(2)}) %all-to-all-start) | async-done | bytes 2097184 | tf_op jit(solution)/shard_map/all_to_all | solution.py:23
  75.0 13.9 %all-to-all-done.3 = bf16[128,2,4096]{2,0,1:T(8,128)(2,1)} async-done(((bf16[128,2,4096]{2,0,1:T(8,128)(2,1)}), bf16[128,2,4096]{2,0,1:T(8,128)(2,1)}, u32[]{:S(2)}, u32[]{:S(2)}) %all-to-all-start.3) | async-done | bytes 2097184 | tf_op jit(solution)/shard_map/all_to_all | solution.py:25
  136.4 9.9 %collective-permute-done.3 = bf16[32,256,128]{2,1,0:T(8,128)(2,1)} collective-permute-done((bf16[32,256,128]{2,1,0:T(8,128)(2,1)}, bf16[32,256,128]{2,1,0:T(8,128)(2,1)}, u32[]{:S(2)}, u32[]{:S(2)}) %collective-permute-start.3) | collective-permute-done | bytes 2097184 | tf_op jit(solution)/shard_map/ppermute | solution.py:18
  152.1 58.5 %collective-permute-done.1 = bf16[32,256,128]{2,1,0:T(8,128)(2,1)} collective-permute-done((bf16[32,256,128]{2,1,0:T(8,128)(2,1)}, bf16[32,256,128]{2,1,0:T(8,128)(2,1)}, u32[]{:S(2)}, u32[]{:S(2)}) %collective-permute-start.1) | collective-permute-done | bytes 2097184 | tf_op jit(solution)/shard_map/ppermute | solution.py:18
  218.0 39.5 %collective-permute-done = bf16[32,256,128]{2,1,0:T(8,128)(2,1)} collective-permute-done((bf16[32,256,128]{2,1,0:T(8,128)(2,1)}, bf16[32,256,128]{2,1,0:T(8,128)(2,1)}, u32[]{:S(2)}, u32[]{:S(2)}) %collective-permute-start) | collective-permute-done | bytes 2097184 | tf_op jit(solution)/shard_map/ppermute | solution.py:18
  266.6 12.7 %exponential_reduce_fusion.3 = (f32[32,256]{1,0:T(8,128)S(1)}, f32[32,256]{1,0:T(8,128)S(1)}, f32[32,256]{1,0:T(8,128)S(1)}, f32[32,256]{1,0:T(8,128)S(1)}, f32[32,256]{1,0:T(8,128)S(1)}) fusion(f32[32,256,256]{1,2,0:T(8,128)} %get-tuple-element.41, f32[32,256]{1,0:T(8,128)S(1)} %maximum_maximum_fusion, pred[256,256]{0,1:T(8,128)(4,1)S(1)} %get-tuple-element.25, ...), kind=kLoop, calls=%fused_computation.21 | loop fusion | flops 41902080 | bytes 42467328 | tf_op jit(solution)/shard_map/reduce_sum | solution.py:69
  279.4 25.9 %collective-permute-start.12 = (bf16[32,256,128]{2,1,0:T(8,128)(2,1)}, bf16[32,256,128]{2,1,0:T(8,128)(2,1)}, u32[]{:S(2)}, u32[]{:S(2)}) collective-permute-start(bf16[32,256,128]{2,1,0:T(8,128)(2,1)} %bitcast.136), channel_id=1, source_target_pairs={{4,0},{6,2},{8,4},{10,6},{12,8},{14,10},{16,12},{18,14},{20,16},{2... | collective-permute-start | bytes 6291464 | tf_op jit(solution)/shard_map/ppermute | solution.py:18
  311.5 36.3 %collective-permute-start.18 = (bf16[32,256,128]{2,1,0:T(8,128)(2,1)}, bf16[32,256,128]{2,1,0:T(8,128)(2,1)}, u32[]{:S(2)}, u32[]{:S(2)}) collective-permute-start(bf16[32,256,128]{2,1,0:T(8,128)(2,1)} %bitcast.134), channel_id=1, source_target_pairs={{6,0},{8,2},{10,4},{12,6},{14,8},{16,10},{18,12},{20,14},{22,16},{... | collective-permute-start | bytes 6291464 | tf_op jit(solution)/shard_map/ppermute | solution.py:18
  352.5 16.5 %collective-permute-done.4 = bf16[32,256,128]{2,1,0:T(8,128)(2,1)} collective-permute-done((bf16[32,256,128]{2,1,0:T(8,128)(2,1)}, bf16[32,256,128]{2,1,0:T(8,128)(2,1)}, u32[]{:S(2)}, u32[]{:S(2)}) %collective-permute-start.4) | collective-permute-done | bytes 2097184 | tf_op jit(solution)/shard_map/ppermute | solution.py:18
  393.0 14.4 %multiply_reduce_fusion = f32[32,256]{1,0:T(8,128)S(1)} fusion(f32[32,256,128]{2,1,0:T(8,128)} %fusion.24, f32[32,256,128]{2,1,0:T(8,128)} %fusion.26, f32[32,256,128]{2,1,0:T(8,128)} %fusion.108, f32[32,256,128]{2,1,0:T(8,128)} %fusion.28, bf16[32,256,128]{2,1,0:T(8,128)(2,1)} %collective-permute-done.7, f32[32,256,256]{1,2,0:T(8,128)} %copy-done, ...), kind=kOutput, calls=%fused_computation.57 | convolution fusion | flops 554688512 | bytes 29491200 | tf_op jit(solution)/shard_map/hqk,hkd->hqd/dot_general | solution.py:78
  407.4 10.3 %multiply_convert_fusion.8 = bf16[32,256,256]{1,2,0:T(8,128)(2,1)} fusion(f32[32,256,256]{1,2,0:T(8,128)} %get-tuple-element.39, f32[32,256]{1,0:T(8,128)S(1)} %multiply_reduce_fusion, f32[32,256]{1,0:T(8,128)S(1)} %log_add_fusion, pred[256,256]{0,1:T(8,128)(4,1)S(1)} %get-tuple-element.24, bf16[256,32,128]{2,1,0:T(8,128)(2,1)} %bitcast.162, ...), kind=kOutput, calls=%fused_computation.12 | convolution fusion | flops 551550976 | bytes 16908288 | tf_op jit(solution)/shard_map/hqd,hkd->hqk/dot_general | solution.py:97
  417.8 11.7 %fusion.64 = f32[32,256,128]{1,2,0:T(8,128)} fusion(bf16[32,256,128]{2,1,0:T(8,128)(2,1)} %collective-permute-done.2, f32[32,256,256]{1,2,0:T(8,128)} %copy-done.5, f32[32,256]{1,0:T(8,128)S(1)} %multiply_reduce_fusion, f32[32,256]{1,0:T(8,128)S(1)} %log_add_fusion, pred[256,256]{0,1:T(8,128)(4,1)S(1)} %get-tuple-element.27, ...), kind=kOutput, calls=%fused_computation.88 | convolution fusion | flops 1088421888 | bytes 19005440 | tf_op jit(solution)/shard_map/hqk,hkd->hqd/dot_general | solution.py:99
  429.4 11.5 %fusion.63 = f32[32,256,128]{1,2,0:T(8,128)} fusion(bf16[32,256,128]{2,1,0:T(8,128)(2,1)} %collective-permute-done.1, f32[32,256,256]{1,2,0:T(8,128)} %copy-done.6, f32[32,256]{1,0:T(8,128)S(1)} %multiply_reduce_fusion, f32[32,256]{1,0:T(8,128)S(1)} %log_add_fusion, pred[256,256]{0,1:T(8,128)(4,1)S(1)} %get-tuple-element.26, ...), kind=kOutput, calls=%fused_computation.87 | convolution fusion | flops 1088421888 | bytes 19005440 | tf_op jit(solution)/shard_map/hqk,hkd->hqd/dot_general | solution.py:99
  440.9 11.4 %fusion.62 = f32[32,256,128]{1,2,0:T(8,128)} fusion(bf16[32,256,128]{2,1,0:T(8,128)(2,1)} %collective-permute-done, f32[32,256,256]{1,2,0:T(8,128)} %get-tuple-element.41, f32[32,256]{1,0:T(8,128)S(1)} %multiply_reduce_fusion, f32[32,256]{1,0:T(8,128)S(1)} %log_add_fusion, pred[256,256]{0,1:T(8,128)(4,1)S(1)} %get-tuple-element.25, ...), kind=kOutput, calls=%fused_computation.86 | convolution fusion | flops 1088421888 | bytes 19005440 | tf_op jit(solution)/shard_map/hqk,hkd->hqd/dot_general | solution.py:99
  458.2 14.7 %multiply_convert_fusion.10 = bf16[32,256,128]{1,2,0:T(8,128)(2,1)} fusion(f32[32,256,128]{1,2,0:T(8,128)} %fusion.64, f32[32,256,128]{1,2,0:T(8,128)} %fusion.63, f32[32,256,128]{1,2,0:T(8,128)} %fusion.106, f32[32,256,128]{1,2,0:T(8,128)} %fusion.62, bf16[32,256,128]{2,1,0:T(8,128)(2,1)} %collective-permute-done.3, f32[32,256,256]{1,2,0:T(8,128)} %copy-done, ...), kind=kOutput, calls=%fused_computation.51 | convolution fusion | flops 1094713344 | bytes 33685504 | tf_op jit(solution)/shard_map/hqk,hkd->hqd/dot_general | solution.py:99
  502.9 15.8 %collective-permute-done.20 = bf16[32,256,128]{2,1,0:T(8,128)(2,1)S(1)} collective-permute-done((bf16[32,256,128]{2,1,0:T(8,128)(2,1)}, bf16[32,256,128]{2,1,0:T(8,128)(2,1)S(1)}, u32[]{:S(2)}, u32[]{:S(2)}) %collective-permute-start.20) | collective-permute-done | bytes 2097184 | tf_op jit(solution)/shard_map/ppermute | solution.py:18
  535.2 9.9 %collective-permute-done.19 = f32[32,256]{1,0:T(8,128)S(1)} collective-permute-done((f32[32,256]{1,0:T(8,128)S(1)}, f32[32,256]{1,0:T(8,128)S(1)}, u32[]{:S(2)}, u32[]{:S(2)}) %collective-permute-start.19) | collective-permute-done | bytes 32800 | tf_op jit(solution)/shard_map/ppermute | solution.py:18
  550.4 10.9 %fusion.68 = f32[32,256,128]{1,2,0:T(8,128)} fusion(bf16[32,256,128]{2,1,0:T(8,128)(2,1)} %collective-permute-done.16, f32[32,256,256]{1,2,0:T(8,128)} %fusion.169, f32[32,256]{1,0:T(8,128)S(1)} %collective-permute-done.19, f32[32,256]{1,0:T(8,128)S(1)} %collective-permute-done.17, pred[256,256]{0,1:T(8,128)(4,1)S(1)} %get-tuple-element.31, ...), kind=kOutput, calls=%fused_computation.92 | convolution fusion | flops 1088421888 | bytes 19005440 | tf_op jit(solution)/shard_map/hqk,hqd->hkd/dot_general | solution.py:119
  565.1 20.9 %collective-permute-done.15 = f32[32,256]{1,0:T(8,128)S(1)} collective-permute-done((f32[32,256]{1,0:T(8,128)S(1)}, f32[32,256]{1,0:T(8,128)S(1)}, u32[]{:S(2)}, u32[]{:S(2)}) %collective-permute-start.15) | collective-permute-done | bytes 32800 | tf_op jit(solution)/shard_map/ppermute | solution.py:18
  589.8 10.9 %fusion.67 = f32[32,256,128]{1,2,0:T(8,128)} fusion(bf16[32,256,128]{2,1,0:T(8,128)(2,1)} %collective-permute-done.12, f32[32,256,256]{1,2,0:T(8,128)} %fusion.170, f32[32,256]{1,0:T(8,128)S(1)} %collective-permute-done.15, f32[32,256]{1,0:T(8,128)S(1)} %collective-permute-done.13, pred[256,256]{0,1:T(8,128)(4,1)S(1)} %get-tuple-element.30, ...), kind=kOutput, calls=%fused_computation.91 | convolution fusion | flops 1088421888 | bytes 19005440 | tf_op jit(solution)/shard_map/hqk,hqd->hkd/dot_general | solution.py:119
  602.9 11.0 %fusion.66 = f32[32,256,128]{1,2,0:T(8,128)} fusion(bf16[32,256,128]{2,1,0:T(8,128)(2,1)} %collective-permute-done.8, f32[32,256,256]{1,2,0:T(8,128)} %fusion.171, f32[32,256]{1,0:T(8,128)S(1)} %collective-permute-done.11, f32[32,256]{1,0:T(8,128)S(1)} %collective-permute-done.9, pred[256,256]{0,1:T(8,128)(4,1)S(1)} %get-tuple-element.29, ...), kind=kOutput, calls=%fused_computation.90 | convolution fusion | flops 1088421888 | bytes 19005440 | tf_op jit(solution)/shard_map/hqk,hqd->hkd/dot_general | solution.py:119
  613.9 13.0 %multiply_convert_fusion.9 = bf16[32,256,128]{1,2,0:T(8,128)(2,1)} fusion(f32[32,256,128]{1,2,0:T(8,128)} %fusion.68, f32[32,256,128]{1,2,0:T(8,128)} %fusion.67, f32[32,256,128]{1,2,0:T(8,128)} %fusion.104, f32[32,256,128]{1,2,0:T(8,128)} %fusion.66, bf16[32,256,128]{2,1,0:T(8,128)(2,1)} %copy-done.12, f32[32,256,256]{1,2,0:T(8,128)} %fusion.172, ...), kind=kOutput, calls=%fused_computation.50 | convolution fusion | flops 1094713344 | bytes 33685504 | tf_op jit(solution)/shard_map/hqk,hqd->hkd/dot_general | solution.py:119
  654.1 11.5 %add_convert_fusion = bf16[32,256,128]{1,2,0:T(8,128)(2,1)S(1)} fusion(f32[32,256,128]{1,2,0:T(8,128)} %fusion.16, f32[32,256,128]{1,2,0:T(8,128)} %fusion.18, f32[32,256,128]{1,2,0:T(8,128)} %fusion.102, f32[32,256,128]{1,2,0:T(8,128)} %fusion.20, bf16[32,256,128]{2,1,0:T(8,128)(2,1)} %collective-permute-done.22, f32[32,256,256]{1,2,0:T(8,128)} %fusion.172, ...), kind=kOutput, calls=%fused_computation.52 | convolution fusion | flops 552599552 | bytes 29458432 | tf_op jit(solution)/shard_map/hqk,hqd->hkd/dot_general | solution.py:121
  (138 shorter events, 236.6 us)
Async XLA Ops:
  32.7 28.0 %all-to-all-start = ((bf16[128,2,4096]{2,0,1:T(8,128)(2,1)}), bf16[128,2,4096]{2,0,1:T(8,128)(2,1)S(1)}, u32[]{:S(2)}, u32[]{:S(2)}) async-start(bf16[128,2,4096]{2,0,1:T(8,128)(2,1)} %bitcast.177), calls=%async_computation | async-start | bytes 4194304 | tf_op jit(solution)/shard_map/all_to_all | solution.py:23
  60.7 28.2 %all-to-all-start.3 = ((bf16[128,2,4096]{2,0,1:T(8,128)(2,1)}), bf16[128,2,4096]{2,0,1:T(8,128)(2,1)}, u32[]{:S(2)}, u32[]{:S(2)}) async-start(bf16[128,2,4096]{2,0,1:T(8,128)(2,1)} %bitcast.176), calls=%async_computation.3 | async-start | bytes 4194304 | tf_op jit(solution)/shard_map/all_to_all | solution.py:25
  71.6 58.4 %collective-permute-start.2 = (bf16[32,256,128]{2,1,0:T(8,128)(2,1)}, bf16[32,256,128]{2,1,0:T(8,128)(2,1)}, u32[]{:S(2)}, u32[]{:S(2)}) collective-permute-start(bf16[32,256,128]{2,1,0:T(8,128)(2,1)} %bitcast.135), channel_id=1, source_target_pairs={{0,6},{2,8},{4,10},{6,12},{8,14},{10,16},{12,18},{14,20},{16,22},{... | collective-permute-start | bytes 6291464 | tf_op jit(solution)/shard_map/ppermute | solution.py:18
  88.9 28.4 %all-to-all-start.2 = ((bf16[128,2,4096]{2,0,1:T(8,128)(2,1)}), bf16[128,2,4096]{2,0,1:T(8,128)(2,1)}, u32[]{:S(2)}, u32[]{:S(2)}) async-start(bf16[128,2,4096]{2,0,1:T(8,128)(2,1)} %bitcast.174), calls=%async_computation.2 | async-start | bytes 4194304 | tf_op jit(solution)/shard_map/all_to_all | solution.py:26
  95.5 50.8 %collective-permute-start.3 = (bf16[32,256,128]{2,1,0:T(8,128)(2,1)}, bf16[32,256,128]{2,1,0:T(8,128)(2,1)}, u32[]{:S(2)}, u32[]{:S(2)}) collective-permute-start(bf16[32,256,128]{2,1,0:T(8,128)(2,1)} %bitcast.135), channel_id=1, source_target_pairs={{0,8},{2,10},{4,12},{6,14},{8,16},{10,18},{12,20},{14,22},{16,24},... | collective-permute-start | bytes 6291464 | tf_op jit(solution)/shard_map/ppermute | solution.py:18
  99.2 111.4 %collective-permute-start.1 = (bf16[32,256,128]{2,1,0:T(8,128)(2,1)}, bf16[32,256,128]{2,1,0:T(8,128)(2,1)}, u32[]{:S(2)}, u32[]{:S(2)}) collective-permute-start(bf16[32,256,128]{2,1,0:T(8,128)(2,1)} %bitcast.135), channel_id=1, source_target_pairs={{0,4},{2,6},{4,8},{6,10},{8,12},{10,14},{12,16},{14,18},{16,20},{1... | collective-permute-start | bytes 6291464 | tf_op jit(solution)/shard_map/ppermute | solution.py:18
  104.0 153.5 %collective-permute-start = (bf16[32,256,128]{2,1,0:T(8,128)(2,1)}, bf16[32,256,128]{2,1,0:T(8,128)(2,1)}, u32[]{:S(2)}, u32[]{:S(2)}) collective-permute-start(bf16[32,256,128]{2,1,0:T(8,128)(2,1)} %bitcast.135), channel_id=1, source_target_pairs={{0,2},{2,4},{4,6},{6,8},{8,10},{10,12},{12,14},{14,16},{16,18},{18... | collective-permute-start | bytes 6291464 | tf_op jit(solution)/shard_map/ppermute | solution.py:18
  114.9 164.4 %collective-permute-start.6 = (bf16[32,256,128]{2,1,0:T(8,128)(2,1)}, bf16[32,256,128]{2,1,0:T(8,128)(2,1)}, u32[]{:S(2)}, u32[]{:S(2)}) collective-permute-start(bf16[32,256,128]{2,1,0:T(8,128)(2,1)} %bitcast.133), channel_id=1, source_target_pairs={{0,6},{2,8},{4,10},{6,12},{8,14},{10,16},{12,18},{14,20},{16,22},{... | collective-permute-start | bytes 6291464 | tf_op jit(solution)/shard_map/ppermute | solution.py:18
  130.0 181.5 %collective-permute-start.5 = (bf16[32,256,128]{2,1,0:T(8,128)(2,1)}, bf16[32,256,128]{2,1,0:T(8,128)(2,1)S(1)}, u32[]{:S(2)}, u32[]{:S(2)}) collective-permute-start(bf16[32,256,128]{2,1,0:T(8,128)(2,1)} %bitcast.133), channel_id=1, source_target_pairs={{0,4},{2,6},{4,8},{6,10},{8,12},{10,14},{12,16},{14,18},{16,20},{1... | collective-permute-start | bytes 6291464 | tf_op jit(solution)/shard_map/ppermute | solution.py:18
  146.3 222.7 %collective-permute-start.4 = (bf16[32,256,128]{2,1,0:T(8,128)(2,1)}, bf16[32,256,128]{2,1,0:T(8,128)(2,1)}, u32[]{:S(2)}, u32[]{:S(2)}) collective-permute-start(bf16[32,256,128]{2,1,0:T(8,128)(2,1)} %bitcast.133), channel_id=1, source_target_pairs={{0,2},{2,4},{4,6},{6,8},{8,10},{10,12},{12,14},{14,16},{16,18},{18... | collective-permute-start | bytes 6291464 | tf_op jit(solution)/shard_map/ppermute | solution.py:18
  210.6 175.7 %collective-permute-start.7 = (bf16[32,256,128]{2,1,0:T(8,128)(2,1)}, bf16[32,256,128]{2,1,0:T(8,128)(2,1)}, u32[]{:S(2)}, u32[]{:S(2)}) collective-permute-start(bf16[32,256,128]{2,1,0:T(8,128)(2,1)} %bitcast.133), channel_id=1, source_target_pairs={{0,8},{2,10},{4,12},{6,14},{8,16},{10,18},{12,20},{14,22},{16,24},... | collective-permute-start | bytes 6291464 | tf_op jit(solution)/shard_map/ppermute | solution.py:18
  257.5 215.3 %collective-permute-start.16 = (bf16[32,256,128]{2,1,0:T(8,128)(2,1)}, bf16[32,256,128]{2,1,0:T(8,128)(2,1)}, u32[]{:S(2)}, u32[]{:S(2)}) collective-permute-start(bf16[32,256,128]{2,1,0:T(8,128)(2,1)} %bitcast.136), channel_id=1, source_target_pairs={{6,0},{8,2},{10,4},{12,6},{14,8},{16,10},{18,12},{20,14},{22,16},{... | collective-permute-start | bytes 6291464 | tf_op jit(solution)/shard_map/ppermute | solution.py:18
  279.4 201.5 %collective-permute-start.12 = (bf16[32,256,128]{2,1,0:T(8,128)(2,1)}, bf16[32,256,128]{2,1,0:T(8,128)(2,1)}, u32[]{:S(2)}, u32[]{:S(2)}) collective-permute-start(bf16[32,256,128]{2,1,0:T(8,128)(2,1)} %bitcast.136), channel_id=1, source_target_pairs={{4,0},{6,2},{8,4},{10,6},{12,8},{14,10},{16,12},{18,14},{20,16},{2... | collective-permute-start | bytes 6291464 | tf_op jit(solution)/shard_map/ppermute | solution.py:18
  311.5 221.5 %collective-permute-start.18 = (bf16[32,256,128]{2,1,0:T(8,128)(2,1)}, bf16[32,256,128]{2,1,0:T(8,128)(2,1)}, u32[]{:S(2)}, u32[]{:S(2)}) collective-permute-start(bf16[32,256,128]{2,1,0:T(8,128)(2,1)} %bitcast.134), channel_id=1, source_target_pairs={{6,0},{8,2},{10,4},{12,6},{14,8},{16,10},{18,12},{20,14},{22,16},{... | collective-permute-start | bytes 6291464 | tf_op jit(solution)/shard_map/ppermute | solution.py:18
  369.0 192.4 %collective-permute-start.14 = (bf16[32,256,128]{2,1,0:T(8,128)(2,1)}, bf16[32,256,128]{2,1,0:T(8,128)(2,1)}, u32[]{:S(2)}, u32[]{:S(2)}) collective-permute-start(bf16[32,256,128]{2,1,0:T(8,128)(2,1)} %bitcast.134), channel_id=1, source_target_pairs={{4,0},{6,2},{8,4},{10,6},{12,8},{14,10},{16,12},{18,14},{20,16},{2... | collective-permute-start | bytes 6291464 | tf_op jit(solution)/shard_map/ppermute | solution.py:18
  386.3 102.8 %collective-permute-start.8 = (bf16[32,256,128]{2,1,0:T(8,128)(2,1)}, bf16[32,256,128]{2,1,0:T(8,128)(2,1)}, u32[]{:S(2)}, u32[]{:S(2)}) collective-permute-start(bf16[32,256,128]{2,1,0:T(8,128)(2,1)} %bitcast.136), channel_id=1, source_target_pairs={{2,0},{4,2},{6,4},{8,6},{10,8},{12,10},{14,12},{16,14},{18,16},{20... | collective-permute-start | bytes 6291464 | tf_op jit(solution)/shard_map/ppermute | solution.py:18
  472.8 45.8 %collective-permute-start.20 = (bf16[32,256,128]{2,1,0:T(8,128)(2,1)}, bf16[32,256,128]{2,1,0:T(8,128)(2,1)S(1)}, u32[]{:S(2)}, u32[]{:S(2)}) collective-permute-start(bf16[32,256,128]{2,1,0:T(8,128)(2,1)} %bitcast.136), channel_id=1, source_target_pairs={{8,0},{10,2},{12,4},{14,6},{16,8},{18,10},{20,12},{22,14},{24,16},... | collective-permute-start | bytes 6291464 | tf_op jit(solution)/shard_map/ppermute | solution.py:18
  480.9 119.9 %collective-permute-start.10 = (bf16[32,256,128]{2,1,0:T(8,128)(2,1)}, bf16[32,256,128]{2,1,0:T(8,128)(2,1)}, u32[]{:S(2)}, u32[]{:S(2)}) collective-permute-start(bf16[32,256,128]{2,1,0:T(8,128)(2,1)} %bitcast.134), channel_id=1, source_target_pairs={{2,0},{4,2},{6,4},{8,6},{10,8},{12,10},{14,12},{16,14},{18,16},{20... | collective-permute-start | bytes 6291464 | tf_op jit(solution)/shard_map/ppermute | solution.py:18
  489.1 56.1 %collective-permute-start.19 = (f32[32,256]{1,0:T(8,128)S(1)}, f32[32,256]{1,0:T(8,128)S(1)}, u32[]{:S(2)}, u32[]{:S(2)}) collective-permute-start(f32[32,256]{1,0:T(8,128)S(1)} %multiply_reduce_fusion), channel_id=1, source_target_pairs={{6,0},{8,2},{10,4},{12,6},{14,8},{16,10},{18,12},{20,14},{22,16},{... | collective-permute-start | bytes 98312 | tf_op jit(solution)/shard_map/ppermute | solution.py:18
  518.7 28.6 %collective-permute-start.17 = (f32[32,256]{1,0:T(8,128)S(1)}, f32[32,256]{1,0:T(8,128)S(1)}, u32[]{:S(2)}, u32[]{:S(2)}) collective-permute-start(f32[32,256]{1,0:T(8,128)S(1)} %log_add_fusion), channel_id=1, source_target_pairs={{6,0},{8,2},{10,4},{12,6},{14,8},{16,10},{18,12},{20,14},{22,16},{... | collective-permute-start | bytes 98312 | tf_op jit(solution)/shard_map/ppermute | solution.py:18
  533.0 80.9 %collective-permute-start.22 = (bf16[32,256,128]{2,1,0:T(8,128)(2,1)}, bf16[32,256,128]{2,1,0:T(8,128)(2,1)}, u32[]{:S(2)}, u32[]{:S(2)}) collective-permute-start(bf16[32,256,128]{2,1,0:T(8,128)(2,1)} %bitcast.134), channel_id=1, source_target_pairs={{8,0},{10,2},{12,4},{14,6},{16,8},{18,10},{20,12},{22,14},{24,16},... | collective-permute-start | bytes 6291464 | tf_op jit(solution)/shard_map/ppermute | solution.py:18
  545.2 40.8 %collective-permute-start.15 = (f32[32,256]{1,0:T(8,128)S(1)}, f32[32,256]{1,0:T(8,128)S(1)}, u32[]{:S(2)}, u32[]{:S(2)}) collective-permute-start(f32[32,256]{1,0:T(8,128)S(1)} %multiply_reduce_fusion), channel_id=1, source_target_pairs={{4,0},{6,2},{8,4},{10,6},{12,8},{14,10},{16,12},{18,14},{20,16},{2... | collective-permute-start | bytes 98312 | tf_op jit(solution)/shard_map/ppermute | solution.py:18
  547.3 40.6 %collective-permute-start.13 = (f32[32,256]{1,0:T(8,128)S(1)}, f32[32,256]{1,0:T(8,128)S(1)}, u32[]{:S(2)}, u32[]{:S(2)}) collective-permute-start(f32[32,256]{1,0:T(8,128)S(1)} %log_add_fusion), channel_id=1, source_target_pairs={{4,0},{6,2},{8,4},{10,6},{12,8},{14,10},{16,12},{18,14},{20,16},{2... | collective-permute-start | bytes 98312 | tf_op jit(solution)/shard_map/ppermute | solution.py:18
  561.3 41.6 %collective-permute-start.11 = (f32[32,256]{1,0:T(8,128)S(1)}, f32[32,256]{1,0:T(8,128)S(1)}, u32[]{:S(2)}, u32[]{:S(2)}) collective-permute-start(f32[32,256]{1,0:T(8,128)S(1)} %multiply_reduce_fusion), channel_id=1, source_target_pairs={{2,0},{4,2},{6,4},{8,6},{10,8},{12,10},{14,12},{16,14},{18,16},{20... | collective-permute-start | bytes 98312 | tf_op jit(solution)/shard_map/ppermute | solution.py:18
  (28 other events, 869.8 us)
where the time goes:
time: 681 us; the launch traced here: 669 us
  matrix products  243 us (36%)
  waiting for transfers between devices  225 us (33%)
  starting transfers between devices  142 us (21%)
  local copies, waits for them, and re-layouts  43.5 us (6%)
  other arithmetic  14.4 us (2%)
    ppermute x24, waiting for transfers between devices, shifted(): lax.ppermute(value, axis, [(source, source + steps) for source in range(l...  171 us
    ppermute x24, starting transfers between devices, shifted(): lax.ppermute(value, axis, [(source, source + steps) for source in range(l...  119 us
    dot_general x5, matrix products, per_device(): jnp.einsum('hqk,hkd->hqd', dscores, k_blk, preferred_element_type=jnp.flo...  55.1 us
    dot_general x9, matrix products, scores(): jnp.einsum('hqd,hkd->hqk', q_blk, k_blk, preferred_element_type=jnp.float32)  48 us
    dot_general x4, matrix products, per_device(): jnp.einsum('hqk,hqd->hkd', dscores, q_blk, preferred_element_type=jnp.flo...  45.8 us
    dot_general x5, matrix products, per_device(): jnp.einsum('hqk,hkd->hqd', probs[index].astype(jnp.bfloat16), value_list[...  40.7 us
    dot_general x4, matrix products, per_device(): jnp.einsum('hqk,hqd->hkd', prob_bf, d_blk, preferred_element_type=jnp.flo...  34.4 us
    unnamed x55, local copies, waits for them, and re-layouts  24 us
  transfers between devices with their start and end apart: 28, of which 10 were waited for; matrix products, arithmetic and copies ran while one was open for 36% of the time, Pallas kernels for 0%

commit v1 on v0

v1 whole, which is shorter than its diff:
```python
import jax
import jax.numpy as jnp
from jax import lax
from jax.experimental import pallas as pl
from jax.experimental.pallas import tpu as pltpu
from jax.sharding import PartitionSpec as P

HEAD_DIM = 128
MAX_DOC = 1024

masked_value = -1e30


def shifted(value, axis, steps):
    count = lax.axis_size(axis)
    leading, last = (max(0, -steps), min(count, count - steps))
    return lax.ppermute(value, axis, [(source, source + steps) for source in range(leading, last)])


def _row(col, tok):
    return jnp.transpose(jnp.broadcast_to(col, (tok, 128)))[0:1, :]


def _query_side_kernel(nblk, tok, scale):
    def kernel(*refs):
        q_ref, d_ref = refs[0], refs[1]
        k_refs = refs[2:2 + nblk]
        v_refs = refs[2 + nblk:2 + 2 * nblk]
        bias_ref = refs[2 + 2 * nblk]
        dq_ref, ld_ref = refs[3 + 2 * nblk], refs[4 + 2 * nblk]
        q = q_ref[...]
        d = d_ref[...]
        logits = []
        for j in range(nblk):
            raw = lax.dot_general(q, k_refs[j][...], (((1,), (1,)), ((), ())),
                                  preferred_element_type=jnp.float32)
            logits.append(raw * scale + bias_ref[:, j * tok:(j + 1) * tok])
        top = logits[0].max(axis=1, keepdims=True)
        for j in range(1, nblk):
            top = jnp.maximum(top, logits[j].max(axis=1, keepdims=True))
        denom = jnp.exp(logits[0] - top).sum(axis=1, keepdims=True)
        for j in range(1, nblk):
            denom = denom + jnp.exp(logits[j] - top).sum(axis=1, keepdims=True)
        lse = top + jnp.log(denom)
        probs = [jnp.exp(item - lse) for item in logits]
        out = None
        for j in range(nblk):
            part = jnp.dot(probs[j].astype(jnp.bfloat16), v_refs[j][...],
                           preferred_element_type=jnp.float32)
            out = part if out is None else out + part
        delta = (d.astype(jnp.float32) * out).sum(axis=1, keepdims=True)
        dq = None
        for j in range(nblk):
            dprobs = lax.dot_general(d, v_refs[j][...], (((1,), (1,)), ((), ())),
                                     preferred_element_type=jnp.float32)
            dscores = (probs[j] * (dprobs - delta)).astype(jnp.bfloat16)
            part = jnp.dot(dscores, k_refs[j][...], preferred_element_type=jnp.float32)
            dq = part if dq is None else dq + part
        dq_ref[...] = (dq * scale).astype(dq_ref.dtype)
        ld_ref[0:1, :] = _row(lse, tok)
        ld_ref[1:2, :] = _row(delta, tok)

    return kernel


def _key_side_kernel(nblk, tok, scale):
    def kernel(*refs):
        k_ref, v_ref = refs[0], refs[1]
        q_refs = refs[2:2 + nblk]
        d_refs = refs[2 + nblk:2 + 2 * nblk]
        ld_refs = refs[2 + 2 * nblk:2 + 3 * nblk]
        bias_ref = refs[2 + 3 * nblk]
        dk_ref, dv_ref = refs[3 + 3 * nblk], refs[4 + 3 * nblk]
        k = k_ref[...]
        v = v_ref[...]
        dk = None
        dv = None
        for j in range(nblk):
            q = q_refs[j][...]
            d = d_refs[j][...]
            lse = ld_refs[j][0:1, :]
            delta = ld_refs[j][1:2, :]
            raw = lax.dot_general(k, q, (((1,), (1,)), ((), ())),
                                  preferred_element_type=jnp.float32)
            logit = raw * scale + bias_ref[:, j * tok:(j + 1) * tok]
            prob = jnp.exp(logit - lse)
            dprobs = lax.dot_general(v, d, (((1,), (1,)), ((), ())),
                                     preferred_element_type=jnp.float32)
            dscores = (prob * (dprobs - delta)).astype(jnp.bfloat16)
            part_k = jnp.dot(dscores, q, preferred_element_type=jnp.float32)
            part_v = jnp.dot(prob.astype(jnp.bfloat16), d, preferred_element_type=jnp.float32)
            dk = part_k if dk is None else dk + part_k
            dv = part_v if dv is None else dv + part_v
        dk_ref[...] = (dk * scale).astype(dk_ref.dtype)
        dv_ref[...] = dv.astype(dv_ref.dtype)

    return kernel


def per_device(attn_q, attn_k, attn_v, attn_dout, doc_ids):
    query, keys, values, dout = (
        lax.all_to_all(attn_q, "head", split_axis=1, concat_axis=0, tiled=True),
        lax.all_to_all(attn_k, "head", split_axis=1, concat_axis=0, tiled=True),
        lax.all_to_all(attn_v, "head", split_axis=1, concat_axis=0, tiled=True),
        lax.all_to_all(attn_dout, "head", split_axis=1, concat_axis=0, tiled=True),
    )
    tok = query.shape[0]
    width = query.shape[1]
    heads_local = width // HEAD_DIM
    ctx_count = lax.axis_size("ctx")
    ctx_pos = lax.axis_index("ctx")
    scale = HEAD_DIM ** (-0.5)
    reach = min(-(-(MAX_DOC - 1) // tok), ctx_count - 1)
    nblk = reach + 1
    row_ids = jnp.arange(tok, dtype=jnp.int32)

    def block_info(owner):
        start = jnp.clip(owner * tok, 0, tok * (ctx_count - 1))
        docs = lax.dynamic_slice_in_dim(doc_ids, start, tok)
        valid = (owner >= 0) & (owner < ctx_count)
        return (owner * tok + row_ids, docs, valid)

    def allowed(q_info, k_info):
        causal = k_info[0][None, :] <= q_info[0][:, None]
        same_doc = k_info[1][None, :] == q_info[1][:, None]
        return causal & same_doc & q_info[2] & k_info[2]

    def bias_of(mask):
        return jnp.where(mask, 0.0, masked_value).astype(jnp.float32)

    own = block_info(ctx_pos)
    key_list, value_list, q_masks = [], [], []
    for shift in range(reach, 0, -1):
        far_k, far_v = shifted((keys, values), "ctx", shift)
        key_list.append(far_k)
        value_list.append(far_v)
        q_masks.append(allowed(own, block_info(ctx_pos - shift)))
    key_list.append(keys)
    value_list.append(values)
    q_masks.append(allowed(own, own))
    q_bias = bias_of(jnp.concatenate(q_masks, axis=1))

    query_list, dout_list, k_masks = [query], [dout], [allowed(own, own).T]
    for shift in range(1, reach + 1):
        far_q, far_d = shifted((query, dout), "ctx", -shift)
        query_list.append(far_q)
        dout_list.append(far_d)
        k_masks.append(allowed(block_info(ctx_pos + shift), own).T)
    k_bias = bias_of(jnp.concatenate(k_masks, axis=1))

    col_spec = pl.BlockSpec((tok, HEAD_DIM), lambda h: (0, h))
    bias_spec = pl.BlockSpec((tok, nblk * tok), lambda h: (0, 0))
    ld_spec = pl.BlockSpec((None, 2, tok), lambda h: (h, 0, 0))
    params = pltpu.CompilerParams(dimension_semantics=("arbitrary",))

    dq, ld = pl.pallas_call(
        _query_side_kernel(nblk, tok, scale),
        out_shape=(
            jax.ShapeDtypeStruct((tok, width), jnp.bfloat16),
            jax.ShapeDtypeStruct((heads_local, 2, tok), jnp.float32),
        ),
        grid=(heads_local,),
        in_specs=[col_spec] * (2 + 2 * nblk) + [bias_spec],
        out_specs=(col_spec, ld_spec),
        compiler_params=params,
        name="attn_query_side",
    )(query, dout, *key_list, *value_list, q_bias)

    ld_list = [ld]
    for shift in range(1, reach + 1):
        ld_list.append(shifted(ld, "ctx", -shift))

    dk, dv = pl.pallas_call(
        _key_side_kernel(nblk, tok, scale),
        out_shape=(
            jax.ShapeDtypeStruct((tok, width), jnp.bfloat16),
            jax.ShapeDtypeStruct((tok, width), jnp.bfloat16),
        ),
        grid=(heads_local,),
        in_specs=[col_spec] * (2 + 2 * nblk) + [ld_spec] * nblk + [bias_spec],
        out_specs=(col_spec, col_spec),
        compiler_params=params,
        name="attn_key_side",
    )(keys, values, *query_list, *dout_list, *ld_list, k_bias)
    return (dq, dk, dv)


def solution(mesh):
    return jax.shard_map(
        per_device,
        mesh=mesh,
        in_specs=(
            P(("ctx", "head"), None),
            P(("ctx", "head"), None),
            P(("ctx", "head"), None),
            P(("ctx", "head"), None),
            P(),
        ),
        out_specs=(P("ctx", "head"), P("ctx", "head"), P("ctx", "head")),
        check_vma=False,
    )
```

time: 681 us -> 584 us (0.86); the launches traced: 669 us -> 580 us
  matrix products: 243 us -> 0 us
  waiting for transfers between devices: 225 us -> 329 us
  Pallas kernels: 0 us -> 95.2 us
  local copies, waits for them, and re-layouts: 43.5 us -> 10.1 us
  starting transfers between devices: 142 us -> 113 us
  blocking collectives: 0 us -> 26.6 us
  other arithmetic: 14.4 us -> 4.08 us
    dot_general x30 -> x0, matrix products: 243 us -> none  [the longest x5 55.1 us: per_device(): jnp.einsum('hqk,hkd->hqd', dscores, k_blk, preferred_element_type=jnp.flo...]
    ppermute x24 -> x20, waiting for transfers between devices: 171 us -> 314 us  [shifted(): lax.ppermute(value, axis, [(source, source + steps) for source in range(l...]
    pallas_call x0 -> x2, Pallas kernels: none -> 95.2 us  [the longest x1 52.5 us: per_device(): pl.pallas_call(_query_side_kernel(nblk, tok, scale), out_shape=(jax.Shape...]
    all_to_all x0 -> x1, blocking collectives: none -> 26.6 us  [per_device(): lax.all_to_all(attn_k, 'head', split_axis=1, concat_axis=0, tiled=True)]
    ppermute x24 -> x20, starting transfers between devices: 119 us -> 94.7 us  [shifted(): lax.ppermute(value, axis, [(source, source + steps) for source in range(l...]
    unnamed x55 -> x16, local copies, waits for them, and re-layouts: 24 us -> 0.64 us
    all_to_all x1 -> x0, waiting for transfers between devices: 20.2 us -> none  [per_device(): lax.all_to_all(attn_k, 'head', split_axis=1, concat_axis=0, tiled=True)]
    all_to_all x1, waiting for transfers between devices: 19.4 us -> 0.01 us  [per_device(): lax.all_to_all(attn_q, 'head', split_axis=1, concat_axis=0, tiled=True)]
  transfers between devices with their start and end apart: 28 -> 23, of which waited for: 10 -> 11; matrix products, arithmetic and copies ran while one was open for 36% -> 2% of each run, Pallas kernels for 0% -> 9%
where the time goes in v1:
time: 584 us; the launch traced here: 580 us
  waiting for transfers between devices  329 us (56%)
  starting transfers between devices  113 us (19%)
  Pallas kernels  95.2 us (16%)
  blocking collectives  26.6 us (5%)
  local copies, waits for them, and re-layouts  10.1 us (2%)
    ppermute x20, waiting for transfers between devices, shifted(): lax.ppermute(value, axis, [(source, source + steps) for source in range(l...  314 us
    ppermute x20, starting transfers between devices, shifted(): lax.ppermute(value, axis, [(source, source + steps) for source in range(l...  94.7 us
    pallas_call x1, Pallas kernels, per_device(): pl.pallas_call(_query_side_kernel(nblk, tok, scale), out_shape=(jax.Shape...  52.5 us
    pallas_call x1, Pallas kernels, per_device(): pl.pallas_call(_key_side_kernel(nblk, tok, scale), out_shape=(jax.ShapeDt...  42.7 us
    all_to_all x1, blocking collectives, per_device(): lax.all_to_all(attn_k, 'head', split_axis=1, concat_axis=0, tiled=True)  26.6 us
    all_to_all x1, waiting for transfers between devices, per_device(): lax.all_to_all(attn_v, 'head', split_axis=1, concat_axis=0, tiled=True)  15 us
  transfers between devices with their start and end apart: 23, of which 11 were waited for; matrix products, arithmetic and copies ran while one was open for 2% of the time, Pallas kernels for 9%

profile of v1, /device:TPU:20, one launch (start us, length us, event | category | flops | bytes accessed | tf_op | source)
XLA Modules:
  0.0 579.8 jit_solution(1413994372472590640)
XLA Ops:
  2.4 26.6 %all_to_all.76 = bf16[128,2,4096]{2,0,1:T(8,128)(2,1)S(1)} all-to-all(bf16[128,2,4096]{2,0,1:T(8,128)(2,1)S(1)} %bitcast.43), channel_id=1, replica_groups=mesh['ctx'=16,'head'=2] {'head'}, dimensions={1} | all-to-all | bytes 4194304 | tf_op jit(solution)/shard_map/all_to_all | solution.py:103
  28.9 3.5 collective-permute-start
  33.9 6.5 %all-to-all-start.3 = ((bf16[128,2,4096]{2,0,1:T(8,128)(2,1)}), bf16[128,2,4096]{2,0,1:T(8,128)(2,1)}, u32[]{:S(2)}, u32[]{:S(2)}) async-start(bf16[128,2,4096]{2,0,1:T(8,128)(2,1)} %bitcast.42), calls=%async_computation.3 | async-start | bytes 4194304 | tf_op jit(solution)/shard_map/all_to_all | solution.py:104
  42.3 3.4 collective-permute-start.2
  47.7 15.0 %all-to-all-done.3 = bf16[128,2,4096]{2,0,1:T(8,128)(2,1)} async-done(((bf16[128,2,4096]{2,0,1:T(8,128)(2,1)}), bf16[128,2,4096]{2,0,1:T(8,128)(2,1)}, u32[]{:S(2)}, u32[]{:S(2)}) %all-to-all-start.3) | async-done | bytes 2097184 | tf_op jit(solution)/shard_map/all_to_all | solution.py:104
  64.6 14.9 %collective-permute-done.refs_2_ = bf16[256,4096]{1,0:T(8,128)(2,1)} collective-permute-done((bf16[256,4096]{1,0:T(8,128)(2,1)S(1)}, bf16[256,4096]{1,0:T(8,128)(2,1)}, u32[]{:S(2)}, u32[]{:S(2)}) %collective-permute-start) | collective-permute-done | bytes 2097184 | tf_op jit(solution)/shard_map/ppermute | solution.py:17
  81.4 3.1 copy.23
  84.5 6.6 %all-to-all-start = ((bf16[128,2,4096]{2,0,1:T(8,128)(2,1)}), bf16[128,2,4096]{2,0,1:T(8,128)(2,1)}, u32[]{:S(2)}, u32[]{:S(2)}) async-start(bf16[128,2,4096]{2,0,1:T(8,128)(2,1)} %bitcast.41), calls=%async_computation | async-start | bytes 4194304 | tf_op jit(solution)/shard_map/all_to_all | solution.py:102
  91.1 29.8 %collective-permute-done.1.refs_3_ = bf16[256,4096]{1,0:T(8,128)(2,1)} collective-permute-done((bf16[256,4096]{1,0:T(8,128)(2,1)S(1)}, bf16[256,4096]{1,0:T(8,128)(2,1)}, u32[]{:S(2)}, u32[]{:S(2)}) %collective-permute-start.1) | collective-permute-done | bytes 2097184 | tf_op jit(solution)/shard_map/ppermute | solution.py:17
  120.9 5.9 %collective-permute-start.6 = (bf16[256,4096]{1,0:T(8,128)(2,1)}, bf16[256,4096]{1,0:T(8,128)(2,1)}, u32[]{:S(2)}, u32[]{:S(2)}) collective-permute-start(bf16[256,4096]{1,0:T(8,128)(2,1)} %bitcast.8.refs_11_.refs_1_), channel_id=1, source_target_pairs={{0,4},{2,6},{4,8},{6,10},{8,12},{10,14},{12,16},{14,18},{16,20},{1... | collective-permute-start | bytes 6291464 | tf_op jit(solution)/shard_map/ppermute | solution.py:17
  126.8 43.5 %collective-permute-done.2.refs_4_ = bf16[256,4096]{1,0:T(8,128)(2,1)} collective-permute-done((bf16[256,4096]{1,0:T(8,128)(2,1)S(1)}, bf16[256,4096]{1,0:T(8,128)(2,1)}, u32[]{:S(2)}, u32[]{:S(2)}) %collective-permute-start.2) | collective-permute-done | bytes 2097184 | tf_op jit(solution)/shard_map/ppermute | solution.py:17
  172.2 39.5 %collective-permute-done.3.refs_5_ = bf16[256,4096]{1,0:T(8,128)(2,1)} collective-permute-done((bf16[256,4096]{1,0:T(8,128)(2,1)S(1)}, bf16[256,4096]{1,0:T(8,128)(2,1)}, u32[]{:S(2)}, u32[]{:S(2)}) %collective-permute-start.3) | collective-permute-done | bytes 2097184 | tf_op jit(solution)/shard_map/ppermute | solution.py:17
  213.6 4.0 collective-permute-start.9
  217.6 44.3 %collective-permute-start.10 = (bf16[256,4096]{1,0:T(8,128)(2,1)}, bf16[256,4096]{1,0:T(8,128)(2,1)}, u32[]{:S(2)}, u32[]{:S(2)}) collective-permute-start(bf16[256,4096]{1,0:T(8,128)(2,1)} %bitcast.1.refs_0_.refs_2_), channel_id=1, source_target_pairs={{6,0},{8,2},{10,4},{12,6},{14,8},{16,10},{18,12},{20,14},{22,16},{... | collective-permute-start | bytes 6291464 | tf_op jit(solution)/shard_map/ppermute | solution.py:17
  262.0 3.1 copy.22
  265.1 5.6 all-to-all-start.1
  271.2 34.0 %collective-permute-done.6.refs_9_ = bf16[256,4096]{1,0:T(8,128)(2,1)} collective-permute-done((bf16[256,4096]{1,0:T(8,128)(2,1)}, bf16[256,4096]{1,0:T(8,128)(2,1)}, u32[]{:S(2)}, u32[]{:S(2)}) %collective-permute-start.6) | collective-permute-done | bytes 2097184 | tf_op jit(solution)/shard_map/ppermute | solution.py:17
  307.6 40.8 %collective-permute-done.7.refs_10_ = bf16[256,4096]{1,0:T(8,128)(2,1)} collective-permute-done((bf16[256,4096]{1,0:T(8,128)(2,1)}, bf16[256,4096]{1,0:T(8,128)(2,1)}, u32[]{:S(2)}, u32[]{:S(2)}) %collective-permute-start.7) | collective-permute-done | bytes 2097184 | tf_op jit(solution)/shard_map/ppermute | solution.py:17
  352.3 5.8 collective-permute-start.14
  358.5 42.4 %collective-permute-done.10.refs_5_ = bf16[256,4096]{1,0:T(8,128)(2,1)} collective-permute-done((bf16[256,4096]{1,0:T(8,128)(2,1)}, bf16[256,4096]{1,0:T(8,128)(2,1)}, u32[]{:S(2)}, u32[]{:S(2)}) %collective-permute-start.10) | collective-permute-done | bytes 2097184 | tf_op jit(solution)/shard_map/ppermute | solution.py:17
  405.3 52.5 %attn_query_side.1 = (bf16[256,4096]{1,0:T(8,128)(2,1)}, f32[32,2,256]{2,1,0:T(2,128)}) custom-call(bf16[256,4096]{1,0:T(8,128)(2,1)} %bitcast.1.refs_0_.refs_2_, bf16[256,4096]{1,0:T(8,128)(2,1)} %bitcast.38, bf16[256,4096]{1,0:T(8,128)(2,1)} %collective-permute-done.refs_2_, bf16[256,4096]{1,0:T(8,128)(2,1)} %collective-permute-done.1.refs_3_, ...), custom_call_target="tpu_custom_call" | custom-call | tf_op jit(solution)/shard_map/attn_query_side/pallas_call | solution.py:156
  463.8 24.9 %collective-permute-done.14.refs_10_ = bf16[256,4096]{1,0:T(8,128)(2,1)} collective-permute-done((bf16[256,4096]{1,0:T(8,128)(2,1)S(1)}, bf16[256,4096]{1,0:T(8,128)(2,1)}, u32[]{:S(2)}, u32[]{:S(2)}) %collective-permute-start.14) | collective-permute-done | bytes 2097184 | tf_op jit(solution)/shard_map/ppermute | solution.py:17
  491.8 41.9 %collective-permute-done.15.refs_11_ = bf16[256,4096]{1,0:T(8,128)(2,1)} collective-permute-done((bf16[256,4096]{1,0:T(8,128)(2,1)S(1)}, bf16[256,4096]{1,0:T(8,128)(2,1)}, u32[]{:S(2)}, u32[]{:S(2)}) %collective-permute-start.15) | collective-permute-done | bytes 2097184 | tf_op jit(solution)/shard_map/ppermute | solution.py:17
  537.1 42.7 %attn_key_side.1 = (bf16[256,4096]{1,0:T(8,128)(2,1)}, bf16[256,4096]{1,0:T(8,128)(2,1)}) custom-call(bf16[256,4096]{1,0:T(8,128)(2,1)} %bitcast.33, bf16[256,4096]{1,0:T(8,128)(2,1)} %bitcast.8.refs_11_.refs_1_, bf16[256,4096]{1,0:T(8,128)(2,1)} %bitcast.1.refs_0_.refs_2_, bf16[256,4096]{1,0:T(8,128)(2,1)} %collective-permute-done.8.refs_3_, ...), custom_call_target="tpu_custom_call" | custom-call | tf_op jit(solution)/shard_map/attn_key_side/pallas_call | solution.py:173
  (62 shorter events, 38.4 us)
Async XLA Ops:
  28.9 50.6 %collective-permute-start = (bf16[256,4096]{1,0:T(8,128)(2,1)S(1)}, bf16[256,4096]{1,0:T(8,128)(2,1)}, u32[]{:S(2)}, u32[]{:S(2)}) collective-permute-start(bf16[256,4096]{1,0:T(8,128)(2,1)S(1)} %bitcast.28), channel_id=1, source_target_pairs={{0,8},{2,10},{4,12},{6,14},{8,16},{10,18},{12,20},{14,22},{16,24},... | collective-permute-start | bytes 6291464 | tf_op jit(solution)/shard_map/ppermute | solution.py:17
  33.9 28.8 %all-to-all-start.3 = ((bf16[128,2,4096]{2,0,1:T(8,128)(2,1)}), bf16[128,2,4096]{2,0,1:T(8,128)(2,1)}, u32[]{:S(2)}, u32[]{:S(2)}) async-start(bf16[128,2,4096]{2,0,1:T(8,128)(2,1)} %bitcast.42), calls=%async_computation.3 | async-start | bytes 4194304 | tf_op jit(solution)/shard_map/all_to_all | solution.py:104
  40.4 80.5 %collective-permute-start.1 = (bf16[256,4096]{1,0:T(8,128)(2,1)S(1)}, bf16[256,4096]{1,0:T(8,128)(2,1)}, u32[]{:S(2)}, u32[]{:S(2)}) collective-permute-start(bf16[256,4096]{1,0:T(8,128)(2,1)S(1)} %bitcast.29), channel_id=1, source_target_pairs={{0,6},{2,8},{4,10},{6,12},{8,14},{10,16},{12,18},{14,20},{16,22},{... | collective-permute-start | bytes 6291464 | tf_op jit(solution)/shard_map/ppermute | solution.py:17
  42.3 128.0 %collective-permute-start.2 = (bf16[256,4096]{1,0:T(8,128)(2,1)S(1)}, bf16[256,4096]{1,0:T(8,128)(2,1)}, u32[]{:S(2)}, u32[]{:S(2)}) collective-permute-start(bf16[256,4096]{1,0:T(8,128)(2,1)S(1)} %bitcast.30), channel_id=1, source_target_pairs={{0,4},{2,6},{4,8},{6,10},{8,12},{10,14},{12,16},{14,18},{16,20},{1... | collective-permute-start | bytes 6291464 | tf_op jit(solution)/shard_map/ppermute | solution.py:17
  45.8 165.9 %collective-permute-start.3 = (bf16[256,4096]{1,0:T(8,128)(2,1)S(1)}, bf16[256,4096]{1,0:T(8,128)(2,1)}, u32[]{:S(2)}, u32[]{:S(2)}) collective-permute-start(bf16[256,4096]{1,0:T(8,128)(2,1)S(1)} %bitcast.31), channel_id=1, source_target_pairs={{0,2},{2,4},{4,6},{6,8},{8,10},{10,12},{12,14},{14,16},{16,18},{18... | collective-permute-start | bytes 6291464 | tf_op jit(solution)/shard_map/ppermute | solution.py:17
  62.7 150.9 %collective-permute-start.4 = (bf16[256,4096]{1,0:T(8,128)(2,1)}, bf16[256,4096]{1,0:T(8,128)(2,1)}, u32[]{:S(2)}, u32[]{:S(2)}) collective-permute-start(bf16[256,4096]{1,0:T(8,128)(2,1)} %bitcast.8.refs_11_.refs_1_), channel_id=1, source_target_pairs={{0,8},{2,10},{4,12},{6,14},{8,16},{10,18},{12,20},{14,22},{16,24},... | collective-permute-start | bytes 6291464 | tf_op jit(solution)/shard_map/ppermute | solution.py:17
  79.5 138.1 %collective-permute-start.5 = (bf16[256,4096]{1,0:T(8,128)(2,1)}, bf16[256,4096]{1,0:T(8,128)(2,1)}, u32[]{:S(2)}, u32[]{:S(2)}) collective-permute-start(bf16[256,4096]{1,0:T(8,128)(2,1)} %bitcast.8.refs_11_.refs_1_), channel_id=1, source_target_pairs={{0,6},{2,8},{4,10},{6,12},{8,14},{10,16},{12,18},{14,20},{16,22},{... | collective-permute-start | bytes 6291464 | tf_op jit(solution)/shard_map/ppermute | solution.py:17
  84.5 87.7 %all-to-all-start = ((bf16[128,2,4096]{2,0,1:T(8,128)(2,1)}), bf16[128,2,4096]{2,0,1:T(8,128)(2,1)}, u32[]{:S(2)}, u32[]{:S(2)}) async-start(bf16[128,2,4096]{2,0,1:T(8,128)(2,1)} %bitcast.41), calls=%async_computation | async-start | bytes 4194304 | tf_op jit(solution)/shard_map/all_to_all | solution.py:102
  120.9 184.4 %collective-permute-start.6 = (bf16[256,4096]{1,0:T(8,128)(2,1)}, bf16[256,4096]{1,0:T(8,128)(2,1)}, u32[]{:S(2)}, u32[]{:S(2)}) collective-permute-start(bf16[256,4096]{1,0:T(8,128)(2,1)} %bitcast.8.refs_11_.refs_1_), channel_id=1, source_target_pairs={{0,4},{2,6},{4,8},{6,10},{8,12},{10,14},{12,16},{14,18},{16,20},{1... | collective-permute-start | bytes 6291464 | tf_op jit(solution)/shard_map/ppermute | solution.py:17
  170.3 178.1 %collective-permute-start.7 = (bf16[256,4096]{1,0:T(8,128)(2,1)}, bf16[256,4096]{1,0:T(8,128)(2,1)}, u32[]{:S(2)}, u32[]{:S(2)}) collective-permute-start(bf16[256,4096]{1,0:T(8,128)(2,1)} %bitcast.8.refs_11_.refs_1_), channel_id=1, source_target_pairs={{0,2},{2,4},{4,6},{6,8},{8,10},{10,12},{12,14},{14,16},{16,18},{18... | collective-permute-start | bytes 6291464 | tf_op jit(solution)/shard_map/ppermute | solution.py:17
  211.7 138.6 %collective-permute-start.8 = (bf16[256,4096]{1,0:T(8,128)(2,1)}, bf16[256,4096]{1,0:T(8,128)(2,1)}, u32[]{:S(2)}, u32[]{:S(2)}) collective-permute-start(bf16[256,4096]{1,0:T(8,128)(2,1)} %bitcast.1.refs_0_.refs_2_), channel_id=1, source_target_pairs={{2,0},{4,2},{6,4},{8,6},{10,8},{12,10},{14,12},{16,14},{18,16},{20... | collective-permute-start | bytes 6291464 | tf_op jit(solution)/shard_map/ppermute | solution.py:17
  213.6 138.6 %collective-permute-start.9 = (bf16[256,4096]{1,0:T(8,128)(2,1)}, bf16[256,4096]{1,0:T(8,128)(2,1)}, u32[]{:S(2)}, u32[]{:S(2)}) collective-permute-start(bf16[256,4096]{1,0:T(8,128)(2,1)} %bitcast.1.refs_0_.refs_2_), channel_id=1, source_target_pairs={{4,0},{6,2},{8,4},{10,6},{12,8},{14,10},{16,12},{18,14},{20,16},{2... | collective-permute-start | bytes 6291464 | tf_op jit(solution)/shard_map/ppermute | solution.py:17
  217.6 183.3 %collective-permute-start.10 = (bf16[256,4096]{1,0:T(8,128)(2,1)}, bf16[256,4096]{1,0:T(8,128)(2,1)}, u32[]{:S(2)}, u32[]{:S(2)}) collective-permute-start(bf16[256,4096]{1,0:T(8,128)(2,1)} %bitcast.1.refs_0_.refs_2_), channel_id=1, source_target_pairs={{6,0},{8,2},{10,4},{12,6},{14,8},{16,10},{18,12},{20,14},{22,16},{... | collective-permute-start | bytes 6291464 | tf_op jit(solution)/shard_map/ppermute | solution.py:17
  265.1 42.5 %all-to-all-start.1 = ((bf16[128,2,4096]{2,0,1:T(8,128)(2,1)}), bf16[128,2,4096]{2,0,1:T(8,128)(2,1)S(1)}, u32[]{:S(2)}, u32[]{:S(2)}) async-start(bf16[128,2,4096]{2,0,1:T(8,128)(2,1)} %bitcast.40), calls=%async_computation.1 | async-start | bytes 4194304 | tf_op jit(solution)/shard_map/all_to_all | solution.py:105
  305.2 152.6 %collective-permute-start.11 = (bf16[256,4096]{1,0:T(8,128)(2,1)}, bf16[256,4096]{1,0:T(8,128)(2,1)}, u32[]{:S(2)}, u32[]{:S(2)}) collective-permute-start(bf16[256,4096]{1,0:T(8,128)(2,1)} %bitcast.1.refs_0_.refs_2_), channel_id=1, source_target_pairs={{8,0},{10,2},{12,4},{14,6},{16,8},{18,10},{20,12},{22,14},{24,16},... | collective-permute-start | bytes 6291464 | tf_op jit(solution)/shard_map/ppermute | solution.py:17
  307.6 97.7 %copy-start.1 = (bf16[128,2,4096]{2,0,1:T(8,128)(2,1)}, bf16[128,2,4096]{2,0,1:T(8,128)(2,1)S(1)}, u32[]{:S(2)}) copy-start(bf16[128,2,4096]{2,0,1:T(8,128)(2,1)S(1)} %all-to-all-done.1) | copy-start | bytes 6291460
  348.4 111.4 %collective-permute-start.12 = (bf16[256,4096]{1,0:T(8,128)(2,1)S(1)}, bf16[256,4096]{1,0:T(8,128)(2,1)}, u32[]{:S(2)}, u32[]{:S(2)}) collective-permute-start(bf16[256,4096]{1,0:T(8,128)(2,1)S(1)} %bitcast.34), channel_id=1, source_target_pairs={{2,0},{4,2},{6,4},{8,6},{10,8},{12,10},{14,12},{16,14},{18,16},{20... | collective-permute-start | bytes 6291464 | tf_op jit(solution)/shard_map/ppermute | solution.py:17
  350.3 111.4 %collective-permute-start.13 = (bf16[256,4096]{1,0:T(8,128)(2,1)S(1)}, bf16[256,4096]{1,0:T(8,128)(2,1)}, u32[]{:S(2)}, u32[]{:S(2)}) collective-permute-start(bf16[256,4096]{1,0:T(8,128)(2,1)S(1)} %bitcast.35), channel_id=1, source_target_pairs={{4,0},{6,2},{8,4},{10,6},{12,8},{14,10},{16,12},{18,14},{20,16},{2... | collective-permute-start | bytes 6291464 | tf_op jit(solution)/shard_map/ppermute | solution.py:17
  352.3 136.4 %collective-permute-start.14 = (bf16[256,4096]{1,0:T(8,128)(2,1)S(1)}, bf16[256,4096]{1,0:T(8,128)(2,1)}, u32[]{:S(2)}, u32[]{:S(2)}) collective-permute-start(bf16[256,4096]{1,0:T(8,128)(2,1)S(1)} %bitcast.36), channel_id=1, source_target_pairs={{6,0},{8,2},{10,4},{12,6},{14,8},{16,10},{18,12},{20,14},{22,16},{... | collective-permute-start | bytes 6291464 | tf_op jit(solution)/shard_map/ppermute | solution.py:17
  400.9 132.8 %collective-permute-start.15 = (bf16[256,4096]{1,0:T(8,128)(2,1)S(1)}, bf16[256,4096]{1,0:T(8,128)(2,1)}, u32[]{:S(2)}, u32[]{:S(2)}) collective-permute-start(bf16[256,4096]{1,0:T(8,128)(2,1)S(1)} %bitcast.37), channel_id=1, source_target_pairs={{8,0},{10,2},{12,4},{14,6},{16,8},{18,10},{20,12},{22,14},{24,16},... | collective-permute-start | bytes 6291464 | tf_op jit(solution)/shard_map/ppermute | solution.py:17
  457.9 75.9 %collective-permute-start.16 = (f32[32,2,256]{2,1,0:T(2,128)}, f32[32,2,256]{2,1,0:T(2,128)S(1)}, u32[]{:S(2)}, u32[]{:S(2)}) collective-permute-start(f32[32,2,256]{2,1,0:T(2,128)} %get-tuple-element.8.refs_12_), channel_id=1, source_target_pairs={{2,0},{4,2},{6,4},{8,6},{10,8},{12,10},{14,12},{16,14},{18,16},{20... | collective-permute-start | bytes 196616 | tf_op jit(solution)/shard_map/ppermute | solution.py:17
  459.8 74.0 %collective-permute-start.17 = (f32[32,2,256]{2,1,0:T(2,128)}, f32[32,2,256]{2,1,0:T(2,128)S(1)}, u32[]{:S(2)}, u32[]{:S(2)}) collective-permute-start(f32[32,2,256]{2,1,0:T(2,128)} %get-tuple-element.8.refs_12_), channel_id=1, source_target_pairs={{4,0},{6,2},{8,4},{10,6},{12,8},{14,10},{16,12},{18,14},{20,16},{2... | collective-permute-start | bytes 196616 | tf_op jit(solution)/shard_map/ppermute | solution.py:17
  461.8 72.1 %collective-permute-start.18 = (f32[32,2,256]{2,1,0:T(2,128)}, f32[32,2,256]{2,1,0:T(2,128)S(1)}, u32[]{:S(2)}, u32[]{:S(2)}) collective-permute-start(f32[32,2,256]{2,1,0:T(2,128)} %get-tuple-element.8.refs_12_), channel_id=1, source_target_pairs={{6,0},{8,2},{10,4},{12,6},{14,8},{16,10},{18,12},{20,14},{22,16},{... | collective-permute-start | bytes 196616 | tf_op jit(solution)/shard_map/ppermute | solution.py:17
  488.7 47.8 %collective-permute-start.19 = (f32[32,2,256]{2,1,0:T(2,128)}, f32[32,2,256]{2,1,0:T(2,128)S(1)}, u32[]{:S(2)}, u32[]{:S(2)}) collective-permute-start(f32[32,2,256]{2,1,0:T(2,128)} %get-tuple-element.8.refs_12_), channel_id=1, source_target_pairs={{8,0},{10,2},{12,4},{14,6},{16,8},{18,10},{20,12},{22,14},{24,16},... | collective-permute-start | bytes 196616 | tf_op jit(solution)/shard_map/ppermute | solution.py:17
  (7 other events, 61.2 us)

commit v2 on v1

v2 whole, which is shorter than its diff:
```python
import jax
import jax.numpy as jnp
import numpy as np
from jax import lax
from jax.experimental import pallas as pl
from jax.experimental.pallas import tpu as pltpu
from jax.sharding import Mesh
from jax.sharding import PartitionSpec as P

HEAD_DIM = 128
MAX_DOC = 1024
PLANE_TOKENS = 1024
TILE = 256

masked_value = -1e30


def shifted(value, axis, steps):
    count = lax.axis_size(axis)
    leading, last = (max(0, -steps), min(count, count - steps))
    return lax.ppermute(value, axis, [(source, source + steps) for source in range(leading, last)])


def _row(col, tok):
    return jnp.transpose(jnp.broadcast_to(col, (tok, 128)))[0:1, :]


def _query_side_kernel(nblk, scale):
    def kernel(*refs):
        q_ref, d_ref = refs[0], refs[1]
        k_refs = refs[2:2 + nblk]
        v_refs = refs[2 + nblk:2 + 2 * nblk]
        bias_ref = refs[2 + 2 * nblk]
        dq_ref, ld_ref = refs[3 + 2 * nblk], refs[4 + 2 * nblk]
        q = q_ref[...]
        d = d_ref[...]
        logits = []
        for j in range(nblk):
            raw = lax.dot_general(q, k_refs[j][...], (((1,), (1,)), ((), ())),
                                  preferred_element_type=jnp.float32)
            logits.append(raw * scale + bias_ref[:, j * TILE:(j + 1) * TILE])
        top = logits[0].max(axis=1, keepdims=True)
        for j in range(1, nblk):
            top = jnp.maximum(top, logits[j].max(axis=1, keepdims=True))
        denom = jnp.exp(logits[0] - top).sum(axis=1, keepdims=True)
        for j in range(1, nblk):
            denom = denom + jnp.exp(logits[j] - top).sum(axis=1, keepdims=True)
        lse = top + jnp.log(denom)
        probs = [jnp.exp(item - lse) for item in logits]
        out = None
        for j in range(nblk):
            part = jnp.dot(probs[j].astype(jnp.bfloat16), v_refs[j][...],
                           preferred_element_type=jnp.float32)
            out = part if out is None else out + part
        delta = (d.astype(jnp.float32) * out).sum(axis=1, keepdims=True)
        dq = None
        for j in range(nblk):
            dprobs = lax.dot_general(d, v_refs[j][...], (((1,), (1,)), ((), ())),
                                     preferred_element_type=jnp.float32)
            dscores = (probs[j] * (dprobs - delta)).astype(jnp.bfloat16)
            part = jnp.dot(dscores, k_refs[j][...], preferred_element_type=jnp.float32)
            dq = part if dq is None else dq + part
        dq_ref[...] = (dq * scale).astype(dq_ref.dtype)
        ld_ref[0:1, :] = _row(lse, TILE)
        ld_ref[1:2, :] = _row(delta, TILE)

    return kernel


def _key_side_kernel(nblk, scale):
    def kernel(*refs):
        k_ref, v_ref = refs[0], refs[1]
        q_refs = refs[2:2 + nblk]
        d_refs = refs[2 + nblk:2 + 2 * nblk]
        ld_refs = refs[2 + 2 * nblk:2 + 3 * nblk]
        bias_ref = refs[2 + 3 * nblk]
        dk_ref, dv_ref = refs[3 + 3 * nblk], refs[4 + 3 * nblk]
        k = k_ref[...]
        v = v_ref[...]
        dk = None
        dv = None
        for j in range(nblk):
            q = q_refs[j][...]
            d = d_refs[j][...]
            lse = ld_refs[j][0:1, :]
            delta = ld_refs[j][1:2, :]
            raw = lax.dot_general(k, q, (((1,), (1,)), ((), ())),
                                  preferred_element_type=jnp.float32)
            logit = raw * scale + bias_ref[:, j * TILE:(j + 1) * TILE]
            prob = jnp.exp(logit - lse)
            dprobs = lax.dot_general(v, d, (((1,), (1,)), ((), ())),
                                     preferred_element_type=jnp.float32)
            dscores = (prob * (dprobs - delta)).astype(jnp.bfloat16)
            part_k = jnp.dot(dscores, q, preferred_element_type=jnp.float32)
            part_v = jnp.dot(prob.astype(jnp.bfloat16), d, preferred_element_type=jnp.float32)
            dk = part_k if dk is None else dk + part_k
            dv = part_v if dv is None else dv + part_v
        dk_ref[...] = (dk * scale).astype(dk_ref.dtype)
        dv_ref[...] = dv.astype(dv_ref.dtype)

    return kernel


def _plan(tok_in, ctx_n, head_n):
    clo_n = 1
    while (clo_n * 2 <= ctx_n and ctx_n % (clo_n * 2) == 0
           and tok_in * clo_n * head_n < PLANE_TOKENS):
        clo_n *= 2
    return clo_n


def _per_device(clo_n, attn_q, attn_k, attn_v, attn_dout, doc_ids):
    tok_in, full_width = attn_q.shape
    head_n = lax.axis_size("head")
    chi_n = lax.axis_size("chi")
    group = clo_n * head_n
    width = full_width // group
    heads_p = width // HEAD_DIM
    plane = tok_in * group
    n_tok = doc_ids.shape[0]
    scale = HEAD_DIM ** (-0.5)
    reach = min(-(-(MAX_DOC - 1) // plane), chi_n - 1)
    tile_reach = -(-(MAX_DOC - 1) // TILE)
    nblk = tile_reach + 1
    n_tiles = plane // TILE
    chi = lax.axis_index("chi")
    plane_start = chi * plane

    def to_plane(x):
        x = x.reshape(tok_in, head_n, clo_n, width).transpose(0, 2, 1, 3).reshape(tok_in, full_width)
        return lax.all_to_all(x, ("clo", "head"), split_axis=1, concat_axis=0, tiled=True)

    keys = to_plane(attn_k)
    values = to_plane(attn_v)
    query = to_plane(attn_q)
    dout = to_plane(attn_dout)

    k_parts, v_parts = [], []
    for shift in range(reach, 0, -1):
        far_k, far_v = shifted((keys, values), "chi", shift)
        k_parts.append(far_k)
        v_parts.append(far_v)
    k_win = jnp.concatenate(k_parts + [keys], axis=0)
    v_win = jnp.concatenate(v_parts + [values], axis=0)

    q_parts, d_parts = [], []
    for shift in range(1, reach + 1):
        far_q, far_d = shifted((query, dout), "chi", -shift)
        q_parts.append(far_q)
        d_parts.append(far_d)
    q_win = jnp.concatenate([query] + q_parts, axis=0)
    d_win = jnp.concatenate([dout] + d_parts, axis=0)

    pad = (reach + 1) * plane
    docs_pad = jnp.concatenate([
        jnp.full((pad,), -1, jnp.int32), doc_ids.astype(jnp.int32), jnp.full((pad,), -1, jnp.int32)])
    span = nblk * TILE
    cols = jnp.arange(span, dtype=jnp.int32)
    rows = jnp.arange(TILE, dtype=jnp.int32)
    q_bias, k_bias = [], []
    for i in range(n_tiles):
        t_start = plane_start + i * TILE
        own_doc = lax.dynamic_slice_in_dim(docs_pad, t_start + pad, TILE)
        own_pos = t_start + rows
        k_start = t_start - tile_reach * TILE
        k_doc = lax.dynamic_slice_in_dim(docs_pad, k_start + pad, span)
        k_pos = k_start + cols
        mask = (k_pos[None, :] <= own_pos[:, None]) & (k_doc[None, :] == own_doc[:, None])
        q_bias.append(jnp.where(mask, 0.0, masked_value).astype(jnp.float32))
        q_doc = lax.dynamic_slice_in_dim(docs_pad, t_start + pad, span)
        q_pos = t_start + cols
        mask = (own_pos[:, None] <= q_pos[None, :]) & (own_doc[:, None] == q_doc[None, :])
        k_bias.append(jnp.where(mask, 0.0, masked_value).astype(jnp.float32))
    q_bias = jnp.concatenate(q_bias, axis=0)
    k_bias = jnp.concatenate(k_bias, axis=0)

    own_spec = pl.BlockSpec((TILE, HEAD_DIM), lambda i, h: (i, h))
    base = reach * n_tiles - tile_reach

    def kwin_spec(j):
        return pl.BlockSpec((TILE, HEAD_DIM), lambda i, h: (base + i + j, h))

    def qwin_spec(j):
        return pl.BlockSpec((TILE, HEAD_DIM), lambda i, h: (i + j, h))

    def ldwin_spec(j):
        return pl.BlockSpec((None, 2, TILE), lambda i, h: (h, 0, i + j))

    bias_spec = pl.BlockSpec((TILE, span), lambda i, h: (i, 0))
    ld_spec = pl.BlockSpec((None, 2, TILE), lambda i, h: (h, 0, i))
    params = pltpu.CompilerParams(dimension_semantics=("arbitrary", "arbitrary"))
    grid = (n_tiles, heads_p)

    dq, ld = pl.pallas_call(
        _query_side_kernel(nblk, scale),
        out_shape=(
            jax.ShapeDtypeStruct((plane, width), jnp.bfloat16),
            jax.ShapeDtypeStruct((heads_p, 2, plane), jnp.float32),
        ),
        grid=grid,
        in_specs=[own_spec, own_spec] + [kwin_spec(j) for j in range(nblk)] * 2 + [bias_spec],
        out_specs=(own_spec, ld_spec),
        compiler_params=params,
        name="attn_query_side",
    )(query, dout, *([k_win] * nblk), *([v_win] * nblk), q_bias)

    ld_parts = [ld]
    for shift in range(1, reach + 1):
        ld_parts.append(shifted(ld, "chi", -shift))
    ld_win = jnp.concatenate(ld_parts, axis=2)

    dk, dv = pl.pallas_call(
        _key_side_kernel(nblk, scale),
        out_shape=(
            jax.ShapeDtypeStruct((plane, width), jnp.bfloat16),
            jax.ShapeDtypeStruct((plane, width), jnp.bfloat16),
        ),
        grid=grid,
        in_specs=[own_spec, own_spec] + [qwin_spec(j) for j in range(nblk)] * 2
        + [ldwin_spec(j) for j in range(nblk)] + [bias_spec],
        out_specs=(own_spec, own_spec),
        compiler_params=params,
        name="attn_key_side",
    )(keys, values, *([q_win] * nblk), *([d_win] * nblk), *([ld_win] * nblk), k_bias)

    def from_plane(x):
        return lax.all_to_all(x, "clo", split_axis=0, concat_axis=1, tiled=True)

    return (from_plane(dq), from_plane(dk), from_plane(dv))


def solution(mesh):
    ctx_n, head_n = mesh.devices.shape
    def fn(attn_q, attn_k, attn_v, attn_dout, doc_ids):
        tok_in = attn_q.shape[0] // (ctx_n * head_n)
        clo_n = _plan(tok_in, ctx_n, head_n)
        chi_n = ctx_n // clo_n
        sub = Mesh(np.asarray(mesh.devices).reshape(chi_n, clo_n, head_n), ("chi", "clo", "head"))
        inner = jax.shard_map(
            lambda *a: _per_device(clo_n, *a),
            mesh=sub,
            in_specs=(
                P(("chi", "clo", "head"), None),
                P(("chi", "clo", "head"), None),
                P(("chi", "clo", "head"), None),
                P(("chi", "clo", "head"), None),
                P(),
            ),
            out_specs=(P(("chi", "clo"), "head"), P(("chi", "clo"), "head"), P(("chi", "clo"), "head")),
            check_vma=False,
        )
        return inner(attn_q, attn_k, attn_v, attn_dout, doc_ids)
    return fn
```

time: 584 us -> 387 us (0.66)
  waiting for transfers between devices: 329 us -> 140 us
  starting transfers between devices: 113 us -> 40.9 us
  other arithmetic: 4.08 us -> 33.4 us
  local copies, waits for them, and re-layouts: 10.1 us -> 38.6 us
    ppermute x20 -> x5, waiting for transfers between devices: 314 us -> 58.5 us  [shifted(): lax.ppermute(value, axis, [(source, source + steps) for source in range(l...]
    ppermute x20 -> x5, starting transfers between devices: 94.7 us -> 14.2 us  [shifted(): lax.ppermute(value, axis, [(source, source + steps) for source in range(l...]
    all_to_all x3 -> x6, waiting for transfers between devices: 15 us -> 81.8 us  [the longest x4 59.9 us: to_plane(): lax.all_to_all(x, ('clo', 'head'), split_axis=1, concat_axis=0, tiled=True)]
    concatenate x2 -> x8, other arithmetic: 0.43 us -> 27.3 us  [the longest x1 4.76 us: _per_device(): d_win = jnp.concatenate([dout] + d_parts, axis=0)]
    reshape x0 -> x4, local copies, waits for them, and re-layouts: none -> 16.8 us  [to_plane(): x.reshape(tok_in, head_n, clo_n, width).transpose(0, 2, 1, 3)]
    transpose x0 -> x4, local copies, waits for them, and re-layouts: none -> 14.7 us  [to_plane(): x.reshape(tok_in, head_n, clo_n, width).transpose(0, 2, 1, 3)]
    all_to_all x3 -> x6, starting transfers between devices: 18.7 us -> 26.7 us  [the longest x4 18.6 us: to_plane(): lax.all_to_all(x, ('clo', 'head'), split_axis=1, concat_axis=0, tiled=True)]
  transfers between devices with their start and end apart: 23 -> 11, of which waited for: 11 -> 7; matrix products, arithmetic and copies ran while one was open for 2% -> 16% of each run, Pallas kernels for 9% -> 26%
where the time goes in v2:
time: 387 us; the launch traced here: 385 us
  waiting for transfers between devices  140 us (36%)
  Pallas kernels  101 us (26%)
  starting transfers between devices  40.9 us (11%)
  local copies, waits for them, and re-layouts  38.6 us (10%)
  other arithmetic  33.4 us (9%)
  blocking collectives  30.2 us (8%)
    all_to_all x4, waiting for transfers between devices, to_plane(): lax.all_to_all(x, ('clo', 'head'), split_axis=1, concat_axis=0, tiled=True)  59.9 us
    ppermute x5, waiting for transfers between devices, shifted(): lax.ppermute(value, axis, [(source, source + steps) for source in range(l...  58.5 us
    pallas_call x1, Pallas kernels, _per_device(): pl.pallas_call(_query_side_kernel(nblk, scale), out_shape=(jax.ShapeDtype...  54.8 us
    pallas_call x1, Pallas kernels, _per_device(): pl.pallas_call(_key_side_kernel(nblk, scale), out_shape=(jax.ShapeDtypeSt...  46.3 us
    all_to_all x1, blocking collectives, from_plane(): return lax.all_to_all(x, 'clo', split_axis=0, concat_axis=1, tiled=True)  30.2 us
    all_to_all x2, waiting for transfers between devices, from_plane(): return lax.all_to_all(x, 'clo', split_axis=0, concat_axis=1, tiled=True)  21.9 us
    all_to_all x4, starting transfers between devices, to_plane(): lax.all_to_all(x, ('clo', 'head'), split_axis=1, concat_axis=0, tiled=True)  18.6 us
    reshape x4, local copies, waits for them, and re-layouts, to_plane(): x.reshape(tok_in, head_n, clo_n, width).transpose(0, 2, 1, 3)  16.8 us
  transfers between devices with their start and end apart: 11, of which 7 were waited for; matrix products, arithmetic and copies ran while one was open for 16% of the time, Pallas kernels for 26%

profile of v2, /device:TPU:20, one launch (start us, length us, event | category | flops | bytes accessed | tf_op | source)
XLA Modules:
  0.0 385.3 jit_solution(9412059792130570776)
XLA Ops:
  6.4 4.2 %all-to-all-start.2 = ((bf16[128,8,1024]{2,0,1:T(8,128)(2,1)}), bf16[128,8,1024]{2,0,1:T(8,128)(2,1)S(1)}, u32[]{:S(2)}, u32[]{:S(2)}) async-start(bf16[128,8,1024]{2,0,1:T(8,128)(2,1)} %bitcast.40), calls=%async_computation.2 | async-start | bytes 4194304 | tf_op jit(solution)/shard_map/all_to_all | solution.py:131
  10.7 4.5 %reshape.110 = bf16[128,2,4,1024]{3,2,1,0:T(4,128)(2,1)} reshape(bf16[128,8192]{1,0:T(8,128)(2,1)} %param.7) | data formatting | bytes 4194304 | tf_op jit(solution)/shard_map/reshape | solution.py:130
  19.2 16.7 %all-to-all-done.2 = bf16[128,8,1024]{2,0,1:T(8,128)(2,1)S(1)} async-done(((bf16[128,8,1024]{2,0,1:T(8,128)(2,1)}), bf16[128,8,1024]{2,0,1:T(8,128)(2,1)S(1)}, u32[]{:S(2)}, u32[]{:S(2)}) %all-to-all-start.2) | async-done | bytes 2097184 | tf_op jit(solution)/shard_map/all_to_all | solution.py:131
  35.9 4.8 %all-to-all-start.3 = ((bf16[128,8,1024]{2,0,1:T(8,128)(2,1)}), bf16[128,8,1024]{2,0,1:T(8,128)(2,1)}, u32[]{:S(2)}, u32[]{:S(2)}) async-start(bf16[128,8,1024]{2,0,1:T(8,128)(2,1)} %bitcast.38), calls=%async_computation.3 | async-start | bytes 4194304 | tf_op jit(solution)/shard_map/all_to_all | solution.py:131
  40.7 4.5 %reshape.107 = bf16[128,2,4,1024]{3,2,1,0:T(4,128)(2,1)} reshape(bf16[128,8192]{1,0:T(8,128)(2,1)} %param.5) | data formatting | bytes 4194304 | tf_op jit(solution)/shard_map/reshape | solution.py:130
  49.2 16.8 %all-to-all-done.3 = bf16[128,8,1024]{2,0,1:T(8,128)(2,1)} async-done(((bf16[128,8,1024]{2,0,1:T(8,128)(2,1)}), bf16[128,8,1024]{2,0,1:T(8,128)(2,1)}, u32[]{:S(2)}, u32[]{:S(2)}) %all-to-all-start.3) | async-done | bytes 2097184 | tf_op jit(solution)/shard_map/all_to_all | solution.py:131
  66.0 4.8 %all-to-all-start = ((bf16[128,8,1024]{2,0,1:T(8,128)(2,1)}), bf16[128,8,1024]{2,0,1:T(8,128)(2,1)}, u32[]{:S(2)}, u32[]{:S(2)}) async-start(bf16[128,8,1024]{2,0,1:T(8,128)(2,1)} %bitcast.36), calls=%async_computation | async-start | bytes 4194304 | tf_op jit(solution)/shard_map/all_to_all | solution.py:131
  70.8 4.5 %reshape.108 = bf16[128,2,4,1024]{3,2,1,0:T(4,128)(2,1)} reshape(bf16[128,8192]{1,0:T(8,128)(2,1)} %param.8) | data formatting | bytes 4194304 | tf_op jit(solution)/shard_map/reshape | solution.py:130
  75.3 4.1 %copy.9 = bf16[128,4,2,1024]{3,0,2,1:T(8,128)(2,1)} copy(bf16[128,4,2,1024]{3,1,2,0:T(4,128)(2,1)} %bitcast.44) | data formatting | bytes 4194304 | tf_op jit(solution)/shard_map/transpose | solution.py:130
  79.6 16.6 %all-to-all-done = bf16[128,8,1024]{2,0,1:T(8,128)(2,1)} async-done(((bf16[128,8,1024]{2,0,1:T(8,128)(2,1)}), bf16[128,8,1024]{2,0,1:T(8,128)(2,1)}, u32[]{:S(2)}, u32[]{:S(2)}) %all-to-all-start) | async-done | bytes 2097184 | tf_op jit(solution)/shard_map/all_to_all | solution.py:131
  96.2 4.8 %all-to-all-start.1 = ((bf16[128,8,1024]{2,0,1:T(8,128)(2,1)}), bf16[128,8,1024]{2,0,1:T(8,128)(2,1)}, u32[]{:S(2)}, u32[]{:S(2)}) async-start(bf16[128,8,1024]{2,0,1:T(8,128)(2,1)} %bitcast.35), calls=%async_computation.1 | async-start | bytes 4194304 | tf_op jit(solution)/shard_map/all_to_all | solution.py:131
  116.6 9.8 %all-to-all-done.1 = bf16[128,8,1024]{2,0,1:T(8,128)(2,1)} async-done(((bf16[128,8,1024]{2,0,1:T(8,128)(2,1)}), bf16[128,8,1024]{2,0,1:T(8,128)(2,1)}, u32[]{:S(2)}, u32[]{:S(2)}) %all-to-all-start.1) | async-done | bytes 2097184 | tf_op jit(solution)/shard_map/all_to_all | solution.py:131
  128.9 4.2 %pad_maximum_fusion.refs_12_ = f32[1024,1280]{1,0:T(8,128)} fusion(f32[256,1280]{1,0:T(8,128)} %get-tuple-element.30, f32[256,1280]{1,0:T(8,128)} %get-tuple-element.31, f32[256,1280]{1,0:T(8,128)} %get-tuple-element.26, f32[256,1280]{1,0:T(8,128)} %get-tuple-element.33), kind=kLoop, calls=%fused_computation | loop fusion | flops 3932160 | bytes 10485760 | tf_op jit(solution)/shard_map/concatenate | solution.py:174
  133.1 18.4 %collective-permute-done = bf16[1024,1024]{1,0:T(8,128)(2,1)} collective-permute-done((bf16[1024,1024]{1,0:T(8,128)(2,1)S(1)}, bf16[1024,1024]{1,0:T(8,128)(2,1)}, u32[]{:S(2)}, u32[]{:S(2)}) %collective-permute-start) | collective-permute-done | bytes 2097184 | tf_op jit(solution)/shard_map/ppermute | solution.py:21
  151.5 4.1 %pad_maximum_fusion.2.refs_2_.refs_3_.refs_4_.refs_5_.refs_6_ = bf16[2048,1024]{1,0:T(8,128)(2,1)} fusion(bf16[1024,1024]{1,0:T(8,128)(2,1)S(1)} %bitcast.33, bf16[1024,1024]{1,0:T(8,128)(2,1)} %collective-permute-done), kind=kLoop, calls=%fused_computation.2 | loop fusion | flops 8388608 | bytes 8388608 | tf_op jit(solution)/shard_map/concatenate | solution.py:143
  155.6 40.1 %collective-permute-done.1 = bf16[1024,1024]{1,0:T(8,128)(2,1)} collective-permute-done((bf16[1024,1024]{1,0:T(8,128)(2,1)}, bf16[1024,1024]{1,0:T(8,128)(2,1)}, u32[]{:S(2)}, u32[]{:S(2)}) %collective-permute-start.1) | collective-permute-done | bytes 2097184 | tf_op jit(solution)/shard_map/ppermute | solution.py:21
  195.6 4.8 %pad_maximum_fusion.3.refs_7_.refs_8_.refs_9_.refs_10_.refs_11_ = bf16[2048,1024]{1,0:T(8,128)(2,1)} fusion(bf16[1024,1024]{1,0:T(8,128)(2,1)} %bitcast.15.refs_1_, bf16[1024,1024]{1,0:T(8,128)(2,1)} %collective-permute-done.1), kind=kLoop, calls=%fused_computation.3 | loop fusion | flops 8388608 | bytes 8388608 | tf_op jit(solution)/shard_map/concatenate | solution.py:144
  200.4 54.8 %attn_query_side.1 = (bf16[1024,1024]{1,0:T(8,128)(2,1)}, f32[8,2,1024]{2,1,0:T(2,128)}) custom-call(bf16[1024,1024]{1,0:T(8,128)(2,1)} %bitcast.3.refs_0_, bf16[1024,1024]{1,0:T(8,128)(2,1)} %bitcast.7.refs_1_, bf16[2048,1024]{1,0:T(8,128)(2,1)} %pad_maximum_fusion.2.refs_2_.refs_3_.refs_4_.refs_5_.refs_6_, ...), custom_call_target="tpu_custom_call" | custom-call | tf_op jit(solution)/shard_map/attn_query_side/pallas_call | solution.py:194
  265.2 4.7 %pad_maximum_fusion.4.refs_2_.refs_3_.refs_4_.refs_5_.refs_6_ = bf16[2048,1024]{1,0:T(8,128)(2,1)} fusion(bf16[1024,1024]{1,0:T(8,128)(2,1)} %collective-permute-done.2, bf16[1024,1024]{1,0:T(8,128)(2,1)} %bitcast.3.refs_0_), kind=kLoop, calls=%fused_computation.4 | loop fusion | flops 8388608 | bytes 8388608 | tf_op jit(solution)/shard_map/concatenate | solution.py:151
  269.9 4.8 %pad_maximum_fusion.5.refs_7_.refs_8_.refs_9_.refs_10_.refs_11_ = bf16[2048,1024]{1,0:T(8,128)(2,1)} fusion(bf16[1024,1024]{1,0:T(8,128)(2,1)} %collective-permute-done.3, bf16[1024,1024]{1,0:T(8,128)(2,1)} %bitcast.7.refs_1_), kind=kLoop, calls=%fused_computation.5 | loop fusion | flops 8388608 | bytes 8388608 | tf_op jit(solution)/shard_map/concatenate | solution.py:152
  275.4 46.3 %attn_key_side.1 = (bf16[1024,1024]{1,0:T(8,128)(2,1)}, bf16[1024,1024]{1,0:T(8,128)(2,1)}) custom-call(bf16[1024,1024]{1,0:T(8,128)(2,1)} %bitcast.34, bf16[1024,1024]{1,0:T(8,128)(2,1)} %bitcast.15.refs_1_, bf16[2048,1024]{1,0:T(8,128)(2,1)} %pad_maximum_fusion.4.refs_2_.refs_3_.refs_4_.refs_5_.refs_6_, ...), custom_call_target="tpu_custom_call" | custom-call | tf_op jit(solution)/shard_map/attn_key_side/pallas_call | solution.py:212
  321.7 30.2 %all_to_all.133 = bf16[4,256,1024]{2,1,0:T(8,128)(2,1)} all-to-all(bf16[4,256,1024]{2,1,0:T(8,128)(2,1)} %bitcast.49), channel_id=1, replica_groups=mesh['chi'=4,'clo'=4,'head'=2] {'clo'}, dimensions={0} | all-to-all | bytes 4194304 | tf_op jit(solution)/shard_map/all_to_all | solution.py:227
  351.9 4.5 %all-to-all-start.6 = ((bf16[4,256,1024]{2,1,0:T(8,128)(2,1)}), bf16[4,256,1024]{2,1,0:T(8,128)(2,1)}, u32[]{:S(2)}, u32[]{:S(2)}) async-start(bf16[4,256,1024]{2,1,0:T(8,128)(2,1)} %bitcast.46), calls=%async_computation.6 | async-start | bytes 4194304 | tf_op jit(solution)/shard_map/all_to_all | solution.py:227
  360.2 21.9 %all-to-all-done.6 = bf16[4,256,1024]{2,1,0:T(8,128)(2,1)} async-done(((bf16[4,256,1024]{2,1,0:T(8,128)(2,1)}), bf16[4,256,1024]{2,1,0:T(8,128)(2,1)}, u32[]{:S(2)}, u32[]{:S(2)}) %all-to-all-start.6) | async-done | bytes 2097184 | tf_op jit(solution)/shard_map/all_to_all | solution.py:227
  (45 shorter events, 49.9 us)
Async XLA Ops:
  6.4 29.5 %all-to-all-start.2 = ((bf16[128,8,1024]{2,0,1:T(8,128)(2,1)}), bf16[128,8,1024]{2,0,1:T(8,128)(2,1)S(1)}, u32[]{:S(2)}, u32[]{:S(2)}) async-start(bf16[128,8,1024]{2,0,1:T(8,128)(2,1)} %bitcast.40), calls=%async_computation.2 | async-start | bytes 4194304 | tf_op jit(solution)/shard_map/all_to_all | solution.py:131
  35.9 115.6 %copy-start = (bf16[128,8,1024]{2,0,1:T(8,128)(2,1)}, bf16[128,8,1024]{2,0,1:T(8,128)(2,1)S(1)}, u32[]{:S(2)}) copy-start(bf16[128,8,1024]{2,0,1:T(8,128)(2,1)S(1)} %all-to-all-done.2) | copy-start | bytes 6291460
  35.9 30.2 %all-to-all-start.3 = ((bf16[128,8,1024]{2,0,1:T(8,128)(2,1)}), bf16[128,8,1024]{2,0,1:T(8,128)(2,1)}, u32[]{:S(2)}, u32[]{:S(2)}) async-start(bf16[128,8,1024]{2,0,1:T(8,128)(2,1)} %bitcast.38), calls=%async_computation.3 | async-start | bytes 4194304 | tf_op jit(solution)/shard_map/all_to_all | solution.py:131
  66.0 30.2 %all-to-all-start = ((bf16[128,8,1024]{2,0,1:T(8,128)(2,1)}), bf16[128,8,1024]{2,0,1:T(8,128)(2,1)}, u32[]{:S(2)}, u32[]{:S(2)}) async-start(bf16[128,8,1024]{2,0,1:T(8,128)(2,1)} %bitcast.36), calls=%async_computation | async-start | bytes 4194304 | tf_op jit(solution)/shard_map/all_to_all | solution.py:131
  75.3 4.1 %copy-start.3 = (s32[4096]{0:T(1024)S(1)}, s32[4096]{0:T(1024)}, u32[]{:S(2)}) copy-start(s32[4096]{0:T(1024)} %param.9) | copy-start | bytes 49156
  96.2 30.2 %all-to-all-start.1 = ((bf16[128,8,1024]{2,0,1:T(8,128)(2,1)}), bf16[128,8,1024]{2,0,1:T(8,128)(2,1)}, u32[]{:S(2)}, u32[]{:S(2)}) async-start(bf16[128,8,1024]{2,0,1:T(8,128)(2,1)} %bitcast.35), calls=%async_computation.1 | async-start | bytes 4194304 | tf_op jit(solution)/shard_map/all_to_all | solution.py:131
  101.0 50.5 %collective-permute-start = (bf16[1024,1024]{1,0:T(8,128)(2,1)S(1)}, bf16[1024,1024]{1,0:T(8,128)(2,1)}, u32[]{:S(2)}, u32[]{:S(2)}) collective-permute-start(bf16[1024,1024]{1,0:T(8,128)(2,1)S(1)} %bitcast.32), channel_id=1, source_target_pairs={{0,8},{8,16},{16,24},{1,9},{9,17},{17,25},{2,10},{10,18},{18,26},{... | collective-permute-start | bytes 6291464 | tf_op jit(solution)/shard_map/ppermute | solution.py:21
  104.6 91.0 %collective-permute-start.1 = (bf16[1024,1024]{1,0:T(8,128)(2,1)}, bf16[1024,1024]{1,0:T(8,128)(2,1)}, u32[]{:S(2)}, u32[]{:S(2)}) collective-permute-start(bf16[1024,1024]{1,0:T(8,128)(2,1)} %bitcast.15.refs_1_), channel_id=1, source_target_pairs={{0,8},{8,16},{16,24},{1,9},{9,17},{17,25},{2,10},{10,18},{18,26},{... | collective-permute-start | bytes 6291464 | tf_op jit(solution)/shard_map/ppermute | solution.py:21
  109.4 155.8 %collective-permute-start.2 = (bf16[1024,1024]{1,0:T(8,128)(2,1)}, bf16[1024,1024]{1,0:T(8,128)(2,1)}, u32[]{:S(2)}, u32[]{:S(2)}) collective-permute-start(bf16[1024,1024]{1,0:T(8,128)(2,1)} %bitcast.3.refs_0_), channel_id=1, source_target_pairs={{8,0},{16,8},{24,16},{9,1},{17,9},{25,17},{10,2},{18,10},{26,18},{... | collective-permute-start | bytes 6291464 | tf_op jit(solution)/shard_map/ppermute | solution.py:21
  126.4 143.6 %collective-permute-start.3 = (bf16[1024,1024]{1,0:T(8,128)(2,1)}, bf16[1024,1024]{1,0:T(8,128)(2,1)}, u32[]{:S(2)}, u32[]{:S(2)}) collective-permute-start(bf16[1024,1024]{1,0:T(8,128)(2,1)} %bitcast.7.refs_1_), channel_id=1, source_target_pairs={{8,0},{16,8},{24,16},{9,1},{17,9},{25,17},{10,2},{18,10},{26,18},{... | collective-permute-start | bytes 6291464 | tf_op jit(solution)/shard_map/ppermute | solution.py:21
  255.2 66.5 %all-to-all-start.4 = ((bf16[4,256,1024]{2,1,0:T(8,128)(2,1)}), bf16[4,256,1024]{2,1,0:T(8,128)(2,1)S(1)}, u32[]{:S(2)}, u32[]{:S(2)}) async-start(bf16[4,256,1024]{2,1,0:T(8,128)(2,1)} %bitcast.45), calls=%async_computation.4 | async-start | bytes 4194304 | tf_op jit(solution)/shard_map/all_to_all | solution.py:227
  258.8 4.1 %copy-start.2 = (f32[8,2,1024]{2,1,0:T(2,128)S(1)}, f32[8,2,1024]{2,1,0:T(2,128)}, u32[]{:S(2)}) copy-start(f32[8,2,1024]{2,1,0:T(2,128)} %get-tuple-element.8) | copy-start | bytes 196612
  262.9 11.8 %collective-permute-start.4 = (f32[8,2,1024]{2,1,0:T(2,128)S(1)}, f32[8,2,1024]{2,1,0:T(2,128)S(1)}, u32[]{:S(2)}, u32[]{:S(2)}) collective-permute-start(f32[8,2,1024]{2,1,0:T(2,128)S(1)} %copy-done.2), channel_id=1, source_target_pairs={{8,0},{16,8},{24,16},{9,1},{17,9},{25,17},{10,2},{18,10},{26,18},{... | collective-permute-start | bytes 196616 | tf_op jit(solution)/shard_map/ppermute | solution.py:21
  351.9 30.2 %all-to-all-start.6 = ((bf16[4,256,1024]{2,1,0:T(8,128)(2,1)}), bf16[4,256,1024]{2,1,0:T(8,128)(2,1)}, u32[]{:S(2)}, u32[]{:S(2)}) async-start(bf16[4,256,1024]{2,1,0:T(8,128)(2,1)} %bitcast.46), calls=%async_computation.6 | async-start | bytes 4194304 | tf_op jit(solution)/shard_map/all_to_all | solution.py:227
  356.3 2.3 copy-start.1

commit v3 on v2

v3 whole, which is shorter than its diff:
```python
import jax
import jax.numpy as jnp
import numpy as np
from jax import lax
from jax.experimental import pallas as pl
from jax.experimental.pallas import tpu as pltpu
from jax.sharding import Mesh
from jax.sharding import PartitionSpec as P

HEAD_DIM = 128
MAX_DOC = 1024
PLANE_TOKENS = 1024
TILE = 256

masked_value = -1e30


def shifted(value, axis, steps):
    count = lax.axis_size(axis)
    leading, last = (max(0, -steps), min(count, count - steps))
    return lax.ppermute(value, axis, [(source, source + steps) for source in range(leading, last)])


def _row(col, tok):
    return jnp.transpose(jnp.broadcast_to(col, (tok, 128)))[0:1, :]


def _query_side_kernel(reach, n_tiles, tile_reach, scale):
    nblk = tile_reach + 1
    npl = reach + 1

    def kernel(flags_ref, *refs):
        q_ref, d_ref = refs[0], refs[1]
        k_refs = refs[2:2 + npl]
        v_refs = refs[2 + npl:2 + 2 * npl]
        bias_ref = refs[2 + 2 * npl]
        dq_ref, ld_ref = refs[3 + 2 * npl], refs[4 + 2 * npl]
        s_scr, m_scr, l_scr, o_scr = refs[5 + 2 * npl:]

        def block(i, j):
            b = reach * n_tiles + i - tile_reach + j
            rows = pl.ds((b % n_tiles) * TILE, TILE)
            return k_refs[b // n_tiles], v_refs[b // n_tiles], rows

        for i in range(n_tiles):
            own_rows = pl.ds(i * TILE, TILE)
            q = q_ref[own_rows, :]
            d = d_ref[own_rows, :]

            def on(j):
                return flags_ref[i * nblk + j] != 0

            def logit(j):
                k_ref, _, rows = block(i, j)
                raw = lax.dot_general(q, k_ref[rows, :], (((1,), (1,)), ((), ())),
                                      preferred_element_type=jnp.float32)
                return raw * scale + bias_ref[own_rows, j * TILE:(j + 1) * TILE]

            s = logit(tile_reach)
            s_scr[tile_reach] = s
            m_scr[...] = s.max(axis=1, keepdims=True)
            for j in range(tile_reach):
                @pl.when(on(j))
                def _():
                    s = logit(j)
                    s_scr[j] = s
                    m_scr[...] = jnp.maximum(m_scr[...], s.max(axis=1, keepdims=True))
            top = m_scr[...]
            l_scr[...] = jnp.exp(s_scr[tile_reach] - top).sum(axis=1, keepdims=True)
            for j in range(tile_reach):
                @pl.when(on(j))
                def _():
                    l_scr[...] += jnp.exp(s_scr[j] - top).sum(axis=1, keepdims=True)
            lse = top + jnp.log(l_scr[...])

            def prob_out(j, first):
                _, v_ref, rows = block(i, j)
                p = jnp.exp(s_scr[j] - lse)
                s_scr[j] = p
                part = jnp.dot(p.astype(jnp.bfloat16), v_ref[rows, :],
                               preferred_element_type=jnp.float32)
                if first:
                    o_scr[...] = part
                else:
                    o_scr[...] += part

            prob_out(tile_reach, True)
            for j in range(tile_reach):
                pl.when(on(j))(lambda j=j: prob_out(j, False))
            delta = (d.astype(jnp.float32) * o_scr[...]).sum(axis=1, keepdims=True)

            def grad(j, first):
                k_ref, v_ref, rows = block(i, j)
                dprobs = lax.dot_general(d, v_ref[rows, :], (((1,), (1,)), ((), ())),
                                         preferred_element_type=jnp.float32)
                dscores = (s_scr[j] * (dprobs - delta)).astype(jnp.bfloat16)
                part = jnp.dot(dscores, k_ref[rows, :], preferred_element_type=jnp.float32)
                if first:
                    o_scr[...] = part
                else:
                    o_scr[...] += part

            grad(tile_reach, True)
            for j in range(tile_reach):
                pl.when(on(j))(lambda j=j: grad(j, False))
            dq_ref[own_rows, :] = (o_scr[...] * scale).astype(dq_ref.dtype)
            ld_ref[0:1, i * TILE:(i + 1) * TILE] = _row(lse, TILE)
            ld_ref[1:2, i * TILE:(i + 1) * TILE] = _row(delta, TILE)

    return kernel


def _key_side_kernel(reach, n_tiles, tile_reach, scale):
    nblk = tile_reach + 1
    npl = reach + 1

    def kernel(flags_ref, *refs):
        k_ref, v_ref = refs[0], refs[1]
        q_refs = refs[2:2 + npl]
        d_refs = refs[2 + npl:2 + 2 * npl]
        ld_refs = refs[2 + 2 * npl:2 + 3 * npl]
        bias_ref = refs[2 + 3 * npl]
        dk_ref, dv_ref = refs[3 + 3 * npl], refs[4 + 3 * npl]
        dk_scr, dv_scr = refs[5 + 3 * npl:]

        for i in range(n_tiles):
            own_rows = pl.ds(i * TILE, TILE)
            k = k_ref[own_rows, :]
            v = v_ref[own_rows, :]

            def step(j, first):
                b = i + j
                p_i, t = b // n_tiles, b % n_tiles
                rows = pl.ds(t * TILE, TILE)
                q = q_refs[p_i][rows, :]
                d = d_refs[p_i][rows, :]
                lse = ld_refs[p_i][0:1, t * TILE:(t + 1) * TILE]
                delta = ld_refs[p_i][1:2, t * TILE:(t + 1) * TILE]
                raw = lax.dot_general(k, q, (((1,), (1,)), ((), ())),
                                      preferred_element_type=jnp.float32)
                logit = raw * scale + bias_ref[own_rows, j * TILE:(j + 1) * TILE]
                prob = jnp.exp(logit - lse)
                dprobs = lax.dot_general(v, d, (((1,), (1,)), ((), ())),
                                         preferred_element_type=jnp.float32)
                dscores = (prob * (dprobs - delta)).astype(jnp.bfloat16)
                part_k = jnp.dot(dscores, q, preferred_element_type=jnp.float32)
                part_v = jnp.dot(prob.astype(jnp.bfloat16), d, preferred_element_type=jnp.float32)
                if first:
                    dk_scr[...] = part_k
                    dv_scr[...] = part_v
                else:
                    dk_scr[...] += part_k
                    dv_scr[...] += part_v

            step(0, True)
            for j in range(1, nblk):
                pl.when(flags_ref[i * nblk + j] != 0)(lambda j=j: step(j, False))
            dk_ref[own_rows, :] = (dk_scr[...] * scale).astype(dk_ref.dtype)
            dv_ref[own_rows, :] = dv_scr[...].astype(dv_ref.dtype)

    return kernel


def _plan(tok_in, ctx_n, head_n):
    clo_n = 1
    while (clo_n * 2 <= ctx_n and ctx_n % (clo_n * 2) == 0
           and tok_in * clo_n * head_n < PLANE_TOKENS):
        clo_n *= 2
    return clo_n


def _per_device(clo_n, attn_q, attn_k, attn_v, attn_dout, doc_ids):
    tok_in, full_width = attn_q.shape
    head_n = lax.axis_size("head")
    chi_n = lax.axis_size("chi")
    group = clo_n * head_n
    width = full_width // group
    heads_p = width // HEAD_DIM
    plane = tok_in * group
    n_tok = doc_ids.shape[0]
    scale = HEAD_DIM ** (-0.5)
    reach = min(-(-(MAX_DOC - 1) // plane), chi_n - 1)
    tile_reach = -(-(MAX_DOC - 1) // TILE)
    nblk = tile_reach + 1
    n_tiles = plane // TILE
    chi = lax.axis_index("chi")
    plane_start = chi * plane

    def to_plane(x):
        x = x.reshape(tok_in, head_n, clo_n, width).transpose(0, 2, 1, 3).reshape(tok_in, full_width)
        return lax.all_to_all(x, ("clo", "head"), split_axis=1, concat_axis=0, tiled=True)

    keys = to_plane(attn_k)
    values = to_plane(attn_v)
    query = to_plane(attn_q)
    dout = to_plane(attn_dout)

    k_parts, v_parts = [], []
    for shift in range(reach, 0, -1):
        far_k, far_v = shifted((keys, values), "chi", shift)
        k_parts.append(far_k)
        v_parts.append(far_v)
    k_parts.append(keys)
    v_parts.append(values)

    q_parts, d_parts = [query], [dout]
    for shift in range(1, reach + 1):
        far_q, far_d = shifted((query, dout), "chi", -shift)
        q_parts.append(far_q)
        d_parts.append(far_d)

    pad = (reach + 1) * plane
    docs_pad = jnp.concatenate([
        jnp.full((pad,), -1, jnp.int32), doc_ids.astype(jnp.int32), jnp.full((pad,), -1, jnp.int32)])
    span = nblk * TILE
    cols = jnp.arange(span, dtype=jnp.int32)
    rows = jnp.arange(TILE, dtype=jnp.int32)
    q_bias, k_bias, q_flags, k_flags = [], [], [], []
    for i in range(n_tiles):
        t_start = plane_start + i * TILE
        own_doc = lax.dynamic_slice_in_dim(docs_pad, t_start + pad, TILE)
        own_pos = t_start + rows
        k_start = t_start - tile_reach * TILE
        k_doc = lax.dynamic_slice_in_dim(docs_pad, k_start + pad, span)
        k_pos = k_start + cols
        mask = (k_pos[None, :] <= own_pos[:, None]) & (k_doc[None, :] == own_doc[:, None])
        q_bias.append(jnp.where(mask, 0.0, masked_value).astype(jnp.float32))
        q_flags.append(mask.reshape(TILE, nblk, TILE).any(axis=(0, 2)))
        q_doc = lax.dynamic_slice_in_dim(docs_pad, t_start + pad, span)
        q_pos = t_start + cols
        mask = (own_pos[:, None] <= q_pos[None, :]) & (own_doc[:, None] == q_doc[None, :])
        k_bias.append(jnp.where(mask, 0.0, masked_value).astype(jnp.float32))
        k_flags.append(mask.reshape(TILE, nblk, TILE).any(axis=(0, 2)))
    q_bias = jnp.concatenate(q_bias, axis=0)
    k_bias = jnp.concatenate(k_bias, axis=0)
    q_flags = jnp.concatenate(q_flags).astype(jnp.int32)
    k_flags = jnp.concatenate(k_flags).astype(jnp.int32)

    plane_spec = pl.BlockSpec((plane, HEAD_DIM), lambda h, f: (0, h))
    ld_spec = pl.BlockSpec((None, 2, plane), lambda h, f: (h, 0, 0))
    bias_spec = pl.BlockSpec((plane, span), lambda h, f: (0, 0))
    params = pltpu.CompilerParams(dimension_semantics=("arbitrary",))
    npl = reach + 1

    dq, ld = pl.pallas_call(
        _query_side_kernel(reach, n_tiles, tile_reach, scale),
        out_shape=(
            jax.ShapeDtypeStruct((plane, width), jnp.bfloat16),
            jax.ShapeDtypeStruct((heads_p, 2, plane), jnp.float32),
        ),
        grid_spec=pltpu.PrefetchScalarGridSpec(
            num_scalar_prefetch=1,
            grid=(heads_p,),
            in_specs=[plane_spec] * (2 + 2 * npl) + [bias_spec],
            out_specs=(plane_spec, ld_spec),
            scratch_shapes=[
                pltpu.VMEM((nblk, TILE, TILE), jnp.float32),
                pltpu.VMEM((TILE, 1), jnp.float32),
                pltpu.VMEM((TILE, 1), jnp.float32),
                pltpu.VMEM((TILE, HEAD_DIM), jnp.float32),
            ],
        ),
        compiler_params=params,
        name="attn_query_side",
    )(q_flags, query, dout, *k_parts, *v_parts, q_bias)

    ld_parts = [ld]
    for shift in range(1, reach + 1):
        ld_parts.append(shifted(ld, "chi", -shift))

    dk, dv = pl.pallas_call(
        _key_side_kernel(reach, n_tiles, tile_reach, scale),
        out_shape=(
            jax.ShapeDtypeStruct((plane, width), jnp.bfloat16),
            jax.ShapeDtypeStruct((plane, width), jnp.bfloat16),
        ),
        grid_spec=pltpu.PrefetchScalarGridSpec(
            num_scalar_prefetch=1,
            grid=(heads_p,),
            in_specs=[plane_spec] * (2 + 2 * npl) + [ld_spec] * npl + [bias_spec],
            out_specs=(plane_spec, plane_spec),
            scratch_shapes=[
                pltpu.VMEM((TILE, HEAD_DIM), jnp.float32),
                pltpu.VMEM((TILE, HEAD_DIM), jnp.float32),
            ],
        ),
        compiler_params=params,
        name="attn_key_side",
    )(k_flags, keys, values, *q_parts, *d_parts, *ld_parts, k_bias)

    def from_plane(x):
        return lax.all_to_all(x, "clo", split_axis=0, concat_axis=1, tiled=True)

    return (from_plane(dq), from_plane(dk), from_plane(dv))


def solution(mesh):
    ctx_n, head_n = mesh.devices.shape
    def fn(attn_q, attn_k, attn_v, attn_dout, doc_ids):
        tok_in = attn_q.shape[0] // (ctx_n * head_n)
        clo_n = _plan(tok_in, ctx_n, head_n)
        chi_n = ctx_n // clo_n
        sub = Mesh(np.asarray(mesh.devices).reshape(chi_n, clo_n, head_n), ("chi", "clo", "head"))
        inner = jax.shard_map(
            lambda *a: _per_device(clo_n, *a),
            mesh=sub,
            in_specs=(
                P(("chi", "clo", "head"), None),
                P(("chi", "clo", "head"), None),
                P(("chi", "clo", "head"), None),
                P(("chi", "clo", "head"), None),
                P(),
            ),
            out_specs=(P(("chi", "clo"), "head"), P(("chi", "clo"), "head"), P(("chi", "clo"), "head")),
            check_vma=False,
        )
        return inner(attn_q, attn_k, attn_v, attn_dout, doc_ids)
    return fn
```

time: 387 us -> 430 us (1.11); the launches traced: 385 us -> 436 us
  Pallas kernels: 101 us -> 132 us
  waiting for transfers between devices: 140 us -> 171 us
  other arithmetic: 33.4 us -> 22.3 us
    ppermute x5, waiting for transfers between devices: 58.5 us -> 96 us  [shifted(): lax.ppermute(value, axis, [(source, source + steps) for source in range(l...]
    pallas_call x2, Pallas kernels: 101 us -> 132 us  [the longest x1 84 us: _per_device(): pl.pallas_call(_query_side_kernel(reach, n_tiles, tile_reach, scale), out...]
    concatenate x5 -> x0, other arithmetic: 19 us -> none  [the longest x1 4.76 us: _per_device(): d_win = jnp.concatenate([dout] + d_parts, axis=0)]
    all_to_all x4, waiting for transfers between devices: 59.9 us -> 52.7 us  [to_plane(): lax.all_to_all(x, ('clo', 'head'), split_axis=1, concat_axis=0, tiled=True)]
    reduce_or x0 -> x2, other arithmetic: none -> 6.11 us  [_per_device(): k_flags.append(mask.reshape(TILE, nblk, TILE).any(axis=(0, 2)))]
  transfers between devices with their start and end apart: 11 -> 11, of which waited for: 7 -> 8; matrix products, arithmetic and copies ran while one was open for 16% -> 12% of each run, Pallas kernels for 26% -> 30%
where the time goes in v3:
time: 430 us; the launch traced here: 436 us
  waiting for transfers between devices  171 us (40%)
  Pallas kernels  132 us (31%)
  starting transfers between devices  40.6 us (9%)
  local copies, waits for them, and re-layouts  39.4 us (9%)
  blocking collectives  30.2 us (7%)
  other arithmetic  22.3 us (5%)
    ppermute x5, waiting for transfers between devices, shifted(): lax.ppermute(value, axis, [(source, source + steps) for source in range(l...  96 us
    pallas_call x1, Pallas kernels, _per_device(): pl.pallas_call(_query_side_kernel(reach, n_tiles, tile_reach, scale), out...  84 us
    all_to_all x4, waiting for transfers between devices, to_plane(): lax.all_to_all(x, ('clo', 'head'), split_axis=1, concat_axis=0, tiled=True)  52.7 us
    pallas_call x1, Pallas kernels, _per_device(): pl.pallas_call(_key_side_kernel(reach, n_tiles, tile_reach, scale), out_s...  47.5 us
    all_to_all x1, blocking collectives, from_plane(): return lax.all_to_all(x, 'clo', split_axis=0, concat_axis=1, tiled=True)  30.2 us
    all_to_all x2, waiting for transfers between devices, from_plane(): return lax.all_to_all(x, 'clo', split_axis=0, concat_axis=1, tiled=True)  21.9 us
    all_to_all x4, starting transfers between devices, to_plane(): lax.all_to_all(x, ('clo', 'head'), split_axis=1, concat_axis=0, tiled=True)  18.6 us
    reshape x4, local copies, waits for them, and re-layouts, to_plane(): x.reshape(tok_in, head_n, clo_n, width).transpose(0, 2, 1, 3)  16.8 us
  transfers between devices with their start and end apart: 11, of which 8 were waited for; matrix products, arithmetic and copies ran while one was open for 12% of the time, Pallas kernels for 30%

profile of v3, /device:TPU:20, one launch (start us, length us, event | category | flops | bytes accessed | tf_op | source)
XLA Modules:
  0.0 435.7 jit_solution(12951802850190240885)
XLA Ops:
  6.4 4.2 all-to-all-start.2
  10.7 4.5 %reshape.282 = bf16[128,2,4,1024]{3,2,1,0:T(4,128)(2,1)} reshape(bf16[128,8192]{1,0:T(8,128)(2,1)} %param.7) | data formatting | bytes 4194304 | tf_op jit(solution)/shard_map/reshape | solution.py:190
  15.1 4.1 copy.18
  19.2 16.7 %all-to-all-done.2 = bf16[128,8,1024]{2,0,1:T(8,128)(2,1)S(1)} async-done(((bf16[128,8,1024]{2,0,1:T(8,128)(2,1)}), bf16[128,8,1024]{2,0,1:T(8,128)(2,1)S(1)}, u32[]{:S(2)}, u32[]{:S(2)}) %all-to-all-start.2) | async-done | bytes 2097184 | tf_op jit(solution)/shard_map/all_to_all | solution.py:191
  35.9 4.8 %all-to-all-start.3 = ((bf16[128,8,1024]{2,0,1:T(8,128)(2,1)}), bf16[128,8,1024]{2,0,1:T(8,128)(2,1)}, u32[]{:S(2)}, u32[]{:S(2)}) async-start(bf16[128,8,1024]{2,0,1:T(8,128)(2,1)} %bitcast.37), calls=%async_computation.3 | async-start | bytes 4194304 | tf_op jit(solution)/shard_map/all_to_all | solution.py:191
  40.7 4.5 %reshape.279 = bf16[128,2,4,1024]{3,2,1,0:T(4,128)(2,1)} reshape(bf16[128,8192]{1,0:T(8,128)(2,1)} %param.5) | data formatting | bytes 4194304 | tf_op jit(solution)/shard_map/reshape | solution.py:190
  45.2 4.1 copy.15
  49.4 16.6 %all-to-all-done.3 = bf16[128,8,1024]{2,0,1:T(8,128)(2,1)} async-done(((bf16[128,8,1024]{2,0,1:T(8,128)(2,1)}), bf16[128,8,1024]{2,0,1:T(8,128)(2,1)}, u32[]{:S(2)}, u32[]{:S(2)}) %all-to-all-start.3) | async-done | bytes 2097184 | tf_op jit(solution)/shard_map/all_to_all | solution.py:191
  66.0 4.8 %all-to-all-start = ((bf16[128,8,1024]{2,0,1:T(8,128)(2,1)}), bf16[128,8,1024]{2,0,1:T(8,128)(2,1)}, u32[]{:S(2)}, u32[]{:S(2)}) async-start(bf16[128,8,1024]{2,0,1:T(8,128)(2,1)} %bitcast.36), calls=%async_computation | async-start | bytes 4194304 | tf_op jit(solution)/shard_map/all_to_all | solution.py:191
  70.8 4.5 %reshape.280 = bf16[128,2,4,1024]{3,2,1,0:T(4,128)(2,1)} reshape(bf16[128,8192]{1,0:T(8,128)(2,1)} %param.8) | data formatting | bytes 4194304 | tf_op jit(solution)/shard_map/reshape | solution.py:190
  75.3 4.1 copy.16
  79.7 16.5 %all-to-all-done = bf16[128,8,1024]{2,0,1:T(8,128)(2,1)} async-done(((bf16[128,8,1024]{2,0,1:T(8,128)(2,1)}), bf16[128,8,1024]{2,0,1:T(8,128)(2,1)}, u32[]{:S(2)}, u32[]{:S(2)}) %all-to-all-start) | async-done | bytes 2097184 | tf_op jit(solution)/shard_map/all_to_all | solution.py:191
  96.2 4.8 %all-to-all-start.1 = ((bf16[128,8,1024]{2,0,1:T(8,128)(2,1)}), bf16[128,8,1024]{2,0,1:T(8,128)(2,1)}, u32[]{:S(2)}, u32[]{:S(2)}) async-start(bf16[128,8,1024]{2,0,1:T(8,128)(2,1)} %bitcast.35), calls=%async_computation.1 | async-start | bytes 4194304 | tf_op jit(solution)/shard_map/all_to_all | solution.py:191
  119.5 3.9 collective-permute-start.2
  129.3 4.2 pad_maximum_fusion.refs_6_
  133.5 21.1 %collective-permute-done.refs_2_ = bf16[1024,1024]{1,0:T(8,128)(2,1)} collective-permute-done((bf16[1024,1024]{1,0:T(8,128)(2,1)S(1)}, bf16[1024,1024]{1,0:T(8,128)(2,1)}, u32[]{:S(2)}, u32[]{:S(2)}) %collective-permute-start) | collective-permute-done | bytes 2097184 | tf_op jit(solution)/shard_map/ppermute | solution.py:21
  154.6 44.2 %collective-permute-done.1.refs_4_ = bf16[1024,1024]{1,0:T(8,128)(2,1)} collective-permute-done((bf16[1024,1024]{1,0:T(8,128)(2,1)}, bf16[1024,1024]{1,0:T(8,128)(2,1)}, u32[]{:S(2)}, u32[]{:S(2)}) %collective-permute-start.1) | collective-permute-done | bytes 2097184 | tf_op jit(solution)/shard_map/ppermute | solution.py:21
  198.8 84.0 %attn_query_side.1 = (bf16[1024,1024]{1,0:T(8,128)(2,1)}, f32[8,2,1024]{2,1,0:T(2,128)}) custom-call(s32[20]{0:T(128)} %add_convert_fusion.flags_ref, bf16[1024,1024]{1,0:T(8,128)(2,1)} %bitcast.3.refs_0_.refs_2_, bf16[1024,1024]{1,0:T(8,128)(2,1)} %bitcast.7.refs_1_.refs_4_, bf16[1024,1024]{1,0:T(8,128)(2,1)} %collective-permute-done.refs_2_, ...), custom_call_target="tpu_custom_call" | custom-call | tf_op jit(solution)/shard_map/attn_query_side/pallas_call | solution.py:245
  286.5 4.0 pad_maximum_fusion.1.refs_8_
  293.3 30.7 %collective-permute-done.4.refs_7_ = f32[8,2,1024]{2,1,0:T(2,128)S(1)} collective-permute-done((f32[8,2,1024]{2,1,0:T(2,128)S(1)}, f32[8,2,1024]{2,1,0:T(2,128)S(1)}, u32[]{:S(2)}, u32[]{:S(2)}) %collective-permute-start.4) | collective-permute-done | bytes 65568 | tf_op jit(solution)/shard_map/ppermute | solution.py:21
  324.6 47.5 %attn_key_side.1 = (bf16[1024,1024]{1,0:T(8,128)(2,1)}, bf16[1024,1024]{1,0:T(8,128)(2,1)}) custom-call(s32[20]{0:T(128)} %add_convert_fusion.1.flags_ref, bf16[1024,1024]{1,0:T(8,128)(2,1)} %bitcast.34, bf16[1024,1024]{1,0:T(8,128)(2,1)} %bitcast.15.refs_5_.refs_1_, bf16[1024,1024]{1,0:T(8,128)(2,1)} %bitcast.3.refs_0_.refs_2_, ...), custom_call_target="tpu_custom_call" | custom-call | tf_op jit(solution)/shard_map/attn_key_side/pallas_call | solution.py:271
  372.2 30.2 %all_to_all.133 = bf16[4,256,1024]{2,1,0:T(8,128)(2,1)} all-to-all(bf16[4,256,1024]{2,1,0:T(8,128)(2,1)} %bitcast.47), channel_id=1, replica_groups=mesh['chi'=4,'clo'=4,'head'=2] {'clo'}, dimensions={0} | all-to-all | bytes 4194304 | tf_op jit(solution)/shard_map/all_to_all | solution.py:292
  402.3 4.4 %all-to-all-start.6 = ((bf16[4,256,1024]{2,1,0:T(8,128)(2,1)}), bf16[4,256,1024]{2,1,0:T(8,128)(2,1)}, u32[]{:S(2)}, u32[]{:S(2)}) async-start(bf16[4,256,1024]{2,1,0:T(8,128)(2,1)} %bitcast.46), calls=%async_computation.6 | async-start | bytes 4194304 | tf_op jit(solution)/shard_map/all_to_all | solution.py:292
  410.6 21.9 %all-to-all-done.6 = bf16[4,256,1024]{2,1,0:T(8,128)(2,1)} async-done(((bf16[4,256,1024]{2,1,0:T(8,128)(2,1)}), bf16[4,256,1024]{2,1,0:T(8,128)(2,1)}, u32[]{:S(2)}, u32[]{:S(2)}) %all-to-all-start.6) | async-done | bytes 2097184 | tf_op jit(solution)/shard_map/all_to_all | solution.py:292
  (90 shorter events, 44.4 us)
Async XLA Ops:
  6.4 29.5 %all-to-all-start.2 = ((bf16[128,8,1024]{2,0,1:T(8,128)(2,1)}), bf16[128,8,1024]{2,0,1:T(8,128)(2,1)S(1)}, u32[]{:S(2)}, u32[]{:S(2)}) async-start(bf16[128,8,1024]{2,0,1:T(8,128)(2,1)} %bitcast.40), calls=%async_computation.2 | async-start | bytes 4194304 | tf_op jit(solution)/shard_map/all_to_all | solution.py:191
  35.9 68.3 %copy-start = (bf16[128,8,1024]{2,0,1:T(8,128)(2,1)}, bf16[128,8,1024]{2,0,1:T(8,128)(2,1)S(1)}, u32[]{:S(2)}) copy-start(bf16[128,8,1024]{2,0,1:T(8,128)(2,1)S(1)} %all-to-all-done.2) | copy-start | bytes 6291460
  35.9 30.1 %all-to-all-start.3 = ((bf16[128,8,1024]{2,0,1:T(8,128)(2,1)}), bf16[128,8,1024]{2,0,1:T(8,128)(2,1)}, u32[]{:S(2)}, u32[]{:S(2)}) async-start(bf16[128,8,1024]{2,0,1:T(8,128)(2,1)} %bitcast.37), calls=%async_computation.3 | async-start | bytes 4194304 | tf_op jit(solution)/shard_map/all_to_all | solution.py:191
  49.2 60.5 %copy-start.5 = (s32[256]{0:T(256)}, s32[256]{0:T(256)S(1)}, u32[]{:S(2)}) copy-start(s32[256]{0:T(256)S(1)} %iota_add_fusion.8) | copy-start | bytes 3076
  49.2 60.5 %copy-start.6 = (s32[256]{0:T(256)}, s32[256]{0:T(256)S(1)}, u32[]{:S(2)}) copy-start(s32[256]{0:T(256)S(1)} %iota_add_fusion.9) | copy-start | bytes 3076
  66.0 30.1 %all-to-all-start = ((bf16[128,8,1024]{2,0,1:T(8,128)(2,1)}), bf16[128,8,1024]{2,0,1:T(8,128)(2,1)}, u32[]{:S(2)}, u32[]{:S(2)}) async-start(bf16[128,8,1024]{2,0,1:T(8,128)(2,1)} %bitcast.36), calls=%async_computation | async-start | bytes 4194304 | tf_op jit(solution)/shard_map/all_to_all | solution.py:191
  70.8 30.2 %copy-start.7 = (s32[256]{0:T(256)}, s32[256]{0:T(256)S(1)}, u32[]{:S(2)}) copy-start(s32[256]{0:T(256)S(1)} %iota_add_fusion.10) | copy-start | bytes 3076
  96.2 30.1 %all-to-all-start.1 = ((bf16[128,8,1024]{2,0,1:T(8,128)(2,1)}), bf16[128,8,1024]{2,0,1:T(8,128)(2,1)}, u32[]{:S(2)}, u32[]{:S(2)}) async-start(bf16[128,8,1024]{2,0,1:T(8,128)(2,1)} %bitcast.35), calls=%async_computation.1 | async-start | bytes 4194304 | tf_op jit(solution)/shard_map/all_to_all | solution.py:191
  101.0 8.8 %copy-start.9 = (s32[256]{0:T(256)}, s32[256]{0:T(256)S(1)}, u32[]{:S(2)}) copy-start(s32[256]{0:T(256)S(1)} %iota_add_fusion.11) | copy-start | bytes 3076
  104.2 50.5 %collective-permute-start = (bf16[1024,1024]{1,0:T(8,128)(2,1)S(1)}, bf16[1024,1024]{1,0:T(8,128)(2,1)}, u32[]{:S(2)}, u32[]{:S(2)}) collective-permute-start(bf16[1024,1024]{1,0:T(8,128)(2,1)S(1)} %bitcast.32), channel_id=1, source_target_pairs={{0,8},{8,16},{16,24},{1,9},{9,17},{17,25},{2,10},{10,18},{18,26},{... | collective-permute-start | bytes 6291464 | tf_op jit(solution)/shard_map/ppermute | solution.py:21
  107.6 91.1 %collective-permute-start.1 = (bf16[1024,1024]{1,0:T(8,128)(2,1)}, bf16[1024,1024]{1,0:T(8,128)(2,1)}, u32[]{:S(2)}, u32[]{:S(2)}) collective-permute-start(bf16[1024,1024]{1,0:T(8,128)(2,1)} %bitcast.15.refs_5_.refs_1_), channel_id=1, source_target_pairs={{0,8},{8,16},{16,24},{1,9},{9,17},{17,25},{2,10},{10,18},{18,26},{... | collective-permute-start | bytes 6291464 | tf_op jit(solution)/shard_map/ppermute | solution.py:21
  116.3 12.4 %copy-start.15 = (pred[5]{0:T(512)(128)(4,1)S(1)}, pred[5]{0:T(512)(128)(4,1)}, u32[]{:S(2)}) copy-start(pred[5]{0:T(512)(128)(4,1)} %get-tuple-element.14) | copy-start | bytes 19
  116.3 12.4 %copy-start.16 = (pred[5]{0:T(512)(128)(4,1)S(1)}, pred[5]{0:T(512)(128)(4,1)}, u32[]{:S(2)}) copy-start(pred[5]{0:T(512)(128)(4,1)} %get-tuple-element.45) | copy-start | bytes 19
  116.3 12.4 %copy-start.17 = (pred[5]{0:T(512)(128)(4,1)S(1)}, pred[5]{0:T(512)(128)(4,1)}, u32[]{:S(2)}) copy-start(pred[5]{0:T(512)(128)(4,1)} %get-tuple-element.18) | copy-start | bytes 19
  116.3 12.4 %copy-start.18 = (pred[5]{0:T(512)(128)(4,1)S(1)}, pred[5]{0:T(512)(128)(4,1)}, u32[]{:S(2)}) copy-start(pred[5]{0:T(512)(128)(4,1)} %get-tuple-element.43) | copy-start | bytes 19
  119.5 173.7 %collective-permute-start.2 = (bf16[1024,1024]{1,0:T(8,128)(2,1)}, bf16[1024,1024]{1,0:T(8,128)(2,1)}, u32[]{:S(2)}, u32[]{:S(2)}) collective-permute-start(bf16[1024,1024]{1,0:T(8,128)(2,1)} %bitcast.3.refs_0_.refs_2_), channel_id=1, source_target_pairs={{8,0},{16,8},{24,16},{9,1},{17,9},{25,17},{10,2},{18,10},{26,18},{... | collective-permute-start | bytes 6291464 | tf_op jit(solution)/shard_map/ppermute | solution.py:21
  126.3 166.9 %collective-permute-start.3 = (bf16[1024,1024]{1,0:T(8,128)(2,1)}, bf16[1024,1024]{1,0:T(8,128)(2,1)}, u32[]{:S(2)}, u32[]{:S(2)}) collective-permute-start(bf16[1024,1024]{1,0:T(8,128)(2,1)} %bitcast.7.refs_1_.refs_4_), channel_id=1, source_target_pairs={{8,0},{16,8},{24,16},{9,1},{17,9},{25,17},{10,2},{18,10},{26,18},{... | collective-permute-start | bytes 6291464 | tf_op jit(solution)/shard_map/ppermute | solution.py:21
  282.8 89.3 %all-to-all-start.4 = ((bf16[4,256,1024]{2,1,0:T(8,128)(2,1)}), bf16[4,256,1024]{2,1,0:T(8,128)(2,1)S(1)}, u32[]{:S(2)}, u32[]{:S(2)}) async-start(bf16[4,256,1024]{2,1,0:T(8,128)(2,1)} %bitcast.45), calls=%async_computation.4 | async-start | bytes 4194304 | tf_op jit(solution)/shard_map/all_to_all | solution.py:292
  286.5 6.2 %copy-start.11 = (pred[5]{0:T(512)(128)(4,1)S(1)}, pred[5]{0:T(512)(128)(4,1)}, u32[]{:S(2)}) copy-start(pred[5]{0:T(512)(128)(4,1)} %get-tuple-element.13) | copy-start | bytes 19
  286.5 6.2 %copy-start.12 = (pred[5]{0:T(512)(128)(4,1)S(1)}, pred[5]{0:T(512)(128)(4,1)}, u32[]{:S(2)}) copy-start(pred[5]{0:T(512)(128)(4,1)} %get-tuple-element.46) | copy-start | bytes 19
  286.5 6.2 %copy-start.13 = (pred[5]{0:T(512)(128)(4,1)S(1)}, pred[5]{0:T(512)(128)(4,1)}, u32[]{:S(2)}) copy-start(pred[5]{0:T(512)(128)(4,1)} %get-tuple-element.17) | copy-start | bytes 19
  286.5 6.2 %copy-start.14 = (pred[5]{0:T(512)(128)(4,1)S(1)}, pred[5]{0:T(512)(128)(4,1)}, u32[]{:S(2)}) copy-start(pred[5]{0:T(512)(128)(4,1)} %get-tuple-element.44) | copy-start | bytes 19
  290.5 33.5 %collective-permute-start.4 = (f32[8,2,1024]{2,1,0:T(2,128)S(1)}, f32[8,2,1024]{2,1,0:T(2,128)S(1)}, u32[]{:S(2)}, u32[]{:S(2)}) collective-permute-start(f32[8,2,1024]{2,1,0:T(2,128)S(1)} %copy-done.2), channel_id=1, source_target_pairs={{8,0},{16,8},{24,16},{9,1},{17,9},{25,17},{10,2},{18,10},{26,18},{... | collective-permute-start | bytes 196616 | tf_op jit(solution)/shard_map/ppermute | solution.py:21
  402.3 30.2 %all-to-all-start.6 = ((bf16[4,256,1024]{2,1,0:T(8,128)(2,1)}), bf16[4,256,1024]{2,1,0:T(8,128)(2,1)}, u32[]{:S(2)}, u32[]{:S(2)}) async-start(bf16[4,256,1024]{2,1,0:T(8,128)(2,1)} %bitcast.46), calls=%async_computation.6 | async-start | bytes 4194304 | tf_op jit(solution)/shard_map/all_to_all | solution.py:292
  (6 other events, 18.1 us)

commit v4 on v2

--- a/solution.py
+++ b/solution.py
@@ -25,18 +25,32 @@
     return jnp.transpose(jnp.broadcast_to(col, (tok, 128)))[0:1, :]
 
 
-def _query_side_kernel(nblk, scale):
+def _pick(refs, plane_idx):
+    value = refs[-1][...]
+    for p in range(len(refs) - 2, -1, -1):
+        value = jnp.where(plane_idx == p, refs[p][...], value)
+    return value
+
+
+def _query_side_kernel(nblk, npl, base, n_tiles, scale):
     def kernel(*refs):
         q_ref, d_ref = refs[0], refs[1]
-        k_refs = refs[2:2 + nblk]
-        v_refs = refs[2 + nblk:2 + 2 * nblk]
-        bias_ref = refs[2 + 2 * nblk]
-        dq_ref, ld_ref = refs[3 + 2 * nblk], refs[4 + 2 * nblk]
+        nref = nblk * npl
+        kp_refs = refs[2:2 + nref]
+        vp_refs = refs[2 + nref:2 + 2 * nref]
+        bias_ref = refs[2 + 2 * nref]
+        dq_ref, ld_ref = refs[3 + 2 * nref], refs[4 + 2 * nref]
+        tile = pl.program_id(0)
+        k_blocks, v_blocks = [], []
+        for j in range(nblk):
+            plane_idx = (base + tile + j) // n_tiles
+            k_blocks.append(_pick(kp_refs[j * npl:(j + 1) * npl], plane_idx))
+            v_blocks.append(_pick(vp_refs[j * npl:(j + 1) * npl], plane_idx))
         q = q_ref[...]
         d = d_ref[...]
         logits = []
         for j in range(nblk):
-            raw = lax.dot_general(q, k_refs[j][...], (((1,), (1,)), ((), ())),
+            raw = lax.dot_general(q, k_blocks[j], (((1,), (1,)), ((), ())),
                                   preferred_element_type=jnp.float32)
             logits.append(raw * scale + bias_ref[:, j * TILE:(j + 1) * TILE])
         top = logits[0].max(axis=1, keepdims=True)
@@ -49,16 +63,16 @@
         probs = [jnp.exp(item - lse) for item in logits]
         out = None
         for j in range(nblk):
-            part = jnp.dot(probs[j].astype(jnp.bfloat16), v_refs[j][...],
+            part = jnp.dot(probs[j].astype(jnp.bfloat16), v_blocks[j],
                            preferred_element_type=jnp.float32)
             out = part if out is None else out + part
         delta = (d.astype(jnp.float32) * out).sum(axis=1, keepdims=True)
         dq = None
         for j in range(nblk):
-            dprobs = lax.dot_general(d, v_refs[j][...], (((1,), (1,)), ((), ())),
+            dprobs = lax.dot_general(d, v_blocks[j], (((1,), (1,)), ((), ())),
                                      preferred_element_type=jnp.float32)
             dscores = (probs[j] * (dprobs - delta)).astype(jnp.bfloat16)
-            part = jnp.dot(dscores, k_refs[j][...], preferred_element_type=jnp.float32)
+            part = jnp.dot(dscores, k_blocks[j], preferred_element_type=jnp.float32)
             dq = part if dq is None else dq + part
         dq_ref[...] = (dq * scale).astype(dq_ref.dtype)
         ld_ref[0:1, :] = _row(lse, TILE)
@@ -67,23 +81,27 @@
     return kernel
 
 
-def _key_side_kernel(nblk, scale):
+def _key_side_kernel(nblk, npl, n_tiles, scale):
     def kernel(*refs):
         k_ref, v_ref = refs[0], refs[1]
-        q_refs = refs[2:2 + nblk]
-        d_refs = refs[2 + nblk:2 + 2 * nblk]
-        ld_refs = refs[2 + 2 * nblk:2 + 3 * nblk]
-        bias_ref = refs[2 + 3 * nblk]
-        dk_ref, dv_ref = refs[3 + 3 * nblk], refs[4 + 3 * nblk]
+        nref = nblk * npl
+        qp_refs = refs[2:2 + nref]
+        dp_refs = refs[2 + nref:2 + 2 * nref]
+        lp_refs = refs[2 + 2 * nref:2 + 3 * nref]
+        bias_ref = refs[2 + 3 * nref]
+        out_ref = refs[3 + 3 * nref]
+        tile = pl.program_id(0)
         k = k_ref[...]
         v = v_ref[...]
         dk = None
         dv = None
         for j in range(nblk):
-            q = q_refs[j][...]
-            d = d_refs[j][...]
-            lse = ld_refs[j][0:1, :]
-            delta = ld_refs[j][1:2, :]
+            plane_idx = (tile + j) // n_tiles
+            q = _pick(qp_refs[j * npl:(j + 1) * npl], plane_idx)
+            d = _pick(dp_refs[j * npl:(j + 1) * npl], plane_idx)
+            ld = _pick(lp_refs[j * npl:(j + 1) * npl], plane_idx)
+            lse = ld[0:1, :]
+            delta = ld[1:2, :]
             raw = lax.dot_general(k, q, (((1,), (1,)), ((), ())),
                                   preferred_element_type=jnp.float32)
             logit = raw * scale + bias_ref[:, j * TILE:(j + 1) * TILE]
@@ -95,8 +113,8 @@
             part_v = jnp.dot(prob.astype(jnp.bfloat16), d, preferred_element_type=jnp.float32)
             dk = part_k if dk is None else dk + part_k
             dv = part_v if dv is None else dv + part_v
-        dk_ref[...] = (dk * scale).astype(dk_ref.dtype)
-        dv_ref[...] = dv.astype(dv_ref.dtype)
+        out_ref[0] = (dk * scale).astype(out_ref.dtype)
+        out_ref[1] = dv.astype(out_ref.dtype)
 
     return kernel
 
@@ -126,30 +144,15 @@
     chi = lax.axis_index("chi")
     plane_start = chi * plane
 
-    def to_plane(x):
-        x = x.reshape(tok_in, head_n, clo_n, width).transpose(0, 2, 1, 3).reshape(tok_in, full_width)
-        return lax.all_to_all(x, ("clo", "head"), split_axis=1, concat_axis=0, tiled=True)
-
-    keys = to_plane(attn_k)
-    values = to_plane(attn_v)
-    query = to_plane(attn_q)
-    dout = to_plane(attn_dout)
-
-    k_parts, v_parts = [], []
-    for shift in range(reach, 0, -1):
-        far_k, far_v = shifted((keys, values), "chi", shift)
-        k_parts.append(far_k)
-        v_parts.append(far_v)
-    k_win = jnp.concatenate(k_parts + [keys], axis=0)
-    v_win = jnp.concatenate(v_parts + [values], axis=0)
-
-    q_parts, d_parts = [], []
-    for shift in range(1, reach + 1):
-        far_q, far_d = shifted((query, dout), "chi", -shift)
-        q_parts.append(far_q)
-        d_parts.append(far_d)
-    q_win = jnp.concatenate([query] + q_parts, axis=0)
-    d_win = jnp.concatenate([dout] + d_parts, axis=0)
+    def to_plane(a, b):
+        x = jnp.stack([a, b]).reshape(2, tok_in, head_n, clo_n, width)
+        x = x.transpose(0, 1, 3, 2, 4).reshape(2, tok_in, full_width)
+        return lax.all_to_all(x, ("clo", "head"), split_axis=2, concat_axis=1, tiled=True)
+
+    kv = to_plane(attn_k, attn_v)
+    kv_parts = [shifted(kv, "chi", shift) for shift in range(reach, 0, -1)] + [kv]
+    qd = to_plane(attn_q, attn_dout)
+    qd_parts = [qd] + [shifted(qd, "chi", -shift) for shift in range(1, reach + 1)]
 
     pad = (reach + 1) * plane
     docs_pad = jnp.concatenate([
@@ -174,59 +177,55 @@
     q_bias = jnp.concatenate(q_bias, axis=0)
     k_bias = jnp.concatenate(k_bias, axis=0)
 
-    own_spec = pl.BlockSpec((TILE, HEAD_DIM), lambda i, h: (i, h))
+    def own_spec(w):
+        return pl.BlockSpec((None, TILE, HEAD_DIM), lambda i, h: (w, i, h))
+
     base = reach * n_tiles - tile_reach
-
-    def kwin_spec(j):
-        return pl.BlockSpec((TILE, HEAD_DIM), lambda i, h: (base + i + j, h))
-
-    def qwin_spec(j):
-        return pl.BlockSpec((TILE, HEAD_DIM), lambda i, h: (i + j, h))
-
-    def ldwin_spec(j):
-        return pl.BlockSpec((None, 2, TILE), lambda i, h: (h, 0, i + j))
-
+    npl = reach + 1
+
+    def clamp_tile(b, p):
+        return jnp.clip(b - p * n_tiles, 0, n_tiles - 1)
+
+    def win_specs(w, shift):
+        return [pl.BlockSpec((None, TILE, HEAD_DIM),
+                             lambda i, h, p=p, j=j: (w, clamp_tile(shift + i + j, p), h))
+                for j in range(nblk) for p in range(npl)]
+
+    ld_win_specs = [pl.BlockSpec((None, 2, TILE), lambda i, h, p=p, j=j: (h, 0, clamp_tile(i + j, p)))
+                    for j in range(nblk) for p in range(npl)]
     bias_spec = pl.BlockSpec((TILE, span), lambda i, h: (i, 0))
     ld_spec = pl.BlockSpec((None, 2, TILE), lambda i, h: (h, 0, i))
     params = pltpu.CompilerParams(dimension_semantics=("arbitrary", "arbitrary"))
     grid = (n_tiles, heads_p)
 
     dq, ld = pl.pallas_call(
-        _query_side_kernel(nblk, scale),
+        _query_side_kernel(nblk, npl, base, n_tiles, scale),
         out_shape=(
             jax.ShapeDtypeStruct((plane, width), jnp.bfloat16),
             jax.ShapeDtypeStruct((heads_p, 2, plane), jnp.float32),
         ),
         grid=grid,
-        in_specs=[own_spec, own_spec] + [kwin_spec(j) for j in range(nblk)] * 2 + [bias_spec],
-        out_specs=(own_spec, ld_spec),
+        in_specs=[own_spec(0), own_spec(1)] + win_specs(0, base) + win_specs(1, base) + [bias_spec],
+        out_specs=(pl.BlockSpec((TILE, HEAD_DIM), lambda i, h: (i, h)), ld_spec),
         compiler_params=params,
         name="attn_query_side",
-    )(query, dout, *([k_win] * nblk), *([v_win] * nblk), q_bias)
-
-    ld_parts = [ld]
-    for shift in range(1, reach + 1):
-        ld_parts.append(shifted(ld, "chi", -shift))
-    ld_win = jnp.concatenate(ld_parts, axis=2)
-
-    dk, dv = pl.pallas_call(
-        _key_side_kernel(nblk, scale),
-        out_shape=(
-            jax.ShapeDtypeStruct((plane, width), jnp.bfloat16),
-            jax.ShapeDtypeStruct((plane, width), jnp.bfloat16),
-        ),
+    )(qd, qd, *(kv_parts * nblk), *(kv_parts * nblk), q_bias)
+
+    ld_parts = [ld] + [shifted(ld, "chi", -shift) for shift in range(1, reach + 1)]
+
+    dkv = pl.pallas_call(
+        _key_side_kernel(nblk, npl, n_tiles, scale),
+        out_shape=jax.ShapeDtypeStruct((2, plane, width), jnp.bfloat16),
         grid=grid,
-        in_specs=[own_spec, own_spec] + [qwin_spec(j) for j in range(nblk)] * 2
-        + [ldwin_spec(j) for j in range(nblk)] + [bias_spec],
-        out_specs=(own_spec, own_spec),
+        in_specs=[own_spec(0), own_spec(1)] + win_specs(0, 0) + win_specs(1, 0) + ld_win_specs + [bias_spec],
+        out_specs=pl.BlockSpec((2, TILE, HEAD_DIM), lambda i, h: (0, i, h)),
         compiler_params=params,
         name="attn_key_side",
-    )(keys, values, *([q_win] * nblk), *([d_win] * nblk), *([ld_win] * nblk), k_bias)
-
-    def from_plane(x):
-        return lax.all_to_all(x, "clo", split_axis=0, concat_axis=1, tiled=True)
-
-    return (from_plane(dq), from_plane(dk), from_plane(dv))
+    )(kv, kv, *(qd_parts * nblk), *(qd_parts * nblk), *(ld_parts * nblk), k_bias)
+
+    dq = lax.all_to_all(dq, "clo", split_axis=0, concat_axis=1, tiled=True)
+    dkv = lax.all_to_all(dkv, "clo", split_axis=1, concat_axis=2, tiled=True)
+    return (dq, dkv[0], dkv[1])
 
 
 def solution(mesh):

time: 387 us -> 419 us (1.083)
  local copies, waits for them, and re-layouts: 38.6 us -> 137 us
  blocking collectives: 30.2 us -> 0 us
  waiting for transfers between devices: 140 us -> 120 us
  other arithmetic: 33.4 us -> 15 us
  Pallas kernels: 101 us -> 115 us
  starting transfers between devices: 40.9 us -> 27.2 us
    reshape x4 -> x2, local copies, waits for them, and re-layouts: 16.8 us -> 70.9 us  [to_plane(): x = x.transpose(0, 1, 3, 2, 4).reshape(2, tok_in, full_width)]
    all_to_all x1 -> x0, blocking collectives: 30.2 us -> none  [from_plane(): return lax.all_to_all(x, 'clo', split_axis=0, concat_axis=1, tiled=True)]
    ppermute x5 -> x3, waiting for transfers between devices: 58.5 us -> 37.3 us  [shifted(): lax.ppermute(value, axis, [(source, source + steps) for source in range(l...]
    concatenate x5 -> x0, other arithmetic: 19 us -> none  [the longest x1 4.76 us: _per_device(): d_win = jnp.concatenate([dout] + d_parts, axis=0)]
    unnamed x8 -> x12, local copies, waits for them, and re-layouts: 0.79 us -> 19.6 us
    all_to_all x3 -> x5, local copies, waits for them, and re-layouts: 6.21 us -> 23.4 us  [the longest x4 21.8 us: to_plane(): lax.all_to_all(x, ('clo', 'head'), split_axis=2, concat_axis=1, tiled=True)]
    pallas_call x2, Pallas kernels: 101 us -> 115 us  [the longest x1 61.1 us: _per_device(): pl.pallas_call(_query_side_kernel(nblk, npl, base, n_tiles, scale), out_s...]
    slice x0 -> x3, local copies, waits for them, and re-layouts: none -> 14.2 us  [_per_device(): return (dq, dkv[0], dkv[1])]
  transfers between devices with their start and end apart: 11 -> 7, of which waited for: 7 -> 4; matrix products, arithmetic and copies ran while one was open for 16% -> 21% of each run, Pallas kernels for 26% -> 28%
where the time goes in v4:
time: 419 us; the launch traced here: 415 us
  local copies, waits for them, and re-layouts  137 us (33%)
  waiting for transfers between devices  120 us (29%)
  Pallas kernels  115 us (27%)
  starting transfers between devices  27.2 us (6%)
  other arithmetic  15 us (4%)
    reshape x2, local copies, waits for them, and re-layouts, to_plane(): x = x.transpose(0, 1, 3, 2, 4).reshape(2, tok_in, full_width)  70.9 us
    pallas_call x1, Pallas kernels, _per_device(): pl.pallas_call(_query_side_kernel(nblk, npl, base, n_tiles, scale), out_s...  61.1 us
    pallas_call x1, Pallas kernels, _per_device(): pl.pallas_call(_key_side_kernel(nblk, npl, n_tiles, scale), out_shape=jax...  54.2 us
    all_to_all x1, waiting for transfers between devices, _per_device(): dkv = lax.all_to_all(dkv, 'clo', split_axis=1, concat_axis=2, tiled=True)  46.4 us
    ppermute x3, waiting for transfers between devices, shifted(): lax.ppermute(value, axis, [(source, source + steps) for source in range(l...  37.3 us
    all_to_all x2, waiting for transfers between devices, to_plane(): lax.all_to_all(x, ('clo', 'head'), split_axis=2, concat_axis=1, tiled=True)  36 us
    all_to_all x4, local copies, waits for them, and re-layouts, to_plane(): lax.all_to_all(x, ('clo', 'head'), split_axis=2, concat_axis=1, tiled=True)  21.8 us
    unnamed x12, local copies, waits for them, and re-layouts  19.6 us
  transfers between devices with their start and end apart: 7, of which 4 were waited for; matrix products, arithmetic and copies ran while one was open for 21% of the time, Pallas kernels for 28%

profile of v4, /device:TPU:20, one launch (start us, length us, event | category | flops | bytes accessed | tf_op | source)
XLA Modules:
  0.0 415.4 jit_solution(15238931674098175523)
XLA Ops:
  0.6 3.2 copy.33
  3.9 4.1 copy.34
  10.3 35.4 %copy.36 = bf16[2,128,8192]{1,0,2:T(2,128)(2,1)} copy(bf16[2,128,8192]{1,2,0:T(8,128)(2,1)S(1)} %bitcast.57) | data formatting | bytes 8388608 | tf_op jit(solution)/shard_map/reshape | solution.py:149
  45.7 4.9 %all-to-all-start.1 = ((bf16[2,128,8192]{1,0,2:T(2,128)(2,1)}), bf16[2,128,8192]{1,0,2:T(2,128)(2,1)}, u32[]{:S(2)}, u32[]{:S(2)}) async-start(bf16[2,128,8192]{1,0,2:T(2,128)(2,1)} %copy.36), calls=%async_computation.1 | async-start | bytes 8388608 | tf_op jit(solution)/shard_map/all_to_all | solution.py:150
  50.7 3.2 copy.27
  53.9 4.1 copy.28
  60.3 35.4 %copy.30 = bf16[2,128,8192]{1,0,2:T(2,128)(2,1)} copy(bf16[2,128,8192]{1,2,0:T(8,128)(2,1)S(1)} %bitcast.58) | data formatting | bytes 8388608 | tf_op jit(solution)/shard_map/reshape | solution.py:149
  95.8 2.7 all-to-all-done.1
  98.5 5.0 %all-to-all-start = ((bf16[2,128,8192]{1,0,2:T(2,128)(2,1)}), bf16[2,128,8192]{1,0,2:T(2,128)(2,1)}, u32[]{:S(2)}, u32[]{:S(2)}) async-start(bf16[2,128,8192]{1,0,2:T(2,128)(2,1)} %copy.30), calls=%async_computation | async-start | bytes 8388608 | tf_op jit(solution)/shard_map/all_to_all | solution.py:150
  103.5 4.7 %copy.37 = bf16[2,128,8192]{1,2,0:T(8,128)(2,1)} copy(bf16[2,128,8192]{1,0,2:T(2,128)(2,1)} %all-to-all-done.1) | data formatting | bytes 8388608 | tf_op jit(solution)/shard_map/all_to_all | solution.py:150
  108.2 6.2 %copy.38 = bf16[2,8,128,1024]{3,2,1,0:T(8,128)(2,1)} copy(bf16[2,8,128,1024]{2,3,1,0:T(8,128)(2,1)} %bitcast.59) | data formatting | bytes 8388608 | tf_op jit(solution)/shard_map/all_to_all | solution.py:150
  114.4 3.5 collective-permute-start
  118.1 33.2 %all-to-all-done = bf16[2,128,8192]{1,0,2:T(2,128)(2,1)} async-done(((bf16[2,128,8192]{1,0,2:T(2,128)(2,1)}), bf16[2,128,8192]{1,0,2:T(2,128)(2,1)}, u32[]{:S(2)}, u32[]{:S(2)}) %all-to-all-start) | async-done | bytes 4194336 | tf_op jit(solution)/shard_map/all_to_all | solution.py:150
  151.3 4.7 %copy.31 = bf16[2,128,8192]{1,2,0:T(8,128)(2,1)} copy(bf16[2,128,8192]{1,0,2:T(2,128)(2,1)} %all-to-all-done) | data formatting | bytes 8388608 | tf_op jit(solution)/shard_map/all_to_all | solution.py:150
  156.0 6.2 %copy.32 = bf16[2,8,128,1024]{3,2,1,0:T(8,128)(2,1)} copy(bf16[2,8,128,1024]{2,3,1,0:T(8,128)(2,1)} %bitcast.60) | data formatting | bytes 8388608 | tf_op jit(solution)/shard_map/all_to_all | solution.py:150
  171.9 37.3 %collective-permute-done.refs_2_.refs_4_.refs_6_.refs_8_.refs_10_.refs_12_.refs_14_.refs_16_.refs_18_.refs_20_ = bf16[2,1024,1024]{2,1,0:T(8,128)(2,1)} collective-permute-done((bf16[2,1024,1024]{2,1,0:T(8,128)(2,1)}, bf16[2,1024,1024]{2,1,0:T(8,128)(2,1)}, u32[]{:S(2)}, u32[]{:S(2)}) %collective-permute-start) | collective-permute-done | bytes 4194336 | tf_op jit(solution)/shard_map/ppermute | solution.py:21
  209.2 61.1 %attn_query_side.1 = (bf16[1024,1024]{1,0:T(8,128)(2,1)}, f32[8,2,1024]{2,1,0:T(2,128)}) custom-call(bf16[2,1024,1024]{2,1,0:T(8,128)(2,1)} %bitcast.45, bf16[2,1024,1024]{2,1,0:T(8,128)(2,1)} %bitcast.46, bf16[2,1024,1024]{2,1,0:T(8,128)(2,1)} %collective-permute-done.refs_2_.refs_4_.refs_6_.refs_8_.refs_10_.refs_12_.refs_14_.refs_16_.refs_18_.refs_20_, ...), custom_call_target="tpu_custom_call" | custom-call | tf_op jit(solution)/shard_map/attn_query_side/pallas_call | solution.py:201
  270.3 3.8 all-to-all-start.2
  276.5 4.0 pad_maximum_fusion.1.refs_32_
  281.1 54.2 %attn_key_side.1 = bf16[2,1024,1024]{2,1,0:T(8,128)(2,1)} custom-call(bf16[2,1024,1024]{2,1,0:T(8,128)(2,1)} %bitcast.42, bf16[2,1024,1024]{2,1,0:T(8,128)(2,1)} %bitcast.43, bf16[2,1024,1024]{2,1,0:T(8,128)(2,1)} %bitcast.47, ...), custom_call_target="tpu_custom_call" | custom-call | tf_op jit(solution)/shard_map/attn_key_side/pallas_call | solution.py:216
  335.3 8.5 %copy.40 = bf16[2,1024,1024]{2,0,1:T(2,128)(2,1)} copy(bf16[2,1024,1024]{2,1,0:T(8,128)(2,1)} %attn_key_side.1) | data formatting | bytes 8388608 | tf_op jit(solution)/shard_map/attn_key_side/pallas_call | solution.py:216
  343.8 5.1 %all-to-all-start.3 = ((bf16[2,1024,1024]{2,0,1:T(2,128)(2,1)}), bf16[2,1024,1024]{2,0,1:T(2,128)(2,1)}, u32[]{:S(2)}, u32[]{:S(2)}) async-start(bf16[2,1024,1024]{2,0,1:T(2,128)(2,1)} %copy.40), calls=%async_computation.3 | async-start | bytes 8388608 | tf_op jit(solution)/shard_map/all_to_all | solution.py:227
  350.4 46.4 %all-to-all-done.3 = bf16[2,1024,1024]{2,0,1:T(2,128)(2,1)} async-done(((bf16[2,1024,1024]{2,0,1:T(2,128)(2,1)}), bf16[2,1024,1024]{2,0,1:T(2,128)(2,1)}, u32[]{:S(2)}, u32[]{:S(2)}) %all-to-all-start.3) | async-done | bytes 4194336 | tf_op jit(solution)/shard_map/all_to_all | solution.py:227
  396.9 8.8 %fusion = (bf16[1,256,4,1024]{3,0,1,2:T(2,128)(2,1)S(1)}, bf16[1,256,4,1024]{3,0,1,2:T(2,128)(2,1)S(1)}) fusion(bf16[2,256,4,1024]{3,0,1,2:T(2,128)(2,1)} %bitcast.17), kind=kLoop, calls=%fused_computation.25 | loop fusion | bytes 8388608 | tf_op jit(solution)/shard_map/slice | solution.py:228
  (39 shorter events, 28.8 us)
Async XLA Ops:
  45.7 52.8 %all-to-all-start.1 = ((bf16[2,128,8192]{1,0,2:T(2,128)(2,1)}), bf16[2,128,8192]{1,0,2:T(2,128)(2,1)}, u32[]{:S(2)}, u32[]{:S(2)}) async-start(bf16[2,128,8192]{1,0,2:T(2,128)(2,1)} %copy.36), calls=%async_computation.1 | async-start | bytes 8388608 | tf_op jit(solution)/shard_map/all_to_all | solution.py:150
  98.5 52.8 %all-to-all-start = ((bf16[2,128,8192]{1,0,2:T(2,128)(2,1)}), bf16[2,128,8192]{1,0,2:T(2,128)(2,1)}, u32[]{:S(2)}, u32[]{:S(2)}) async-start(bf16[2,128,8192]{1,0,2:T(2,128)(2,1)} %copy.30), calls=%async_computation | async-start | bytes 8388608 | tf_op jit(solution)/shard_map/all_to_all | solution.py:150
  108.2 9.8 %copy-start.2 = (s32[4096]{0:T(1024)S(1)}, s32[4096]{0:T(1024)}, u32[]{:S(2)}) copy-start(s32[4096]{0:T(1024)} %param.9) | copy-start | bytes 49156
  114.4 94.8 %collective-permute-start = (bf16[2,1024,1024]{2,1,0:T(8,128)(2,1)}, bf16[2,1024,1024]{2,1,0:T(8,128)(2,1)}, u32[]{:S(2)}, u32[]{:S(2)}) collective-permute-start(bf16[2,1024,1024]{2,1,0:T(8,128)(2,1)} %bitcast.31), channel_id=1, source_target_pairs={{0,8},{8,16},{16,24},{1,9},{9,17},{17,25},{2,10},{10,18},{18,26},{... | collective-permute-start | bytes 12582920 | tf_op jit(solution)/shard_map/ppermute | solution.py:21
  162.2 118.3 %collective-permute-start.1 = (bf16[2,1024,1024]{2,1,0:T(8,128)(2,1)}, bf16[2,1024,1024]{2,1,0:T(8,128)(2,1)}, u32[]{:S(2)}, u32[]{:S(2)}) collective-permute-start(bf16[2,1024,1024]{2,1,0:T(8,128)(2,1)} %bitcast.44), channel_id=1, source_target_pairs={{8,0},{16,8},{24,16},{9,1},{17,9},{25,17},{10,2},{18,10},{26,18},{... | collective-permute-start | bytes 12582920 | tf_op jit(solution)/shard_map/ppermute | solution.py:21
  270.3 3.8 copy-start
  270.3 73.5 %all-to-all-start.2 = ((bf16[4,256,1024]{2,1,0:T(8,128)(2,1)}), bf16[4,256,1024]{2,1,0:T(8,128)(2,1)S(1)}, u32[]{:S(2)}, u32[]{:S(2)}) async-start(bf16[4,256,1024]{2,1,0:T(8,128)(2,1)} %bitcast.68), calls=%async_computation.2 | async-start | bytes 4194304 | tf_op jit(solution)/shard_map/all_to_all | solution.py:226
  274.1 6.4 %collective-permute-start.2 = (f32[8,2,1024]{2,1,0:T(2,128)S(1)}, f32[8,2,1024]{2,1,0:T(2,128)S(1)}, u32[]{:S(2)}, u32[]{:S(2)}) collective-permute-start(f32[8,2,1024]{2,1,0:T(2,128)S(1)} %copy-done), channel_id=1, source_target_pairs={{8,0},{16,8},{24,16},{9,1},{17,9},{25,17},{10,2},{18,10},{26,18},{... | collective-permute-start | bytes 196616 | tf_op jit(solution)/shard_map/ppermute | solution.py:21
  280.5 0.6 copy-start.1
  343.8 53.1 %all-to-all-start.3 = ((bf16[2,1024,1024]{2,0,1:T(2,128)(2,1)}), bf16[2,1024,1024]{2,0,1:T(2,128)(2,1)}, u32[]{:S(2)}, u32[]{:S(2)}) async-start(bf16[2,1024,1024]{2,0,1:T(2,128)(2,1)} %copy.40), calls=%async_computation.3 | async-start | bytes 8388608 | tf_op jit(solution)/shard_map/all_to_all | solution.py:227

commit v5 on v2

--- a/solution.py
+++ b/solution.py
@@ -126,30 +126,16 @@
     chi = lax.axis_index("chi")
     plane_start = chi * plane
 
-    def to_plane(x):
-        x = x.reshape(tok_in, head_n, clo_n, width).transpose(0, 2, 1, 3).reshape(tok_in, full_width)
+    def to_plane(a, b):
+        a = a.reshape(tok_in, head_n, clo_n, 1, width)
+        b = b.reshape(tok_in, head_n, clo_n, 1, width)
+        x = jnp.concatenate([a, b], axis=3).transpose(0, 2, 1, 3, 4).reshape(tok_in, 2 * full_width)
         return lax.all_to_all(x, ("clo", "head"), split_axis=1, concat_axis=0, tiled=True)
 
-    keys = to_plane(attn_k)
-    values = to_plane(attn_v)
-    query = to_plane(attn_q)
-    dout = to_plane(attn_dout)
-
-    k_parts, v_parts = [], []
-    for shift in range(reach, 0, -1):
-        far_k, far_v = shifted((keys, values), "chi", shift)
-        k_parts.append(far_k)
-        v_parts.append(far_v)
-    k_win = jnp.concatenate(k_parts + [keys], axis=0)
-    v_win = jnp.concatenate(v_parts + [values], axis=0)
-
-    q_parts, d_parts = [], []
-    for shift in range(1, reach + 1):
-        far_q, far_d = shifted((query, dout), "chi", -shift)
-        q_parts.append(far_q)
-        d_parts.append(far_d)
-    q_win = jnp.concatenate([query] + q_parts, axis=0)
-    d_win = jnp.concatenate([dout] + d_parts, axis=0)
+    kv = to_plane(attn_k, attn_v)
+    kv_win = jnp.concatenate([shifted(kv, "chi", shift) for shift in range(reach, 0, -1)] + [kv], axis=0)
+    qd = to_plane(attn_q, attn_dout)
+    qd_win = jnp.concatenate([qd] + [shifted(qd, "chi", -shift) for shift in range(1, reach + 1)], axis=0)
 
     pad = (reach + 1) * plane
     docs_pad = jnp.concatenate([
@@ -177,11 +163,14 @@
     own_spec = pl.BlockSpec((TILE, HEAD_DIM), lambda i, h: (i, h))
     base = reach * n_tiles - tile_reach
 
-    def kwin_spec(j):
-        return pl.BlockSpec((TILE, HEAD_DIM), lambda i, h: (base + i + j, h))
-
-    def qwin_spec(j):
-        return pl.BlockSpec((TILE, HEAD_DIM), lambda i, h: (i + j, h))
+    def col_spec(off):
+        return pl.BlockSpec((TILE, HEAD_DIM), lambda i, h: (i, h + off))
+
+    def kwin_spec(j, off):
+        return pl.BlockSpec((TILE, HEAD_DIM), lambda i, h: (base + i + j, h + off))
+
+    def qwin_spec(j, off):
+        return pl.BlockSpec((TILE, HEAD_DIM), lambda i, h: (i + j, h + off))
 
     def ldwin_spec(j):
         return pl.BlockSpec((None, 2, TILE), lambda i, h: (h, 0, i + j))
@@ -198,11 +187,12 @@
             jax.ShapeDtypeStruct((heads_p, 2, plane), jnp.float32),
         ),
         grid=grid,
-        in_specs=[own_spec, own_spec] + [kwin_spec(j) for j in range(nblk)] * 2 + [bias_spec],
+        in_specs=[col_spec(0), col_spec(heads_p)] + [kwin_spec(j, 0) for j in range(nblk)]
+        + [kwin_spec(j, heads_p) for j in range(nblk)] + [bias_spec],
         out_specs=(own_spec, ld_spec),
         compiler_params=params,
         name="attn_query_side",
-    )(query, dout, *([k_win] * nblk), *([v_win] * nblk), q_bias)
+    )(qd, qd, *([kv_win] * (2 * nblk)), q_bias)
 
     ld_parts = [ld]
     for shift in range(1, reach + 1):
@@ -216,12 +206,12 @@
             jax.ShapeDtypeStruct((plane, width), jnp.bfloat16),
         ),
         grid=grid,
-        in_specs=[own_spec, own_spec] + [qwin_spec(j) for j in range(nblk)] * 2
-        + [ldwin_spec(j) for j in range(nblk)] + [bias_spec],
+        in_specs=[col_spec(0), col_spec(heads_p)] + [qwin_spec(j, 0) for j in range(nblk)]
+        + [qwin_spec(j, heads_p) for j in range(nblk)] + [ldwin_spec(j) for j in range(nblk)] + [bias_spec],
         out_specs=(own_spec, own_spec),
         compiler_params=params,
         name="attn_key_side",
-    )(keys, values, *([q_win] * nblk), *([d_win] * nblk), *([ld_win] * nblk), k_bias)
+    )(kv, kv, *([qd_win] * (2 * nblk)), *([ld_win] * nblk), k_bias)
 
     def from_plane(x):
         return lax.all_to_all(x, "clo", split_axis=0, concat_axis=1, tiled=True)

time: 387 us -> 377 us (0.974)
  waiting for transfers between devices: 140 us -> 124 us
  starting transfers between devices: 40.9 us -> 26.4 us
  local copies, waits for them, and re-layouts: 38.6 us -> 51 us
  other arithmetic: 33.4 us -> 38.1 us
  Pallas kernels: 101 us -> 105 us
    ppermute x5 -> x3, waiting for transfers between devices: 58.5 us -> 37.2 us  [shifted(): lax.ppermute(value, axis, [(source, source + steps) for source in range(l...]
    all_to_all x0 -> x2, local copies, waits for them, and re-layouts: none -> 15.6 us  [to_plane(): lax.all_to_all(x, ('clo', 'head'), split_axis=1, concat_axis=0, tiled=True)]
    transpose x0 -> x2, other arithmetic: none -> 9.46 us  [to_plane(): jnp.concatenate([a, b], axis=3).transpose(0, 2, 1, 3, 4)]
    all_to_all x4 -> x2, starting transfers between devices: 18.6 us -> 9.96 us  [to_plane(): lax.all_to_all(x, ('clo', 'head'), split_axis=1, concat_axis=0, tiled=True)]
    ppermute x5 -> x3, starting transfers between devices: 14.2 us -> 8.39 us  [shifted(): lax.ppermute(value, axis, [(source, source + steps) for source in range(l...]
    all_to_all x4 -> x2, waiting for transfers between devices: 59.9 us -> 65.3 us  [to_plane(): lax.all_to_all(x, ('clo', 'head'), split_axis=1, concat_axis=0, tiled=True)]
    transpose x4 -> x2, local copies, waits for them, and re-layouts: 14.7 us -> 12.6 us  [to_plane(): jnp.concatenate([a, b], axis=3).transpose(0, 2, 1, 3, 4)]
    concatenate x4 -> x2, other arithmetic: 18.3 us -> 16.7 us  [the longest x1 8.37 us: _per_device(): jnp.concatenate([qd] + [shifted(qd, 'chi', -shift) for shift in range(1,...]
  transfers between devices with their start and end apart: 11 -> 7, of which waited for: 7 -> 4; matrix products, arithmetic and copies ran while one was open for 16% -> 14% of each run, Pallas kernels for 26% -> 28%
where the time goes in v5:
time: 377 us; the launch traced here: 376 us
  waiting for transfers between devices  124 us (33%)
  Pallas kernels  105 us (28%)
  local copies, waits for them, and re-layouts  51 us (14%)
  other arithmetic  38.1 us (10%)
  blocking collectives  30.2 us (8%)
  starting transfers between devices  26.4 us (7%)
    all_to_all x2, waiting for transfers between devices, to_plane(): lax.all_to_all(x, ('clo', 'head'), split_axis=1, concat_axis=0, tiled=True)  65.3 us
    pallas_call x1, Pallas kernels, _per_device(): pl.pallas_call(_query_side_kernel(nblk, scale), out_shape=(jax.ShapeDtype...  56.9 us
    pallas_call x1, Pallas kernels, _per_device(): pl.pallas_call(_key_side_kernel(nblk, scale), out_shape=(jax.ShapeDtypeSt...  47.9 us
    ppermute x3, waiting for transfers between devices, shifted(): lax.ppermute(value, axis, [(source, source + steps) for source in range(l...  37.2 us
    all_to_all x1, blocking collectives, from_plane(): return lax.all_to_all(x, 'clo', split_axis=0, concat_axis=1, tiled=True)  30.2 us
    all_to_all x2, waiting for transfers between devices, from_plane(): return lax.all_to_all(x, 'clo', split_axis=0, concat_axis=1, tiled=True)  21.9 us
    all_to_all x2, local copies, waits for them, and re-layouts, to_plane(): lax.all_to_all(x, ('clo', 'head'), split_axis=1, concat_axis=0, tiled=True)  15.6 us
    transpose x2, local copies, waits for them, and re-layouts, to_plane(): jnp.concatenate([a, b], axis=3).transpose(0, 2, 1, 3, 4)  12.6 us
  transfers between devices with their start and end apart: 7, of which 4 were waited for; matrix products, arithmetic and copies ran while one was open for 14% of the time, Pallas kernels for 28%

profile of v5, /device:TPU:20, one launch (start us, length us, event | category | flops | bytes accessed | tf_op | source)
XLA Modules:
  0.0 375.8 jit_solution(6097894514822171659)
XLA Ops:
  0.6 3.3 reshape.100
  4.0 4.5 %reshape.99 = bf16[128,2,4,1,1024]{4,2,1,0,3:T(4,128)(2,1)} reshape(bf16[128,8192]{1,0:T(8,128)(2,1)} %param.6) | data formatting | bytes 4194304 | tf_op jit(solution)/shard_map/reshape | solution.py:130
  8.4 4.7 %maximum_bitcast_fusion.1 = bf16[128,4,2,2,1024]{4,1,2,0,3:T(4,128)(2,1)S(1)} fusion(bf16[128,2,4,1,1024]{4,2,1,0,3:T(4,128)(2,1)S(1)} %reshape.100, bf16[128,2,4,1,1024]{4,2,1,0,3:T(4,128)(2,1)} %reshape.99), kind=kLoop, calls=%fused_computation.5 | loop fusion | flops 2097152 | bytes 8388608 | tf_op jit(solution)/shard_map/transpose | solution.py:132
  13.2 6.3 %copy.9 = bf16[128,4,2,2,1024]{4,3,0,2,1:T(2,128)(2,1)} copy(bf16[128,4,2,2,1024]{4,1,2,0,3:T(4,128)(2,1)S(1)} %maximum_bitcast_fusion.1) | data formatting | bytes 8388608 | tf_op jit(solution)/shard_map/transpose | solution.py:132
  19.5 7.8 %all_to_all.74 = bf16[128,8,2048]{2,0,1:T(8,128)(2,1)} reshape(bf16[128,4,2,2,1024]{4,3,0,2,1:T(2,128)(2,1)} %copy.9) | data formatting | bytes 8388608 | tf_op jit(solution)/shard_map/all_to_all | solution.py:133
  27.3 5.0 %all-to-all-start.1 = ((bf16[128,8,2048]{2,0,1:T(8,128)(2,1)}), bf16[128,8,2048]{2,0,1:T(8,128)(2,1)}, u32[]{:S(2)}, u32[]{:S(2)}) async-start(bf16[128,8,2048]{2,0,1:T(8,128)(2,1)} %all_to_all.74), calls=%async_computation.1 | async-start | bytes 8388608 | tf_op jit(solution)/shard_map/all_to_all | solution.py:133
  35.5 4.5 %reshape.98 = bf16[128,2,4,1,1024]{4,2,1,0,3:T(4,128)(2,1)} reshape(bf16[128,8192]{1,0:T(8,128)(2,1)} %param.8) | data formatting | bytes 4194304 | tf_op jit(solution)/shard_map/reshape | solution.py:131
  40.0 4.7 %maximum_bitcast_fusion = bf16[128,4,2,2,1024]{4,1,2,0,3:T(4,128)(2,1)S(1)} fusion(bf16[128,2,4,1,1024]{4,2,1,0,3:T(4,128)(2,1)} %reshape.98, bf16[128,2,4,1,1024]{4,2,1,0,3:T(4,128)(2,1)S(1)} %reshape.97), kind=kLoop, calls=%fused_computation.4 | loop fusion | flops 2097152 | bytes 8388608 | tf_op jit(solution)/shard_map/transpose | solution.py:132
  44.7 6.3 %copy.8 = bf16[128,4,2,2,1024]{4,3,0,2,1:T(2,128)(2,1)} copy(bf16[128,4,2,2,1024]{4,1,2,0,3:T(4,128)(2,1)S(1)} %maximum_bitcast_fusion) | data formatting | bytes 8388608 | tf_op jit(solution)/shard_map/transpose | solution.py:132
  51.1 7.8 %all_to_all.70 = bf16[128,8,2048]{2,0,1:T(8,128)(2,1)} reshape(bf16[128,4,2,2,1024]{4,3,0,2,1:T(2,128)(2,1)} %copy.8) | data formatting | bytes 8388608 | tf_op jit(solution)/shard_map/all_to_all | solution.py:133
  58.9 21.1 %all-to-all-done.1 = bf16[128,8,2048]{2,0,1:T(8,128)(2,1)} async-done(((bf16[128,8,2048]{2,0,1:T(8,128)(2,1)}), bf16[128,8,2048]{2,0,1:T(8,128)(2,1)}, u32[]{:S(2)}, u32[]{:S(2)}) %all-to-all-start.1) | async-done | bytes 4194336 | tf_op jit(solution)/shard_map/all_to_all | solution.py:133
  80.0 5.0 %all-to-all-start = ((bf16[128,8,2048]{2,0,1:T(8,128)(2,1)}), bf16[128,8,2048]{2,0,1:T(8,128)(2,1)}, u32[]{:S(2)}, u32[]{:S(2)}) async-start(bf16[128,8,2048]{2,0,1:T(8,128)(2,1)} %all_to_all.70), calls=%async_computation | async-start | bytes 8388608 | tf_op jit(solution)/shard_map/all_to_all | solution.py:133
  85.0 3.5 collective-permute-start
  88.7 44.2 %all-to-all-done = bf16[128,8,2048]{2,0,1:T(8,128)(2,1)} async-done(((bf16[128,8,2048]{2,0,1:T(8,128)(2,1)}), bf16[128,8,2048]{2,0,1:T(8,128)(2,1)}, u32[]{:S(2)}, u32[]{:S(2)}) %all-to-all-start) | async-done | bytes 4194336 | tf_op jit(solution)/shard_map/all_to_all | solution.py:133
  142.7 37.2 %collective-permute-done = bf16[1024,2048]{1,0:T(8,128)(2,1)} collective-permute-done((bf16[1024,2048]{1,0:T(8,128)(2,1)}, bf16[1024,2048]{1,0:T(8,128)(2,1)}, u32[]{:S(2)}, u32[]{:S(2)}) %collective-permute-start) | collective-permute-done | bytes 4194336 | tf_op jit(solution)/shard_map/ppermute | solution.py:21
  179.9 8.4 %pad_maximum_fusion.refs_2_.refs_3_.refs_4_.refs_5_.refs_6_.refs_7_.refs_8_.refs_9_.refs_10_.refs_11_ = bf16[2048,2048]{1,0:T(8,128)(2,1)} fusion(bf16[1024,2048]{1,0:T(8,128)(2,1)} %bitcast.5.refs_0_.refs_1_, bf16[1024,2048]{1,0:T(8,128)(2,1)} %collective-permute-done), kind=kLoop, calls=%fused_computation | loop fusion | flops 16777216 | bytes 16777216 | tf_op jit(solution)/shard_map/concatenate | solution.py:136
  188.2 56.9 %attn_query_side.1 = (bf16[1024,1024]{1,0:T(8,128)(2,1)}, f32[8,2,1024]{2,1,0:T(2,128)}) custom-call(bf16[1024,2048]{1,0:T(8,128)(2,1)} %bitcast.2.refs_0_.refs_1_, bf16[1024,2048]{1,0:T(8,128)(2,1)} %bitcast.2.refs_0_.refs_1_, bf16[2048,2048]{1,0:T(8,128)(2,1)} %pad_maximum_fusion.refs_2_.refs_3_.refs_4_.refs_5_.refs_6_.refs_7_.refs_8_.refs_9_.refs_10_.refs_11_, ...), custom_call_target="tpu_custom_call" | custom-call | tf_op jit(solution)/shard_map/attn_query_side/pallas_call | solution.py:183
  245.1 3.6 all-to-all-start.2
  248.8 4.1 %pad_maximum_fusion.3.refs_17_ = f32[1024,1280]{1,0:T(8,128)} fusion(f32[256,1280]{1,0:T(8,128)S(1)} %get-tuple-element.29, f32[256,1280]{1,0:T(8,128)} %get-tuple-element.32, f32[256,1280]{1,0:T(8,128)} %get-tuple-element.25, f32[256,1280]{1,0:T(8,128)} %get-tuple-element.34), kind=kLoop, calls=%fused_computation.3 | loop fusion | flops 3932160 | bytes 10485760 | tf_op jit(solution)/shard_map/concatenate | solution.py:161
  255.3 8.4 %pad_maximum_fusion.1.refs_2_.refs_3_.refs_4_.refs_5_.refs_6_.refs_7_.refs_8_.refs_9_.refs_10_.refs_11_ = bf16[2048,2048]{1,0:T(8,128)(2,1)} fusion(bf16[1024,2048]{1,0:T(8,128)(2,1)} %collective-permute-done.1, bf16[1024,2048]{1,0:T(8,128)(2,1)} %bitcast.2.refs_0_.refs_1_), kind=kLoop, calls=%fused_computation.1 | loop fusion | flops 16777216 | bytes 16777216 | tf_op jit(solution)/shard_map/concatenate | solution.py:138
  264.3 47.9 %attn_key_side.1 = (bf16[1024,1024]{1,0:T(8,128)(2,1)}, bf16[1024,1024]{1,0:T(8,128)(2,1)}) custom-call(bf16[1024,2048]{1,0:T(8,128)(2,1)} %bitcast.5.refs_0_.refs_1_, bf16[1024,2048]{1,0:T(8,128)(2,1)} %bitcast.5.refs_0_.refs_1_, bf16[2048,2048]{1,0:T(8,128)(2,1)} %pad_maximum_fusion.1.refs_2_.refs_3_.refs_4_.refs_5_.refs_6_.refs_7_.refs_8_.refs_9_.refs_10_.refs_11_, ...), custom_call_target="tpu_custom_call" | custom-call | tf_op jit(solution)/shard_map/attn_key_side/pallas_call | solution.py:202
  312.3 30.2 %all_to_all.95 = bf16[4,256,1024]{2,1,0:T(8,128)(2,1)} all-to-all(bf16[4,256,1024]{2,1,0:T(8,128)(2,1)} %bitcast.32), channel_id=1, replica_groups=mesh['chi'=4,'clo'=4,'head'=2] {'clo'}, dimensions={0} | all-to-all | bytes 4194304 | tf_op jit(solution)/shard_map/all_to_all | solution.py:217
  342.4 4.5 %all-to-all-start.4 = ((bf16[4,256,1024]{2,1,0:T(8,128)(2,1)}), bf16[4,256,1024]{2,1,0:T(8,128)(2,1)}, u32[]{:S(2)}, u32[]{:S(2)}) async-start(bf16[4,256,1024]{2,1,0:T(8,128)(2,1)} %bitcast.29), calls=%async_computation.4 | async-start | bytes 4194304 | tf_op jit(solution)/shard_map/all_to_all | solution.py:217
  350.7 21.9 %all-to-all-done.4 = bf16[4,256,1024]{2,1,0:T(8,128)(2,1)} async-done(((bf16[4,256,1024]{2,1,0:T(8,128)(2,1)}), bf16[4,256,1024]{2,1,0:T(8,128)(2,1)}, u32[]{:S(2)}, u32[]{:S(2)}) %all-to-all-start.4) | async-done | bytes 2097184 | tf_op jit(solution)/shard_map/all_to_all | solution.py:217
  (35 shorter events, 23.3 us)
Async XLA Ops:
  27.3 52.8 %all-to-all-start.1 = ((bf16[128,8,2048]{2,0,1:T(8,128)(2,1)}), bf16[128,8,2048]{2,0,1:T(8,128)(2,1)}, u32[]{:S(2)}, u32[]{:S(2)}) async-start(bf16[128,8,2048]{2,0,1:T(8,128)(2,1)} %all_to_all.74), calls=%async_computation.1 | async-start | bytes 8388608 | tf_op jit(solution)/shard_map/all_to_all | solution.py:133
  58.9 29.7 %copy-start.2 = (s32[4096]{0:T(1024)S(1)}, s32[4096]{0:T(1024)}, u32[]{:S(2)}) copy-start(s32[4096]{0:T(1024)} %param.9) | copy-start | bytes 49156
  80.0 52.8 %all-to-all-start = ((bf16[128,8,2048]{2,0,1:T(8,128)(2,1)}), bf16[128,8,2048]{2,0,1:T(8,128)(2,1)}, u32[]{:S(2)}, u32[]{:S(2)}) async-start(bf16[128,8,2048]{2,0,1:T(8,128)(2,1)} %all_to_all.70), calls=%async_computation | async-start | bytes 8388608 | tf_op jit(solution)/shard_map/all_to_all | solution.py:133
  85.0 94.8 %collective-permute-start = (bf16[1024,2048]{1,0:T(8,128)(2,1)}, bf16[1024,2048]{1,0:T(8,128)(2,1)}, u32[]{:S(2)}, u32[]{:S(2)}) collective-permute-start(bf16[1024,2048]{1,0:T(8,128)(2,1)} %bitcast.5.refs_0_.refs_1_), channel_id=1, source_target_pairs={{0,8},{8,16},{16,24},{1,9},{9,17},{17,25},{2,10},{10,18},{18,26},{... | collective-permute-start | bytes 12582920 | tf_op jit(solution)/shard_map/ppermute | solution.py:21
  132.9 122.4 %collective-permute-start.1 = (bf16[1024,2048]{1,0:T(8,128)(2,1)}, bf16[1024,2048]{1,0:T(8,128)(2,1)}, u32[]{:S(2)}, u32[]{:S(2)}) collective-permute-start(bf16[1024,2048]{1,0:T(8,128)(2,1)} %bitcast.2.refs_0_.refs_1_), channel_id=1, source_target_pairs={{8,0},{16,8},{24,16},{9,1},{17,9},{25,17},{10,2},{18,10},{26,18},{... | collective-permute-start | bytes 12582920 | tf_op jit(solution)/shard_map/ppermute | solution.py:21
  245.1 67.1 %all-to-all-start.2 = ((bf16[4,256,1024]{2,1,0:T(8,128)(2,1)}), bf16[4,256,1024]{2,1,0:T(8,128)(2,1)S(1)}, u32[]{:S(2)}, u32[]{:S(2)}) async-start(bf16[4,256,1024]{2,1,0:T(8,128)(2,1)} %bitcast.28), calls=%async_computation.2 | async-start | bytes 4194304 | tf_op jit(solution)/shard_map/all_to_all | solution.py:217
  248.8 4.1 %copy-start.1 = (f32[8,2,1024]{2,1,0:T(2,128)S(1)}, f32[8,2,1024]{2,1,0:T(2,128)}, u32[]{:S(2)}) copy-start(f32[8,2,1024]{2,1,0:T(2,128)} %get-tuple-element.8) | copy-start | bytes 196612
  252.9 10.7 %collective-permute-start.2 = (f32[8,2,1024]{2,1,0:T(2,128)S(1)}, f32[8,2,1024]{2,1,0:T(2,128)S(1)}, u32[]{:S(2)}, u32[]{:S(2)}) collective-permute-start(f32[8,2,1024]{2,1,0:T(2,128)S(1)} %copy-done.1), channel_id=1, source_target_pairs={{8,0},{16,8},{24,16},{9,1},{17,9},{25,17},{10,2},{18,10},{26,18},{... | collective-permute-start | bytes 196616 | tf_op jit(solution)/shard_map/ppermute | solution.py:21
  342.4 30.2 %all-to-all-start.4 = ((bf16[4,256,1024]{2,1,0:T(8,128)(2,1)}), bf16[4,256,1024]{2,1,0:T(8,128)(2,1)}, u32[]{:S(2)}, u32[]{:S(2)}) async-start(bf16[4,256,1024]{2,1,0:T(8,128)(2,1)} %bitcast.29), calls=%async_computation.4 | async-start | bytes 4194304 | tf_op jit(solution)/shard_map/all_to_all | solution.py:217
  346.9 2.3 copy-start

commit v6 on v5

--- a/solution.py
+++ b/solution.py
@@ -74,7 +74,7 @@
         d_refs = refs[2 + nblk:2 + 2 * nblk]
         ld_refs = refs[2 + 2 * nblk:2 + 3 * nblk]
         bias_ref = refs[2 + 3 * nblk]
-        dk_ref, dv_ref = refs[3 + 3 * nblk], refs[4 + 3 * nblk]
+        out_ref = refs[3 + 3 * nblk]
         k = k_ref[...]
         v = v_ref[...]
         dk = None
@@ -95,8 +95,8 @@
             part_v = jnp.dot(prob.astype(jnp.bfloat16), d, preferred_element_type=jnp.float32)
             dk = part_k if dk is None else dk + part_k
             dv = part_v if dv is None else dv + part_v
-        dk_ref[...] = (dk * scale).astype(dk_ref.dtype)
-        dv_ref[...] = dv.astype(dv_ref.dtype)
+        out_ref[:, 0:HEAD_DIM] = (dk * scale).astype(out_ref.dtype)
+        out_ref[:, HEAD_DIM:2 * HEAD_DIM] = dv.astype(out_ref.dtype)
 
     return kernel
 
@@ -199,24 +199,41 @@
         ld_parts.append(shifted(ld, "chi", -shift))
     ld_win = jnp.concatenate(ld_parts, axis=2)
 
-    dk, dv = pl.pallas_call(
-        _key_side_kernel(nblk, scale),
-        out_shape=(
-            jax.ShapeDtypeStruct((plane, width), jnp.bfloat16),
-            jax.ShapeDtypeStruct((plane, width), jnp.bfloat16),
-        ),
-        grid=grid,
-        in_specs=[col_spec(0), col_spec(heads_p)] + [qwin_spec(j, 0) for j in range(nblk)]
-        + [qwin_spec(j, heads_p) for j in range(nblk)] + [ldwin_spec(j) for j in range(nblk)] + [bias_spec],
-        out_specs=(own_spec, own_spec),
-        compiler_params=params,
-        name="attn_key_side",
-    )(kv, kv, *([qd_win] * (2 * nblk)), *([ld_win] * nblk), k_bias)
-
     def from_plane(x):
         return lax.all_to_all(x, "clo", split_axis=0, concat_axis=1, tiled=True)
 
-    return (from_plane(dq), from_plane(dk), from_plane(dv))
+    groups = 2 if heads_p % 2 == 0 else 1
+    hg = heads_p // groups
+    dkv_parts = []
+    for g in range(groups):
+        off = g * hg
+
+        def gcol(extra, off=off):
+            return pl.BlockSpec((TILE, HEAD_DIM), lambda i, h: (i, h + off + extra))
+
+        def gwin(j, extra, off=off):
+            return pl.BlockSpec((TILE, HEAD_DIM), lambda i, h: (i + j, h + off + extra))
+
+        def gld(j, off=off):
+            return pl.BlockSpec((None, 2, TILE), lambda i, h: (h + off, 0, i + j))
+
+        dkv_g = pl.pallas_call(
+            _key_side_kernel(nblk, scale),
+            out_shape=jax.ShapeDtypeStruct((plane, 2 * hg * HEAD_DIM), jnp.bfloat16),
+            grid=(n_tiles, hg),
+            in_specs=[gcol(0), gcol(heads_p)] + [gwin(j, 0) for j in range(nblk)]
+            + [gwin(j, heads_p) for j in range(nblk)] + [gld(j) for j in range(nblk)] + [bias_spec],
+            out_specs=pl.BlockSpec((TILE, 2 * HEAD_DIM), lambda i, h: (i, h)),
+            compiler_params=params,
+            name="attn_key_side",
+        )(kv, kv, *([qd_win] * (2 * nblk)), *([ld_win] * nblk), k_bias)
+        dkv_parts.append(from_plane(dkv_g).reshape(-1, clo_n, 1, hg, 2, HEAD_DIM))
+
+    dkv = jnp.concatenate(dkv_parts, axis=2)
+    rows = dkv.shape[0]
+    attn_dk = dkv[:, :, :, :, 0, :].reshape(rows, clo_n * width)
+    attn_dv = dkv[:, :, :, :, 1, :].reshape(rows, clo_n * width)
+    return (from_plane(dq), attn_dk, attn_dv)
 
 
 def solution(mesh):

time: 377 us -> 371 us (0.984)
  blocking collectives: 30.2 us -> 0 us
  local copies, waits for them, and re-layouts: 51 us -> 67.9 us
  starting transfers between devices: 26.4 us -> 31.1 us
    all_to_all x1 -> x0, blocking collectives: 30.2 us -> none  [from_plane(): return lax.all_to_all(x, 'clo', split_axis=0, concat_axis=1, tiled=True)]
    reshape x0 -> x2, local copies, waits for them, and re-layouts: none -> 7.66 us  [_per_device(): dkv_parts.append(from_plane(dkv_g).reshape(-1, clo_n, 1, hg, 2, HEAD_DIM))]
    another operation x0 -> x2, local copies, waits for them, and re-layouts: none -> 7.25 us  [the longest x1 4.47 us: _per_device(): attn_dk = dkv[:, :, :, :, 0, :].reshape(rows, clo_n * width)]
    all_to_all x2 -> x3, starting transfers between devices: 8.07 us -> 12.8 us  [from_plane(): return lax.all_to_all(x, 'clo', split_axis=0, concat_axis=1, tiled=True)]
    all_to_all x3 -> x1, local copies, waits for them, and re-layouts: 6.21 us -> 1.56 us  [from_plane(): return lax.all_to_all(x, 'clo', split_axis=0, concat_axis=1, tiled=True)]
    pallas_call x1 -> x2, Pallas kernels: 47.9 us -> 51 us  [_per_device(): pl.pallas_call(_key_side_kernel(nblk, scale), out_shape=jax.ShapeDtypeStr...]
    all_to_all x2 -> x3, waiting for transfers between devices: 21.9 us -> 21 us  [from_plane(): return lax.all_to_all(x, 'clo', split_axis=0, concat_axis=1, tiled=True)]
  transfers between devices with their start and end apart: 7 -> 8, of which waited for: 4 -> 5; matrix products, arithmetic and copies ran while one was open for 14% -> 14% of each run, Pallas kernels for 28% -> 29%
where the time goes in v6:
time: 371 us; the launch traced here: 369 us
  waiting for transfers between devices  124 us (33%)
  Pallas kernels  108 us (29%)
  local copies, waits for them, and re-layouts  67.9 us (18%)
  other arithmetic  37.3 us (10%)
  starting transfers between devices  31.1 us (8%)
    all_to_all x2, waiting for transfers between devices, to_plane(): lax.all_to_all(x, ('clo', 'head'), split_axis=1, concat_axis=0, tiled=True)  65.3 us
    pallas_call x1, Pallas kernels, _per_device(): pl.pallas_call(_query_side_kernel(nblk, scale), out_shape=(jax.ShapeDtype...  56.9 us
    pallas_call x2, Pallas kernels, _per_device(): pl.pallas_call(_key_side_kernel(nblk, scale), out_shape=jax.ShapeDtypeStr...  51 us
    ppermute x3, waiting for transfers between devices, shifted(): lax.ppermute(value, axis, [(source, source + steps) for source in range(l...  37.2 us
    all_to_all x3, waiting for transfers between devices, from_plane(): return lax.all_to_all(x, 'clo', split_axis=0, concat_axis=1, tiled=True)  21 us
    all_to_all x2, local copies, waits for them, and re-layouts, to_plane(): lax.all_to_all(x, ('clo', 'head'), split_axis=1, concat_axis=0, tiled=True)  15.6 us
    all_to_all x3, starting transfers between devices, from_plane(): return lax.all_to_all(x, 'clo', split_axis=0, concat_axis=1, tiled=True)  12.8 us
    transpose x2, local copies, waits for them, and re-layouts, to_plane(): jnp.concatenate([a, b], axis=3).transpose(0, 2, 1, 3, 4)  12.6 us
  transfers between devices with their start and end apart: 8, of which 5 were waited for; matrix products, arithmetic and copies ran while one was open for 14% of the time, Pallas kernels for 29%

profile of v6, /device:TPU:20, one launch (start us, length us, event | category | flops | bytes accessed | tf_op | source)
XLA Modules:
  0.0 368.7 jit_solution(18123651710129653338)
XLA Ops:
  4.0 4.5 %reshape.108 = bf16[128,2,4,1,1024]{4,2,1,0,3:T(4,128)(2,1)} reshape(bf16[128,8192]{1,0:T(8,128)(2,1)} %param.7) | data formatting | bytes 4194304 | tf_op jit(solution)/shard_map/reshape | solution.py:131
  8.4 4.7 %maximum_bitcast_fusion.1 = bf16[128,4,2,2,1024]{4,1,2,0,3:T(4,128)(2,1)S(1)} fusion(bf16[128,2,4,1,1024]{4,2,1,0,3:T(4,128)(2,1)} %reshape.108, bf16[128,2,4,1,1024]{4,2,1,0,3:T(4,128)(2,1)S(1)} %reshape.107), kind=kLoop, calls=%fused_computation.5 | loop fusion | flops 2097152 | bytes 8388608 | tf_op jit(solution)/shard_map/transpose | solution.py:132
  13.2 6.3 %copy.9 = bf16[128,4,2,2,1024]{4,3,0,2,1:T(2,128)(2,1)} copy(bf16[128,4,2,2,1024]{4,1,2,0,3:T(4,128)(2,1)S(1)} %maximum_bitcast_fusion.1) | data formatting | bytes 8388608 | tf_op jit(solution)/shard_map/transpose | solution.py:132
  19.5 7.8 %all_to_all.70 = bf16[128,8,2048]{2,0,1:T(8,128)(2,1)} reshape(bf16[128,4,2,2,1024]{4,3,0,2,1:T(2,128)(2,1)} %copy.9) | data formatting | bytes 8388608 | tf_op jit(solution)/shard_map/all_to_all | solution.py:133
  27.2 4.9 %all-to-all-start.1 = ((bf16[128,8,2048]{2,0,1:T(8,128)(2,1)}), bf16[128,8,2048]{2,0,1:T(8,128)(2,1)}, u32[]{:S(2)}, u32[]{:S(2)}) async-start(bf16[128,8,2048]{2,0,1:T(8,128)(2,1)} %all_to_all.70), calls=%async_computation.1 | async-start | bytes 8388608 | tf_op jit(solution)/shard_map/all_to_all | solution.py:133
  35.5 4.5 %reshape.106 = bf16[128,2,4,1,1024]{4,2,1,0,3:T(4,128)(2,1)} reshape(bf16[128,8192]{1,0:T(8,128)(2,1)} %param.8) | data formatting | bytes 4194304 | tf_op jit(solution)/shard_map/reshape | solution.py:131
  40.0 4.7 %maximum_bitcast_fusion = bf16[128,4,2,2,1024]{4,1,2,0,3:T(4,128)(2,1)S(1)} fusion(bf16[128,2,4,1,1024]{4,2,1,0,3:T(4,128)(2,1)} %reshape.106, bf16[128,2,4,1,1024]{4,2,1,0,3:T(4,128)(2,1)S(1)} %reshape.105), kind=kLoop, calls=%fused_computation.4 | loop fusion | flops 2097152 | bytes 8388608 | tf_op jit(solution)/shard_map/transpose | solution.py:132
  44.7 6.3 %copy.8 = bf16[128,4,2,2,1024]{4,3,0,2,1:T(2,128)(2,1)} copy(bf16[128,4,2,2,1024]{4,1,2,0,3:T(4,128)(2,1)S(1)} %maximum_bitcast_fusion) | data formatting | bytes 8388608 | tf_op jit(solution)/shard_map/transpose | solution.py:132
  51.0 7.8 %all_to_all.66 = bf16[128,8,2048]{2,0,1:T(8,128)(2,1)} reshape(bf16[128,4,2,2,1024]{4,3,0,2,1:T(2,128)(2,1)} %copy.8) | data formatting | bytes 8388608 | tf_op jit(solution)/shard_map/all_to_all | solution.py:133
  58.9 21.1 %all-to-all-done.1 = bf16[128,8,2048]{2,0,1:T(8,128)(2,1)} async-done(((bf16[128,8,2048]{2,0,1:T(8,128)(2,1)}), bf16[128,8,2048]{2,0,1:T(8,128)(2,1)}, u32[]{:S(2)}, u32[]{:S(2)}) %all-to-all-start.1) | async-done | bytes 4194336 | tf_op jit(solution)/shard_map/all_to_all | solution.py:133
  80.0 5.0 %all-to-all-start = ((bf16[128,8,2048]{2,0,1:T(8,128)(2,1)}), bf16[128,8,2048]{2,0,1:T(8,128)(2,1)}, u32[]{:S(2)}, u32[]{:S(2)}) async-start(bf16[128,8,2048]{2,0,1:T(8,128)(2,1)} %all_to_all.66), calls=%async_computation | async-start | bytes 8388608 | tf_op jit(solution)/shard_map/all_to_all | solution.py:133
  88.7 44.2 %all-to-all-done = bf16[128,8,2048]{2,0,1:T(8,128)(2,1)} async-done(((bf16[128,8,2048]{2,0,1:T(8,128)(2,1)}), bf16[128,8,2048]{2,0,1:T(8,128)(2,1)}, u32[]{:S(2)}, u32[]{:S(2)}) %all-to-all-start) | async-done | bytes 4194336 | tf_op jit(solution)/shard_map/all_to_all | solution.py:133
  142.6 37.2 %collective-permute-done = bf16[1024,2048]{1,0:T(8,128)(2,1)} collective-permute-done((bf16[1024,2048]{1,0:T(8,128)(2,1)}, bf16[1024,2048]{1,0:T(8,128)(2,1)}, u32[]{:S(2)}, u32[]{:S(2)}) %collective-permute-start) | collective-permute-done | bytes 4194336 | tf_op jit(solution)/shard_map/ppermute | solution.py:21
  179.8 8.4 %pad_maximum_fusion.refs_2_.refs_3_.refs_4_.refs_5_.refs_6_.refs_7_.refs_8_.refs_9_.refs_10_.refs_11_ = bf16[2048,2048]{1,0:T(8,128)(2,1)} fusion(bf16[1024,2048]{1,0:T(8,128)(2,1)} %bitcast.5.refs_0_.refs_1_, bf16[1024,2048]{1,0:T(8,128)(2,1)} %collective-permute-done), kind=kLoop, calls=%fused_computation | loop fusion | flops 16777216 | bytes 16777216 | tf_op jit(solution)/shard_map/concatenate | solution.py:136
  188.2 56.9 %attn_query_side.1 = (bf16[1024,1024]{1,0:T(8,128)(2,1)}, f32[8,2,1024]{2,1,0:T(2,128)}) custom-call(bf16[1024,2048]{1,0:T(8,128)(2,1)} %bitcast.2.refs_0_.refs_1_, bf16[1024,2048]{1,0:T(8,128)(2,1)} %bitcast.2.refs_0_.refs_1_, bf16[2048,2048]{1,0:T(8,128)(2,1)} %pad_maximum_fusion.refs_2_.refs_3_.refs_4_.refs_5_.refs_6_.refs_7_.refs_8_.refs_9_.refs_10_.refs_11_, ...), custom_call_target="tpu_custom_call" | custom-call | tf_op jit(solution)/shard_map/attn_query_side/pallas_call | solution.py:183
  248.7 4.0 %pad_maximum_fusion.3.refs_17_ = f32[1024,1280]{1,0:T(8,128)} fusion(f32[256,1280]{1,0:T(8,128)S(1)} %get-tuple-element.27, f32[256,1280]{1,0:T(8,128)} %get-tuple-element.30, f32[256,1280]{1,0:T(8,128)} %get-tuple-element.23, f32[256,1280]{1,0:T(8,128)} %get-tuple-element.32), kind=kLoop, calls=%fused_computation.3 | loop fusion | flops 3932160 | bytes 10485760 | tf_op jit(solution)/shard_map/concatenate | solution.py:161
  255.1 8.4 %pad_maximum_fusion.1.refs_2_.refs_3_.refs_4_.refs_5_.refs_6_.refs_7_.refs_8_.refs_9_.refs_10_.refs_11_ = bf16[2048,2048]{1,0:T(8,128)(2,1)} fusion(bf16[1024,2048]{1,0:T(8,128)(2,1)} %collective-permute-done.1, bf16[1024,2048]{1,0:T(8,128)(2,1)} %bitcast.2.refs_0_.refs_1_), kind=kLoop, calls=%fused_computation.1 | loop fusion | flops 16777216 | bytes 16777216 | tf_op jit(solution)/shard_map/concatenate | solution.py:138
  265.0 25.6 %attn_key_side.3 = bf16[1024,1024]{1,0:T(8,128)(2,1)} custom-call(bf16[1024,2048]{1,0:T(8,128)(2,1)} %bitcast.5.refs_0_.refs_1_, bf16[1024,2048]{1,0:T(8,128)(2,1)} %bitcast.5.refs_0_.refs_1_, bf16[2048,2048]{1,0:T(8,128)(2,1)} %pad_maximum_fusion.1.refs_2_.refs_3_.refs_4_.refs_5_.refs_6_.refs_7_.refs_8_.refs_9_.refs_10_.refs_11_, ...), custom_call_target="tpu_custom_call" | custom-call | tf_op jit(solution)/shard_map/attn_key_side/pallas_call | solution.py:220
  290.6 4.5 %all-to-all-start.4 = ((bf16[4,256,1024]{2,1,0:T(8,128)(2,1)}), bf16[4,256,1024]{2,1,0:T(8,128)(2,1)}, u32[]{:S(2)}, u32[]{:S(2)}) async-start(bf16[4,256,1024]{2,1,0:T(8,128)(2,1)} %bitcast.31), calls=%async_computation.4 | async-start | bytes 4194304 | tf_op jit(solution)/shard_map/all_to_all | solution.py:203
  295.1 25.4 %attn_key_side.2 = bf16[1024,1024]{1,0:T(8,128)(2,1)} custom-call(bf16[1024,2048]{1,0:T(8,128)(2,1)} %bitcast.5.refs_0_.refs_1_, bf16[1024,2048]{1,0:T(8,128)(2,1)} %bitcast.5.refs_0_.refs_1_, bf16[2048,2048]{1,0:T(8,128)(2,1)} %pad_maximum_fusion.1.refs_2_.refs_3_.refs_4_.refs_5_.refs_6_.refs_7_.refs_8_.refs_9_.refs_10_.refs_11_, ...), custom_call_target="tpu_custom_call" | custom-call | tf_op jit(solution)/shard_map/attn_key_side/pallas_call | solution.py:220
  320.9 4.7 %all-to-all-start.3 = ((bf16[4,256,1024]{2,1,0:T(8,128)(2,1)}), bf16[4,256,1024]{2,1,0:T(8,128)(2,1)}, u32[]{:S(2)}, u32[]{:S(2)}) async-start(bf16[4,256,1024]{2,1,0:T(8,128)(2,1)} %bitcast.30), calls=%async_computation.3 | async-start | bytes 4194304 | tf_op jit(solution)/shard_map/all_to_all | solution.py:203
  330.4 20.7 %all-to-all-done.3 = bf16[4,256,1024]{2,1,0:T(8,128)(2,1)} async-done(((bf16[4,256,1024]{2,1,0:T(8,128)(2,1)}), bf16[4,256,1024]{2,1,0:T(8,128)(2,1)}, u32[]{:S(2)}, u32[]{:S(2)}) %all-to-all-start.3) | async-done | bytes 2097184 | tf_op jit(solution)/shard_map/all_to_all | solution.py:203
  351.1 4.4 %reshape.109 = bf16[256,4,1,4,2,128]{5,4,3,0,1,2:T(2,128)(2,1)} reshape(bf16[256,4,1024]{2,0,1:T(8,128)(2,1)} %bitcast.11) | data formatting | bytes 4194304 | tf_op jit(solution)/shard_map/reshape | solution.py:230
  361.5 4.5 %reshape_squeeze.6 = bf16[256,4096]{1,0:T(8,128)(2,1)} reshape(bf16[256,4,2,4,1,128]{5,3,2,1,0,4:T(4,128)(2,1)} %get-tuple-element.8) | data formatting | bytes 4194304 | tf_op jit(solution)/shard_map/reshape;squeeze | solution.py:234
  (41 shorter events, 41.3 us)
Async XLA Ops:
  27.2 52.8 %all-to-all-start.1 = ((bf16[128,8,2048]{2,0,1:T(8,128)(2,1)}), bf16[128,8,2048]{2,0,1:T(8,128)(2,1)}, u32[]{:S(2)}, u32[]{:S(2)}) async-start(bf16[128,8,2048]{2,0,1:T(8,128)(2,1)} %all_to_all.70), calls=%async_computation.1 | async-start | bytes 8388608 | tf_op jit(solution)/shard_map/all_to_all | solution.py:133
  58.9 29.7 %copy-start.1 = (s32[4096]{0:T(1024)S(1)}, s32[4096]{0:T(1024)}, u32[]{:S(2)}) copy-start(s32[4096]{0:T(1024)} %param.9) | copy-start | bytes 49156
  80.0 52.8 %all-to-all-start = ((bf16[128,8,2048]{2,0,1:T(8,128)(2,1)}), bf16[128,8,2048]{2,0,1:T(8,128)(2,1)}, u32[]{:S(2)}, u32[]{:S(2)}) async-start(bf16[128,8,2048]{2,0,1:T(8,128)(2,1)} %all_to_all.66), calls=%async_computation | async-start | bytes 8388608 | tf_op jit(solution)/shard_map/all_to_all | solution.py:133
  85.0 94.8 %collective-permute-start = (bf16[1024,2048]{1,0:T(8,128)(2,1)}, bf16[1024,2048]{1,0:T(8,128)(2,1)}, u32[]{:S(2)}, u32[]{:S(2)}) collective-permute-start(bf16[1024,2048]{1,0:T(8,128)(2,1)} %bitcast.5.refs_0_.refs_1_), channel_id=1, source_target_pairs={{0,8},{8,16},{16,24},{1,9},{9,17},{17,25},{2,10},{10,18},{18,26},{... | collective-permute-start | bytes 12582920 | tf_op jit(solution)/shard_map/ppermute | solution.py:21
  132.8 122.3 %collective-permute-start.1 = (bf16[1024,2048]{1,0:T(8,128)(2,1)}, bf16[1024,2048]{1,0:T(8,128)(2,1)}, u32[]{:S(2)}, u32[]{:S(2)}) collective-permute-start(bf16[1024,2048]{1,0:T(8,128)(2,1)} %bitcast.2.refs_0_.refs_1_), channel_id=1, source_target_pairs={{8,0},{16,8},{24,16},{9,1},{17,9},{25,17},{10,2},{18,10},{26,18},{... | collective-permute-start | bytes 12582920 | tf_op jit(solution)/shard_map/ppermute | solution.py:21
  245.1 45.5 %all-to-all-start.2 = ((bf16[4,256,1024]{2,1,0:T(8,128)(2,1)}), bf16[4,256,1024]{2,1,0:T(8,128)(2,1)S(1)}, u32[]{:S(2)}, u32[]{:S(2)}) async-start(bf16[4,256,1024]{2,1,0:T(8,128)(2,1)} %bitcast.33), calls=%async_computation.2 | async-start | bytes 4194304 | tf_op jit(solution)/shard_map/all_to_all | solution.py:203
  252.8 11.6 %collective-permute-start.2 = (f32[8,2,1024]{2,1,0:T(2,128)}, f32[8,2,1024]{2,1,0:T(2,128)S(1)}, u32[]{:S(2)}, u32[]{:S(2)}) collective-permute-start(f32[8,2,1024]{2,1,0:T(2,128)} %get-tuple-element.6), channel_id=1, source_target_pairs={{8,0},{16,8},{24,16},{9,1},{17,9},{25,17},{10,2},{18,10},{26,18},{... | collective-permute-start | bytes 196616 | tf_op jit(solution)/shard_map/ppermute | solution.py:21
  264.4 0.7 copy-start
  290.6 30.2 %all-to-all-start.4 = ((bf16[4,256,1024]{2,1,0:T(8,128)(2,1)}), bf16[4,256,1024]{2,1,0:T(8,128)(2,1)}, u32[]{:S(2)}, u32[]{:S(2)}) async-start(bf16[4,256,1024]{2,1,0:T(8,128)(2,1)} %bitcast.31), calls=%async_computation.4 | async-start | bytes 4194304 | tf_op jit(solution)/shard_map/all_to_all | solution.py:203
  320.9 30.2 %all-to-all-start.3 = ((bf16[4,256,1024]{2,1,0:T(8,128)(2,1)}), bf16[4,256,1024]{2,1,0:T(8,128)(2,1)}, u32[]{:S(2)}, u32[]{:S(2)}) async-start(bf16[4,256,1024]{2,1,0:T(8,128)(2,1)} %bitcast.30), calls=%async_computation.3 | async-start | bytes 4194304 | tf_op jit(solution)/shard_map/all_to_all | solution.py:203

commit v7 on v6

--- a/solution.py
+++ b/solution.py
@@ -133,7 +133,14 @@
         return lax.all_to_all(x, ("clo", "head"), split_axis=1, concat_axis=0, tiled=True)
 
     kv = to_plane(attn_k, attn_v)
-    kv_win = jnp.concatenate([shifted(kv, "chi", shift) for shift in range(reach, 0, -1)] + [kv], axis=0)
+    split = reach == 1 and tile_reach * TILE == plane and n_tiles % 2 == 0
+    if split:
+        half = plane // 2
+        prev_late = shifted(kv[half:], "chi", 1)
+        early_src, prev_late = lax.optimization_barrier((kv[:half], prev_late))
+        prev_early = shifted(early_src, "chi", 1)
+    else:
+        kv_win = jnp.concatenate([shifted(kv, "chi", shift) for shift in range(reach, 0, -1)] + [kv], axis=0)
     qd = to_plane(attn_q, attn_dout)
     qd_win = jnp.concatenate([qd] + [shifted(qd, "chi", -shift) for shift in range(1, reach + 1)], axis=0)
 
@@ -180,19 +187,38 @@
     params = pltpu.CompilerParams(dimension_semantics=("arbitrary", "arbitrary"))
     grid = (n_tiles, heads_p)
 
-    dq, ld = pl.pallas_call(
-        _query_side_kernel(nblk, scale),
-        out_shape=(
-            jax.ShapeDtypeStruct((plane, width), jnp.bfloat16),
-            jax.ShapeDtypeStruct((heads_p, 2, plane), jnp.float32),
-        ),
-        grid=grid,
-        in_specs=[col_spec(0), col_spec(heads_p)] + [kwin_spec(j, 0) for j in range(nblk)]
-        + [kwin_spec(j, heads_p) for j in range(nblk)] + [bias_spec],
-        out_specs=(own_spec, ld_spec),
-        compiler_params=params,
-        name="attn_query_side",
-    )(qd, qd, *([kv_win] * (2 * nblk)), q_bias)
+    def query_side(window, i_off, count, w_base):
+        def gcol(extra):
+            return pl.BlockSpec((TILE, HEAD_DIM), lambda i, h: (i + i_off, h + extra))
+
+        def gwin(j, extra):
+            return pl.BlockSpec((TILE, HEAD_DIM), lambda i, h: (w_base + i + j, h + extra))
+
+        return pl.pallas_call(
+            _query_side_kernel(nblk, scale),
+            out_shape=(
+                jax.ShapeDtypeStruct((count * TILE, width), jnp.bfloat16),
+                jax.ShapeDtypeStruct((heads_p, 2, count * TILE), jnp.float32),
+            ),
+            grid=(count, heads_p),
+            in_specs=[gcol(0), gcol(heads_p)] + [gwin(j, 0) for j in range(nblk)]
+            + [gwin(j, heads_p) for j in range(nblk)]
+            + [pl.BlockSpec((TILE, span), lambda i, h: (i + i_off, 0))],
+            out_specs=(own_spec, ld_spec),
+            compiler_params=params,
+            name="attn_query_side",
+        )(qd, qd, *([window] * (2 * nblk)), q_bias)
+
+    if split:
+        late = n_tiles // 2
+        dq_late, ld_late = query_side(jnp.concatenate([prev_late, kv], axis=0), late, n_tiles - late, 0)
+        dq_late, ld_late, prev_early = lax.optimization_barrier((dq_late, ld_late, prev_early))
+        dq_early, ld_early = query_side(
+            jnp.concatenate([prev_early, prev_late, kv[:half]], axis=0), 0, late, 0)
+        dq = jnp.concatenate([dq_early, dq_late], axis=0)
+        ld = jnp.concatenate([ld_early, ld_late], axis=2)
+    else:
+        dq, ld = query_side(kv_win, 0, n_tiles, base)
 
     ld_parts = [ld]
     for shift in range(1, reach + 1):

time: 371 us -> 351 us (0.946)
  waiting for transfers between devices: 124 us -> 86 us
  other arithmetic: 37.3 us -> 44.6 us
  starting transfers between devices: 31.1 us -> 35.6 us
    ppermute x3 -> x4, waiting for transfers between devices: 37.2 us -> 3.84 us  [shifted(): lax.ppermute(value, axis, [(source, source + steps) for source in range(l...]
    concatenate x1 -> x4, other arithmetic: 8.36 us -> 14.8 us  [the longest x1 6.63 us: _per_device(): jnp.concatenate([prev_late, kv], axis=0)]
    ppermute x3 -> x4, starting transfers between devices: 8.39 us -> 12.8 us  [shifted(): lax.ppermute(value, axis, [(source, source + steps) for source in range(l...]
    all_to_all x2, waiting for transfers between devices: 65.3 us -> 61.1 us  [to_plane(): lax.all_to_all(x, ('clo', 'head'), split_axis=1, concat_axis=0, tiled=True)]
    slice x0 -> x1, local copies, waits for them, and re-layouts: none -> 4.01 us  [_per_device(): prev_late = shifted(kv[half:], 'chi', 1)]
    pallas_call x1 -> x2, Pallas kernels: 56.9 us -> 59.2 us  [query_side(): pl.pallas_call(_query_side_kernel(nblk, scale), out_shape=(jax.ShapeDtype...]
  transfers between devices with their start and end apart: 8 -> 9, of which waited for: 5 -> 6; matrix products, arithmetic and copies ran while one was open for 14% -> 18% of each run, Pallas kernels for 29% -> 32%
where the time goes in v7:
time: 351 us; the launch traced here: 349 us
  Pallas kernels  110 us (31%)
  waiting for transfers between devices  86 us (25%)
  local copies, waits for them, and re-layouts  71.2 us (20%)
  other arithmetic  44.6 us (13%)
  starting transfers between devices  35.6 us (10%)
    all_to_all x2, waiting for transfers between devices, to_plane(): lax.all_to_all(x, ('clo', 'head'), split_axis=1, concat_axis=0, tiled=True)  61.1 us
    pallas_call x2, Pallas kernels, query_side(): pl.pallas_call(_query_side_kernel(nblk, scale), out_shape=(jax.ShapeDtype...  59.2 us
    pallas_call x2, Pallas kernels, _per_device(): pl.pallas_call(_key_side_kernel(nblk, scale), out_shape=jax.ShapeDtypeStr...  51 us
    all_to_all x3, waiting for transfers between devices, from_plane(): return lax.all_to_all(x, 'clo', split_axis=0, concat_axis=1, tiled=True)  21 us
    all_to_all x2, local copies, waits for them, and re-layouts, to_plane(): lax.all_to_all(x, ('clo', 'head'), split_axis=1, concat_axis=0, tiled=True)  15.6 us
    ppermute x4, starting transfers between devices, shifted(): lax.ppermute(value, axis, [(source, source + steps) for source in range(l...  12.8 us
    all_to_all x3, starting transfers between devices, from_plane(): return lax.all_to_all(x, 'clo', split_axis=0, concat_axis=1, tiled=True)  12.8 us
    transpose x2, local copies, waits for them, and re-layouts, to_plane(): jnp.concatenate([a, b], axis=3).transpose(0, 2, 1, 3, 4)  12.6 us
  transfers between devices with their start and end apart: 9, of which 6 were waited for; matrix products, arithmetic and copies ran while one was open for 18% of the time, Pallas kernels for 32%

profile of v7, /device:TPU:20, one launch (start us, length us, event | category | flops | bytes accessed | tf_op | source)
XLA Modules:
  0.0 348.5 jit_solution(2970246361987330445)
XLA Ops:
  4.0 4.5 %reshape.110 = bf16[128,2,4,1,1024]{4,2,1,0,3:T(4,128)(2,1)} reshape(bf16[128,8192]{1,0:T(8,128)(2,1)} %param.7) | data formatting | bytes 4194304 | tf_op jit(solution)/shard_map/reshape | solution.py:131
  8.4 4.7 %maximum_bitcast_fusion.1 = bf16[128,4,2,2,1024]{4,1,2,0,3:T(4,128)(2,1)S(1)} fusion(bf16[128,2,4,1,1024]{4,2,1,0,3:T(4,128)(2,1)} %reshape.110, bf16[128,2,4,1,1024]{4,2,1,0,3:T(4,128)(2,1)S(1)} %reshape.109), kind=kLoop, calls=%fused_computation.6 | loop fusion | flops 2097152 | bytes 8388608 | tf_op jit(solution)/shard_map/transpose | solution.py:132
  13.2 6.3 %copy.9 = bf16[128,4,2,2,1024]{4,3,0,2,1:T(2,128)(2,1)} copy(bf16[128,4,2,2,1024]{4,1,2,0,3:T(4,128)(2,1)S(1)} %maximum_bitcast_fusion.1) | data formatting | bytes 8388608 | tf_op jit(solution)/shard_map/transpose | solution.py:132
  19.5 7.8 %all_to_all.70 = bf16[128,8,2048]{2,0,1:T(8,128)(2,1)} reshape(bf16[128,4,2,2,1024]{4,3,0,2,1:T(2,128)(2,1)} %copy.9) | data formatting | bytes 8388608 | tf_op jit(solution)/shard_map/all_to_all | solution.py:133
  27.3 4.9 %all-to-all-start.1 = ((bf16[128,8,2048]{2,0,1:T(8,128)(2,1)}), bf16[128,8,2048]{2,0,1:T(8,128)(2,1)}, u32[]{:S(2)}, u32[]{:S(2)}) async-start(bf16[128,8,2048]{2,0,1:T(8,128)(2,1)} %all_to_all.70), calls=%async_computation.1 | async-start | bytes 8388608 | tf_op jit(solution)/shard_map/all_to_all | solution.py:133
  35.5 4.5 %reshape.108 = bf16[128,2,4,1,1024]{4,2,1,0,3:T(4,128)(2,1)} reshape(bf16[128,8192]{1,0:T(8,128)(2,1)} %param.8) | data formatting | bytes 4194304 | tf_op jit(solution)/shard_map/reshape | solution.py:131
  40.0 4.7 %maximum_bitcast_fusion = bf16[128,4,2,2,1024]{4,1,2,0,3:T(4,128)(2,1)S(1)} fusion(bf16[128,2,4,1,1024]{4,2,1,0,3:T(4,128)(2,1)} %reshape.108, bf16[128,2,4,1,1024]{4,2,1,0,3:T(4,128)(2,1)S(1)} %reshape.107), kind=kLoop, calls=%fused_computation.5 | loop fusion | flops 2097152 | bytes 8388608 | tf_op jit(solution)/shard_map/transpose | solution.py:132
  44.8 6.3 %copy.8 = bf16[128,4,2,2,1024]{4,3,0,2,1:T(2,128)(2,1)} copy(bf16[128,4,2,2,1024]{4,1,2,0,3:T(4,128)(2,1)S(1)} %maximum_bitcast_fusion) | data formatting | bytes 8388608 | tf_op jit(solution)/shard_map/transpose | solution.py:132
  51.1 7.9 %all_to_all.66 = bf16[128,8,2048]{2,0,1:T(8,128)(2,1)} reshape(bf16[128,4,2,2,1024]{4,3,0,2,1:T(2,128)(2,1)} %copy.8) | data formatting | bytes 8388608 | tf_op jit(solution)/shard_map/all_to_all | solution.py:133
  58.9 21.1 %all-to-all-done.1 = bf16[128,8,2048]{2,0,1:T(8,128)(2,1)} async-done(((bf16[128,8,2048]{2,0,1:T(8,128)(2,1)}), bf16[128,8,2048]{2,0,1:T(8,128)(2,1)}, u32[]{:S(2)}, u32[]{:S(2)}) %all-to-all-start.1) | async-done | bytes 4194336 | tf_op jit(solution)/shard_map/all_to_all | solution.py:133
  80.1 5.0 %all-to-all-start = ((bf16[128,8,2048]{2,0,1:T(8,128)(2,1)}), bf16[128,8,2048]{2,0,1:T(8,128)(2,1)}, u32[]{:S(2)}, u32[]{:S(2)}) async-start(bf16[128,8,2048]{2,0,1:T(8,128)(2,1)} %all_to_all.66), calls=%async_computation | async-start | bytes 8388608 | tf_op jit(solution)/shard_map/all_to_all | solution.py:133
  92.9 40.0 %all-to-all-done = bf16[128,8,2048]{2,0,1:T(8,128)(2,1)} async-done(((bf16[128,8,2048]{2,0,1:T(8,128)(2,1)}), bf16[128,8,2048]{2,0,1:T(8,128)(2,1)}, u32[]{:S(2)}, u32[]{:S(2)}) %all-to-all-start) | async-done | bytes 4194336 | tf_op jit(solution)/shard_map/all_to_all | solution.py:133
  139.0 4.8 %collective-permute-start.1 = (bf16[512,2048]{1,0:T(8,128)(2,1)S(1)}, bf16[512,2048]{1,0:T(8,128)(2,1)}, u32[]{:S(2)}, u32[]{:S(2)}) collective-permute-start(bf16[512,2048]{1,0:T(8,128)(2,1)S(1)} %bitcast.36), channel_id=1, source_target_pairs={{0,8},{8,16},{16,24},{1,9},{9,17},{17,25},{2,10},{10,18},{18,26},{... | collective-permute-start | bytes 6291464 | tf_op jit(solution)/shard_map/ppermute | solution.py:21
  148.8 6.6 %pad_maximum_fusion.1.refs_2_.refs_3_.refs_4_.refs_5_.refs_6_.refs_7_.refs_8_.refs_9_.refs_10_.refs_11_ = bf16[1536,2048]{1,0:T(8,128)(2,1)} fusion(bf16[1024,2048]{1,0:T(8,128)(2,1)} %bitcast.8.refs_0_.refs_1_, bf16[512,2048]{1,0:T(8,128)(2,1)} %collective-permute-done), kind=kLoop, calls=%fused_computation.1 | loop fusion | flops 12582912 | bytes 12582912 | tf_op jit(solution)/shard_map/concatenate | solution.py:214
  155.5 29.6 %attn_query_side.2 = (bf16[512,1024]{1,0:T(8,128)(2,1)}, f32[8,2,512]{2,1,0:T(2,128)}) custom-call(bf16[1024,2048]{1,0:T(8,128)(2,1)} %bitcast.2.refs_0_.refs_1_, bf16[1024,2048]{1,0:T(8,128)(2,1)} %bitcast.2.refs_0_.refs_1_, bf16[1536,2048]{1,0:T(8,128)(2,1)} %pad_maximum_fusion.1.refs_2_.refs_3_.refs_4_.refs_5_.refs_6_.refs_7_.refs_8_.refs_9_.refs_10_.refs_11_, ...), custom_call_target="tpu_custom_call" | custom-call | tf_op jit(solution)/shard_map/attn_query_side/pallas_call | solution.py:197
  188.0 5.4 %pad_maximum_fusion.2.refs_2_.refs_3_.refs_4_.refs_5_.refs_6_.refs_7_.refs_8_.refs_9_.refs_10_.refs_11_ = bf16[1536,2048]{1,0:T(8,128)(2,1)} fusion(bf16[512,2048]{1,0:T(8,128)(2,1)S(1)} %bitcast.37, bf16[512,2048]{1,0:T(8,128)(2,1)} %collective-permute-done, bf16[512,2048]{1,0:T(8,128)(2,1)} %collective-permute-done.1), kind=kLoop, calls=%fused_computation.2 | loop fusion | flops 18874368 | bytes 12582912 | tf_op jit(solution)/shard_map/concatenate | solution.py:217
  193.4 29.6 %attn_query_side.3 = (bf16[512,1024]{1,0:T(8,128)(2,1)}, f32[8,2,512]{2,1,0:T(2,128)}) custom-call(bf16[1024,2048]{1,0:T(8,128)(2,1)} %bitcast.2.refs_0_.refs_1_, bf16[1024,2048]{1,0:T(8,128)(2,1)} %bitcast.2.refs_0_.refs_1_, bf16[1536,2048]{1,0:T(8,128)(2,1)} %pad_maximum_fusion.2.refs_2_.refs_3_.refs_4_.refs_5_.refs_6_.refs_7_.refs_8_.refs_9_.refs_10_.refs_11_, ...), custom_call_target="tpu_custom_call" | custom-call | tf_op jit(solution)/shard_map/attn_query_side/pallas_call | solution.py:197
  235.7 8.4 %pad_maximum_fusion.refs_2_.refs_3_.refs_4_.refs_5_.refs_6_.refs_7_.refs_8_.refs_9_.refs_10_.refs_11_ = bf16[2048,2048]{1,0:T(8,128)(2,1)} fusion(bf16[1024,2048]{1,0:T(8,128)(2,1)} %collective-permute-done.2, bf16[1024,2048]{1,0:T(8,128)(2,1)} %bitcast.2.refs_0_.refs_1_), kind=kLoop, calls=%fused_computation | loop fusion | flops 16777216 | bytes 16777216 | tf_op jit(solution)/shard_map/concatenate | solution.py:145
  244.8 25.6 %attn_key_side.3 = bf16[1024,1024]{1,0:T(8,128)(2,1)} custom-call(bf16[1024,2048]{1,0:T(8,128)(2,1)} %bitcast.8.refs_0_.refs_1_, bf16[1024,2048]{1,0:T(8,128)(2,1)} %bitcast.8.refs_0_.refs_1_, bf16[2048,2048]{1,0:T(8,128)(2,1)} %pad_maximum_fusion.refs_2_.refs_3_.refs_4_.refs_5_.refs_6_.refs_7_.refs_8_.refs_9_.refs_10_.refs_11_, ...), custom_call_target="tpu_custom_call" | custom-call | tf_op jit(solution)/shard_map/attn_key_side/pallas_call | solution.py:246
  270.4 4.5 %all-to-all-start.4 = ((bf16[4,256,1024]{2,1,0:T(8,128)(2,1)}), bf16[4,256,1024]{2,1,0:T(8,128)(2,1)}, u32[]{:S(2)}, u32[]{:S(2)}) async-start(bf16[4,256,1024]{2,1,0:T(8,128)(2,1)} %bitcast.33), calls=%async_computation.4 | async-start | bytes 4194304 | tf_op jit(solution)/shard_map/all_to_all | solution.py:229
  274.9 25.4 %attn_key_side.2 = bf16[1024,1024]{1,0:T(8,128)(2,1)} custom-call(bf16[1024,2048]{1,0:T(8,128)(2,1)} %bitcast.8.refs_0_.refs_1_, bf16[1024,2048]{1,0:T(8,128)(2,1)} %bitcast.8.refs_0_.refs_1_, bf16[2048,2048]{1,0:T(8,128)(2,1)} %pad_maximum_fusion.refs_2_.refs_3_.refs_4_.refs_5_.refs_6_.refs_7_.refs_8_.refs_9_.refs_10_.refs_11_, ...), custom_call_target="tpu_custom_call" | custom-call | tf_op jit(solution)/shard_map/attn_key_side/pallas_call | solution.py:246
  300.7 4.7 %all-to-all-start.3 = ((bf16[4,256,1024]{2,1,0:T(8,128)(2,1)}), bf16[4,256,1024]{2,1,0:T(8,128)(2,1)}, u32[]{:S(2)}, u32[]{:S(2)}) async-start(bf16[4,256,1024]{2,1,0:T(8,128)(2,1)} %bitcast.32), calls=%async_computation.3 | async-start | bytes 4194304 | tf_op jit(solution)/shard_map/all_to_all | solution.py:229
  310.2 20.7 %all-to-all-done.3 = bf16[4,256,1024]{2,1,0:T(8,128)(2,1)} async-done(((bf16[4,256,1024]{2,1,0:T(8,128)(2,1)}), bf16[4,256,1024]{2,1,0:T(8,128)(2,1)}, u32[]{:S(2)}, u32[]{:S(2)}) %all-to-all-start.3) | async-done | bytes 2097184 | tf_op jit(solution)/shard_map/all_to_all | solution.py:229
  341.3 4.5 %reshape_squeeze.6 = bf16[256,4096]{1,0:T(8,128)(2,1)} reshape(bf16[256,4,2,4,1,128]{5,3,2,1,0,4:T(4,128)(2,1)} %get-tuple-element.22) | data formatting | bytes 4194304 | tf_op jit(solution)/shard_map/reshape;squeeze | solution.py:260
  (61 shorter events, 60.0 us)
Async XLA Ops:
  27.3 52.8 %all-to-all-start.1 = ((bf16[128,8,2048]{2,0,1:T(8,128)(2,1)}), bf16[128,8,2048]{2,0,1:T(8,128)(2,1)}, u32[]{:S(2)}, u32[]{:S(2)}) async-start(bf16[128,8,2048]{2,0,1:T(8,128)(2,1)} %all_to_all.70), calls=%async_computation.1 | async-start | bytes 8388608 | tf_op jit(solution)/shard_map/all_to_all | solution.py:133
  80.1 52.8 %all-to-all-start = ((bf16[128,8,2048]{2,0,1:T(8,128)(2,1)}), bf16[128,8,2048]{2,0,1:T(8,128)(2,1)}, u32[]{:S(2)}, u32[]{:S(2)}) async-start(bf16[128,8,2048]{2,0,1:T(8,128)(2,1)} %all_to_all.66), calls=%async_computation | async-start | bytes 8388608 | tf_op jit(solution)/shard_map/all_to_all | solution.py:133
  85.1 7.5 %copy-start.7 = (s32[4096]{0:T(1024)S(1)}, s32[4096]{0:T(1024)}, u32[]{:S(2)}) copy-start(s32[4096]{0:T(1024)} %param.9) | copy-start | bytes 49156
  89.1 49.9 %collective-permute-start = (bf16[512,2048]{1,0:T(8,128)(2,1)}, bf16[512,2048]{1,0:T(8,128)(2,1)}, u32[]{:S(2)}, u32[]{:S(2)}) collective-permute-start(bf16[512,2048]{1,0:T(8,128)(2,1)} %bitcast.7), channel_id=1, source_target_pairs={{0,8},{8,16},{16,24},{1,9},{9,17},{17,25},{2,10},{10,18},{18,26},{... | collective-permute-start | bytes 6291464 | tf_op jit(solution)/shard_map/ppermute | solution.py:21
  132.9 102.8 %collective-permute-start.2 = (bf16[1024,2048]{1,0:T(8,128)(2,1)}, bf16[1024,2048]{1,0:T(8,128)(2,1)}, u32[]{:S(2)}, u32[]{:S(2)}) collective-permute-start(bf16[1024,2048]{1,0:T(8,128)(2,1)} %bitcast.2.refs_0_.refs_1_), channel_id=1, source_target_pairs={{8,0},{16,8},{24,16},{9,1},{17,9},{25,17},{10,2},{18,10},{26,18},{... | collective-permute-start | bytes 12582920 | tf_op jit(solution)/shard_map/ppermute | solution.py:21
  139.0 49.0 %collective-permute-start.1 = (bf16[512,2048]{1,0:T(8,128)(2,1)S(1)}, bf16[512,2048]{1,0:T(8,128)(2,1)}, u32[]{:S(2)}, u32[]{:S(2)}) collective-permute-start(bf16[512,2048]{1,0:T(8,128)(2,1)S(1)} %bitcast.36), channel_id=1, source_target_pairs={{0,8},{8,16},{16,24},{1,9},{9,17},{17,25},{2,10},{10,18},{18,26},{... | collective-permute-start | bytes 6291464 | tf_op jit(solution)/shard_map/ppermute | solution.py:21
  143.8 2.5 copy-start.1
  143.8 2.4 copy-start.2
  193.4 29.6 %copy-start.3 = (bf16[512,1024]{1,0:T(8,128)(2,1)S(1)}, bf16[512,1024]{1,0:T(8,128)(2,1)}, u32[]{:S(2)}) copy-start(bf16[512,1024]{1,0:T(8,128)(2,1)} %get-tuple-element.18) | copy-start | bytes 3145732
  225.7 44.7 %all-to-all-start.2 = ((bf16[4,256,1024]{2,1,0:T(8,128)(2,1)}), bf16[4,256,1024]{2,1,0:T(8,128)(2,1)S(1)}, u32[]{:S(2)}, u32[]{:S(2)}) async-start(bf16[4,256,1024]{2,1,0:T(8,128)(2,1)} %bitcast.35), calls=%async_computation.2 | async-start | bytes 4194304 | tf_op jit(solution)/shard_map/all_to_all | solution.py:229
  229.3 4.1 %copy-start.4 = (f32[8,2,512]{2,1,0:T(2,128)S(1)}, f32[8,2,512]{2,1,0:T(2,128)}, u32[]{:S(2)}) copy-start(f32[8,2,512]{2,1,0:T(2,128)} %get-tuple-element.20) | copy-start | bytes 98308
  229.3 4.1 %copy-start.6 = (f32[8,2,512]{2,1,0:T(2,128)S(1)}, f32[8,2,512]{2,1,0:T(2,128)}, u32[]{:S(2)}) copy-start(f32[8,2,512]{2,1,0:T(2,128)} %get-tuple-element.19) | copy-start | bytes 98308
  233.5 10.7 %collective-permute-start.3 = (f32[8,2,1024]{2,1,0:T(2,128)S(1)}, f32[8,2,1024]{2,1,0:T(2,128)S(1)}, u32[]{:S(2)}, u32[]{:S(2)}) collective-permute-start(f32[8,2,1024]{2,1,0:T(2,128)S(1)} %pad_maximum_fusion.6), channel_id=1, source_target_pairs={{8,0},{16,8},{24,16},{9,1},{17,9},{25,17},{10,2},{18,10},{26,18},{... | collective-permute-start | bytes 196616 | tf_op jit(solution)/shard_map/ppermute | solution.py:21
  235.7 8.4 %copy-start.5 = (f32[8,2,512]{2,1,0:T(2,128)S(1)}, f32[8,2,512]{2,1,0:T(2,128)}, u32[]{:S(2)}) copy-start(f32[8,2,512]{2,1,0:T(2,128)} %get-tuple-element.20) | copy-start | bytes 98308
  244.2 0.7 copy-start
  270.4 30.2 %all-to-all-start.4 = ((bf16[4,256,1024]{2,1,0:T(8,128)(2,1)}), bf16[4,256,1024]{2,1,0:T(8,128)(2,1)}, u32[]{:S(2)}, u32[]{:S(2)}) async-start(bf16[4,256,1024]{2,1,0:T(8,128)(2,1)} %bitcast.33), calls=%async_computation.4 | async-start | bytes 4194304 | tf_op jit(solution)/shard_map/all_to_all | solution.py:229
  300.7 30.2 %all-to-all-start.3 = ((bf16[4,256,1024]{2,1,0:T(8,128)(2,1)}), bf16[4,256,1024]{2,1,0:T(8,128)(2,1)}, u32[]{:S(2)}, u32[]{:S(2)}) async-start(bf16[4,256,1024]{2,1,0:T(8,128)(2,1)} %bitcast.32), calls=%async_computation.3 | async-start | bytes 4194304 | tf_op jit(solution)/shard_map/all_to_all | solution.py:229

commit v8 on v7

--- a/solution.py
+++ b/solution.py
@@ -141,9 +141,6 @@
         prev_early = shifted(early_src, "chi", 1)
     else:
         kv_win = jnp.concatenate([shifted(kv, "chi", shift) for shift in range(reach, 0, -1)] + [kv], axis=0)
-    qd = to_plane(attn_q, attn_dout)
-    qd_win = jnp.concatenate([qd] + [shifted(qd, "chi", -shift) for shift in range(1, reach + 1)], axis=0)
-
     pad = (reach + 1) * plane
     docs_pad = jnp.concatenate([
         jnp.full((pad,), -1, jnp.int32), doc_ids.astype(jnp.int32), jnp.full((pad,), -1, jnp.int32)])
@@ -166,6 +163,10 @@
         k_bias.append(jnp.where(mask, 0.0, masked_value).astype(jnp.float32))
     q_bias = jnp.concatenate(q_bias, axis=0)
     k_bias = jnp.concatenate(k_bias, axis=0)
+    attn_q, attn_dout, q_bias, k_bias, kv = lax.optimization_barrier((attn_q, attn_dout, q_bias, k_bias, kv))
+    qd = to_plane(attn_q, attn_dout)
+    qd_win = jnp.concatenate([qd] + [shifted(qd, "chi", -shift) for shift in range(1, reach + 1)], axis=0)
+
 
     own_spec = pl.BlockSpec((TILE, HEAD_DIM), lambda i, h: (i, h))
     base = reach * n_tiles - tile_reach

time: 351 us -> 379 us (1.080)
  waiting for transfers between devices: 86 us -> 115 us
  other arithmetic: 44.6 us -> 39.1 us
  local copies, waits for them, and re-layouts: 71.2 us -> 75.6 us
    all_to_all x2, waiting for transfers between devices: 61.1 us -> 79.9 us  [to_plane(): lax.all_to_all(x, ('clo', 'head'), split_axis=1, concat_axis=0, tiled=True)]
    ppermute x4, waiting for transfers between devices: 3.84 us -> 16.3 us  [shifted(): lax.ppermute(value, axis, [(source, source + steps) for source in range(l...]
  transfers between devices with their start and end apart: 9 -> 9, of which waited for: 6 -> 7; matrix products, arithmetic and copies ran while one was open for 18% -> 12% of each run, Pallas kernels for 32% -> 29%
where the time goes in v8:
time: 379 us; the launch traced here: 376 us
  waiting for transfers between devices  115 us (30%)
  Pallas kernels  110 us (29%)
  local copies, waits for them, and re-layouts  75.6 us (20%)
  other arithmetic  39.1 us (10%)
  starting transfers between devices  34.7 us (9%)
    all_to_all x2, waiting for transfers between devices, to_plane(): lax.all_to_all(x, ('clo', 'head'), split_axis=1, concat_axis=0, tiled=True)  79.9 us
    pallas_call x2, Pallas kernels, query_side(): pl.pallas_call(_query_side_kernel(nblk, scale), out_shape=(jax.ShapeDtype...  59.2 us
    pallas_call x2, Pallas kernels, _per_device(): pl.pallas_call(_key_side_kernel(nblk, scale), out_shape=jax.ShapeDtypeStr...  51 us
    all_to_all x3, waiting for transfers between devices, from_plane(): return lax.all_to_all(x, 'clo', split_axis=0, concat_axis=1, tiled=True)  19 us
    ppermute x4, waiting for transfers between devices, shifted(): lax.ppermute(value, axis, [(source, source + steps) for source in range(l...  16.3 us
    all_to_all x2, local copies, waits for them, and re-layouts, to_plane(): lax.all_to_all(x, ('clo', 'head'), split_axis=1, concat_axis=0, tiled=True)  15.6 us
    all_to_all x3, starting transfers between devices, from_plane(): return lax.all_to_all(x, 'clo', split_axis=0, concat_axis=1, tiled=True)  12.9 us
    transpose x2, local copies, waits for them, and re-layouts, to_plane(): jnp.concatenate([a, b], axis=3).transpose(0, 2, 1, 3, 4)  12.7 us
  transfers between devices with their start and end apart: 9, of which 7 were waited for; matrix products, arithmetic and copies ran while one was open for 12% of the time, Pallas kernels for 29%

profile of v8, /device:TPU:20, one launch (start us, length us, event | category | flops | bytes accessed | tf_op | source)
XLA Modules:
  0.0 375.8 jit_solution(10309149346745750564)
XLA Ops:
  4.0 4.5 %reshape.107 = bf16[128,2,4,1,1024]{4,2,1,0,3:T(4,128)(2,1)} reshape(bf16[128,8192]{1,0:T(8,128)(2,1)} %param.6) | data formatting | bytes 4194304 | tf_op jit(solution)/shard_map/reshape | solution.py:130
  8.4 4.7 %maximum_bitcast_fusion = bf16[128,4,2,2,1024]{4,1,2,0,3:T(4,128)(2,1)S(1)} fusion(bf16[128,2,4,1,1024]{4,2,1,0,3:T(4,128)(2,1)S(1)} %reshape.108, bf16[128,2,4,1,1024]{4,2,1,0,3:T(4,128)(2,1)} %reshape.107), kind=kLoop, calls=%fused_computation.5 | loop fusion | flops 2097152 | bytes 8388608 | tf_op jit(solution)/shard_map/transpose | solution.py:132
  13.2 6.3 %copy.8 = bf16[128,4,2,2,1024]{4,3,0,2,1:T(2,128)(2,1)} copy(bf16[128,4,2,2,1024]{4,1,2,0,3:T(4,128)(2,1)S(1)} %maximum_bitcast_fusion) | data formatting | bytes 8388608 | tf_op jit(solution)/shard_map/transpose | solution.py:132
  19.5 7.8 %all_to_all.66 = bf16[128,8,2048]{2,0,1:T(8,128)(2,1)} reshape(bf16[128,4,2,2,1024]{4,3,0,2,1:T(2,128)(2,1)} %copy.8) | data formatting | bytes 8388608 | tf_op jit(solution)/shard_map/all_to_all | solution.py:133
  27.3 5.1 %all-to-all-start = ((bf16[128,8,2048]{2,0,1:T(8,128)(2,1)}), bf16[128,8,2048]{2,0,1:T(8,128)(2,1)}, u32[]{:S(2)}, u32[]{:S(2)}) async-start(bf16[128,8,2048]{2,0,1:T(8,128)(2,1)} %all_to_all.66), calls=%async_computation | async-start | bytes 8388608 | tf_op jit(solution)/shard_map/all_to_all | solution.py:133
  39.8 40.4 %all-to-all-done = bf16[128,8,2048]{2,0,1:T(8,128)(2,1)} async-done(((bf16[128,8,2048]{2,0,1:T(8,128)(2,1)}), bf16[128,8,2048]{2,0,1:T(8,128)(2,1)}, u32[]{:S(2)}, u32[]{:S(2)}) %all-to-all-start) | async-done | bytes 4194336 | tf_op jit(solution)/shard_map/all_to_all | solution.py:133
  83.5 4.5 %reshape.109 = bf16[128,2,4,1,1024]{4,2,1,0,3:T(4,128)(2,1)} reshape(bf16[128,8192]{1,0:T(8,128)(2,1)} %param.5) | data formatting | bytes 4194304 | tf_op jit(solution)/shard_map/reshape | solution.py:130
  88.0 4.7 %maximum_bitcast_fusion.1 = bf16[128,4,2,2,1024]{4,1,2,0,3:T(4,128)(2,1)S(1)} fusion(bf16[128,2,4,1,1024]{4,2,1,0,3:T(4,128)(2,1)S(1)} %reshape.110, bf16[128,2,4,1,1024]{4,2,1,0,3:T(4,128)(2,1)} %reshape.109), kind=kLoop, calls=%fused_computation.6 | loop fusion | flops 2097152 | bytes 8388608 | tf_op jit(solution)/shard_map/transpose | solution.py:132
  92.8 6.3 %copy.9 = bf16[128,4,2,2,1024]{4,3,0,2,1:T(2,128)(2,1)} copy(bf16[128,4,2,2,1024]{4,1,2,0,3:T(4,128)(2,1)S(1)} %maximum_bitcast_fusion.1) | data formatting | bytes 8388608 | tf_op jit(solution)/shard_map/transpose | solution.py:132
  99.1 7.8 %all_to_all.70 = bf16[128,8,2048]{2,0,1:T(8,128)(2,1)} reshape(bf16[128,4,2,2,1024]{4,3,0,2,1:T(2,128)(2,1)} %copy.9) | data formatting | bytes 8388608 | tf_op jit(solution)/shard_map/all_to_all | solution.py:133
  106.9 5.0 %all-to-all-start.1 = ((bf16[128,8,2048]{2,0,1:T(8,128)(2,1)}), bf16[128,8,2048]{2,0,1:T(8,128)(2,1)}, u32[]{:S(2)}, u32[]{:S(2)}) async-start(bf16[128,8,2048]{2,0,1:T(8,128)(2,1)} %all_to_all.70), calls=%async_computation.1 | async-start | bytes 8388608 | tf_op jit(solution)/shard_map/all_to_all | solution.py:133
  111.9 4.8 %fusion.1 = (bf16[4,128,2048]{2,1,0:T(8,128)(2,1)}, bf16[4,128,2048]{2,1,0:T(8,128)(2,1)}) fusion(bf16[8,128,2048]{2,1,0:T(8,128)(2,1)} %bitcast.1), kind=kLoop, calls=%fused_computation.36 | loop fusion | bytes 8388608 | tf_op jit(solution)/shard_map/slice | solution.py:139
  120.2 39.5 %all-to-all-done.1 = bf16[128,8,2048]{2,0,1:T(8,128)(2,1)} async-done(((bf16[128,8,2048]{2,0,1:T(8,128)(2,1)}), bf16[128,8,2048]{2,0,1:T(8,128)(2,1)}, u32[]{:S(2)}, u32[]{:S(2)}) %all-to-all-start.1) | async-done | bytes 4194336 | tf_op jit(solution)/shard_map/all_to_all | solution.py:133
  173.5 5.9 %pad_maximum_fusion.1.refs_2_.refs_3_.refs_4_.refs_5_.refs_6_.refs_7_.refs_8_.refs_9_.refs_10_.refs_11_ = bf16[1536,2048]{1,0:T(8,128)(2,1)} fusion(bf16[1024,2048]{1,0:T(8,128)(2,1)} %bitcast.2.refs_0_.refs_1_, bf16[512,2048]{1,0:T(8,128)(2,1)S(1)} %copy-done.2), kind=kLoop, calls=%fused_computation.1 | loop fusion | flops 12582912 | bytes 12582912 | tf_op jit(solution)/shard_map/concatenate | solution.py:215
  179.4 29.6 %attn_query_side.2 = (bf16[512,1024]{1,0:T(8,128)(2,1)}, f32[8,2,512]{2,1,0:T(2,128)}) custom-call(bf16[1024,2048]{1,0:T(8,128)(2,1)} %bitcast.5.refs_0_.refs_1_, bf16[1024,2048]{1,0:T(8,128)(2,1)} %bitcast.5.refs_0_.refs_1_, bf16[1536,2048]{1,0:T(8,128)(2,1)} %pad_maximum_fusion.1.refs_2_.refs_3_.refs_4_.refs_5_.refs_6_.refs_7_.refs_8_.refs_9_.refs_10_.refs_11_, ...), custom_call_target="tpu_custom_call" | custom-call | tf_op jit(solution)/shard_map/attn_query_side/pallas_call | solution.py:198
  209.0 8.0 %collective-permute-done.1 = bf16[512,2048]{1,0:T(8,128)(2,1)} collective-permute-done((bf16[512,2048]{1,0:T(8,128)(2,1)}, bf16[512,2048]{1,0:T(8,128)(2,1)}, u32[]{:S(2)}, u32[]{:S(2)}) %collective-permute-start.1) | collective-permute-done | bytes 2097184 | tf_op jit(solution)/shard_map/ppermute | solution.py:21
  217.0 5.4 %pad_maximum_fusion.2.refs_2_.refs_3_.refs_4_.refs_5_.refs_6_.refs_7_.refs_8_.refs_9_.refs_10_.refs_11_ = bf16[1536,2048]{1,0:T(8,128)(2,1)} fusion(bf16[512,2048]{1,0:T(8,128)(2,1)S(1)} %slice.25, bf16[512,2048]{1,0:T(8,128)(2,1)} %copy-done.1, bf16[512,2048]{1,0:T(8,128)(2,1)} %collective-permute-done.1), kind=kLoop, calls=%fused_computation.2 | loop fusion | flops 18874368 | bytes 12582912 | tf_op jit(solution)/shard_map/concatenate | solution.py:218
  222.4 29.6 %attn_query_side.3 = (bf16[512,1024]{1,0:T(8,128)(2,1)}, f32[8,2,512]{2,1,0:T(2,128)}) custom-call(bf16[1024,2048]{1,0:T(8,128)(2,1)} %bitcast.5.refs_0_.refs_1_, bf16[1024,2048]{1,0:T(8,128)(2,1)} %bitcast.5.refs_0_.refs_1_, bf16[1536,2048]{1,0:T(8,128)(2,1)} %pad_maximum_fusion.2.refs_2_.refs_3_.refs_4_.refs_5_.refs_6_.refs_7_.refs_8_.refs_9_.refs_10_.refs_11_, ...), custom_call_target="tpu_custom_call" | custom-call | tf_op jit(solution)/shard_map/attn_query_side/pallas_call | solution.py:198
  264.9 8.4 %pad_maximum_fusion.refs_2_.refs_3_.refs_4_.refs_5_.refs_6_.refs_7_.refs_8_.refs_9_.refs_10_.refs_11_ = bf16[2048,2048]{1,0:T(8,128)(2,1)} fusion(bf16[1024,2048]{1,0:T(8,128)(2,1)} %collective-permute-done.2, bf16[1024,2048]{1,0:T(8,128)(2,1)} %bitcast.5.refs_0_.refs_1_), kind=kLoop, calls=%fused_computation | loop fusion | flops 16777216 | bytes 16777216 | tf_op jit(solution)/shard_map/concatenate | solution.py:168
  273.4 25.4 %attn_key_side.2 = bf16[1024,1024]{1,0:T(8,128)(2,1)} custom-call(bf16[1024,2048]{1,0:T(8,128)(2,1)} %bitcast.2.refs_0_.refs_1_, bf16[1024,2048]{1,0:T(8,128)(2,1)} %bitcast.2.refs_0_.refs_1_, bf16[2048,2048]{1,0:T(8,128)(2,1)} %pad_maximum_fusion.refs_2_.refs_3_.refs_4_.refs_5_.refs_6_.refs_7_.refs_8_.refs_9_.refs_10_.refs_11_, ...), custom_call_target="tpu_custom_call" | custom-call | tf_op jit(solution)/shard_map/attn_key_side/pallas_call | solution.py:247
  303.3 25.6 %attn_key_side.3 = bf16[1024,1024]{1,0:T(8,128)(2,1)} custom-call(bf16[1024,2048]{1,0:T(8,128)(2,1)} %bitcast.2.refs_0_.refs_1_, bf16[1024,2048]{1,0:T(8,128)(2,1)} %bitcast.2.refs_0_.refs_1_, bf16[2048,2048]{1,0:T(8,128)(2,1)} %pad_maximum_fusion.refs_2_.refs_3_.refs_4_.refs_5_.refs_6_.refs_7_.refs_8_.refs_9_.refs_10_.refs_11_, ...), custom_call_target="tpu_custom_call" | custom-call | tf_op jit(solution)/shard_map/attn_key_side/pallas_call | solution.py:247
  329.0 4.7 %all-to-all-start.4 = ((bf16[4,256,1024]{2,1,0:T(8,128)(2,1)}), bf16[4,256,1024]{2,1,0:T(8,128)(2,1)}, u32[]{:S(2)}, u32[]{:S(2)}) async-start(bf16[4,256,1024]{2,1,0:T(8,128)(2,1)} %bitcast.32), calls=%async_computation.4 | async-start | bytes 4194304 | tf_op jit(solution)/shard_map/all_to_all | solution.py:230
  340.5 18.8 %all-to-all-done.4 = bf16[4,256,1024]{2,1,0:T(8,128)(2,1)} async-done(((bf16[4,256,1024]{2,1,0:T(8,128)(2,1)}), bf16[4,256,1024]{2,1,0:T(8,128)(2,1)}, u32[]{:S(2)}, u32[]{:S(2)}) %all-to-all-start.4) | async-done | bytes 2097184 | tf_op jit(solution)/shard_map/all_to_all | solution.py:230
  368.5 4.5 %reshape_squeeze.6 = bf16[256,4096]{1,0:T(8,128)(2,1)} reshape(bf16[256,4,2,4,1,128]{5,3,2,1,0,4:T(4,128)(2,1)} %get-tuple-element.32) | data formatting | bytes 4194304 | tf_op jit(solution)/shard_map/reshape;squeeze | solution.py:261
  (60 shorter events, 67.3 us)
Async XLA Ops:
  27.3 5.1 %copy-start.6 = (s32[4096]{0:T(1024)S(1)}, s32[4096]{0:T(1024)}, u32[]{:S(2)}) copy-start(s32[4096]{0:T(1024)} %param.9) | copy-start | bytes 49156
  27.3 52.9 %all-to-all-start = ((bf16[128,8,2048]{2,0,1:T(8,128)(2,1)}), bf16[128,8,2048]{2,0,1:T(8,128)(2,1)}, u32[]{:S(2)}, u32[]{:S(2)}) async-start(bf16[128,8,2048]{2,0,1:T(8,128)(2,1)} %all_to_all.66), calls=%async_computation | async-start | bytes 8388608 | tf_op jit(solution)/shard_map/all_to_all | solution.py:133
  106.9 52.8 %all-to-all-start.1 = ((bf16[128,8,2048]{2,0,1:T(8,128)(2,1)}), bf16[128,8,2048]{2,0,1:T(8,128)(2,1)}, u32[]{:S(2)}, u32[]{:S(2)}) async-start(bf16[128,8,2048]{2,0,1:T(8,128)(2,1)} %all_to_all.70), calls=%async_computation.1 | async-start | bytes 8388608 | tf_op jit(solution)/shard_map/all_to_all | solution.py:133
  116.7 49.8 %collective-permute-start = (bf16[512,2048]{1,0:T(8,128)(2,1)}, bf16[512,2048]{1,0:T(8,128)(2,1)S(1)}, u32[]{:S(2)}, u32[]{:S(2)}) collective-permute-start(bf16[512,2048]{1,0:T(8,128)(2,1)} %bitcast.8), channel_id=1, source_target_pairs={{0,8},{8,16},{16,24},{1,9},{9,17},{17,25},{2,10},{10,18},{18,26},{... | collective-permute-start | bytes 6291464 | tf_op jit(solution)/shard_map/ppermute | solution.py:21
  159.7 105.2 %collective-permute-start.2 = (bf16[1024,2048]{1,0:T(8,128)(2,1)}, bf16[1024,2048]{1,0:T(8,128)(2,1)}, u32[]{:S(2)}, u32[]{:S(2)}) collective-permute-start(bf16[1024,2048]{1,0:T(8,128)(2,1)} %bitcast.5.refs_0_.refs_1_), channel_id=1, source_target_pairs={{8,0},{16,8},{24,16},{9,1},{17,9},{25,17},{10,2},{18,10},{26,18},{... | collective-permute-start | bytes 12582920 | tf_op jit(solution)/shard_map/ppermute | solution.py:21
  166.5 1.3 copy-start.1
  167.8 49.2 %collective-permute-start.1 = (bf16[512,2048]{1,0:T(8,128)(2,1)}, bf16[512,2048]{1,0:T(8,128)(2,1)}, u32[]{:S(2)}, u32[]{:S(2)}) collective-permute-start(bf16[512,2048]{1,0:T(8,128)(2,1)} %bitcast.37), channel_id=1, source_target_pairs={{0,8},{8,16},{16,24},{1,9},{9,17},{17,25},{2,10},{10,18},{18,26},{... | collective-permute-start | bytes 6291464 | tf_op jit(solution)/shard_map/ppermute | solution.py:21
  171.3 2.2 copy-start.2
  222.4 29.6 %copy-start.3 = (bf16[512,1024]{1,0:T(8,128)(2,1)S(1)}, bf16[512,1024]{1,0:T(8,128)(2,1)}, u32[]{:S(2)}) copy-start(bf16[512,1024]{1,0:T(8,128)(2,1)} %get-tuple-element.27) | copy-start | bytes 3145732
  254.8 3.8 copy-start.4
  254.8 3.8 %copy-start.5 = (f32[8,2,512]{2,1,0:T(2,128)S(1)}, f32[8,2,512]{2,1,0:T(2,128)}, u32[]{:S(2)}) copy-start(f32[8,2,512]{2,1,0:T(2,128)} %get-tuple-element.28) | copy-start | bytes 98308
  254.8 44.1 %all-to-all-start.2 = ((bf16[4,256,1024]{2,1,0:T(8,128)(2,1)}), bf16[4,256,1024]{2,1,0:T(8,128)(2,1)S(1)}, u32[]{:S(2)}, u32[]{:S(2)}) async-start(bf16[4,256,1024]{2,1,0:T(8,128)(2,1)} %bitcast.35), calls=%async_computation.2 | async-start | bytes 4194304 | tf_op jit(solution)/shard_map/all_to_all | solution.py:230
  258.6 6.3 %collective-permute-start.3 = (f32[8,2,1024]{2,1,0:T(2,128)S(1)}, f32[8,2,1024]{2,1,0:T(2,128)S(1)}, u32[]{:S(2)}, u32[]{:S(2)}) collective-permute-start(f32[8,2,1024]{2,1,0:T(2,128)S(1)} %pad_maximum_fusion.6), channel_id=1, source_target_pairs={{8,0},{16,8},{24,16},{9,1},{17,9},{25,17},{10,2},{18,10},{26,18},{... | collective-permute-start | bytes 196616 | tf_op jit(solution)/shard_map/ppermute | solution.py:21
  264.9 8.5 %copy-start = (f32[8,2,2048]{2,1,0:T(2,128)}, f32[8,2,2048]{2,1,0:T(2,128)S(1)}, u32[]{:S(2)}) copy-start(f32[8,2,2048]{2,1,0:T(2,128)S(1)} %constant_dynamic-update-slice_fusion.refs_12_.refs_13_.refs_14_.refs_15_.refs_16_) | copy-start | bytes 393220
  298.8 30.2 %all-to-all-start.3 = ((bf16[4,256,1024]{2,1,0:T(8,128)(2,1)}), bf16[4,256,1024]{2,1,0:T(8,128)(2,1)}, u32[]{:S(2)}, u32[]{:S(2)}) async-start(bf16[4,256,1024]{2,1,0:T(8,128)(2,1)} %bitcast.33), calls=%async_computation.3 | async-start | bytes 4194304 | tf_op jit(solution)/shard_map/all_to_all | solution.py:230
  329.0 30.3 %all-to-all-start.4 = ((bf16[4,256,1024]{2,1,0:T(8,128)(2,1)}), bf16[4,256,1024]{2,1,0:T(8,128)(2,1)}, u32[]{:S(2)}, u32[]{:S(2)}) async-start(bf16[4,256,1024]{2,1,0:T(8,128)(2,1)} %bitcast.32), calls=%async_computation.4 | async-start | bytes 4194304 | tf_op jit(solution)/shard_map/all_to_all | solution.py:230

commit v9 on v8

--- a/solution.py
+++ b/solution.py
@@ -126,13 +126,15 @@
     chi = lax.axis_index("chi")
     plane_start = chi * plane
 
-    def to_plane(a, b):
+    def to_plane(a, b, tied=None):
         a = a.reshape(tok_in, head_n, clo_n, 1, width)
         b = b.reshape(tok_in, head_n, clo_n, 1, width)
         x = jnp.concatenate([a, b], axis=3).transpose(0, 2, 1, 3, 4).reshape(tok_in, 2 * full_width)
-        return lax.all_to_all(x, ("clo", "head"), split_axis=1, concat_axis=0, tiled=True)
-
-    kv = to_plane(attn_k, attn_v)
+        if tied is not None:
+            x, tied = lax.optimization_barrier((x, tied))
+        return lax.all_to_all(x, ("clo", "head"), split_axis=1, concat_axis=0, tiled=True), tied
+
+    kv, _ = to_plane(attn_k, attn_v)
     split = reach == 1 and tile_reach * TILE == plane and n_tiles % 2 == 0
     if split:
         half = plane // 2
@@ -163,8 +165,7 @@
         k_bias.append(jnp.where(mask, 0.0, masked_value).astype(jnp.float32))
     q_bias = jnp.concatenate(q_bias, axis=0)
     k_bias = jnp.concatenate(k_bias, axis=0)
-    attn_q, attn_dout, q_bias, k_bias, kv = lax.optimization_barrier((attn_q, attn_dout, q_bias, k_bias, kv))
-    qd = to_plane(attn_q, attn_dout)
+    qd, (q_bias, k_bias) = to_plane(attn_q, attn_dout, (q_bias, k_bias))
     qd_win = jnp.concatenate([qd] + [shifted(qd, "chi", -shift) for shift in range(1, reach + 1)], axis=0)
 
 

time: 379 us -> 351 us (0.926)
  waiting for transfers between devices: 115 us -> 94.3 us
  local copies, waits for them, and re-layouts: 75.6 us -> 67.7 us
    all_to_all x2, waiting for transfers between devices: 79.9 us -> 64.9 us  [to_plane(): lax.all_to_all(x, ('clo', 'head'), split_axis=1, concat_axis=0, tiled=True)]
    ppermute x4, waiting for transfers between devices: 16.3 us -> 8.19 us  [shifted(): lax.ppermute(value, axis, [(source, source + steps) for source in range(l...]
    unnamed x17 -> x15, local copies, waits for them, and re-layouts: 3.62 us -> 10.2 us
    reshape x2 -> x1, local copies, waits for them, and re-layouts: 8.97 us -> 3.32 us  [to_plane(): a = a.reshape(tok_in, head_n, clo_n, 1, width)]
  transfers between devices with their start and end apart: 9 -> 9, of which waited for: 7 -> 5; matrix products, arithmetic and copies ran while one was open for 12% -> 18% of each run, Pallas kernels for 29% -> 32%
where the time goes in v9:
time: 351 us; the launch traced here: 348 us
  Pallas kernels  110 us (31%)
  waiting for transfers between devices  94.3 us (27%)
  local copies, waits for them, and re-layouts  67.7 us (19%)
  other arithmetic  39 us (11%)
  starting transfers between devices  36.1 us (10%)
    all_to_all x2, waiting for transfers between devices, to_plane(): lax.all_to_all(x, ('clo', 'head'), split_axis=1, concat_axis=0, tiled=True)  64.9 us
    pallas_call x2, Pallas kernels, query_side(): pl.pallas_call(_query_side_kernel(nblk, scale), out_shape=(jax.ShapeDtype...  59.2 us
    pallas_call x2, Pallas kernels, _per_device(): pl.pallas_call(_key_side_kernel(nblk, scale), out_shape=jax.ShapeDtypeStr...  51 us
    all_to_all x3, waiting for transfers between devices, from_plane(): return lax.all_to_all(x, 'clo', split_axis=0, concat_axis=1, tiled=True)  21.2 us
    all_to_all x2, local copies, waits for them, and re-layouts, to_plane(): lax.all_to_all(x, ('clo', 'head'), split_axis=1, concat_axis=0, tiled=True)  14.3 us
    ppermute x4, starting transfers between devices, shifted(): lax.ppermute(value, axis, [(source, source + steps) for source in range(l...  13.3 us
    all_to_all x3, starting transfers between devices, from_plane(): return lax.all_to_all(x, 'clo', split_axis=0, concat_axis=1, tiled=True)  12.9 us
    transpose x2, local copies, waits for them, and re-layouts, to_plane(): jnp.concatenate([a, b], axis=3).transpose(0, 2, 1, 3, 4)  11 us
  transfers between devices with their start and end apart: 9, of which 5 were waited for; matrix products, arithmetic and copies ran while one was open for 18% of the time, Pallas kernels for 32%

profile of v9, /device:TPU:20, one launch (start us, length us, event | category | flops | bytes accessed | tf_op | source)
XLA Modules:
  0.0 348.2 jit_solution(17049775728068196522)
XLA Ops:
  4.0 4.5 %reshape.112 = bf16[128,2,4,1,1024]{4,2,1,0,3:T(4,128)(2,1)} reshape(bf16[128,8192]{1,0:T(8,128)(2,1)} %param.7) | data formatting | bytes 4194304 | tf_op jit(solution)/shard_map/reshape | solution.py:131
  8.4 4.7 %maximum_bitcast_fusion.1 = bf16[128,4,2,2,1024]{4,1,2,0,3:T(4,128)(2,1)S(1)} fusion(bf16[128,2,4,1,1024]{4,2,1,0,3:T(4,128)(2,1)} %reshape.112, bf16[128,2,4,1,1024]{4,2,1,0,3:T(4,128)(2,1)S(1)} %reshape.111), kind=kLoop, calls=%fused_computation.6 | loop fusion | flops 2097152 | bytes 8388608 | tf_op jit(solution)/shard_map/transpose | solution.py:132
  13.2 6.3 %copy.21 = bf16[128,4,2,2,1024]{4,3,0,2,1:T(2,128)(2,1)} copy(bf16[128,4,2,2,1024]{4,1,2,0,3:T(4,128)(2,1)S(1)} %maximum_bitcast_fusion.1) | data formatting | bytes 8388608 | tf_op jit(solution)/shard_map/transpose | solution.py:132
  19.5 7.8 %all_to_all.70 = bf16[128,8,2048]{2,0,1:T(8,128)(2,1)} reshape(bf16[128,4,2,2,1024]{4,3,0,2,1:T(2,128)(2,1)} %copy.21) | data formatting | bytes 8388608 | tf_op jit(solution)/shard_map/all_to_all | solution.py:135
  27.3 4.9 %all-to-all-start.1 = ((bf16[128,8,2048]{2,0,1:T(8,128)(2,1)}), bf16[128,8,2048]{2,0,1:T(8,128)(2,1)}, u32[]{:S(2)}, u32[]{:S(2)}) async-start(bf16[128,8,2048]{2,0,1:T(8,128)(2,1)} %all_to_all.70), calls=%async_computation.1 | async-start | bytes 8388608 | tf_op jit(solution)/shard_map/all_to_all | solution.py:135
  43.5 4.6 %copy.19 = bf16[128,4,2,2,1024]{0,4,3,2,1:T(8,128)(2,1)} copy(bf16[128,4,2,2,1024]{0,4,1,2,3:T(8,128)(2,1)} %maximum_bitcast_fusion) | data formatting | bytes 8388608 | tf_op jit(solution)/shard_map/transpose | solution.py:132
  55.5 24.5 %all-to-all-done.1 = bf16[128,8,2048]{2,0,1:T(8,128)(2,1)} async-done(((bf16[128,8,2048]{2,0,1:T(8,128)(2,1)}), bf16[128,8,2048]{2,0,1:T(8,128)(2,1)}, u32[]{:S(2)}, u32[]{:S(2)}) %all-to-all-start.1) | async-done | bytes 4194336 | tf_op jit(solution)/shard_map/all_to_all | solution.py:135
  80.0 5.0 %all-to-all-start = ((bf16[128,8,2048]{0,2,1:T(8,128)(2,1)}), bf16[128,8,2048]{0,2,1:T(8,128)(2,1)}, u32[]{:S(2)}, u32[]{:S(2)}) async-start(bf16[128,8,2048]{0,2,1:T(8,128)(2,1)} %bitcast.39), calls=%async_computation | async-start | bytes 8388608 | tf_op jit(solution)/shard_map/all_to_all | solution.py:135
  92.5 40.4 %all-to-all-done = bf16[128,8,2048]{0,2,1:T(8,128)(2,1)} async-done(((bf16[128,8,2048]{0,2,1:T(8,128)(2,1)}), bf16[128,8,2048]{0,2,1:T(8,128)(2,1)}, u32[]{:S(2)}, u32[]{:S(2)}) %all-to-all-start) | async-done | bytes 4194336 | tf_op jit(solution)/shard_map/all_to_all | solution.py:135
  132.9 6.6 %copy.20 = bf16[8,128,2048]{2,1,0:T(8,128)(2,1)} copy(bf16[8,128,2048]{1,2,0:T(8,128)(2,1)} %bitcast.5) | data formatting | bytes 8388608 | tf_op jit(solution)/shard_map/all_to_all | solution.py:135
  141.8 5.5 %collective-permute-start.1 = (bf16[512,2048]{1,0:T(8,128)(2,1)S(1)}, bf16[512,2048]{1,0:T(8,128)(2,1)}, u32[]{:S(2)}, u32[]{:S(2)}) collective-permute-start(bf16[512,2048]{1,0:T(8,128)(2,1)S(1)} %bitcast.46), channel_id=1, source_target_pairs={{0,8},{8,16},{16,24},{1,9},{9,17},{17,25},{2,10},{10,18},{18,26},{... | collective-permute-start | bytes 6291464 | tf_op jit(solution)/shard_map/ppermute | solution.py:21
  147.3 6.6 %pad_maximum_fusion.1.refs_2_.refs_3_.refs_4_.refs_5_.refs_6_.refs_7_.refs_8_.refs_9_.refs_10_.refs_11_ = bf16[1536,2048]{1,0:T(8,128)(2,1)} fusion(bf16[1024,2048]{1,0:T(8,128)(2,1)} %bitcast.11.refs_0_.refs_1_, bf16[512,2048]{1,0:T(8,128)(2,1)} %collective-permute-done), kind=kLoop, calls=%fused_computation.1 | loop fusion | flops 12582912 | bytes 12582912 | tf_op jit(solution)/shard_map/concatenate | solution.py:216
  154.0 29.6 %attn_query_side.2 = (bf16[512,1024]{1,0:T(8,128)(2,1)}, f32[8,2,512]{2,1,0:T(2,128)}) custom-call(bf16[1024,2048]{1,0:T(8,128)(2,1)} %bitcast.34, bf16[1024,2048]{1,0:T(8,128)(2,1)} %bitcast.35, bf16[1536,2048]{1,0:T(8,128)(2,1)} %pad_maximum_fusion.1.refs_2_.refs_3_.refs_4_.refs_5_.refs_6_.refs_7_.refs_8_.refs_9_.refs_10_.refs_11_, ...), custom_call_target="tpu_custom_call" | custom-call | tf_op jit(solution)/shard_map/attn_query_side/pallas_call | solution.py:199
  183.5 8.2 %collective-permute-done.1 = bf16[512,2048]{1,0:T(8,128)(2,1)} collective-permute-done((bf16[512,2048]{1,0:T(8,128)(2,1)S(1)}, bf16[512,2048]{1,0:T(8,128)(2,1)}, u32[]{:S(2)}, u32[]{:S(2)}) %collective-permute-start.1) | collective-permute-done | bytes 2097184 | tf_op jit(solution)/shard_map/ppermute | solution.py:21
  191.7 5.4 %pad_maximum_fusion.2.refs_2_.refs_3_.refs_4_.refs_5_.refs_6_.refs_7_.refs_8_.refs_9_.refs_10_.refs_11_ = bf16[1536,2048]{1,0:T(8,128)(2,1)} fusion(bf16[512,2048]{1,0:T(8,128)(2,1)S(1)} %bitcast.47, bf16[512,2048]{1,0:T(8,128)(2,1)} %collective-permute-done, bf16[512,2048]{1,0:T(8,128)(2,1)} %collective-permute-done.1), kind=kLoop, calls=%fused_computation.2 | loop fusion | flops 18874368 | bytes 12582912 | tf_op jit(solution)/shard_map/concatenate | solution.py:219
  197.1 29.6 %attn_query_side.3 = (bf16[512,1024]{1,0:T(8,128)(2,1)}, f32[8,2,512]{2,1,0:T(2,128)}) custom-call(bf16[1024,2048]{1,0:T(8,128)(2,1)} %bitcast.36, bf16[1024,2048]{1,0:T(8,128)(2,1)} %bitcast.37, bf16[1536,2048]{1,0:T(8,128)(2,1)} %pad_maximum_fusion.2.refs_2_.refs_3_.refs_4_.refs_5_.refs_6_.refs_7_.refs_8_.refs_9_.refs_10_.refs_11_, ...), custom_call_target="tpu_custom_call" | custom-call | tf_op jit(solution)/shard_map/attn_query_side/pallas_call | solution.py:199
  235.2 8.4 %pad_maximum_fusion.refs_2_.refs_3_.refs_4_.refs_5_.refs_6_.refs_7_.refs_8_.refs_9_.refs_10_.refs_11_ = bf16[2048,2048]{1,0:T(8,128)(2,1)} fusion(bf16[1024,2048]{1,0:T(8,128)(2,1)} %collective-permute-done.2, bf16[1024,2048]{1,0:T(8,128)(2,1)} %bitcast.38), kind=kLoop, calls=%fused_computation | loop fusion | flops 16777216 | bytes 16777216 | tf_op jit(solution)/shard_map/concatenate | solution.py:169
  244.3 25.6 %attn_key_side.3 = bf16[1024,1024]{1,0:T(8,128)(2,1)} custom-call(bf16[1024,2048]{1,0:T(8,128)(2,1)} %bitcast.11.refs_0_.refs_1_, bf16[1024,2048]{1,0:T(8,128)(2,1)} %bitcast.11.refs_0_.refs_1_, bf16[2048,2048]{1,0:T(8,128)(2,1)} %pad_maximum_fusion.refs_2_.refs_3_.refs_4_.refs_5_.refs_6_.refs_7_.refs_8_.refs_9_.refs_10_.refs_11_, ...), custom_call_target="tpu_custom_call" | custom-call | tf_op jit(solution)/shard_map/attn_key_side/pallas_call | solution.py:248
  269.9 4.7 %all-to-all-start.4 = ((bf16[4,256,1024]{2,1,0:T(8,128)(2,1)}), bf16[4,256,1024]{2,1,0:T(8,128)(2,1)}, u32[]{:S(2)}, u32[]{:S(2)}) async-start(bf16[4,256,1024]{2,1,0:T(8,128)(2,1)} %bitcast.41), calls=%async_computation.4 | async-start | bytes 4194304 | tf_op jit(solution)/shard_map/all_to_all | solution.py:231
  274.6 25.4 %attn_key_side.2 = bf16[1024,1024]{1,0:T(8,128)(2,1)} custom-call(bf16[1024,2048]{1,0:T(8,128)(2,1)} %bitcast.11.refs_0_.refs_1_, bf16[1024,2048]{1,0:T(8,128)(2,1)} %bitcast.11.refs_0_.refs_1_, bf16[2048,2048]{1,0:T(8,128)(2,1)} %pad_maximum_fusion.refs_2_.refs_3_.refs_4_.refs_5_.refs_6_.refs_7_.refs_8_.refs_9_.refs_10_.refs_11_, ...), custom_call_target="tpu_custom_call" | custom-call | tf_op jit(solution)/shard_map/attn_key_side/pallas_call | solution.py:248
  300.4 4.5 %all-to-all-start.3 = ((bf16[4,256,1024]{2,1,0:T(8,128)(2,1)}), bf16[4,256,1024]{2,1,0:T(8,128)(2,1)}, u32[]{:S(2)}, u32[]{:S(2)}) async-start(bf16[4,256,1024]{2,1,0:T(8,128)(2,1)} %bitcast.40), calls=%async_computation.3 | async-start | bytes 4194304 | tf_op jit(solution)/shard_map/all_to_all | solution.py:231
  309.6 21.0 %all-to-all-done.3 = bf16[4,256,1024]{2,1,0:T(8,128)(2,1)} async-done(((bf16[4,256,1024]{2,1,0:T(8,128)(2,1)}), bf16[4,256,1024]{2,1,0:T(8,128)(2,1)}, u32[]{:S(2)}, u32[]{:S(2)}) %all-to-all-start.3) | async-done | bytes 2097184 | tf_op jit(solution)/shard_map/all_to_all | solution.py:231
  330.6 4.4 %reshape.113 = bf16[256,4,1,4,2,128]{5,4,3,0,1,2:T(2,128)(2,1)} reshape(bf16[256,4,1024]{2,0,1:T(8,128)(2,1)} %bitcast.16) | data formatting | bytes 4194304 | tf_op jit(solution)/shard_map/reshape | solution.py:258
  340.9 4.5 %reshape_squeeze.6 = bf16[256,4096]{1,0:T(8,128)(2,1)} reshape(bf16[256,4,2,4,1,128]{5,3,2,1,0,4:T(4,128)(2,1)} %get-tuple-element.28) | data formatting | bytes 4194304 | tf_op jit(solution)/shard_map/reshape;squeeze | solution.py:262
  (55 shorter events, 54.6 us)
Async XLA Ops:
  27.3 52.8 %all-to-all-start.1 = ((bf16[128,8,2048]{2,0,1:T(8,128)(2,1)}), bf16[128,8,2048]{2,0,1:T(8,128)(2,1)}, u32[]{:S(2)}, u32[]{:S(2)}) async-start(bf16[128,8,2048]{2,0,1:T(8,128)(2,1)} %all_to_all.70), calls=%async_computation.1 | async-start | bytes 8388608 | tf_op jit(solution)/shard_map/all_to_all | solution.py:135
  43.5 4.6 %copy-start.4 = (s32[4096]{0:T(1024)S(1)}, s32[4096]{0:T(1024)}, u32[]{:S(2)}) copy-start(s32[4096]{0:T(1024)} %param.9) | copy-start | bytes 49156
  80.0 52.8 %all-to-all-start = ((bf16[128,8,2048]{0,2,1:T(8,128)(2,1)}), bf16[128,8,2048]{0,2,1:T(8,128)(2,1)}, u32[]{:S(2)}, u32[]{:S(2)}) async-start(bf16[128,8,2048]{0,2,1:T(8,128)(2,1)} %bitcast.39), calls=%async_computation | async-start | bytes 8388608 | tf_op jit(solution)/shard_map/all_to_all | solution.py:135
  89.0 52.7 %collective-permute-start = (bf16[512,2048]{1,0:T(8,128)(2,1)}, bf16[512,2048]{1,0:T(8,128)(2,1)}, u32[]{:S(2)}, u32[]{:S(2)}) collective-permute-start(bf16[512,2048]{1,0:T(8,128)(2,1)} %bitcast.10), channel_id=1, source_target_pairs={{0,8},{8,16},{16,24},{1,9},{9,17},{17,25},{2,10},{10,18},{18,26},{... | collective-permute-start | bytes 6291464 | tf_op jit(solution)/shard_map/ppermute | solution.py:21
  139.4 95.8 %collective-permute-start.2 = (bf16[1024,2048]{1,0:T(8,128)(2,1)}, bf16[1024,2048]{1,0:T(8,128)(2,1)}, u32[]{:S(2)}, u32[]{:S(2)}) collective-permute-start(bf16[1024,2048]{1,0:T(8,128)(2,1)} %bitcast.33), channel_id=1, source_target_pairs={{8,0},{16,8},{24,16},{9,1},{17,9},{25,17},{10,2},{18,10},{26,18},{... | collective-permute-start | bytes 12582920 | tf_op jit(solution)/shard_map/ppermute | solution.py:21
  141.8 49.9 %collective-permute-start.1 = (bf16[512,2048]{1,0:T(8,128)(2,1)S(1)}, bf16[512,2048]{1,0:T(8,128)(2,1)}, u32[]{:S(2)}, u32[]{:S(2)}) collective-permute-start(bf16[512,2048]{1,0:T(8,128)(2,1)S(1)} %bitcast.46), channel_id=1, source_target_pairs={{0,8},{8,16},{16,24},{1,9},{9,17},{17,25},{2,10},{10,18},{18,26},{... | collective-permute-start | bytes 6291464 | tf_op jit(solution)/shard_map/ppermute | solution.py:21
  197.1 29.6 %copy-start.1 = (bf16[512,1024]{1,0:T(8,128)(2,1)S(1)}, bf16[512,1024]{1,0:T(8,128)(2,1)}, u32[]{:S(2)}) copy-start(bf16[512,1024]{1,0:T(8,128)(2,1)} %get-tuple-element.23) | copy-start | bytes 3145732
  229.5 3.8 %copy-start.2 = (f32[8,2,512]{2,1,0:T(2,128)S(1)}, f32[8,2,512]{2,1,0:T(2,128)}, u32[]{:S(2)}) copy-start(f32[8,2,512]{2,1,0:T(2,128)} %get-tuple-element.25) | copy-start | bytes 98308
  229.5 3.8 %copy-start.3 = (f32[8,2,512]{2,1,0:T(2,128)S(1)}, f32[8,2,512]{2,1,0:T(2,128)}, u32[]{:S(2)}) copy-start(f32[8,2,512]{2,1,0:T(2,128)} %get-tuple-element.24) | copy-start | bytes 98308
  229.5 40.4 %all-to-all-start.2 = ((bf16[4,256,1024]{2,1,0:T(8,128)(2,1)}), bf16[4,256,1024]{2,1,0:T(8,128)(2,1)S(1)}, u32[]{:S(2)}, u32[]{:S(2)}) async-start(bf16[4,256,1024]{2,1,0:T(8,128)(2,1)} %bitcast.43), calls=%async_computation.2 | async-start | bytes 4194304 | tf_op jit(solution)/shard_map/all_to_all | solution.py:231
  233.3 10.4 %collective-permute-start.3 = (f32[8,2,1024]{2,1,0:T(2,128)S(1)}, f32[8,2,1024]{2,1,0:T(2,128)S(1)}, u32[]{:S(2)}, u32[]{:S(2)}) collective-permute-start(f32[8,2,1024]{2,1,0:T(2,128)S(1)} %pad_maximum_fusion.6), channel_id=1, source_target_pairs={{8,0},{16,8},{24,16},{9,1},{17,9},{25,17},{10,2},{18,10},{26,18},{... | collective-permute-start | bytes 196616 | tf_op jit(solution)/shard_map/ppermute | solution.py:21
  243.7 0.7 copy-start
  269.9 30.4 %all-to-all-start.4 = ((bf16[4,256,1024]{2,1,0:T(8,128)(2,1)}), bf16[4,256,1024]{2,1,0:T(8,128)(2,1)}, u32[]{:S(2)}, u32[]{:S(2)}) async-start(bf16[4,256,1024]{2,1,0:T(8,128)(2,1)} %bitcast.41), calls=%async_computation.4 | async-start | bytes 4194304 | tf_op jit(solution)/shard_map/all_to_all | solution.py:231
  300.4 30.2 %all-to-all-start.3 = ((bf16[4,256,1024]{2,1,0:T(8,128)(2,1)}), bf16[4,256,1024]{2,1,0:T(8,128)(2,1)}, u32[]{:S(2)}, u32[]{:S(2)}) async-start(bf16[4,256,1024]{2,1,0:T(8,128)(2,1)} %bitcast.40), calls=%async_computation.3 | async-start | bytes 4194304 | tf_op jit(solution)/shard_map/all_to_all | solution.py:231

commit v10 on v9

--- a/solution.py
+++ b/solution.py
@@ -42,11 +42,13 @@
         top = logits[0].max(axis=1, keepdims=True)
         for j in range(1, nblk):
             top = jnp.maximum(top, logits[j].max(axis=1, keepdims=True))
-        denom = jnp.exp(logits[0] - top).sum(axis=1, keepdims=True)
+        expd = [jnp.exp(item - top) for item in logits]
+        denom = expd[0].sum(axis=1, keepdims=True)
         for j in range(1, nblk):
-            denom = denom + jnp.exp(logits[j] - top).sum(axis=1, keepdims=True)
+            denom = denom + expd[j].sum(axis=1, keepdims=True)
         lse = top + jnp.log(denom)
-        probs = [jnp.exp(item - lse) for item in logits]
+        inv = 1.0 / denom
+        probs = [item * inv for item in expd]
         out = None
         for j in range(nblk):
             part = jnp.dot(probs[j].astype(jnp.bfloat16), v_refs[j][...],

time: 351 us -> 351 us (level)
  transfers between devices with their start and end apart: 9 -> 9, of which waited for: 5 -> 5; matrix products, arithmetic and copies ran while one was open for 18% -> 18% of each run, Pallas kernels for 32% -> 31%
where the time goes in v10:
time: 351 us; the launch traced here: 348 us
  Pallas kernels  110 us (31%)
  waiting for transfers between devices  94.6 us (27%)
  local copies, waits for them, and re-layouts  67.7 us (19%)
  other arithmetic  39 us (11%)
  starting transfers between devices  36.1 us (10%)
    all_to_all x2, waiting for transfers between devices, to_plane(): lax.all_to_all(x, ('clo', 'head'), split_axis=1, concat_axis=0, tiled=True)  64.9 us
    pallas_call x2, Pallas kernels, query_side(): pl.pallas_call(_query_side_kernel(nblk, scale), out_shape=(jax.ShapeDtype...  58.5 us
    pallas_call x2, Pallas kernels, _per_device(): pl.pallas_call(_key_side_kernel(nblk, scale), out_shape=jax.ShapeDtypeStr...  51 us
    all_to_all x3, waiting for transfers between devices, from_plane(): return lax.all_to_all(x, 'clo', split_axis=0, concat_axis=1, tiled=True)  21.2 us
    all_to_all x2, local copies, waits for them, and re-layouts, to_plane(): lax.all_to_all(x, ('clo', 'head'), split_axis=1, concat_axis=0, tiled=True)  14.3 us
    ppermute x4, starting transfers between devices, shifted(): lax.ppermute(value, axis, [(source, source + steps) for source in range(l...  13.3 us
    all_to_all x3, starting transfers between devices, from_plane(): return lax.all_to_all(x, 'clo', split_axis=0, concat_axis=1, tiled=True)  12.9 us
    transpose x2, local copies, waits for them, and re-layouts, to_plane(): jnp.concatenate([a, b], axis=3).transpose(0, 2, 1, 3, 4)  11 us
  transfers between devices with their start and end apart: 9, of which 5 were waited for; matrix products, arithmetic and copies ran while one was open for 18% of the time, Pallas kernels for 31%

profile of v10, /device:TPU:20, one launch (start us, length us, event | category | flops | bytes accessed | tf_op | source)
XLA Modules:
  0.0 347.9 jit_solution(1107802781086019226)
XLA Ops:
  4.0 4.5 %reshape.112 = bf16[128,2,4,1,1024]{4,2,1,0,3:T(4,128)(2,1)} reshape(bf16[128,8192]{1,0:T(8,128)(2,1)} %param.7) | data formatting | bytes 4194304 | tf_op jit(solution)/shard_map/reshape | solution.py:133
  8.4 4.7 %maximum_bitcast_fusion.1 = bf16[128,4,2,2,1024]{4,1,2,0,3:T(4,128)(2,1)S(1)} fusion(bf16[128,2,4,1,1024]{4,2,1,0,3:T(4,128)(2,1)} %reshape.112, bf16[128,2,4,1,1024]{4,2,1,0,3:T(4,128)(2,1)S(1)} %reshape.111), kind=kLoop, calls=%fused_computation.6 | loop fusion | flops 2097152 | bytes 8388608 | tf_op jit(solution)/shard_map/transpose | solution.py:134
  13.2 6.3 %copy.21 = bf16[128,4,2,2,1024]{4,3,0,2,1:T(2,128)(2,1)} copy(bf16[128,4,2,2,1024]{4,1,2,0,3:T(4,128)(2,1)S(1)} %maximum_bitcast_fusion.1) | data formatting | bytes 8388608 | tf_op jit(solution)/shard_map/transpose | solution.py:134
  19.5 7.8 %all_to_all.70 = bf16[128,8,2048]{2,0,1:T(8,128)(2,1)} reshape(bf16[128,4,2,2,1024]{4,3,0,2,1:T(2,128)(2,1)} %copy.21) | data formatting | bytes 8388608 | tf_op jit(solution)/shard_map/all_to_all | solution.py:137
  27.3 4.9 %all-to-all-start.1 = ((bf16[128,8,2048]{2,0,1:T(8,128)(2,1)}), bf16[128,8,2048]{2,0,1:T(8,128)(2,1)}, u32[]{:S(2)}, u32[]{:S(2)}) async-start(bf16[128,8,2048]{2,0,1:T(8,128)(2,1)} %all_to_all.70), calls=%async_computation.1 | async-start | bytes 8388608 | tf_op jit(solution)/shard_map/all_to_all | solution.py:137
  43.5 4.6 %copy.19 = bf16[128,4,2,2,1024]{0,4,3,2,1:T(8,128)(2,1)} copy(bf16[128,4,2,2,1024]{0,4,1,2,3:T(8,128)(2,1)} %maximum_bitcast_fusion) | data formatting | bytes 8388608 | tf_op jit(solution)/shard_map/transpose | solution.py:134
  55.5 24.5 %all-to-all-done.1 = bf16[128,8,2048]{2,0,1:T(8,128)(2,1)} async-done(((bf16[128,8,2048]{2,0,1:T(8,128)(2,1)}), bf16[128,8,2048]{2,0,1:T(8,128)(2,1)}, u32[]{:S(2)}, u32[]{:S(2)}) %all-to-all-start.1) | async-done | bytes 4194336 | tf_op jit(solution)/shard_map/all_to_all | solution.py:137
  80.0 5.0 %all-to-all-start = ((bf16[128,8,2048]{0,2,1:T(8,128)(2,1)}), bf16[128,8,2048]{0,2,1:T(8,128)(2,1)}, u32[]{:S(2)}, u32[]{:S(2)}) async-start(bf16[128,8,2048]{0,2,1:T(8,128)(2,1)} %bitcast.39), calls=%async_computation | async-start | bytes 8388608 | tf_op jit(solution)/shard_map/all_to_all | solution.py:137
  92.5 40.4 %all-to-all-done = bf16[128,8,2048]{0,2,1:T(8,128)(2,1)} async-done(((bf16[128,8,2048]{0,2,1:T(8,128)(2,1)}), bf16[128,8,2048]{0,2,1:T(8,128)(2,1)}, u32[]{:S(2)}, u32[]{:S(2)}) %all-to-all-start) | async-done | bytes 4194336 | tf_op jit(solution)/shard_map/all_to_all | solution.py:137
  132.9 6.6 %copy.20 = bf16[8,128,2048]{2,1,0:T(8,128)(2,1)} copy(bf16[8,128,2048]{1,2,0:T(8,128)(2,1)} %bitcast.5) | data formatting | bytes 8388608 | tf_op jit(solution)/shard_map/all_to_all | solution.py:137
  141.8 5.5 %collective-permute-start.1 = (bf16[512,2048]{1,0:T(8,128)(2,1)S(1)}, bf16[512,2048]{1,0:T(8,128)(2,1)}, u32[]{:S(2)}, u32[]{:S(2)}) collective-permute-start(bf16[512,2048]{1,0:T(8,128)(2,1)S(1)} %bitcast.46), channel_id=1, source_target_pairs={{0,8},{8,16},{16,24},{1,9},{9,17},{17,25},{2,10},{10,18},{18,26},{... | collective-permute-start | bytes 6291464 | tf_op jit(solution)/shard_map/ppermute | solution.py:21
  147.3 6.6 %pad_maximum_fusion.1.refs_2_.refs_3_.refs_4_.refs_5_.refs_6_.refs_7_.refs_8_.refs_9_.refs_10_.refs_11_ = bf16[1536,2048]{1,0:T(8,128)(2,1)} fusion(bf16[1024,2048]{1,0:T(8,128)(2,1)} %bitcast.11.refs_0_.refs_1_, bf16[512,2048]{1,0:T(8,128)(2,1)} %collective-permute-done), kind=kLoop, calls=%fused_computation.1 | loop fusion | flops 12582912 | bytes 12582912 | tf_op jit(solution)/shard_map/concatenate | solution.py:218
  154.0 29.3 %attn_query_side.2 = (bf16[512,1024]{1,0:T(8,128)(2,1)}, f32[8,2,512]{2,1,0:T(2,128)}) custom-call(bf16[1024,2048]{1,0:T(8,128)(2,1)} %bitcast.34, bf16[1024,2048]{1,0:T(8,128)(2,1)} %bitcast.35, bf16[1536,2048]{1,0:T(8,128)(2,1)} %pad_maximum_fusion.1.refs_2_.refs_3_.refs_4_.refs_5_.refs_6_.refs_7_.refs_8_.refs_9_.refs_10_.refs_11_, ...), custom_call_target="tpu_custom_call" | custom-call | tf_op jit(solution)/shard_map/attn_query_side/pallas_call | solution.py:201
  183.2 8.5 %collective-permute-done.1 = bf16[512,2048]{1,0:T(8,128)(2,1)} collective-permute-done((bf16[512,2048]{1,0:T(8,128)(2,1)S(1)}, bf16[512,2048]{1,0:T(8,128)(2,1)}, u32[]{:S(2)}, u32[]{:S(2)}) %collective-permute-start.1) | collective-permute-done | bytes 2097184 | tf_op jit(solution)/shard_map/ppermute | solution.py:21
  191.7 5.4 %pad_maximum_fusion.2.refs_2_.refs_3_.refs_4_.refs_5_.refs_6_.refs_7_.refs_8_.refs_9_.refs_10_.refs_11_ = bf16[1536,2048]{1,0:T(8,128)(2,1)} fusion(bf16[512,2048]{1,0:T(8,128)(2,1)S(1)} %bitcast.47, bf16[512,2048]{1,0:T(8,128)(2,1)} %collective-permute-done, bf16[512,2048]{1,0:T(8,128)(2,1)} %collective-permute-done.1), kind=kLoop, calls=%fused_computation.2 | loop fusion | flops 18874368 | bytes 12582912 | tf_op jit(solution)/shard_map/concatenate | solution.py:221
  197.1 29.3 %attn_query_side.3 = (bf16[512,1024]{1,0:T(8,128)(2,1)}, f32[8,2,512]{2,1,0:T(2,128)}) custom-call(bf16[1024,2048]{1,0:T(8,128)(2,1)} %bitcast.36, bf16[1024,2048]{1,0:T(8,128)(2,1)} %bitcast.37, bf16[1536,2048]{1,0:T(8,128)(2,1)} %pad_maximum_fusion.2.refs_2_.refs_3_.refs_4_.refs_5_.refs_6_.refs_7_.refs_8_.refs_9_.refs_10_.refs_11_, ...), custom_call_target="tpu_custom_call" | custom-call | tf_op jit(solution)/shard_map/attn_query_side/pallas_call | solution.py:201
  234.9 8.4 %pad_maximum_fusion.refs_2_.refs_3_.refs_4_.refs_5_.refs_6_.refs_7_.refs_8_.refs_9_.refs_10_.refs_11_ = bf16[2048,2048]{1,0:T(8,128)(2,1)} fusion(bf16[1024,2048]{1,0:T(8,128)(2,1)} %collective-permute-done.2, bf16[1024,2048]{1,0:T(8,128)(2,1)} %bitcast.38), kind=kLoop, calls=%fused_computation | loop fusion | flops 16777216 | bytes 16777216 | tf_op jit(solution)/shard_map/concatenate | solution.py:171
  244.0 25.6 %attn_key_side.3 = bf16[1024,1024]{1,0:T(8,128)(2,1)} custom-call(bf16[1024,2048]{1,0:T(8,128)(2,1)} %bitcast.11.refs_0_.refs_1_, bf16[1024,2048]{1,0:T(8,128)(2,1)} %bitcast.11.refs_0_.refs_1_, bf16[2048,2048]{1,0:T(8,128)(2,1)} %pad_maximum_fusion.refs_2_.refs_3_.refs_4_.refs_5_.refs_6_.refs_7_.refs_8_.refs_9_.refs_10_.refs_11_, ...), custom_call_target="tpu_custom_call" | custom-call | tf_op jit(solution)/shard_map/attn_key_side/pallas_call | solution.py:250
  269.6 4.7 %all-to-all-start.4 = ((bf16[4,256,1024]{2,1,0:T(8,128)(2,1)}), bf16[4,256,1024]{2,1,0:T(8,128)(2,1)}, u32[]{:S(2)}, u32[]{:S(2)}) async-start(bf16[4,256,1024]{2,1,0:T(8,128)(2,1)} %bitcast.41), calls=%async_computation.4 | async-start | bytes 4194304 | tf_op jit(solution)/shard_map/all_to_all | solution.py:233
  274.3 25.4 %attn_key_side.2 = bf16[1024,1024]{1,0:T(8,128)(2,1)} custom-call(bf16[1024,2048]{1,0:T(8,128)(2,1)} %bitcast.11.refs_0_.refs_1_, bf16[1024,2048]{1,0:T(8,128)(2,1)} %bitcast.11.refs_0_.refs_1_, bf16[2048,2048]{1,0:T(8,128)(2,1)} %pad_maximum_fusion.refs_2_.refs_3_.refs_4_.refs_5_.refs_6_.refs_7_.refs_8_.refs_9_.refs_10_.refs_11_, ...), custom_call_target="tpu_custom_call" | custom-call | tf_op jit(solution)/shard_map/attn_key_side/pallas_call | solution.py:250
  300.0 4.5 %all-to-all-start.3 = ((bf16[4,256,1024]{2,1,0:T(8,128)(2,1)}), bf16[4,256,1024]{2,1,0:T(8,128)(2,1)}, u32[]{:S(2)}, u32[]{:S(2)}) async-start(bf16[4,256,1024]{2,1,0:T(8,128)(2,1)} %bitcast.40), calls=%async_computation.3 | async-start | bytes 4194304 | tf_op jit(solution)/shard_map/all_to_all | solution.py:233
  309.3 21.0 %all-to-all-done.3 = bf16[4,256,1024]{2,1,0:T(8,128)(2,1)} async-done(((bf16[4,256,1024]{2,1,0:T(8,128)(2,1)}), bf16[4,256,1024]{2,1,0:T(8,128)(2,1)}, u32[]{:S(2)}, u32[]{:S(2)}) %all-to-all-start.3) | async-done | bytes 2097184 | tf_op jit(solution)/shard_map/all_to_all | solution.py:233
  330.2 4.4 %reshape.113 = bf16[256,4,1,4,2,128]{5,4,3,0,1,2:T(2,128)(2,1)} reshape(bf16[256,4,1024]{2,0,1:T(8,128)(2,1)} %bitcast.16) | data formatting | bytes 4194304 | tf_op jit(solution)/shard_map/reshape | solution.py:260
  340.6 4.5 %reshape_squeeze.6 = bf16[256,4096]{1,0:T(8,128)(2,1)} reshape(bf16[256,4,2,4,1,128]{5,3,2,1,0,4:T(4,128)(2,1)} %get-tuple-element.28) | data formatting | bytes 4194304 | tf_op jit(solution)/shard_map/reshape;squeeze | solution.py:264
  (55 shorter events, 54.6 us)
Async XLA Ops:
  27.3 52.8 %all-to-all-start.1 = ((bf16[128,8,2048]{2,0,1:T(8,128)(2,1)}), bf16[128,8,2048]{2,0,1:T(8,128)(2,1)}, u32[]{:S(2)}, u32[]{:S(2)}) async-start(bf16[128,8,2048]{2,0,1:T(8,128)(2,1)} %all_to_all.70), calls=%async_computation.1 | async-start | bytes 8388608 | tf_op jit(solution)/shard_map/all_to_all | solution.py:137
  43.5 4.6 %copy-start.4 = (s32[4096]{0:T(1024)S(1)}, s32[4096]{0:T(1024)}, u32[]{:S(2)}) copy-start(s32[4096]{0:T(1024)} %param.9) | copy-start | bytes 49156
  80.0 52.8 %all-to-all-start = ((bf16[128,8,2048]{0,2,1:T(8,128)(2,1)}), bf16[128,8,2048]{0,2,1:T(8,128)(2,1)}, u32[]{:S(2)}, u32[]{:S(2)}) async-start(bf16[128,8,2048]{0,2,1:T(8,128)(2,1)} %bitcast.39), calls=%async_computation | async-start | bytes 8388608 | tf_op jit(solution)/shard_map/all_to_all | solution.py:137
  89.0 52.7 %collective-permute-start = (bf16[512,2048]{1,0:T(8,128)(2,1)}, bf16[512,2048]{1,0:T(8,128)(2,1)}, u32[]{:S(2)}, u32[]{:S(2)}) collective-permute-start(bf16[512,2048]{1,0:T(8,128)(2,1)} %bitcast.10), channel_id=1, source_target_pairs={{0,8},{8,16},{16,24},{1,9},{9,17},{17,25},{2,10},{10,18},{18,26},{... | collective-permute-start | bytes 6291464 | tf_op jit(solution)/shard_map/ppermute | solution.py:21
  139.4 95.5 %collective-permute-start.2 = (bf16[1024,2048]{1,0:T(8,128)(2,1)}, bf16[1024,2048]{1,0:T(8,128)(2,1)}, u32[]{:S(2)}, u32[]{:S(2)}) collective-permute-start(bf16[1024,2048]{1,0:T(8,128)(2,1)} %bitcast.33), channel_id=1, source_target_pairs={{8,0},{16,8},{24,16},{9,1},{17,9},{25,17},{10,2},{18,10},{26,18},{... | collective-permute-start | bytes 12582920 | tf_op jit(solution)/shard_map/ppermute | solution.py:21
  141.8 49.9 %collective-permute-start.1 = (bf16[512,2048]{1,0:T(8,128)(2,1)S(1)}, bf16[512,2048]{1,0:T(8,128)(2,1)}, u32[]{:S(2)}, u32[]{:S(2)}) collective-permute-start(bf16[512,2048]{1,0:T(8,128)(2,1)S(1)} %bitcast.46), channel_id=1, source_target_pairs={{0,8},{8,16},{16,24},{1,9},{9,17},{17,25},{2,10},{10,18},{18,26},{... | collective-permute-start | bytes 6291464 | tf_op jit(solution)/shard_map/ppermute | solution.py:21
  197.1 29.3 %copy-start.1 = (bf16[512,1024]{1,0:T(8,128)(2,1)S(1)}, bf16[512,1024]{1,0:T(8,128)(2,1)}, u32[]{:S(2)}) copy-start(bf16[512,1024]{1,0:T(8,128)(2,1)} %get-tuple-element.23) | copy-start | bytes 3145732
  229.1 3.8 %copy-start.2 = (f32[8,2,512]{2,1,0:T(2,128)S(1)}, f32[8,2,512]{2,1,0:T(2,128)}, u32[]{:S(2)}) copy-start(f32[8,2,512]{2,1,0:T(2,128)} %get-tuple-element.25) | copy-start | bytes 98308
  229.1 3.8 %copy-start.3 = (f32[8,2,512]{2,1,0:T(2,128)S(1)}, f32[8,2,512]{2,1,0:T(2,128)}, u32[]{:S(2)}) copy-start(f32[8,2,512]{2,1,0:T(2,128)} %get-tuple-element.24) | copy-start | bytes 98308
  229.1 40.4 %all-to-all-start.2 = ((bf16[4,256,1024]{2,1,0:T(8,128)(2,1)}), bf16[4,256,1024]{2,1,0:T(8,128)(2,1)S(1)}, u32[]{:S(2)}, u32[]{:S(2)}) async-start(bf16[4,256,1024]{2,1,0:T(8,128)(2,1)} %bitcast.43), calls=%async_computation.2 | async-start | bytes 4194304 | tf_op jit(solution)/shard_map/all_to_all | solution.py:233
  233.0 10.4 %collective-permute-start.3 = (f32[8,2,1024]{2,1,0:T(2,128)S(1)}, f32[8,2,1024]{2,1,0:T(2,128)S(1)}, u32[]{:S(2)}, u32[]{:S(2)}) collective-permute-start(f32[8,2,1024]{2,1,0:T(2,128)S(1)} %pad_maximum_fusion.6), channel_id=1, source_target_pairs={{8,0},{16,8},{24,16},{9,1},{17,9},{25,17},{10,2},{18,10},{26,18},{... | collective-permute-start | bytes 196616 | tf_op jit(solution)/shard_map/ppermute | solution.py:21
  243.3 0.7 copy-start
  269.6 30.4 %all-to-all-start.4 = ((bf16[4,256,1024]{2,1,0:T(8,128)(2,1)}), bf16[4,256,1024]{2,1,0:T(8,128)(2,1)}, u32[]{:S(2)}, u32[]{:S(2)}) async-start(bf16[4,256,1024]{2,1,0:T(8,128)(2,1)} %bitcast.41), calls=%async_computation.4 | async-start | bytes 4194304 | tf_op jit(solution)/shard_map/all_to_all | solution.py:233
  300.0 30.2 %all-to-all-start.3 = ((bf16[4,256,1024]{2,1,0:T(8,128)(2,1)}), bf16[4,256,1024]{2,1,0:T(8,128)(2,1)}, u32[]{:S(2)}, u32[]{:S(2)}) async-start(bf16[4,256,1024]{2,1,0:T(8,128)(2,1)} %bitcast.40), calls=%async_computation.3 | async-start | bytes 4194304 | tf_op jit(solution)/shard_map/all_to_all | solution.py:233

commit v11 on v10

--- a/solution.py
+++ b/solution.py
@@ -257,13 +257,15 @@
             compiler_params=params,
             name="attn_key_side",
         )(kv, kv, *([qd_win] * (2 * nblk)), *([ld_win] * nblk), k_bias)
-        dkv_parts.append(from_plane(dkv_g).reshape(-1, clo_n, 1, hg, 2, HEAD_DIM))
-
-    dkv = jnp.concatenate(dkv_parts, axis=2)
-    rows = dkv.shape[0]
-    attn_dk = dkv[:, :, :, :, 0, :].reshape(rows, clo_n * width)
-    attn_dv = dkv[:, :, :, :, 1, :].reshape(rows, clo_n * width)
-    return (from_plane(dq), attn_dk, attn_dv)
+        dkv_parts.append(from_plane(dkv_g).reshape(-1, clo_n, hg, 2, HEAD_DIM))
+
+    rows = dkv_parts[0].shape[0]
+    attn_dk = jnp.zeros((rows, clo_n, groups, hg, HEAD_DIM), jnp.bfloat16)
+    attn_dv = jnp.zeros((rows, clo_n, groups, hg, HEAD_DIM), jnp.bfloat16)
+    for g, part in enumerate(dkv_parts):
+        attn_dk = attn_dk.at[:, :, g].set(part[:, :, :, 0, :])
+        attn_dv = attn_dv.at[:, :, g].set(part[:, :, :, 1, :])
+    return (from_plane(dq), attn_dk.reshape(rows, clo_n * width), attn_dv.reshape(rows, clo_n * width))
 
 
 def solution(mesh):

time: 351 us -> 351 us (level)
  waiting for transfers between devices: 94.6 us -> 90.3 us
    another operation x2 -> x0, local copies, waits for them, and re-layouts: 7.25 us -> none  [the longest x1 4.47 us: _per_device(): attn_dk = dkv[:, :, :, :, 0, :].reshape(rows, clo_n * width)]
    slice x1 -> x2, local copies, waits for them, and re-layouts: 2.45 us -> 7.61 us  [_per_device(): attn_dv = attn_dv.at[:, :, g].set(part[:, :, :, 1, :])]
    reshape x2 -> x4, local copies, waits for them, and re-layouts: 7.66 us -> 12.1 us  [the longest x2 6.46 us: _per_device(): dkv_parts.append(from_plane(dkv_g).reshape(-1, clo_n, hg, 2, HEAD_DIM))]
    all_to_all x3, waiting for transfers between devices: 21.2 us -> 16.9 us  [from_plane(): return lax.all_to_all(x, 'clo', split_axis=0, concat_axis=1, tiled=True)]
    unnamed x15 -> x20, local copies, waits for them, and re-layouts: 10.2 us -> 11.3 us
  transfers between devices with their start and end apart: 9 -> 9, of which waited for: 5 -> 5; matrix products, arithmetic and copies ran while one was open for 18% -> 19% of each run, Pallas kernels for 31% -> 31%
where the time goes in v11:
time: 351 us; the launch traced here: 349 us
  Pallas kernels  110 us (31%)
  waiting for transfers between devices  90.3 us (26%)
  local copies, waits for them, and re-layouts  69.8 us (20%)
  other arithmetic  42 us (12%)
  starting transfers between devices  36.1 us (10%)
    all_to_all x2, waiting for transfers between devices, to_plane(): lax.all_to_all(x, ('clo', 'head'), split_axis=1, concat_axis=0, tiled=True)  64.9 us
    pallas_call x2, Pallas kernels, query_side(): pl.pallas_call(_query_side_kernel(nblk, scale), out_shape=(jax.ShapeDtype...  58.5 us
    pallas_call x2, Pallas kernels, _per_device(): pl.pallas_call(_key_side_kernel(nblk, scale), out_shape=jax.ShapeDtypeStr...  51 us
    all_to_all x3, waiting for transfers between devices, from_plane(): return lax.all_to_all(x, 'clo', split_axis=0, concat_axis=1, tiled=True)  16.9 us
    all_to_all x2, local copies, waits for them, and re-layouts, to_plane(): lax.all_to_all(x, ('clo', 'head'), split_axis=1, concat_axis=0, tiled=True)  14.3 us
    ppermute x4, starting transfers between devices, shifted(): lax.ppermute(value, axis, [(source, source + steps) for source in range(l...  13.3 us
    all_to_all x3, starting transfers between devices, from_plane(): return lax.all_to_all(x, 'clo', split_axis=0, concat_axis=1, tiled=True)  12.9 us
    unnamed x20, local copies, waits for them, and re-layouts  11.3 us
  transfers between devices with their start and end apart: 9, of which 5 were waited for; matrix products, arithmetic and copies ran while one was open for 19% of the time, Pallas kernels for 31%

profile of v11, /device:TPU:20, one launch (start us, length us, event | category | flops | bytes accessed | tf_op | source)
XLA Modules:
  0.0 348.7 jit_solution(15121764151550318135)
XLA Ops:
  4.0 4.5 %reshape.284 = bf16[128,2,4,1,1024]{4,2,1,0,3:T(4,128)(2,1)} reshape(bf16[128,8192]{1,0:T(8,128)(2,1)} %param.15) | data formatting | bytes 4194304 | tf_op jit(solution)/shard_map/reshape | solution.py:133
  8.4 4.7 %maximum_bitcast_fusion.1 = bf16[128,4,2,2,1024]{4,1,2,0,3:T(4,128)(2,1)S(1)} fusion(bf16[128,2,4,1,1024]{4,2,1,0,3:T(4,128)(2,1)} %reshape.284, bf16[128,2,4,1,1024]{4,2,1,0,3:T(4,128)(2,1)S(1)} %reshape.283), kind=kLoop, calls=%fused_computation.6 | loop fusion | flops 2097152 | bytes 8388608 | tf_op jit(solution)/shard_map/transpose | solution.py:134
  13.2 6.3 %copy.25 = bf16[128,4,2,2,1024]{4,3,0,2,1:T(2,128)(2,1)} copy(bf16[128,4,2,2,1024]{4,1,2,0,3:T(4,128)(2,1)S(1)} %maximum_bitcast_fusion.1) | data formatting | bytes 8388608 | tf_op jit(solution)/shard_map/transpose | solution.py:134
  19.5 7.8 %all_to_all.70 = bf16[128,8,2048]{2,0,1:T(8,128)(2,1)} reshape(bf16[128,4,2,2,1024]{4,3,0,2,1:T(2,128)(2,1)} %copy.25) | data formatting | bytes 8388608 | tf_op jit(solution)/shard_map/all_to_all | solution.py:137
  27.3 5.0 %all-to-all-start.1 = ((bf16[128,8,2048]{2,0,1:T(8,128)(2,1)}), bf16[128,8,2048]{2,0,1:T(8,128)(2,1)}, u32[]{:S(2)}, u32[]{:S(2)}) async-start(bf16[128,8,2048]{2,0,1:T(8,128)(2,1)} %all_to_all.70), calls=%async_computation.1 | async-start | bytes 8388608 | tf_op jit(solution)/shard_map/all_to_all | solution.py:137
  35.5 4.1 %copy.22 = bf16[128,8192]{0,1:T(8,128)(2,1)} copy(bf16[128,8192]{1,0:T(8,128)(2,1)} %param.16) | data formatting | bytes 4194304 | tf_op args[3]
  43.5 4.6 %copy.23 = bf16[128,4,2,2,1024]{0,4,3,2,1:T(8,128)(2,1)} copy(bf16[128,4,2,2,1024]{0,4,1,2,3:T(8,128)(2,1)} %maximum_bitcast_fusion) | data formatting | bytes 8388608 | tf_op jit(solution)/shard_map/transpose | solution.py:134
  55.6 24.5 %all-to-all-done.1 = bf16[128,8,2048]{2,0,1:T(8,128)(2,1)} async-done(((bf16[128,8,2048]{2,0,1:T(8,128)(2,1)}), bf16[128,8,2048]{2,0,1:T(8,128)(2,1)}, u32[]{:S(2)}, u32[]{:S(2)}) %all-to-all-start.1) | async-done | bytes 4194336 | tf_op jit(solution)/shard_map/all_to_all | solution.py:137
  80.1 5.0 %all-to-all-start = ((bf16[128,8,2048]{0,2,1:T(8,128)(2,1)}), bf16[128,8,2048]{0,2,1:T(8,128)(2,1)}, u32[]{:S(2)}, u32[]{:S(2)}) async-start(bf16[128,8,2048]{0,2,1:T(8,128)(2,1)} %bitcast.47), calls=%async_computation | async-start | bytes 8388608 | tf_op jit(solution)/shard_map/all_to_all | solution.py:137
  85.1 4.0 %fusion = (bf16[4,128,2048]{2,1,0:T(8,128)(2,1)}, bf16[4,128,2048]{2,1,0:T(8,128)(2,1)S(1)}) fusion(bf16[8,128,2048]{2,1,0:T(8,128)(2,1)} %bitcast.8), kind=kLoop, calls=%fused_computation.39 | loop fusion | bytes 8388608 | tf_op jit(solution)/shard_map/slice | solution.py:143
  92.6 40.4 %all-to-all-done = bf16[128,8,2048]{0,2,1:T(8,128)(2,1)} async-done(((bf16[128,8,2048]{0,2,1:T(8,128)(2,1)}), bf16[128,8,2048]{0,2,1:T(8,128)(2,1)}, u32[]{:S(2)}, u32[]{:S(2)}) %all-to-all-start) | async-done | bytes 4194336 | tf_op jit(solution)/shard_map/all_to_all | solution.py:137
  132.9 6.5 %copy.24 = bf16[8,128,2048]{2,1,0:T(8,128)(2,1)} copy(bf16[8,128,2048]{1,2,0:T(8,128)(2,1)} %bitcast.5) | data formatting | bytes 8388608 | tf_op jit(solution)/shard_map/all_to_all | solution.py:137
  141.8 5.5 %collective-permute-start.1 = (bf16[512,2048]{1,0:T(8,128)(2,1)S(1)}, bf16[512,2048]{1,0:T(8,128)(2,1)}, u32[]{:S(2)}, u32[]{:S(2)}) collective-permute-start(bf16[512,2048]{1,0:T(8,128)(2,1)S(1)} %bitcast.54), channel_id=1, source_target_pairs={{0,8},{8,16},{16,24},{1,9},{9,17},{17,25},{2,10},{10,18},{18,26},{... | collective-permute-start | bytes 6291464 | tf_op jit(solution)/shard_map/ppermute | solution.py:21
  147.4 6.6 %pad_maximum_fusion.1.refs_2_.refs_3_.refs_4_.refs_5_.refs_6_.refs_7_.refs_8_.refs_9_.refs_10_.refs_11_ = bf16[1536,2048]{1,0:T(8,128)(2,1)} fusion(bf16[1024,2048]{1,0:T(8,128)(2,1)} %bitcast.11.refs_0_.refs_1_, bf16[512,2048]{1,0:T(8,128)(2,1)} %collective-permute-done), kind=kLoop, calls=%fused_computation.1 | loop fusion | flops 12582912 | bytes 12582912 | tf_op jit(solution)/shard_map/concatenate | solution.py:218
  154.0 29.3 %attn_query_side.2 = (bf16[512,1024]{1,0:T(8,128)(2,1)}, f32[8,2,512]{2,1,0:T(2,128)}) custom-call(bf16[1024,2048]{1,0:T(8,128)(2,1)} %bitcast.42, bf16[1024,2048]{1,0:T(8,128)(2,1)} %bitcast.43, bf16[1536,2048]{1,0:T(8,128)(2,1)} %pad_maximum_fusion.1.refs_2_.refs_3_.refs_4_.refs_5_.refs_6_.refs_7_.refs_8_.refs_9_.refs_10_.refs_11_, ...), custom_call_target="tpu_custom_call" | custom-call | tf_op jit(solution)/shard_map/attn_query_side/pallas_call | solution.py:201
  183.3 8.5 %collective-permute-done.1 = bf16[512,2048]{1,0:T(8,128)(2,1)} collective-permute-done((bf16[512,2048]{1,0:T(8,128)(2,1)S(1)}, bf16[512,2048]{1,0:T(8,128)(2,1)}, u32[]{:S(2)}, u32[]{:S(2)}) %collective-permute-start.1) | collective-permute-done | bytes 2097184 | tf_op jit(solution)/shard_map/ppermute | solution.py:21
  191.7 5.4 %pad_maximum_fusion.2.refs_2_.refs_3_.refs_4_.refs_5_.refs_6_.refs_7_.refs_8_.refs_9_.refs_10_.refs_11_ = bf16[1536,2048]{1,0:T(8,128)(2,1)} fusion(bf16[512,2048]{1,0:T(8,128)(2,1)S(1)} %bitcast.55, bf16[512,2048]{1,0:T(8,128)(2,1)} %collective-permute-done, bf16[512,2048]{1,0:T(8,128)(2,1)} %collective-permute-done.1), kind=kLoop, calls=%fused_computation.2 | loop fusion | flops 18874368 | bytes 12582912 | tf_op jit(solution)/shard_map/concatenate | solution.py:221
  197.2 29.3 %attn_query_side.3 = (bf16[512,1024]{1,0:T(8,128)(2,1)}, f32[8,2,512]{2,1,0:T(2,128)}) custom-call(bf16[1024,2048]{1,0:T(8,128)(2,1)} %bitcast.44, bf16[1024,2048]{1,0:T(8,128)(2,1)} %bitcast.45, bf16[1536,2048]{1,0:T(8,128)(2,1)} %pad_maximum_fusion.2.refs_2_.refs_3_.refs_4_.refs_5_.refs_6_.refs_7_.refs_8_.refs_9_.refs_10_.refs_11_, ...), custom_call_target="tpu_custom_call" | custom-call | tf_op jit(solution)/shard_map/attn_query_side/pallas_call | solution.py:201
  234.9 8.4 %pad_maximum_fusion.refs_2_.refs_3_.refs_4_.refs_5_.refs_6_.refs_7_.refs_8_.refs_9_.refs_10_.refs_11_ = bf16[2048,2048]{1,0:T(8,128)(2,1)} fusion(bf16[1024,2048]{1,0:T(8,128)(2,1)} %collective-permute-done.2, bf16[1024,2048]{1,0:T(8,128)(2,1)} %bitcast.46), kind=kLoop, calls=%fused_computation | loop fusion | flops 16777216 | bytes 16777216 | tf_op jit(solution)/shard_map/concatenate | solution.py:171
  244.0 25.4 %attn_key_side.2 = bf16[1024,1024]{1,0:T(8,128)(2,1)} custom-call(bf16[1024,2048]{1,0:T(8,128)(2,1)} %bitcast.11.refs_0_.refs_1_, bf16[1024,2048]{1,0:T(8,128)(2,1)} %bitcast.11.refs_0_.refs_1_, bf16[2048,2048]{1,0:T(8,128)(2,1)} %pad_maximum_fusion.refs_2_.refs_3_.refs_4_.refs_5_.refs_6_.refs_7_.refs_8_.refs_9_.refs_10_.refs_11_, ...), custom_call_target="tpu_custom_call" | custom-call | tf_op jit(solution)/shard_map/attn_key_side/pallas_call | solution.py:250
  269.5 4.7 %all-to-all-start.3 = ((bf16[4,256,1024]{2,1,0:T(8,128)(2,1)}), bf16[4,256,1024]{2,1,0:T(8,128)(2,1)}, u32[]{:S(2)}, u32[]{:S(2)}) async-start(bf16[4,256,1024]{2,1,0:T(8,128)(2,1)} %bitcast.49), calls=%async_computation.3 | async-start | bytes 4194304 | tf_op jit(solution)/shard_map/all_to_all | solution.py:233
  274.2 25.6 %attn_key_side.3 = bf16[1024,1024]{1,0:T(8,128)(2,1)} custom-call(bf16[1024,2048]{1,0:T(8,128)(2,1)} %bitcast.11.refs_0_.refs_1_, bf16[1024,2048]{1,0:T(8,128)(2,1)} %bitcast.11.refs_0_.refs_1_, bf16[2048,2048]{1,0:T(8,128)(2,1)} %pad_maximum_fusion.refs_2_.refs_3_.refs_4_.refs_5_.refs_6_.refs_7_.refs_8_.refs_9_.refs_10_.refs_11_, ...), custom_call_target="tpu_custom_call" | custom-call | tf_op jit(solution)/shard_map/attn_key_side/pallas_call | solution.py:250
  299.9 4.5 %all-to-all-start.4 = ((bf16[4,256,1024]{2,1,0:T(8,128)(2,1)}), bf16[4,256,1024]{2,1,0:T(8,128)(2,1)}, u32[]{:S(2)}, u32[]{:S(2)}) async-start(bf16[4,256,1024]{2,1,0:T(8,128)(2,1)} %bitcast.48), calls=%async_computation.4 | async-start | bytes 4194304 | tf_op jit(solution)/shard_map/all_to_all | solution.py:233
  313.3 16.8 %all-to-all-done.4 = bf16[4,256,1024]{2,1,0:T(8,128)(2,1)} async-done(((bf16[4,256,1024]{2,1,0:T(8,128)(2,1)}), bf16[4,256,1024]{2,1,0:T(8,128)(2,1)}, u32[]{:S(2)}, u32[]{:S(2)}) %all-to-all-start.4) | async-done | bytes 2097184 | tf_op jit(solution)/shard_map/all_to_all | solution.py:233
  (62 shorter events, 60.4 us)
Async XLA Ops:
  27.3 52.8 %all-to-all-start.1 = ((bf16[128,8,2048]{2,0,1:T(8,128)(2,1)}), bf16[128,8,2048]{2,0,1:T(8,128)(2,1)}, u32[]{:S(2)}, u32[]{:S(2)}) async-start(bf16[128,8,2048]{2,0,1:T(8,128)(2,1)} %all_to_all.70), calls=%async_computation.1 | async-start | bytes 8388608 | tf_op jit(solution)/shard_map/all_to_all | solution.py:137
  43.5 4.7 %copy-start.5 = (s32[4096]{0:T(1024)S(1)}, s32[4096]{0:T(1024)}, u32[]{:S(2)}) copy-start(s32[4096]{0:T(1024)} %param.17) | copy-start | bytes 49156
  80.1 52.8 %all-to-all-start = ((bf16[128,8,2048]{0,2,1:T(8,128)(2,1)}), bf16[128,8,2048]{0,2,1:T(8,128)(2,1)}, u32[]{:S(2)}, u32[]{:S(2)}) async-start(bf16[128,8,2048]{0,2,1:T(8,128)(2,1)} %bitcast.47), calls=%async_computation | async-start | bytes 8388608 | tf_op jit(solution)/shard_map/all_to_all | solution.py:137
  89.1 52.7 %collective-permute-start = (bf16[512,2048]{1,0:T(8,128)(2,1)}, bf16[512,2048]{1,0:T(8,128)(2,1)}, u32[]{:S(2)}, u32[]{:S(2)}) collective-permute-start(bf16[512,2048]{1,0:T(8,128)(2,1)} %bitcast.10), channel_id=1, source_target_pairs={{0,8},{8,16},{16,24},{1,9},{9,17},{17,25},{2,10},{10,18},{18,26},{... | collective-permute-start | bytes 6291464 | tf_op jit(solution)/shard_map/ppermute | solution.py:21
  139.5 95.5 %collective-permute-start.2 = (bf16[1024,2048]{1,0:T(8,128)(2,1)}, bf16[1024,2048]{1,0:T(8,128)(2,1)}, u32[]{:S(2)}, u32[]{:S(2)}) collective-permute-start(bf16[1024,2048]{1,0:T(8,128)(2,1)} %bitcast.41), channel_id=1, source_target_pairs={{8,0},{16,8},{24,16},{9,1},{17,9},{25,17},{10,2},{18,10},{26,18},{... | collective-permute-start | bytes 12582920 | tf_op jit(solution)/shard_map/ppermute | solution.py:21
  141.8 49.9 %collective-permute-start.1 = (bf16[512,2048]{1,0:T(8,128)(2,1)S(1)}, bf16[512,2048]{1,0:T(8,128)(2,1)}, u32[]{:S(2)}, u32[]{:S(2)}) collective-permute-start(bf16[512,2048]{1,0:T(8,128)(2,1)S(1)} %bitcast.54), channel_id=1, source_target_pairs={{0,8},{8,16},{16,24},{1,9},{9,17},{17,25},{2,10},{10,18},{18,26},{... | collective-permute-start | bytes 6291464 | tf_op jit(solution)/shard_map/ppermute | solution.py:21
  197.2 29.3 %copy-start.2 = (bf16[512,1024]{1,0:T(8,128)(2,1)S(1)}, bf16[512,1024]{1,0:T(8,128)(2,1)}, u32[]{:S(2)}) copy-start(bf16[512,1024]{1,0:T(8,128)(2,1)} %get-tuple-element.71) | copy-start | bytes 3145732
  229.2 3.8 %copy-start.3 = (f32[8,2,512]{2,1,0:T(2,128)S(1)}, f32[8,2,512]{2,1,0:T(2,128)}, u32[]{:S(2)}) copy-start(f32[8,2,512]{2,1,0:T(2,128)} %get-tuple-element.73) | copy-start | bytes 98308
  229.2 3.8 %copy-start.4 = (f32[8,2,512]{2,1,0:T(2,128)S(1)}, f32[8,2,512]{2,1,0:T(2,128)}, u32[]{:S(2)}) copy-start(f32[8,2,512]{2,1,0:T(2,128)} %get-tuple-element.72) | copy-start | bytes 98308
  229.2 40.3 %all-to-all-start.2 = ((bf16[4,256,1024]{2,1,0:T(8,128)(2,1)}), bf16[4,256,1024]{2,1,0:T(8,128)(2,1)S(1)}, u32[]{:S(2)}, u32[]{:S(2)}) async-start(bf16[4,256,1024]{2,1,0:T(8,128)(2,1)} %bitcast.51), calls=%async_computation.2 | async-start | bytes 4194304 | tf_op jit(solution)/shard_map/all_to_all | solution.py:233
  233.0 10.4 %collective-permute-start.3 = (f32[8,2,1024]{2,1,0:T(2,128)S(1)}, f32[8,2,1024]{2,1,0:T(2,128)S(1)}, u32[]{:S(2)}, u32[]{:S(2)}) collective-permute-start(f32[8,2,1024]{2,1,0:T(2,128)S(1)} %pad_maximum_fusion.8), channel_id=1, source_target_pairs={{8,0},{16,8},{24,16},{9,1},{17,9},{25,17},{10,2},{18,10},{26,18},{... | collective-permute-start | bytes 196616 | tf_op jit(solution)/shard_map/ppermute | solution.py:21
  243.4 0.7 copy-start
  269.5 30.4 %all-to-all-start.3 = ((bf16[4,256,1024]{2,1,0:T(8,128)(2,1)}), bf16[4,256,1024]{2,1,0:T(8,128)(2,1)}, u32[]{:S(2)}, u32[]{:S(2)}) async-start(bf16[4,256,1024]{2,1,0:T(8,128)(2,1)} %bitcast.49), calls=%async_computation.3 | async-start | bytes 4194304 | tf_op jit(solution)/shard_map/all_to_all | solution.py:233
  299.9 30.2 %all-to-all-start.4 = ((bf16[4,256,1024]{2,1,0:T(8,128)(2,1)}), bf16[4,256,1024]{2,1,0:T(8,128)(2,1)}, u32[]{:S(2)}, u32[]{:S(2)}) async-start(bf16[4,256,1024]{2,1,0:T(8,128)(2,1)} %bitcast.48), calls=%async_computation.4 | async-start | bytes 4194304 | tf_op jit(solution)/shard_map/all_to_all | solution.py:233
  341.8 2.2 copy-start.1

commit v12 on v11

--- a/solution.py
+++ b/solution.py
@@ -232,7 +232,7 @@
     def from_plane(x):
         return lax.all_to_all(x, "clo", split_axis=0, concat_axis=1, tiled=True)
 
-    groups = 2 if heads_p % 2 == 0 else 1
+    groups = 4 if heads_p % 4 == 0 else (2 if heads_p % 2 == 0 else 1)
     hg = heads_p // groups
     dkv_parts = []
     for g in range(groups):

time: 351 us -> 370 us (1.054)
  local copies, waits for them, and re-layouts: 69.8 us -> 85.6 us
  waiting for transfers between devices: 90.3 us -> 82.5 us
  starting transfers between devices: 36.1 us -> 42.1 us
  Pallas kernels: 110 us -> 115 us
    scatter x0 -> x8, local copies, waits for them, and re-layouts: none -> 13.3 us  [the longest x4 7.15 us: _per_device(): attn_dv = attn_dv.at[:, :, g].set(part[:, :, :, 1, :])]
    all_to_all x3 -> x5, waiting for transfers between devices: 16.9 us -> 4.64 us  [from_plane(): return lax.all_to_all(x, 'clo', split_axis=0, concat_axis=1, tiled=True)]
    all_to_all x3 -> x5, starting transfers between devices: 12.9 us -> 18.9 us  [from_plane(): return lax.all_to_all(x, 'clo', split_axis=0, concat_axis=1, tiled=True)]
    pallas_call x2 -> x4, Pallas kernels: 51 us -> 56.4 us  [_per_device(): pl.pallas_call(_key_side_kernel(nblk, scale), out_shape=jax.ShapeDtypeStr...]
    ppermute x4, waiting for transfers between devices: 8.48 us -> 13 us  [shifted(): lax.ppermute(value, axis, [(source, source + steps) for source in range(l...]
    slice x2 -> x4, local copies, waits for them, and re-layouts: 7.61 us -> 9.66 us  [_per_device(): attn_dv = attn_dv.at[:, :, g].set(part[:, :, :, 1, :])]
    unnamed x20 -> x26, local copies, waits for them, and re-layouts: 11.3 us -> 11.5 us
  transfers between devices with their start and end apart: 9 -> 11, of which waited for: 5 -> 7; matrix products, arithmetic and copies ran while one was open for 19% -> 26% of each run, Pallas kernels for 31% -> 28%
where the time goes in v12:
time: 370 us; the launch traced here: 366 us
  Pallas kernels  115 us (31%)
  local copies, waits for them, and re-layouts  85.6 us (23%)
  waiting for transfers between devices  82.5 us (22%)
  starting transfers between devices  42.1 us (11%)
  other arithmetic  40.1 us (11%)
    all_to_all x2, waiting for transfers between devices, to_plane(): lax.all_to_all(x, ('clo', 'head'), split_axis=1, concat_axis=0, tiled=True)  64.9 us
    pallas_call x2, Pallas kernels, query_side(): pl.pallas_call(_query_side_kernel(nblk, scale), out_shape=(jax.ShapeDtype...  58.5 us
    pallas_call x4, Pallas kernels, _per_device(): pl.pallas_call(_key_side_kernel(nblk, scale), out_shape=jax.ShapeDtypeStr...  56.4 us
    all_to_all x5, starting transfers between devices, from_plane(): return lax.all_to_all(x, 'clo', split_axis=0, concat_axis=1, tiled=True)  18.9 us
    all_to_all x2, local copies, waits for them, and re-layouts, to_plane(): lax.all_to_all(x, ('clo', 'head'), split_axis=1, concat_axis=0, tiled=True)  14.3 us
    ppermute x4, starting transfers between devices, shifted(): lax.ppermute(value, axis, [(source, source + steps) for source in range(l...  13.3 us
    ppermute x4, waiting for transfers between devices, shifted(): lax.ppermute(value, axis, [(source, source + steps) for source in range(l...  13 us
    unnamed x26, local copies, waits for them, and re-layouts  11.5 us
  transfers between devices with their start and end apart: 11, of which 7 were waited for; matrix products, arithmetic and copies ran while one was open for 26% of the time, Pallas kernels for 28%

profile of v12, /device:TPU:20, one launch (start us, length us, event | category | flops | bytes accessed | tf_op | source)
XLA Modules:
  0.0 366.2 jit_solution(18224223876005040557)
XLA Ops:
  4.0 4.5 %reshape.454 = bf16[128,2,4,1,1024]{4,2,1,0,3:T(4,128)(2,1)} reshape(bf16[128,8192]{1,0:T(8,128)(2,1)} %param.23) | data formatting | bytes 4194304 | tf_op jit(solution)/shard_map/reshape | solution.py:133
  8.4 4.7 %maximum_bitcast_fusion.1 = bf16[128,4,2,2,1024]{4,1,2,0,3:T(4,128)(2,1)S(1)} fusion(bf16[128,2,4,1,1024]{4,2,1,0,3:T(4,128)(2,1)} %reshape.454, bf16[128,2,4,1,1024]{4,2,1,0,3:T(4,128)(2,1)S(1)} %reshape.453), kind=kLoop, calls=%fused_computation.6 | loop fusion | flops 2097152 | bytes 8388608 | tf_op jit(solution)/shard_map/transpose | solution.py:134
  13.2 6.3 %copy.33 = bf16[128,4,2,2,1024]{4,3,0,2,1:T(2,128)(2,1)} copy(bf16[128,4,2,2,1024]{4,1,2,0,3:T(4,128)(2,1)S(1)} %maximum_bitcast_fusion.1) | data formatting | bytes 8388608 | tf_op jit(solution)/shard_map/transpose | solution.py:134
  19.5 7.8 %all_to_all.94 = bf16[128,8,2048]{2,0,1:T(8,128)(2,1)} reshape(bf16[128,4,2,2,1024]{4,3,0,2,1:T(2,128)(2,1)} %copy.33) | data formatting | bytes 8388608 | tf_op jit(solution)/shard_map/all_to_all | solution.py:137
  27.3 4.9 %all-to-all-start.1 = ((bf16[128,8,2048]{2,0,1:T(8,128)(2,1)}), bf16[128,8,2048]{2,0,1:T(8,128)(2,1)}, u32[]{:S(2)}, u32[]{:S(2)}) async-start(bf16[128,8,2048]{2,0,1:T(8,128)(2,1)} %all_to_all.94), calls=%async_computation.1 | async-start | bytes 8388608 | tf_op jit(solution)/shard_map/all_to_all | solution.py:137
  43.5 4.6 %copy.31 = bf16[128,4,2,2,1024]{0,4,3,2,1:T(8,128)(2,1)} copy(bf16[128,4,2,2,1024]{0,4,1,2,3:T(8,128)(2,1)} %maximum_bitcast_fusion) | data formatting | bytes 8388608 | tf_op jit(solution)/shard_map/transpose | solution.py:134
  55.6 24.5 %all-to-all-done.1 = bf16[128,8,2048]{2,0,1:T(8,128)(2,1)} async-done(((bf16[128,8,2048]{2,0,1:T(8,128)(2,1)}), bf16[128,8,2048]{2,0,1:T(8,128)(2,1)}, u32[]{:S(2)}, u32[]{:S(2)}) %all-to-all-start.1) | async-done | bytes 4194336 | tf_op jit(solution)/shard_map/all_to_all | solution.py:137
  80.1 5.0 %all-to-all-start = ((bf16[128,8,2048]{0,2,1:T(8,128)(2,1)}), bf16[128,8,2048]{0,2,1:T(8,128)(2,1)}, u32[]{:S(2)}, u32[]{:S(2)}) async-start(bf16[128,8,2048]{0,2,1:T(8,128)(2,1)} %bitcast.73), calls=%async_computation | async-start | bytes 8388608 | tf_op jit(solution)/shard_map/all_to_all | solution.py:137
  92.5 40.4 %all-to-all-done = bf16[128,8,2048]{0,2,1:T(8,128)(2,1)} async-done(((bf16[128,8,2048]{0,2,1:T(8,128)(2,1)}), bf16[128,8,2048]{0,2,1:T(8,128)(2,1)}, u32[]{:S(2)}, u32[]{:S(2)}) %all-to-all-start) | async-done | bytes 4194336 | tf_op jit(solution)/shard_map/all_to_all | solution.py:137
  132.9 6.5 %copy.32 = bf16[8,128,2048]{2,1,0:T(8,128)(2,1)} copy(bf16[8,128,2048]{1,2,0:T(8,128)(2,1)} %bitcast.5) | data formatting | bytes 8388608 | tf_op jit(solution)/shard_map/all_to_all | solution.py:137
  141.8 5.5 %collective-permute-start.1 = (bf16[512,2048]{1,0:T(8,128)(2,1)S(1)}, bf16[512,2048]{1,0:T(8,128)(2,1)}, u32[]{:S(2)}, u32[]{:S(2)}) collective-permute-start(bf16[512,2048]{1,0:T(8,128)(2,1)S(1)} %bitcast.78), channel_id=1, source_target_pairs={{0,8},{8,16},{16,24},{1,9},{9,17},{17,25},{2,10},{10,18},{18,26},{... | collective-permute-start | bytes 6291464 | tf_op jit(solution)/shard_map/ppermute | solution.py:21
  147.3 6.6 %pad_maximum_fusion.1.refs_2_.refs_3_.refs_4_.refs_5_.refs_6_.refs_7_.refs_8_.refs_9_.refs_10_.refs_11_ = bf16[1536,2048]{1,0:T(8,128)(2,1)} fusion(bf16[1024,2048]{1,0:T(8,128)(2,1)} %bitcast.11.refs_0_.refs_1_, bf16[512,2048]{1,0:T(8,128)(2,1)} %collective-permute-done), kind=kLoop, calls=%fused_computation.1 | loop fusion | flops 12582912 | bytes 12582912 | tf_op jit(solution)/shard_map/concatenate | solution.py:218
  153.9 29.3 %attn_query_side.2 = (bf16[512,1024]{1,0:T(8,128)(2,1)}, f32[8,2,512]{2,1,0:T(2,128)}) custom-call(bf16[1024,2048]{1,0:T(8,128)(2,1)} %bitcast.68, bf16[1024,2048]{1,0:T(8,128)(2,1)} %bitcast.69, bf16[1536,2048]{1,0:T(8,128)(2,1)} %pad_maximum_fusion.1.refs_2_.refs_3_.refs_4_.refs_5_.refs_6_.refs_7_.refs_8_.refs_9_.refs_10_.refs_11_, ...), custom_call_target="tpu_custom_call" | custom-call | tf_op jit(solution)/shard_map/attn_query_side/pallas_call | solution.py:201
  183.2 8.5 %collective-permute-done.1 = bf16[512,2048]{1,0:T(8,128)(2,1)} collective-permute-done((bf16[512,2048]{1,0:T(8,128)(2,1)S(1)}, bf16[512,2048]{1,0:T(8,128)(2,1)}, u32[]{:S(2)}, u32[]{:S(2)}) %collective-permute-start.1) | collective-permute-done | bytes 2097184 | tf_op jit(solution)/shard_map/ppermute | solution.py:21
  191.7 5.5 %pad_maximum_fusion.2.refs_2_.refs_3_.refs_4_.refs_5_.refs_6_.refs_7_.refs_8_.refs_9_.refs_10_.refs_11_ = bf16[1536,2048]{1,0:T(8,128)(2,1)} fusion(bf16[512,2048]{1,0:T(8,128)(2,1)S(1)} %bitcast.79, bf16[512,2048]{1,0:T(8,128)(2,1)} %collective-permute-done, bf16[512,2048]{1,0:T(8,128)(2,1)} %collective-permute-done.1), kind=kLoop, calls=%fused_computation.2 | loop fusion | flops 18874368 | bytes 12582912 | tf_op jit(solution)/shard_map/concatenate | solution.py:221
  197.2 29.2 %attn_query_side.3 = (bf16[512,1024]{1,0:T(8,128)(2,1)}, f32[8,2,512]{2,1,0:T(2,128)}) custom-call(bf16[1024,2048]{1,0:T(8,128)(2,1)} %bitcast.70, bf16[1024,2048]{1,0:T(8,128)(2,1)} %bitcast.71, bf16[1536,2048]{1,0:T(8,128)(2,1)} %pad_maximum_fusion.2.refs_2_.refs_3_.refs_4_.refs_5_.refs_6_.refs_7_.refs_8_.refs_9_.refs_10_.refs_11_, ...), custom_call_target="tpu_custom_call" | custom-call | tf_op jit(solution)/shard_map/attn_query_side/pallas_call | solution.py:201
  229.9 4.5 %collective-permute-done.2 = bf16[1024,2048]{1,0:T(8,128)(2,1)} collective-permute-done((bf16[1024,2048]{1,0:T(8,128)(2,1)}, bf16[1024,2048]{1,0:T(8,128)(2,1)}, u32[]{:S(2)}, u32[]{:S(2)}) %collective-permute-start.2) | collective-permute-done | bytes 4194336 | tf_op jit(solution)/shard_map/ppermute | solution.py:21
  234.4 8.4 %pad_maximum_fusion.refs_2_.refs_3_.refs_4_.refs_5_.refs_6_.refs_7_.refs_8_.refs_9_.refs_10_.refs_11_ = bf16[2048,2048]{1,0:T(8,128)(2,1)} fusion(bf16[1024,2048]{1,0:T(8,128)(2,1)} %collective-permute-done.2, bf16[1024,2048]{1,0:T(8,128)(2,1)} %bitcast.72), kind=kLoop, calls=%fused_computation | loop fusion | flops 16777216 | bytes 16777216 | tf_op jit(solution)/shard_map/concatenate | solution.py:171
  243.5 14.1 %attn_key_side.5 = bf16[1024,512]{1,0:T(8,128)(2,1)} custom-call(bf16[1024,2048]{1,0:T(8,128)(2,1)} %bitcast.11.refs_0_.refs_1_, bf16[1024,2048]{1,0:T(8,128)(2,1)} %bitcast.11.refs_0_.refs_1_, bf16[2048,2048]{1,0:T(8,128)(2,1)} %pad_maximum_fusion.refs_2_.refs_3_.refs_4_.refs_5_.refs_6_.refs_7_.refs_8_.refs_9_.refs_10_.refs_11_, ...), custom_call_target="tpu_custom_call" | custom-call | tf_op jit(solution)/shard_map/attn_key_side/pallas_call | solution.py:250
  261.4 14.1 %attn_key_side.4 = bf16[1024,512]{1,0:T(8,128)(2,1)} custom-call(bf16[1024,2048]{1,0:T(8,128)(2,1)} %bitcast.11.refs_0_.refs_1_, bf16[1024,2048]{1,0:T(8,128)(2,1)} %bitcast.11.refs_0_.refs_1_, bf16[2048,2048]{1,0:T(8,128)(2,1)} %pad_maximum_fusion.refs_2_.refs_3_.refs_4_.refs_5_.refs_6_.refs_7_.refs_8_.refs_9_.refs_10_.refs_11_, ...), custom_call_target="tpu_custom_call" | custom-call | tf_op jit(solution)/shard_map/attn_key_side/pallas_call | solution.py:250
  279.1 14.1 %attn_key_side.6 = bf16[1024,512]{1,0:T(8,128)(2,1)} custom-call(bf16[1024,2048]{1,0:T(8,128)(2,1)} %bitcast.11.refs_0_.refs_1_, bf16[1024,2048]{1,0:T(8,128)(2,1)} %bitcast.11.refs_0_.refs_1_, bf16[2048,2048]{1,0:T(8,128)(2,1)} %pad_maximum_fusion.refs_2_.refs_3_.refs_4_.refs_5_.refs_6_.refs_7_.refs_8_.refs_9_.refs_10_.refs_11_, ...), custom_call_target="tpu_custom_call" | custom-call | tf_op jit(solution)/shard_map/attn_key_side/pallas_call | solution.py:250
  300.1 14.1 %attn_key_side.7 = bf16[1024,512]{1,0:T(8,128)(2,1)} custom-call(bf16[1024,2048]{1,0:T(8,128)(2,1)} %bitcast.11.refs_0_.refs_1_, bf16[1024,2048]{1,0:T(8,128)(2,1)} %bitcast.11.refs_0_.refs_1_, bf16[2048,2048]{1,0:T(8,128)(2,1)} %pad_maximum_fusion.refs_2_.refs_3_.refs_4_.refs_5_.refs_6_.refs_7_.refs_8_.refs_9_.refs_10_.refs_11_, ...), custom_call_target="tpu_custom_call" | custom-call | tf_op jit(solution)/shard_map/attn_key_side/pallas_call | solution.py:250
  349.0 4.6 %reshape.468 = bf16[256,4096]{1,0:T(8,128)(2,1)} reshape(bf16[256,4,4,2,128]{4,3,2,1,0:T(2,128)(2,1)} %fusion) | data formatting | bytes 4194304 | tf_op jit(solution)/shard_map/reshape | solution.py:268
  360.1 4.5 %reshape.463 = bf16[256,4096]{1,0:T(8,128)(2,1)} reshape(bf16[256,4,4,2,128]{4,3,2,1,0:T(2,128)(2,1)} %fusion.3) | data formatting | bytes 4194304 | tf_op jit(solution)/shard_map/reshape | solution.py:268
  (84 shorter events, 93.0 us)
Async XLA Ops:
  27.3 52.8 %all-to-all-start.1 = ((bf16[128,8,2048]{2,0,1:T(8,128)(2,1)}), bf16[128,8,2048]{2,0,1:T(8,128)(2,1)}, u32[]{:S(2)}, u32[]{:S(2)}) async-start(bf16[128,8,2048]{2,0,1:T(8,128)(2,1)} %all_to_all.94), calls=%async_computation.1 | async-start | bytes 8388608 | tf_op jit(solution)/shard_map/all_to_all | solution.py:137
  43.5 4.6 %copy-start.9 = (s32[4096]{0:T(1024)S(1)}, s32[4096]{0:T(1024)}, u32[]{:S(2)}) copy-start(s32[4096]{0:T(1024)} %param.25) | copy-start | bytes 49156
  80.1 52.8 %all-to-all-start = ((bf16[128,8,2048]{0,2,1:T(8,128)(2,1)}), bf16[128,8,2048]{0,2,1:T(8,128)(2,1)}, u32[]{:S(2)}, u32[]{:S(2)}) async-start(bf16[128,8,2048]{0,2,1:T(8,128)(2,1)} %bitcast.73), calls=%async_computation | async-start | bytes 8388608 | tf_op jit(solution)/shard_map/all_to_all | solution.py:137
  89.1 52.7 %collective-permute-start = (bf16[512,2048]{1,0:T(8,128)(2,1)}, bf16[512,2048]{1,0:T(8,128)(2,1)}, u32[]{:S(2)}, u32[]{:S(2)}) collective-permute-start(bf16[512,2048]{1,0:T(8,128)(2,1)} %bitcast.10), channel_id=1, source_target_pairs={{0,8},{8,16},{16,24},{1,9},{9,17},{17,25},{2,10},{10,18},{18,26},{... | collective-permute-start | bytes 6291464 | tf_op jit(solution)/shard_map/ppermute | solution.py:21
  139.4 95.0 %collective-permute-start.2 = (bf16[1024,2048]{1,0:T(8,128)(2,1)}, bf16[1024,2048]{1,0:T(8,128)(2,1)}, u32[]{:S(2)}, u32[]{:S(2)}) collective-permute-start(bf16[1024,2048]{1,0:T(8,128)(2,1)} %bitcast.67), channel_id=1, source_target_pairs={{8,0},{16,8},{24,16},{9,1},{17,9},{25,17},{10,2},{18,10},{26,18},{... | collective-permute-start | bytes 12582920 | tf_op jit(solution)/shard_map/ppermute | solution.py:21
  141.8 49.9 %collective-permute-start.1 = (bf16[512,2048]{1,0:T(8,128)(2,1)S(1)}, bf16[512,2048]{1,0:T(8,128)(2,1)}, u32[]{:S(2)}, u32[]{:S(2)}) collective-permute-start(bf16[512,2048]{1,0:T(8,128)(2,1)S(1)} %bitcast.78), channel_id=1, source_target_pairs={{0,8},{8,16},{16,24},{1,9},{9,17},{17,25},{2,10},{10,18},{18,26},{... | collective-permute-start | bytes 6291464 | tf_op jit(solution)/shard_map/ppermute | solution.py:21
  197.2 29.2 %copy-start.8 = (f32[8,2,512]{2,1,0:T(2,128)S(1)}, f32[8,2,512]{2,1,0:T(2,128)}, u32[]{:S(2)}) copy-start(f32[8,2,512]{2,1,0:T(2,128)} %get-tuple-element.121) | copy-start | bytes 98308
  227.2 15.6 %collective-permute-start.3 = (f32[8,2,1024]{2,1,0:T(2,128)S(1)}, f32[8,2,1024]{2,1,0:T(2,128)S(1)}, u32[]{:S(2)}, u32[]{:S(2)}) collective-permute-start(f32[8,2,1024]{2,1,0:T(2,128)S(1)} %pad_maximum_fusion.6), channel_id=1, source_target_pairs={{8,0},{16,8},{24,16},{9,1},{17,9},{25,17},{10,2},{18,10},{26,18},{... | collective-permute-start | bytes 196616 | tf_op jit(solution)/shard_map/ppermute | solution.py:21
  242.9 0.7 copy-start
  257.6 18.0 %all-to-all-start.4 = ((bf16[4,256,512]{2,1,0:T(8,128)(2,1)}), bf16[4,256,512]{2,1,0:T(8,128)(2,1)S(1)}, u32[]{:S(2)}, u32[]{:S(2)}) async-start(bf16[4,256,512]{2,1,0:T(8,128)(2,1)} %bitcast.82), calls=%async_computation.4 | async-start | bytes 2097152 | tf_op jit(solution)/shard_map/all_to_all | solution.py:233
  275.6 18.0 %all-to-all-start.3 = ((bf16[4,256,512]{2,1,0:T(8,128)(2,1)}), bf16[4,256,512]{2,1,0:T(8,128)(2,1)S(1)}, u32[]{:S(2)}, u32[]{:S(2)}) async-start(bf16[4,256,512]{2,1,0:T(8,128)(2,1)} %bitcast.81), calls=%async_computation.3 | async-start | bytes 2097152 | tf_op jit(solution)/shard_map/all_to_all | solution.py:233
  293.5 6.6 %copy-start.1 = (bf16[4,256,512]{2,1,0:T(8,128)(2,1)}, bf16[4,256,512]{2,1,0:T(8,128)(2,1)S(1)}, u32[]{:S(2)}) copy-start(bf16[4,256,512]{2,1,0:T(8,128)(2,1)S(1)} %all-to-all-done.3) | copy-start | bytes 3145732
  293.5 22.0 %all-to-all-start.5 = ((bf16[4,256,512]{2,1,0:T(8,128)(2,1)}), bf16[4,256,512]{2,1,0:T(8,128)(2,1)S(1)}, u32[]{:S(2)}, u32[]{:S(2)}) async-start(bf16[4,256,512]{2,1,0:T(8,128)(2,1)} %bitcast.80), calls=%async_computation.5 | async-start | bytes 2097152 | tf_op jit(solution)/shard_map/all_to_all | solution.py:233
  315.5 18.8 %all-to-all-start.6 = ((bf16[4,256,512]{2,1,0:T(8,128)(2,1)}), bf16[4,256,512]{2,1,0:T(8,128)(2,1)}, u32[]{:S(2)}, u32[]{:S(2)}) async-start(bf16[4,256,512]{2,1,0:T(8,128)(2,1)} %bitcast.24), calls=%async_computation.6 | async-start | bytes 2097152 | tf_op jit(solution)/shard_map/all_to_all | solution.py:233
  334.3 30.3 %all-to-all-start.2 = ((bf16[4,256,1024]{2,1,0:T(8,128)(2,1)}), bf16[4,256,1024]{2,1,0:T(8,128)(2,1)S(1)}, u32[]{:S(2)}, u32[]{:S(2)}) async-start(bf16[4,256,1024]{2,1,0:T(8,128)(2,1)} %bitcast.74), calls=%async_computation.2 | async-start | bytes 4194304 | tf_op jit(solution)/shard_map/all_to_all | solution.py:233
  339.5 3.7 %copy-start.5 = (bf16[256,4,2,1,128]{4,3,2,0,1:T(2,128)(2,1)S(1)}, bf16[256,4,2,1,128]{4,3,2,0,1:T(2,128)(2,1)}, u32[]{:S(2)}) copy-start(bf16[256,4,2,1,128]{4,3,2,0,1:T(2,128)(2,1)} %get-tuple-element.129) | copy-start | bytes 1572868
  339.6 4.9 %copy-start.7 = (bf16[256,4,2,1,128]{4,3,2,0,1:T(2,128)(2,1)S(1)}, bf16[256,4,2,1,128]{4,3,2,0,1:T(2,128)(2,1)}, u32[]{:S(2)}) copy-start(bf16[256,4,2,1,128]{4,3,2,0,1:T(2,128)(2,1)} %get-tuple-element.127) | copy-start | bytes 1572868
  349.0 4.6 %copy-start.2 = (bf16[256,4,2,1,128]{4,3,2,0,1:T(2,128)(2,1)S(1)}, bf16[256,4,2,1,128]{4,3,2,0,1:T(2,128)(2,1)}, u32[]{:S(2)}) copy-start(bf16[256,4,2,1,128]{4,3,2,0,1:T(2,128)(2,1)} %get-tuple-element.132) | copy-start | bytes 1572868
  353.6 2.9 copy-start.3
  353.9 3.8 %copy-start.4 = (bf16[256,4,2,1,128]{4,3,2,0,1:T(2,128)(2,1)S(1)}, bf16[256,4,2,1,128]{4,3,2,0,1:T(2,128)(2,1)}, u32[]{:S(2)}) copy-start(bf16[256,4,2,1,128]{4,3,2,0,1:T(2,128)(2,1)} %get-tuple-element.128) | copy-start | bytes 1572868
  356.5 2.4 copy-start.6

commit v13 on v9

--- a/solution.py
+++ b/solution.py
@@ -25,13 +25,34 @@
     return jnp.transpose(jnp.broadcast_to(col, (tok, 128)))[0:1, :]
 
 
-def _query_side_kernel(nblk, scale):
+class _Picked:
+    def __init__(self, refs, starts, tile):
+        self.refs, self.starts, self.tile = refs, starts, tile
+
+    def __getitem__(self, idx):
+        value = self.refs[-1][idx]
+        for p in range(len(self.refs) - 2, -1, -1):
+            value = jnp.where(self.tile < self.starts[p + 1], self.refs[p][idx], value)
+        return value
+
+
+def _query_side_kernel(nblk, scale, layout=None):
     def kernel(*refs):
         q_ref, d_ref = refs[0], refs[1]
-        k_refs = refs[2:2 + nblk]
-        v_refs = refs[2 + nblk:2 + 2 * nblk]
-        bias_ref = refs[2 + 2 * nblk]
-        dq_ref, ld_ref = refs[3 + 2 * nblk], refs[4 + 2 * nblk]
+        if layout is None:
+            k_refs = refs[2:2 + nblk]
+            v_refs = refs[2 + nblk:2 + 2 * nblk]
+            rest = refs[2 + 2 * nblk:]
+        else:
+            tile = pl.program_id(0)
+            at = 2
+            k_refs, v_refs = [], []
+            for group in (k_refs, v_refs):
+                for j, starts in enumerate(layout):
+                    group.append(_Picked(refs[at:at + len(starts)], starts, tile + j))
+                    at += len(starts)
+            rest = refs[at:]
+        bias_ref, dq_ref, ld_ref = rest
         q = q_ref[...]
         d = d_ref[...]
         logits = []
@@ -211,12 +232,43 @@
             name="attn_query_side",
         )(qd, qd, *([window] * (2 * nblk)), q_bias)
 
+    def query_side_pieces(pieces, i_off, count):
+        layout, specs, args = [], [], []
+        for extra in (0, heads_p):
+            for j in range(nblk):
+                starts = []
+                for arr, first, n in pieces:
+                    if first <= j + count - 1 and j <= first + n - 1:
+                        starts.append(first)
+                        specs.append(pl.BlockSpec(
+                            (TILE, HEAD_DIM),
+                            lambda i, h, j=j, first=first, n=n, extra=extra:
+                                (jnp.clip(i + j - first, 0, n - 1), h + extra)))
+                        args.append(arr)
+                if extra == 0:
+                    layout.append(starts)
+        return pl.pallas_call(
+            _query_side_kernel(nblk, scale, layout),
+            out_shape=(
+                jax.ShapeDtypeStruct((count * TILE, width), jnp.bfloat16),
+                jax.ShapeDtypeStruct((heads_p, 2, count * TILE), jnp.float32),
+            ),
+            grid=(count, heads_p),
+            in_specs=[pl.BlockSpec((TILE, HEAD_DIM), lambda i, h: (i + i_off, h)),
+                      pl.BlockSpec((TILE, HEAD_DIM), lambda i, h: (i + i_off, h + heads_p))]
+            + specs + [pl.BlockSpec((TILE, span), lambda i, h: (i + i_off, 0))],
+            out_specs=(own_spec, ld_spec),
+            compiler_params=params,
+            name="attn_query_side",
+        )(qd, qd, *args, q_bias)
+
     if split:
         late = n_tiles // 2
-        dq_late, ld_late = query_side(jnp.concatenate([prev_late, kv], axis=0), late, n_tiles - late, 0)
+        h_t = half // TILE
+        dq_late, ld_late = query_side_pieces([(prev_late, 0, h_t), (kv, h_t, n_tiles)], late, n_tiles - late)
         dq_late, ld_late, prev_early = lax.optimization_barrier((dq_late, ld_late, prev_early))
-        dq_early, ld_early = query_side(
-            jnp.concatenate([prev_early, prev_late, kv[:half]], axis=0), 0, late, 0)
+        dq_early, ld_early = query_side_pieces(
+            [(prev_early, 0, h_t), (prev_late, h_t, h_t), (kv, 2 * h_t, n_tiles)], 0, late)
         dq = jnp.concatenate([dq_early, dq_late], axis=0)
         ld = jnp.concatenate([ld_early, ld_late], axis=2)
     else:

time: 351 us -> 349 us (level)
  other arithmetic: 39 us -> 26.9 us
  waiting for transfers between devices: 94.3 us -> 99 us
    concatenate x2 -> x0, other arithmetic: 12.1 us -> none  [the longest x1 6.65 us: _per_device(): jnp.concatenate([prev_late, kv], axis=0)]
    ppermute x4, waiting for transfers between devices: 8.19 us -> 15.9 us  [shifted(): lax.ppermute(value, axis, [(source, source + steps) for source in range(l...]
    unnamed x15 -> x17, local copies, waits for them, and re-layouts: 10.2 us -> 9.88 us
  transfers between devices with their start and end apart: 9 -> 9, of which waited for: 5 -> 5; matrix products, arithmetic and copies ran while one was open for 18% -> 15% of each run, Pallas kernels for 32% -> 33%
where the time goes in v13:
time: 349 us; the launch traced here: 345 us
  Pallas kernels  113 us (32%)
  waiting for transfers between devices  99 us (28%)
  local copies, waits for them, and re-layouts  69.1 us (20%)
  starting transfers between devices  36.1 us (10%)
  other arithmetic  26.9 us (8%)
    all_to_all x2, waiting for transfers between devices, to_plane(): lax.all_to_all(x, ('clo', 'head'), split_axis=1, concat_axis=0, tiled=True)  64.1 us
    pallas_call x2, Pallas kernels, query_side_pieces(): pl.pallas_call(_query_side_kernel(nblk, scale, layout), out_shape=(jax.Sh...  62.1 us
    pallas_call x2, Pallas kernels, _per_device(): pl.pallas_call(_key_side_kernel(nblk, scale), out_shape=jax.ShapeDtypeStr...  51 us
    all_to_all x3, waiting for transfers between devices, from_plane(): return lax.all_to_all(x, 'clo', split_axis=0, concat_axis=1, tiled=True)  19.1 us
    ppermute x4, waiting for transfers between devices, shifted(): lax.ppermute(value, axis, [(source, source + steps) for source in range(l...  15.9 us
    all_to_all x2, local copies, waits for them, and re-layouts, to_plane(): lax.all_to_all(x, ('clo', 'head'), split_axis=1, concat_axis=0, tiled=True)  14.3 us
    ppermute x4, starting transfers between devices, shifted(): lax.ppermute(value, axis, [(source, source + steps) for source in range(l...  13.2 us
    all_to_all x3, starting transfers between devices, from_plane(): return lax.all_to_all(x, 'clo', split_axis=0, concat_axis=1, tiled=True)  12.9 us
  transfers between devices with their start and end apart: 9, of which 5 were waited for; matrix products, arithmetic and copies ran while one was open for 15% of the time, Pallas kernels for 33%

profile of v13, /device:TPU:20, one launch (start us, length us, event | category | flops | bytes accessed | tf_op | source)
XLA Modules:
  0.0 345.1 jit_solution(11171006416001144491)
XLA Ops:
  4.0 4.5 %reshape.111 = bf16[128,2,4,1,1024]{4,2,1,0,3:T(4,128)(2,1)} reshape(bf16[128,8192]{1,0:T(8,128)(2,1)} %param.6) | data formatting | bytes 4194304 | tf_op jit(solution)/shard_map/reshape | solution.py:151
  8.4 4.7 %maximum_bitcast_fusion.1 = bf16[128,4,2,2,1024]{4,1,2,0,3:T(4,128)(2,1)S(1)} fusion(bf16[128,2,4,1,1024]{4,2,1,0,3:T(4,128)(2,1)S(1)} %reshape.112, bf16[128,2,4,1,1024]{4,2,1,0,3:T(4,128)(2,1)} %reshape.111), kind=kLoop, calls=%fused_computation.4 | loop fusion | flops 2097152 | bytes 8388608 | tf_op jit(solution)/shard_map/transpose | solution.py:153
  13.2 6.3 %copy.21 = bf16[128,4,2,2,1024]{4,3,0,2,1:T(2,128)(2,1)} copy(bf16[128,4,2,2,1024]{4,1,2,0,3:T(4,128)(2,1)S(1)} %maximum_bitcast_fusion.1) | data formatting | bytes 8388608 | tf_op jit(solution)/shard_map/transpose | solution.py:153
  19.4 7.8 %all_to_all.70 = bf16[128,8,2048]{2,0,1:T(8,128)(2,1)} reshape(bf16[128,4,2,2,1024]{4,3,0,2,1:T(2,128)(2,1)} %copy.21) | data formatting | bytes 8388608 | tf_op jit(solution)/shard_map/all_to_all | solution.py:156
  27.2 4.9 %all-to-all-start.1 = ((bf16[128,8,2048]{2,0,1:T(8,128)(2,1)}), bf16[128,8,2048]{2,0,1:T(8,128)(2,1)}, u32[]{:S(2)}, u32[]{:S(2)}) async-start(bf16[128,8,2048]{2,0,1:T(8,128)(2,1)} %all_to_all.70), calls=%async_computation.1 | async-start | bytes 8388608 | tf_op jit(solution)/shard_map/all_to_all | solution.py:156
  35.4 4.1 %copy.17 = bf16[128,8192]{0,1:T(8,128)(2,1)} copy(bf16[128,8192]{1,0:T(8,128)(2,1)} %param.5) | data formatting | bytes 4194304 | tf_op args[0]
  43.4 4.6 %copy.19 = bf16[128,4,2,2,1024]{0,4,3,2,1:T(8,128)(2,1)} copy(bf16[128,4,2,2,1024]{0,4,1,2,3:T(8,128)(2,1)} %maximum_bitcast_fusion) | data formatting | bytes 8388608 | tf_op jit(solution)/shard_map/transpose | solution.py:153
  55.5 24.5 %all-to-all-done.1 = bf16[128,8,2048]{2,0,1:T(8,128)(2,1)} async-done(((bf16[128,8,2048]{2,0,1:T(8,128)(2,1)}), bf16[128,8,2048]{2,0,1:T(8,128)(2,1)}, u32[]{:S(2)}, u32[]{:S(2)}) %all-to-all-start.1) | async-done | bytes 4194336 | tf_op jit(solution)/shard_map/all_to_all | solution.py:156
  80.0 5.0 %all-to-all-start = ((bf16[128,8,2048]{0,2,1:T(8,128)(2,1)}), bf16[128,8,2048]{0,2,1:T(8,128)(2,1)}, u32[]{:S(2)}, u32[]{:S(2)}) async-start(bf16[128,8,2048]{0,2,1:T(8,128)(2,1)} %bitcast.39), calls=%async_computation | async-start | bytes 8388608 | tf_op jit(solution)/shard_map/all_to_all | solution.py:156
  85.0 4.8 %fusion.1 = (bf16[4,128,2048]{2,1,0:T(8,128)(2,1)}, bf16[4,128,2048]{2,1,0:T(8,128)(2,1)}) fusion(bf16[8,128,2048]{2,1,0:T(8,128)(2,1)} %bitcast.8), kind=kLoop, calls=%fused_computation.34 | loop fusion | bytes 8388608 | tf_op jit(solution)/shard_map/slice | solution.py:162
  93.3 39.5 %all-to-all-done = bf16[128,8,2048]{0,2,1:T(8,128)(2,1)} async-done(((bf16[128,8,2048]{0,2,1:T(8,128)(2,1)}), bf16[128,8,2048]{0,2,1:T(8,128)(2,1)}, u32[]{:S(2)}, u32[]{:S(2)}) %all-to-all-start) | async-done | bytes 4194336 | tf_op jit(solution)/shard_map/all_to_all | solution.py:156
  132.8 6.5 %copy.20 = bf16[8,128,2048]{2,1,0:T(8,128)(2,1)} copy(bf16[8,128,2048]{1,2,0:T(8,128)(2,1)} %bitcast.5) | data formatting | bytes 8388608 | tf_op jit(solution)/shard_map/all_to_all | solution.py:156
  141.7 5.5 %collective-permute-start.1 = (bf16[512,2048]{1,0:T(8,128)(2,1)}, bf16[512,2048]{1,0:T(8,128)(2,1)}, u32[]{:S(2)}, u32[]{:S(2)}) collective-permute-start(bf16[512,2048]{1,0:T(8,128)(2,1)} %bitcast.47), channel_id=1, source_target_pairs={{0,8},{8,16},{16,24},{1,9},{9,17},{17,25},{2,10},{10,18},{18,26},{... | collective-permute-start | bytes 6291464 | tf_op jit(solution)/shard_map/ppermute | solution.py:21
  147.2 31.2 %attn_query_side.2 = (bf16[512,1024]{1,0:T(8,128)(2,1)}, f32[8,2,512]{2,1,0:T(2,128)}) custom-call(bf16[1024,2048]{1,0:T(8,128)(2,1)} %bitcast.34, bf16[1024,2048]{1,0:T(8,128)(2,1)} %bitcast.35, bf16[512,2048]{1,0:T(8,128)(2,1)} %copy-done, bf16[512,2048]{1,0:T(8,128)(2,1)} %copy-done, ...), custom_call_target="tpu_custom_call" | custom-call | tf_op jit(solution)/shard_map/attn_query_side/pallas_call | solution.py:250
  178.4 13.5 %collective-permute-done.1.refs_2_.refs_3_.refs_9_.refs_10_ = bf16[512,2048]{1,0:T(8,128)(2,1)} collective-permute-done((bf16[512,2048]{1,0:T(8,128)(2,1)}, bf16[512,2048]{1,0:T(8,128)(2,1)}, u32[]{:S(2)}, u32[]{:S(2)}) %collective-permute-start.1) | collective-permute-done | bytes 2097184 | tf_op jit(solution)/shard_map/ppermute | solution.py:21
  191.9 30.9 %attn_query_side.3 = (bf16[512,1024]{1,0:T(8,128)(2,1)}, f32[8,2,512]{2,1,0:T(2,128)}) custom-call(bf16[1024,2048]{1,0:T(8,128)(2,1)} %bitcast.36, bf16[1024,2048]{1,0:T(8,128)(2,1)} %bitcast.37, bf16[512,2048]{1,0:T(8,128)(2,1)} %collective-permute-done.1.refs_2_.refs_3_.refs_9_.refs_10_, ...), custom_call_target="tpu_custom_call" | custom-call | tf_op jit(solution)/shard_map/attn_query_side/pallas_call | solution.py:250
  233.6 8.4 %pad_maximum_fusion.refs_2_.refs_3_.refs_4_.refs_5_.refs_6_.refs_7_.refs_8_.refs_9_.refs_10_.refs_11_ = bf16[2048,2048]{1,0:T(8,128)(2,1)} fusion(bf16[1024,2048]{1,0:T(8,128)(2,1)} %collective-permute-done.2, bf16[1024,2048]{1,0:T(8,128)(2,1)} %bitcast.38), kind=kLoop, calls=%fused_computation | loop fusion | flops 16777216 | bytes 16777216 | tf_op jit(solution)/shard_map/concatenate | solution.py:190
  242.7 25.4 %attn_key_side.2 = bf16[1024,1024]{1,0:T(8,128)(2,1)} custom-call(bf16[1024,2048]{1,0:T(8,128)(2,1)} %bitcast.11.refs_4_.refs_5_.refs_6_.refs_7_.refs_10_.refs_11_.refs_12_.refs_13_.refs_8_.refs_14_.refs_15_.refs_0_.refs_1_, ...), custom_call_target="tpu_custom_call" | custom-call | tf_op jit(solution)/shard_map/attn_key_side/pallas_call | solution.py:300
  268.1 4.7 %all-to-all-start.3 = ((bf16[4,256,1024]{2,1,0:T(8,128)(2,1)}), bf16[4,256,1024]{2,1,0:T(8,128)(2,1)}, u32[]{:S(2)}, u32[]{:S(2)}) async-start(bf16[4,256,1024]{2,1,0:T(8,128)(2,1)} %bitcast.41), calls=%async_computation.3 | async-start | bytes 4194304 | tf_op jit(solution)/shard_map/all_to_all | solution.py:283
  272.8 25.6 %attn_key_side.3 = bf16[1024,1024]{1,0:T(8,128)(2,1)} custom-call(bf16[1024,2048]{1,0:T(8,128)(2,1)} %bitcast.11.refs_4_.refs_5_.refs_6_.refs_7_.refs_10_.refs_11_.refs_12_.refs_13_.refs_8_.refs_14_.refs_15_.refs_0_.refs_1_, ...), custom_call_target="tpu_custom_call" | custom-call | tf_op jit(solution)/shard_map/attn_key_side/pallas_call | solution.py:300
  298.4 4.5 %all-to-all-start.4 = ((bf16[4,256,1024]{2,1,0:T(8,128)(2,1)}), bf16[4,256,1024]{2,1,0:T(8,128)(2,1)}, u32[]{:S(2)}, u32[]{:S(2)}) async-start(bf16[4,256,1024]{2,1,0:T(8,128)(2,1)} %bitcast.40), calls=%async_computation.4 | async-start | bytes 4194304 | tf_op jit(solution)/shard_map/all_to_all | solution.py:283
  309.6 19.0 %all-to-all-done.4 = bf16[4,256,1024]{2,1,0:T(8,128)(2,1)} async-done(((bf16[4,256,1024]{2,1,0:T(8,128)(2,1)}), bf16[4,256,1024]{2,1,0:T(8,128)(2,1)}, u32[]{:S(2)}, u32[]{:S(2)}) %all-to-all-start.4) | async-done | bytes 2097184 | tf_op jit(solution)/shard_map/all_to_all | solution.py:283
  333.8 4.0 %fusion = (bf16[256,4,2,4,1,128]{5,3,2,1,0,4:T(4,128)(2,1)S(1)}, bf16[256,4,2,4,1,128]{5,3,2,1,0,4:T(4,128)(2,1)}) fusion(bf16[256,4,2,4,2,128]{5,3,2,1,0,4:T(4,128)(2,1)} %copy_dynamic-update-slice_fusion), kind=kLoop, calls=%fused_computation.33 | loop fusion | bytes 8388608 | tf_op jit(solution)/shard_map/slice | solution.py:315
  337.8 4.5 %reshape_squeeze.6 = bf16[256,4096]{1,0:T(8,128)(2,1)} reshape(bf16[256,4,2,4,1,128]{5,3,2,1,0,4:T(4,128)(2,1)} %get-tuple-element.28) | data formatting | bytes 4194304 | tf_op jit(solution)/shard_map/reshape;squeeze | solution.py:314
  (55 shorter events, 49.7 us)
Async XLA Ops:
  27.2 52.8 %all-to-all-start.1 = ((bf16[128,8,2048]{2,0,1:T(8,128)(2,1)}), bf16[128,8,2048]{2,0,1:T(8,128)(2,1)}, u32[]{:S(2)}, u32[]{:S(2)}) async-start(bf16[128,8,2048]{2,0,1:T(8,128)(2,1)} %all_to_all.70), calls=%async_computation.1 | async-start | bytes 8388608 | tf_op jit(solution)/shard_map/all_to_all | solution.py:156
  43.4 4.7 %copy-start.5 = (s32[4096]{0:T(1024)S(1)}, s32[4096]{0:T(1024)}, u32[]{:S(2)}) copy-start(s32[4096]{0:T(1024)} %param.9) | copy-start | bytes 49156
  80.0 52.8 %all-to-all-start = ((bf16[128,8,2048]{0,2,1:T(8,128)(2,1)}), bf16[128,8,2048]{0,2,1:T(8,128)(2,1)}, u32[]{:S(2)}, u32[]{:S(2)}) async-start(bf16[128,8,2048]{0,2,1:T(8,128)(2,1)} %bitcast.39), calls=%async_computation | async-start | bytes 8388608 | tf_op jit(solution)/shard_map/all_to_all | solution.py:156
  89.8 51.8 %collective-permute-start = (bf16[512,2048]{1,0:T(8,128)(2,1)}, bf16[512,2048]{1,0:T(8,128)(2,1)S(1)}, u32[]{:S(2)}, u32[]{:S(2)}) collective-permute-start(bf16[512,2048]{1,0:T(8,128)(2,1)} %bitcast.10), channel_id=1, source_target_pairs={{0,8},{8,16},{16,24},{1,9},{9,17},{17,25},{2,10},{10,18},{18,26},{... | collective-permute-start | bytes 6291464 | tf_op jit(solution)/shard_map/ppermute | solution.py:21
  139.3 94.3 %collective-permute-start.2 = (bf16[1024,2048]{1,0:T(8,128)(2,1)}, bf16[1024,2048]{1,0:T(8,128)(2,1)}, u32[]{:S(2)}, u32[]{:S(2)}) collective-permute-start(bf16[1024,2048]{1,0:T(8,128)(2,1)} %bitcast.33), channel_id=1, source_target_pairs={{8,0},{16,8},{24,16},{9,1},{17,9},{25,17},{10,2},{18,10},{26,18},{... | collective-permute-start | bytes 12582920 | tf_op jit(solution)/shard_map/ppermute | solution.py:21
  141.6 5.5 %copy-start = (bf16[512,2048]{1,0:T(8,128)(2,1)}, bf16[512,2048]{1,0:T(8,128)(2,1)S(1)}, u32[]{:S(2)}) copy-start(bf16[512,2048]{1,0:T(8,128)(2,1)S(1)} %collective-permute-done.refs_2_.refs_3_.refs_8_.refs_9_.refs_4_.refs_5_.refs_6_.refs_11_.refs_12_.refs_13_) | copy-start | bytes 6291460
  141.7 50.2 %collective-permute-start.1 = (bf16[512,2048]{1,0:T(8,128)(2,1)}, bf16[512,2048]{1,0:T(8,128)(2,1)}, u32[]{:S(2)}, u32[]{:S(2)}) collective-permute-start(bf16[512,2048]{1,0:T(8,128)(2,1)} %bitcast.47), channel_id=1, source_target_pairs={{0,8},{8,16},{16,24},{1,9},{9,17},{17,25},{2,10},{10,18},{18,26},{... | collective-permute-start | bytes 6291464 | tf_op jit(solution)/shard_map/ppermute | solution.py:21
  191.9 30.9 %copy-start.2 = (bf16[512,1024]{1,0:T(8,128)(2,1)S(1)}, bf16[512,1024]{1,0:T(8,128)(2,1)}, u32[]{:S(2)}) copy-start(bf16[512,1024]{1,0:T(8,128)(2,1)} %get-tuple-element.23) | copy-start | bytes 3145732
  225.5 3.8 %copy-start.3 = (f32[8,2,512]{2,1,0:T(2,128)S(1)}, f32[8,2,512]{2,1,0:T(2,128)}, u32[]{:S(2)}) copy-start(f32[8,2,512]{2,1,0:T(2,128)} %get-tuple-element.25) | copy-start | bytes 98308
  225.5 3.8 %copy-start.4 = (f32[8,2,512]{2,1,0:T(2,128)S(1)}, f32[8,2,512]{2,1,0:T(2,128)}, u32[]{:S(2)}) copy-start(f32[8,2,512]{2,1,0:T(2,128)} %get-tuple-element.24) | copy-start | bytes 98308
  225.5 42.6 %all-to-all-start.2 = ((bf16[4,256,1024]{2,1,0:T(8,128)(2,1)}), bf16[4,256,1024]{2,1,0:T(8,128)(2,1)S(1)}, u32[]{:S(2)}, u32[]{:S(2)}) async-start(bf16[4,256,1024]{2,1,0:T(8,128)(2,1)} %bitcast.43), calls=%async_computation.2 | async-start | bytes 4194304 | tf_op jit(solution)/shard_map/all_to_all | solution.py:283
  229.3 12.7 %collective-permute-start.3 = (f32[8,2,1024]{2,1,0:T(2,128)S(1)}, f32[8,2,1024]{2,1,0:T(2,128)S(1)}, u32[]{:S(2)}, u32[]{:S(2)}) collective-permute-start(f32[8,2,1024]{2,1,0:T(2,128)S(1)} %pad_maximum_fusion.4), channel_id=1, source_target_pairs={{8,0},{16,8},{24,16},{9,1},{17,9},{25,17},{10,2},{18,10},{26,18},{... | collective-permute-start | bytes 196616 | tf_op jit(solution)/shard_map/ppermute | solution.py:21
  242.0 0.7 copy-start.1
  268.1 30.3 %all-to-all-start.3 = ((bf16[4,256,1024]{2,1,0:T(8,128)(2,1)}), bf16[4,256,1024]{2,1,0:T(8,128)(2,1)}, u32[]{:S(2)}, u32[]{:S(2)}) async-start(bf16[4,256,1024]{2,1,0:T(8,128)(2,1)} %bitcast.41), calls=%async_computation.3 | async-start | bytes 4194304 | tf_op jit(solution)/shard_map/all_to_all | solution.py:283
  298.4 30.2 %all-to-all-start.4 = ((bf16[4,256,1024]{2,1,0:T(8,128)(2,1)}), bf16[4,256,1024]{2,1,0:T(8,128)(2,1)}, u32[]{:S(2)}, u32[]{:S(2)}) async-start(bf16[4,256,1024]{2,1,0:T(8,128)(2,1)} %bitcast.40), calls=%async_computation.4 | async-start | bytes 4194304 | tf_op jit(solution)/shard_map/all_to_all | solution.py:283

commit v14 on v13

--- a/solution.py
+++ b/solution.py
@@ -88,14 +88,24 @@
     return kernel
 
 
-def _key_side_kernel(nblk, scale):
+def _key_side_kernel(nblk, scale, layout=None):
     def kernel(*refs):
         k_ref, v_ref = refs[0], refs[1]
-        q_refs = refs[2:2 + nblk]
-        d_refs = refs[2 + nblk:2 + 2 * nblk]
-        ld_refs = refs[2 + 2 * nblk:2 + 3 * nblk]
-        bias_ref = refs[2 + 3 * nblk]
-        out_ref = refs[3 + 3 * nblk]
+        if layout is None:
+            q_refs = refs[2:2 + nblk]
+            d_refs = refs[2 + nblk:2 + 2 * nblk]
+            rest = refs[2 + 2 * nblk:]
+        else:
+            tile = pl.program_id(0)
+            at = 2
+            q_refs, d_refs = [], []
+            for group in (q_refs, d_refs):
+                for j, starts in enumerate(layout):
+                    group.append(_Picked(refs[at:at + len(starts)], starts, tile + j))
+                    at += len(starts)
+            rest = refs[at:]
+        ld_refs = rest[:nblk]
+        bias_ref, out_ref = rest[nblk:]
         k = k_ref[...]
         v = v_ref[...]
         dk = None
@@ -187,7 +197,7 @@
     q_bias = jnp.concatenate(q_bias, axis=0)
     k_bias = jnp.concatenate(k_bias, axis=0)
     qd, (q_bias, k_bias) = to_plane(attn_q, attn_dout, (q_bias, k_bias))
-    qd_win = jnp.concatenate([qd] + [shifted(qd, "chi", -shift) for shift in range(1, reach + 1)], axis=0)
+    qd_parts = [qd] + [shifted(qd, "chi", -shift) for shift in range(1, reach + 1)]
 
 
     own_spec = pl.BlockSpec((TILE, HEAD_DIM), lambda i, h: (i, h))
@@ -297,16 +307,31 @@
         def gld(j, off=off):
             return pl.BlockSpec((None, 2, TILE), lambda i, h: (h + off, 0, i + j))
 
+        layout, q_specs, q_args = [], [], []
+        for extra in (0, heads_p):
+            for j in range(nblk):
+                starts = []
+                for p, arr in enumerate(qd_parts):
+                    first = p * n_tiles
+                    if first <= j + n_tiles - 1 and j <= first + n_tiles - 1:
+                        starts.append(first)
+                        q_specs.append(pl.BlockSpec(
+                            (TILE, HEAD_DIM),
+                            lambda i, h, j=j, first=first, extra=extra, off=off:
+                                (jnp.clip(i + j - first, 0, n_tiles - 1), h + off + extra)))
+                        q_args.append(arr)
+                if extra == 0:
+                    layout.append(starts)
+
         dkv_g = pl.pallas_call(
-            _key_side_kernel(nblk, scale),
+            _key_side_kernel(nblk, scale, layout),
             out_shape=jax.ShapeDtypeStruct((plane, 2 * hg * HEAD_DIM), jnp.bfloat16),
             grid=(n_tiles, hg),
-            in_specs=[gcol(0), gcol(heads_p)] + [gwin(j, 0) for j in range(nblk)]
-            + [gwin(j, heads_p) for j in range(nblk)] + [gld(j) for j in range(nblk)] + [bias_spec],
+            in_specs=[gcol(0), gcol(heads_p)] + q_specs + [gld(j) for j in range(nblk)] + [bias_spec],
             out_specs=pl.BlockSpec((TILE, 2 * HEAD_DIM), lambda i, h: (i, h)),
             compiler_params=params,
             name="attn_key_side",
-        )(kv, kv, *([qd_win] * (2 * nblk)), *([ld_win] * nblk), k_bias)
+        )(kv, kv, *q_args, *([ld_win] * nblk), k_bias)
         dkv_parts.append(from_plane(dkv_g).reshape(-1, clo_n, 1, hg, 2, HEAD_DIM))
 
     dkv = jnp.concatenate(dkv_parts, axis=2)

time: 349 us -> 348 us (level)
  other arithmetic: 26.9 us -> 18.5 us
  Pallas kernels: 113 us -> 118 us
  waiting for transfers between devices: 99 us -> 103 us
    concatenate x1 -> x0, other arithmetic: 8.4 us -> none  [_per_device(): jnp.concatenate([qd] + [shifted(qd, 'chi', -shift) for shift in range(1,...]
    pallas_call x2, Pallas kernels: 51 us -> 56.1 us  [_per_device(): pl.pallas_call(_key_side_kernel(nblk, scale, layout), out_shape=jax.Shape...]
  transfers between devices with their start and end apart: 9 -> 9, of which waited for: 5 -> 5; matrix products, arithmetic and copies ran while one was open for 15% -> 12% of each run, Pallas kernels for 33% -> 34%
where the time goes in v14:
time: 348 us; the launch traced here: 345 us
  Pallas kernels  118 us (34%)
  waiting for transfers between devices  103 us (30%)
  local copies, waits for them, and re-layouts  68.4 us (20%)
  starting transfers between devices  36.1 us (10%)
  other arithmetic  18.5 us (5%)
    all_to_all x2, waiting for transfers between devices, to_plane(): lax.all_to_all(x, ('clo', 'head'), split_axis=1, concat_axis=0, tiled=True)  64.1 us
    pallas_call x2, Pallas kernels, query_side_pieces(): pl.pallas_call(_query_side_kernel(nblk, scale, layout), out_shape=(jax.Sh...  62.1 us
    pallas_call x2, Pallas kernels, _per_device(): pl.pallas_call(_key_side_kernel(nblk, scale, layout), out_shape=jax.Shape...  56.1 us
    all_to_all x3, waiting for transfers between devices, from_plane(): return lax.all_to_all(x, 'clo', split_axis=0, concat_axis=1, tiled=True)  21 us
    ppermute x4, waiting for transfers between devices, shifted(): lax.ppermute(value, axis, [(source, source + steps) for source in range(l...  18 us
    all_to_all x2, local copies, waits for them, and re-layouts, to_plane(): lax.all_to_all(x, ('clo', 'head'), split_axis=1, concat_axis=0, tiled=True)  14.3 us
    ppermute x4, starting transfers between devices, shifted(): lax.ppermute(value, axis, [(source, source + steps) for source in range(l...  13.2 us
    all_to_all x3, starting transfers between devices, from_plane(): return lax.all_to_all(x, 'clo', split_axis=0, concat_axis=1, tiled=True)  12.9 us
  transfers between devices with their start and end apart: 9, of which 5 were waited for; matrix products, arithmetic and copies ran while one was open for 12% of the time, Pallas kernels for 34%

profile of v14, /device:TPU:20, one launch (start us, length us, event | category | flops | bytes accessed | tf_op | source)
XLA Modules:
  0.0 345.1 jit_solution(6552982711897466546)
XLA Ops:
  4.0 4.5 %reshape.112 = bf16[128,2,4,1,1024]{4,2,1,0,3:T(4,128)(2,1)} reshape(bf16[128,8192]{1,0:T(8,128)(2,1)} %param.7) | data formatting | bytes 4194304 | tf_op jit(solution)/shard_map/reshape | solution.py:162
  8.4 4.7 %maximum_bitcast_fusion.1 = bf16[128,4,2,2,1024]{4,1,2,0,3:T(4,128)(2,1)S(1)} fusion(bf16[128,2,4,1,1024]{4,2,1,0,3:T(4,128)(2,1)} %reshape.112, bf16[128,2,4,1,1024]{4,2,1,0,3:T(4,128)(2,1)S(1)} %reshape.111), kind=kLoop, calls=%fused_computation.3 | loop fusion | flops 2097152 | bytes 8388608 | tf_op jit(solution)/shard_map/transpose | solution.py:163
  13.2 6.3 %copy.21 = bf16[128,4,2,2,1024]{4,3,0,2,1:T(2,128)(2,1)} copy(bf16[128,4,2,2,1024]{4,1,2,0,3:T(4,128)(2,1)S(1)} %maximum_bitcast_fusion.1) | data formatting | bytes 8388608 | tf_op jit(solution)/shard_map/transpose | solution.py:163
  19.4 7.8 %all_to_all.70 = bf16[128,8,2048]{2,0,1:T(8,128)(2,1)} reshape(bf16[128,4,2,2,1024]{4,3,0,2,1:T(2,128)(2,1)} %copy.21) | data formatting | bytes 8388608 | tf_op jit(solution)/shard_map/all_to_all | solution.py:166
  27.2 4.9 %all-to-all-start.1 = ((bf16[128,8,2048]{2,0,1:T(8,128)(2,1)}), bf16[128,8,2048]{2,0,1:T(8,128)(2,1)}, u32[]{:S(2)}, u32[]{:S(2)}) async-start(bf16[128,8,2048]{2,0,1:T(8,128)(2,1)} %all_to_all.70), calls=%async_computation.1 | async-start | bytes 8388608 | tf_op jit(solution)/shard_map/all_to_all | solution.py:166
  35.4 4.1 %copy.18 = bf16[128,8192]{0,1:T(8,128)(2,1)} copy(bf16[128,8192]{1,0:T(8,128)(2,1)} %param.8) | data formatting | bytes 4194304 | tf_op args[3]
  43.4 4.6 %copy.19 = bf16[128,4,2,2,1024]{0,4,3,2,1:T(8,128)(2,1)} copy(bf16[128,4,2,2,1024]{0,4,1,2,3:T(8,128)(2,1)} %maximum_bitcast_fusion) | data formatting | bytes 8388608 | tf_op jit(solution)/shard_map/transpose | solution.py:163
  55.4 24.5 %all-to-all-done.1 = bf16[128,8,2048]{2,0,1:T(8,128)(2,1)} async-done(((bf16[128,8,2048]{2,0,1:T(8,128)(2,1)}), bf16[128,8,2048]{2,0,1:T(8,128)(2,1)}, u32[]{:S(2)}, u32[]{:S(2)}) %all-to-all-start.1) | async-done | bytes 4194336 | tf_op jit(solution)/shard_map/all_to_all | solution.py:166
  80.0 5.0 %all-to-all-start = ((bf16[128,8,2048]{0,2,1:T(8,128)(2,1)}), bf16[128,8,2048]{0,2,1:T(8,128)(2,1)}, u32[]{:S(2)}, u32[]{:S(2)}) async-start(bf16[128,8,2048]{0,2,1:T(8,128)(2,1)} %bitcast.54), calls=%async_computation | async-start | bytes 8388608 | tf_op jit(solution)/shard_map/all_to_all | solution.py:166
  85.0 4.8 %fusion.1 = (bf16[4,128,2048]{2,1,0:T(8,128)(2,1)}, bf16[4,128,2048]{2,1,0:T(8,128)(2,1)}) fusion(bf16[8,128,2048]{2,1,0:T(8,128)(2,1)} %bitcast.8), kind=kLoop, calls=%fused_computation.33 | loop fusion | bytes 8388608 | tf_op jit(solution)/shard_map/slice | solution.py:172
  93.3 39.5 %all-to-all-done = bf16[128,8,2048]{0,2,1:T(8,128)(2,1)} async-done(((bf16[128,8,2048]{0,2,1:T(8,128)(2,1)}), bf16[128,8,2048]{0,2,1:T(8,128)(2,1)}, u32[]{:S(2)}, u32[]{:S(2)}) %all-to-all-start) | async-done | bytes 4194336 | tf_op jit(solution)/shard_map/all_to_all | solution.py:166
  132.8 6.5 %copy.20 = bf16[8,128,2048]{2,1,0:T(8,128)(2,1)} copy(bf16[8,128,2048]{1,2,0:T(8,128)(2,1)} %bitcast.5) | data formatting | bytes 8388608 | tf_op jit(solution)/shard_map/all_to_all | solution.py:166
  141.7 5.5 %collective-permute-start.1 = (bf16[512,2048]{1,0:T(8,128)(2,1)}, bf16[512,2048]{1,0:T(8,128)(2,1)}, u32[]{:S(2)}, u32[]{:S(2)}) collective-permute-start(bf16[512,2048]{1,0:T(8,128)(2,1)} %bitcast.62), channel_id=1, source_target_pairs={{0,8},{8,16},{16,24},{1,9},{9,17},{17,25},{2,10},{10,18},{18,26},{... | collective-permute-start | bytes 6291464 | tf_op jit(solution)/shard_map/ppermute | solution.py:21
  147.2 31.2 %attn_query_side.2 = (bf16[512,1024]{1,0:T(8,128)(2,1)}, f32[8,2,512]{2,1,0:T(2,128)}) custom-call(bf16[1024,2048]{1,0:T(8,128)(2,1)} %bitcast.34, bf16[1024,2048]{1,0:T(8,128)(2,1)} %bitcast.35, bf16[512,2048]{1,0:T(8,128)(2,1)} %copy-done, bf16[512,2048]{1,0:T(8,128)(2,1)} %copy-done, ...), custom_call_target="tpu_custom_call" | custom-call | tf_op jit(solution)/shard_map/attn_query_side/pallas_call | solution.py:260
  178.4 13.5 %collective-permute-done.1.refs_2_.refs_3_.refs_9_.refs_10_ = bf16[512,2048]{1,0:T(8,128)(2,1)} collective-permute-done((bf16[512,2048]{1,0:T(8,128)(2,1)}, bf16[512,2048]{1,0:T(8,128)(2,1)}, u32[]{:S(2)}, u32[]{:S(2)}) %collective-permute-start.1) | collective-permute-done | bytes 2097184 | tf_op jit(solution)/shard_map/ppermute | solution.py:21
  191.9 30.9 %attn_query_side.3 = (bf16[512,1024]{1,0:T(8,128)(2,1)}, f32[8,2,512]{2,1,0:T(2,128)}) custom-call(bf16[1024,2048]{1,0:T(8,128)(2,1)} %bitcast.36, bf16[1024,2048]{1,0:T(8,128)(2,1)} %bitcast.37, bf16[512,2048]{1,0:T(8,128)(2,1)} %collective-permute-done.1.refs_2_.refs_3_.refs_9_.refs_10_, ...), custom_call_target="tpu_custom_call" | custom-call | tf_op jit(solution)/shard_map/attn_query_side/pallas_call | solution.py:260
  231.3 4.5 %collective-permute-done.3 = f32[8,2,1024]{2,1,0:T(2,128)S(1)} collective-permute-done((f32[8,2,1024]{2,1,0:T(2,128)S(1)}, f32[8,2,1024]{2,1,0:T(2,128)S(1)}, u32[]{:S(2)}, u32[]{:S(2)}) %collective-permute-start.3) | collective-permute-done | bytes 65568 | tf_op jit(solution)/shard_map/ppermute | solution.py:21
  236.5 28.1 %attn_key_side.3 = bf16[1024,1024]{1,0:T(8,128)(2,1)} custom-call(bf16[1024,2048]{1,0:T(8,128)(2,1)} %bitcast.11.refs_4_.refs_5_.refs_6_.refs_7_.refs_10_.refs_11_.refs_12_.refs_13_.refs_8_.refs_14_.refs_15_.refs_0_.refs_1_, ...), custom_call_target="tpu_custom_call" | custom-call | tf_op jit(solution)/shard_map/attn_key_side/pallas_call | solution.py:326
  264.5 4.7 %all-to-all-start.4 = ((bf16[4,256,1024]{2,1,0:T(8,128)(2,1)}), bf16[4,256,1024]{2,1,0:T(8,128)(2,1)}, u32[]{:S(2)}, u32[]{:S(2)}) async-start(bf16[4,256,1024]{2,1,0:T(8,128)(2,1)} %bitcast.56), calls=%async_computation.4 | async-start | bytes 4194304 | tf_op jit(solution)/shard_map/all_to_all | solution.py:293
  269.2 28.0 %attn_key_side.2 = bf16[1024,1024]{1,0:T(8,128)(2,1)} custom-call(bf16[1024,2048]{1,0:T(8,128)(2,1)} %bitcast.11.refs_4_.refs_5_.refs_6_.refs_7_.refs_10_.refs_11_.refs_12_.refs_13_.refs_8_.refs_14_.refs_15_.refs_0_.refs_1_, ...), custom_call_target="tpu_custom_call" | custom-call | tf_op jit(solution)/shard_map/attn_key_side/pallas_call | solution.py:326
  297.3 4.5 %all-to-all-start.3 = ((bf16[4,256,1024]{2,1,0:T(8,128)(2,1)}), bf16[4,256,1024]{2,1,0:T(8,128)(2,1)}, u32[]{:S(2)}, u32[]{:S(2)}) async-start(bf16[4,256,1024]{2,1,0:T(8,128)(2,1)} %bitcast.55), calls=%async_computation.3 | async-start | bytes 4194304 | tf_op jit(solution)/shard_map/all_to_all | solution.py:293
  306.6 21.0 %all-to-all-done.3 = bf16[4,256,1024]{2,1,0:T(8,128)(2,1)} async-done(((bf16[4,256,1024]{2,1,0:T(8,128)(2,1)}), bf16[4,256,1024]{2,1,0:T(8,128)(2,1)}, u32[]{:S(2)}, u32[]{:S(2)}) %all-to-all-start.3) | async-done | bytes 2097184 | tf_op jit(solution)/shard_map/all_to_all | solution.py:293
  327.5 4.4 %reshape.113 = bf16[256,4,1,4,2,128]{5,4,3,0,1,2:T(2,128)(2,1)} reshape(bf16[256,4,1024]{2,0,1:T(8,128)(2,1)} %bitcast.16) | data formatting | bytes 4194304 | tf_op jit(solution)/shard_map/reshape | solution.py:335
  337.9 4.5 %reshape_squeeze.6 = bf16[256,4096]{1,0:T(8,128)(2,1)} reshape(bf16[256,4,2,4,1,128]{5,3,2,1,0,4:T(4,128)(2,1)} %get-tuple-element.28) | data formatting | bytes 4194304 | tf_op jit(solution)/shard_map/reshape;squeeze | solution.py:339
  (54 shorter events, 46.2 us)
Async XLA Ops:
  27.2 52.8 %all-to-all-start.1 = ((bf16[128,8,2048]{2,0,1:T(8,128)(2,1)}), bf16[128,8,2048]{2,0,1:T(8,128)(2,1)}, u32[]{:S(2)}, u32[]{:S(2)}) async-start(bf16[128,8,2048]{2,0,1:T(8,128)(2,1)} %all_to_all.70), calls=%async_computation.1 | async-start | bytes 8388608 | tf_op jit(solution)/shard_map/all_to_all | solution.py:166
  43.4 4.6 %copy-start.5 = (s32[4096]{0:T(1024)S(1)}, s32[4096]{0:T(1024)}, u32[]{:S(2)}) copy-start(s32[4096]{0:T(1024)} %param.9) | copy-start | bytes 49156
  80.0 52.8 %all-to-all-start = ((bf16[128,8,2048]{0,2,1:T(8,128)(2,1)}), bf16[128,8,2048]{0,2,1:T(8,128)(2,1)}, u32[]{:S(2)}, u32[]{:S(2)}) async-start(bf16[128,8,2048]{0,2,1:T(8,128)(2,1)} %bitcast.54), calls=%async_computation | async-start | bytes 8388608 | tf_op jit(solution)/shard_map/all_to_all | solution.py:166
  89.8 51.9 %collective-permute-start = (bf16[512,2048]{1,0:T(8,128)(2,1)}, bf16[512,2048]{1,0:T(8,128)(2,1)S(1)}, u32[]{:S(2)}, u32[]{:S(2)}) collective-permute-start(bf16[512,2048]{1,0:T(8,128)(2,1)} %bitcast.10), channel_id=1, source_target_pairs={{0,8},{8,16},{16,24},{1,9},{9,17},{17,25},{2,10},{10,18},{18,26},{... | collective-permute-start | bytes 6291464 | tf_op jit(solution)/shard_map/ppermute | solution.py:21
  139.3 96.5 %collective-permute-start.2 = (bf16[1024,2048]{1,0:T(8,128)(2,1)}, bf16[1024,2048]{1,0:T(8,128)(2,1)}, u32[]{:S(2)}, u32[]{:S(2)}) collective-permute-start(bf16[1024,2048]{1,0:T(8,128)(2,1)} %bitcast.33), channel_id=1, source_target_pairs={{8,0},{16,8},{24,16},{9,1},{17,9},{25,17},{10,2},{18,10},{26,18},{... | collective-permute-start | bytes 12582920 | tf_op jit(solution)/shard_map/ppermute | solution.py:21
  141.7 5.5 %copy-start = (bf16[512,2048]{1,0:T(8,128)(2,1)}, bf16[512,2048]{1,0:T(8,128)(2,1)S(1)}, u32[]{:S(2)}) copy-start(bf16[512,2048]{1,0:T(8,128)(2,1)S(1)} %collective-permute-done.refs_2_.refs_3_.refs_8_.refs_9_.refs_4_.refs_5_.refs_6_.refs_11_.refs_12_.refs_13_) | copy-start | bytes 6291460
  141.7 50.2 %collective-permute-start.1 = (bf16[512,2048]{1,0:T(8,128)(2,1)}, bf16[512,2048]{1,0:T(8,128)(2,1)}, u32[]{:S(2)}, u32[]{:S(2)}) collective-permute-start(bf16[512,2048]{1,0:T(8,128)(2,1)} %bitcast.62), channel_id=1, source_target_pairs={{0,8},{8,16},{16,24},{1,9},{9,17},{17,25},{2,10},{10,18},{18,26},{... | collective-permute-start | bytes 6291464 | tf_op jit(solution)/shard_map/ppermute | solution.py:21
  191.9 30.9 %copy-start.2 = (bf16[512,1024]{1,0:T(8,128)(2,1)S(1)}, bf16[512,1024]{1,0:T(8,128)(2,1)}, u32[]{:S(2)}) copy-start(bf16[512,1024]{1,0:T(8,128)(2,1)} %get-tuple-element.23) | copy-start | bytes 3145732
  225.5 3.8 %copy-start.3 = (f32[8,2,512]{2,1,0:T(2,128)S(1)}, f32[8,2,512]{2,1,0:T(2,128)}, u32[]{:S(2)}) copy-start(f32[8,2,512]{2,1,0:T(2,128)} %get-tuple-element.25) | copy-start | bytes 98308
  225.5 3.8 %copy-start.4 = (f32[8,2,512]{2,1,0:T(2,128)S(1)}, f32[8,2,512]{2,1,0:T(2,128)}, u32[]{:S(2)}) copy-start(f32[8,2,512]{2,1,0:T(2,128)} %get-tuple-element.24) | copy-start | bytes 98308
  225.5 39.0 %all-to-all-start.2 = ((bf16[4,256,1024]{2,1,0:T(8,128)(2,1)}), bf16[4,256,1024]{2,1,0:T(8,128)(2,1)S(1)}, u32[]{:S(2)}, u32[]{:S(2)}) async-start(bf16[4,256,1024]{2,1,0:T(8,128)(2,1)} %bitcast.58), calls=%async_computation.2 | async-start | bytes 4194304 | tf_op jit(solution)/shard_map/all_to_all | solution.py:293
  229.3 6.5 %collective-permute-start.3 = (f32[8,2,1024]{2,1,0:T(2,128)S(1)}, f32[8,2,1024]{2,1,0:T(2,128)S(1)}, u32[]{:S(2)}, u32[]{:S(2)}) collective-permute-start(f32[8,2,1024]{2,1,0:T(2,128)S(1)} %pad_maximum_fusion.3), channel_id=1, source_target_pairs={{8,0},{16,8},{24,16},{9,1},{17,9},{25,17},{10,2},{18,10},{26,18},{... | collective-permute-start | bytes 196616 | tf_op jit(solution)/shard_map/ppermute | solution.py:21
  235.8 0.7 copy-start.1
  264.5 32.7 %all-to-all-start.4 = ((bf16[4,256,1024]{2,1,0:T(8,128)(2,1)}), bf16[4,256,1024]{2,1,0:T(8,128)(2,1)}, u32[]{:S(2)}, u32[]{:S(2)}) async-start(bf16[4,256,1024]{2,1,0:T(8,128)(2,1)} %bitcast.56), calls=%async_computation.4 | async-start | bytes 4194304 | tf_op jit(solution)/shard_map/all_to_all | solution.py:293
  297.3 30.2 %all-to-all-start.3 = ((bf16[4,256,1024]{2,1,0:T(8,128)(2,1)}), bf16[4,256,1024]{2,1,0:T(8,128)(2,1)}, u32[]{:S(2)}, u32[]{:S(2)}) async-start(bf16[4,256,1024]{2,1,0:T(8,128)(2,1)} %bitcast.55), calls=%async_computation.3 | async-start | bytes 4194304 | tf_op jit(solution)/shard_map/all_to_all | solution.py:293

commit v15 on v14

--- a/solution.py
+++ b/solution.py
@@ -104,8 +104,15 @@
                     group.append(_Picked(refs[at:at + len(starts)], starts, tile + j))
                     at += len(starts)
             rest = refs[at:]
-        ld_refs = rest[:nblk]
-        bias_ref, out_ref = rest[nblk:]
+        if layout is None:
+            ld_refs = rest[:nblk]
+            rest = rest[nblk:]
+        else:
+            ld_refs = []
+            for j, starts in enumerate(layout):
+                ld_refs.append(_Picked(rest[:len(starts)], starts, tile + j))
+                rest = rest[len(starts):]
+        bias_ref, out_ref = rest
         k = k_ref[...]
         v = v_ref[...]
         dk = None
@@ -322,16 +329,26 @@
                         q_args.append(arr)
                 if extra == 0:
                     layout.append(starts)
+        ld_specs, ld_args = [], []
+        for j in range(nblk):
+            for p, arr in enumerate(ld_parts):
+                first = p * n_tiles
+                if first <= j + n_tiles - 1 and j <= first + n_tiles - 1:
+                    ld_specs.append(pl.BlockSpec(
+                        (None, 2, TILE),
+                        lambda i, h, j=j, first=first, off=off:
+                            (h + off, 0, jnp.clip(i + j - first, 0, n_tiles - 1))))
+                    ld_args.append(arr)
 
         dkv_g = pl.pallas_call(
             _key_side_kernel(nblk, scale, layout),
             out_shape=jax.ShapeDtypeStruct((plane, 2 * hg * HEAD_DIM), jnp.bfloat16),
             grid=(n_tiles, hg),
-            in_specs=[gcol(0), gcol(heads_p)] + q_specs + [gld(j) for j in range(nblk)] + [bias_spec],
+            in_specs=[gcol(0), gcol(heads_p)] + q_specs + ld_specs + [bias_spec],
             out_specs=pl.BlockSpec((TILE, 2 * HEAD_DIM), lambda i, h: (i, h)),
             compiler_params=params,
             name="attn_key_side",
-        )(kv, kv, *q_args, *([ld_win] * nblk), k_bias)
+        )(kv, kv, *q_args, *ld_args, k_bias)
         dkv_parts.append(from_plane(dkv_g).reshape(-1, clo_n, 1, hg, 2, HEAD_DIM))
 
     dkv = jnp.concatenate(dkv_parts, axis=2)

time: 348 us -> 347 us (level)
    unnamed x17 -> x18, local copies, waits for them, and re-layouts: 10.2 us -> 10.2 us
  transfers between devices with their start and end apart: 9 -> 9, of which waited for: 5 -> 6; matrix products, arithmetic and copies ran while one was open for 12% -> 12% of each run, Pallas kernels for 34% -> 34%
where the time goes in v15:
time: 347 us; the launch traced here: 345 us
  Pallas kernels  118 us (34%)
  waiting for transfers between devices  103 us (30%)
  local copies, waits for them, and re-layouts  68.3 us (20%)
  starting transfers between devices  36.1 us (10%)
  other arithmetic  18.5 us (5%)
    all_to_all x2, waiting for transfers between devices, to_plane(): lax.all_to_all(x, ('clo', 'head'), split_axis=1, concat_axis=0, tiled=True)  64.1 us
    pallas_call x2, Pallas kernels, query_side_pieces(): pl.pallas_call(_query_side_kernel(nblk, scale, layout), out_shape=(jax.Sh...  62.1 us
    pallas_call x2, Pallas kernels, _per_device(): pl.pallas_call(_key_side_kernel(nblk, scale, layout), out_shape=jax.Shape...  55.6 us
    all_to_all x3, waiting for transfers between devices, from_plane(): return lax.all_to_all(x, 'clo', split_axis=0, concat_axis=1, tiled=True)  21 us
    ppermute x4, waiting for transfers between devices, shifted(): lax.ppermute(value, axis, [(source, source + steps) for source in range(l...  18.1 us
    all_to_all x2, local copies, waits for them, and re-layouts, to_plane(): lax.all_to_all(x, ('clo', 'head'), split_axis=1, concat_axis=0, tiled=True)  14.2 us
    ppermute x4, starting transfers between devices, shifted(): lax.ppermute(value, axis, [(source, source + steps) for source in range(l...  13.2 us
    all_to_all x3, starting transfers between devices, from_plane(): return lax.all_to_all(x, 'clo', split_axis=0, concat_axis=1, tiled=True)  12.9 us
  transfers between devices with their start and end apart: 9, of which 6 were waited for; matrix products, arithmetic and copies ran while one was open for 12% of the time, Pallas kernels for 34%

profile of v15, /device:TPU:20, one launch (start us, length us, event | category | flops | bytes accessed | tf_op | source)
XLA Modules:
  0.0 344.6 jit_solution(1512494843454990400)
XLA Ops:
  4.0 4.5 %reshape.112 = bf16[128,2,4,1,1024]{4,2,1,0,3:T(4,128)(2,1)} reshape(bf16[128,8192]{1,0:T(8,128)(2,1)} %param.7) | data formatting | bytes 4194304 | tf_op jit(solution)/shard_map/reshape | solution.py:169
  8.4 4.7 %maximum_bitcast_fusion.1 = bf16[128,4,2,2,1024]{4,1,2,0,3:T(4,128)(2,1)S(1)} fusion(bf16[128,2,4,1,1024]{4,2,1,0,3:T(4,128)(2,1)} %reshape.112, bf16[128,2,4,1,1024]{4,2,1,0,3:T(4,128)(2,1)S(1)} %reshape.111), kind=kLoop, calls=%fused_computation.3 | loop fusion | flops 2097152 | bytes 8388608 | tf_op jit(solution)/shard_map/transpose | solution.py:170
  13.2 6.3 %copy.21 = bf16[128,4,2,2,1024]{4,3,0,2,1:T(2,128)(2,1)} copy(bf16[128,4,2,2,1024]{4,1,2,0,3:T(4,128)(2,1)S(1)} %maximum_bitcast_fusion.1) | data formatting | bytes 8388608 | tf_op jit(solution)/shard_map/transpose | solution.py:170
  19.4 7.8 %all_to_all.70 = bf16[128,8,2048]{2,0,1:T(8,128)(2,1)} reshape(bf16[128,4,2,2,1024]{4,3,0,2,1:T(2,128)(2,1)} %copy.21) | data formatting | bytes 8388608 | tf_op jit(solution)/shard_map/all_to_all | solution.py:173
  27.2 4.9 %all-to-all-start.1 = ((bf16[128,8,2048]{2,0,1:T(8,128)(2,1)}), bf16[128,8,2048]{2,0,1:T(8,128)(2,1)}, u32[]{:S(2)}, u32[]{:S(2)}) async-start(bf16[128,8,2048]{2,0,1:T(8,128)(2,1)} %all_to_all.70), calls=%async_computation.1 | async-start | bytes 8388608 | tf_op jit(solution)/shard_map/all_to_all | solution.py:173
  35.4 4.1 %copy.18 = bf16[128,8192]{0,1:T(8,128)(2,1)} copy(bf16[128,8192]{1,0:T(8,128)(2,1)} %param.8) | data formatting | bytes 4194304 | tf_op args[3]
  39.5 3.9 %maximum_bitcast_fusion = bf16[128,4,2,2,1024]{0,4,1,2,3:T(8,128)(2,1)} fusion(bf16[128,2,4,1,1024]{0,4,2,1,3:T(8,128)(2,1)} %bitcast.60, bf16[128,2,4,1,1024]{0,4,2,1,3:T(8,128)(2,1)S(1)} %bitcast.59), kind=kLoop, calls=%fused_computation.2 | loop fusion | flops 2097152 | bytes 8388608 | tf_op jit(solution)/shard_map/transpose | solution.py:170
  43.4 4.6 %copy.19 = bf16[128,4,2,2,1024]{0,4,3,2,1:T(8,128)(2,1)} copy(bf16[128,4,2,2,1024]{0,4,1,2,3:T(8,128)(2,1)} %maximum_bitcast_fusion) | data formatting | bytes 8388608 | tf_op jit(solution)/shard_map/transpose | solution.py:170
  55.4 24.6 %all-to-all-done.1 = bf16[128,8,2048]{2,0,1:T(8,128)(2,1)} async-done(((bf16[128,8,2048]{2,0,1:T(8,128)(2,1)}), bf16[128,8,2048]{2,0,1:T(8,128)(2,1)}, u32[]{:S(2)}, u32[]{:S(2)}) %all-to-all-start.1) | async-done | bytes 4194336 | tf_op jit(solution)/shard_map/all_to_all | solution.py:173
  80.0 5.0 %all-to-all-start = ((bf16[128,8,2048]{0,2,1:T(8,128)(2,1)}), bf16[128,8,2048]{0,2,1:T(8,128)(2,1)}, u32[]{:S(2)}, u32[]{:S(2)}) async-start(bf16[128,8,2048]{0,2,1:T(8,128)(2,1)} %bitcast.54), calls=%async_computation | async-start | bytes 8388608 | tf_op jit(solution)/shard_map/all_to_all | solution.py:173
  85.0 4.8 %fusion.1 = (bf16[4,128,2048]{2,1,0:T(8,128)(2,1)}, bf16[4,128,2048]{2,1,0:T(8,128)(2,1)}) fusion(bf16[8,128,2048]{2,1,0:T(8,128)(2,1)} %bitcast.8), kind=kLoop, calls=%fused_computation.31 | loop fusion | bytes 8388608 | tf_op jit(solution)/shard_map/slice | solution.py:179
  93.3 39.5 %all-to-all-done = bf16[128,8,2048]{0,2,1:T(8,128)(2,1)} async-done(((bf16[128,8,2048]{0,2,1:T(8,128)(2,1)}), bf16[128,8,2048]{0,2,1:T(8,128)(2,1)}, u32[]{:S(2)}, u32[]{:S(2)}) %all-to-all-start) | async-done | bytes 4194336 | tf_op jit(solution)/shard_map/all_to_all | solution.py:173
  132.8 6.5 %copy.20 = bf16[8,128,2048]{2,1,0:T(8,128)(2,1)} copy(bf16[8,128,2048]{1,2,0:T(8,128)(2,1)} %bitcast.5) | data formatting | bytes 8388608 | tf_op jit(solution)/shard_map/all_to_all | solution.py:173
  141.7 5.5 %collective-permute-start.1 = (bf16[512,2048]{1,0:T(8,128)(2,1)}, bf16[512,2048]{1,0:T(8,128)(2,1)}, u32[]{:S(2)}, u32[]{:S(2)}) collective-permute-start(bf16[512,2048]{1,0:T(8,128)(2,1)} %bitcast.62), channel_id=1, source_target_pairs={{0,8},{8,16},{16,24},{1,9},{9,17},{17,25},{2,10},{10,18},{18,26},{... | collective-permute-start | bytes 6291464 | tf_op jit(solution)/shard_map/ppermute | solution.py:21
  147.1 31.2 %attn_query_side.2 = (bf16[512,1024]{1,0:T(8,128)(2,1)}, f32[8,2,512]{2,1,0:T(2,128)}) custom-call(bf16[1024,2048]{1,0:T(8,128)(2,1)} %bitcast.34, bf16[1024,2048]{1,0:T(8,128)(2,1)} %bitcast.35, bf16[512,2048]{1,0:T(8,128)(2,1)} %copy-done, bf16[512,2048]{1,0:T(8,128)(2,1)} %copy-done, ...), custom_call_target="tpu_custom_call" | custom-call | tf_op jit(solution)/shard_map/attn_query_side/pallas_call | solution.py:267
  178.3 13.5 %collective-permute-done.1.refs_2_.refs_3_.refs_9_.refs_10_ = bf16[512,2048]{1,0:T(8,128)(2,1)} collective-permute-done((bf16[512,2048]{1,0:T(8,128)(2,1)}, bf16[512,2048]{1,0:T(8,128)(2,1)}, u32[]{:S(2)}, u32[]{:S(2)}) %collective-permute-start.1) | collective-permute-done | bytes 2097184 | tf_op jit(solution)/shard_map/ppermute | solution.py:21
  191.8 30.9 %attn_query_side.3 = (bf16[512,1024]{1,0:T(8,128)(2,1)}, f32[8,2,512]{2,1,0:T(2,128)}) custom-call(bf16[1024,2048]{1,0:T(8,128)(2,1)} %bitcast.36, bf16[1024,2048]{1,0:T(8,128)(2,1)} %bitcast.37, bf16[512,2048]{1,0:T(8,128)(2,1)} %collective-permute-done.1.refs_2_.refs_3_.refs_9_.refs_10_, ...), custom_call_target="tpu_custom_call" | custom-call | tf_op jit(solution)/shard_map/attn_query_side/pallas_call | solution.py:267
  236.4 27.8 %attn_key_side.3 = bf16[1024,1024]{1,0:T(8,128)(2,1)} custom-call(bf16[1024,2048]{1,0:T(8,128)(2,1)} %bitcast.11.refs_4_.refs_5_.refs_6_.refs_7_.refs_10_.refs_11_.refs_12_.refs_13_.refs_8_.refs_14_.refs_15_.refs_0_.refs_1_, ...), custom_call_target="tpu_custom_call" | custom-call | tf_op jit(solution)/shard_map/attn_key_side/pallas_call | solution.py:343
  264.2 4.7 %all-to-all-start.4 = ((bf16[4,256,1024]{2,1,0:T(8,128)(2,1)}), bf16[4,256,1024]{2,1,0:T(8,128)(2,1)}, u32[]{:S(2)}, u32[]{:S(2)}) async-start(bf16[4,256,1024]{2,1,0:T(8,128)(2,1)} %bitcast.56), calls=%async_computation.4 | async-start | bytes 4194304 | tf_op jit(solution)/shard_map/all_to_all | solution.py:300
  268.9 27.8 %attn_key_side.2 = bf16[1024,1024]{1,0:T(8,128)(2,1)} custom-call(bf16[1024,2048]{1,0:T(8,128)(2,1)} %bitcast.11.refs_4_.refs_5_.refs_6_.refs_7_.refs_10_.refs_11_.refs_12_.refs_13_.refs_8_.refs_14_.refs_15_.refs_0_.refs_1_, ...), custom_call_target="tpu_custom_call" | custom-call | tf_op jit(solution)/shard_map/attn_key_side/pallas_call | solution.py:343
  296.7 4.5 %all-to-all-start.3 = ((bf16[4,256,1024]{2,1,0:T(8,128)(2,1)}), bf16[4,256,1024]{2,1,0:T(8,128)(2,1)}, u32[]{:S(2)}, u32[]{:S(2)}) async-start(bf16[4,256,1024]{2,1,0:T(8,128)(2,1)} %bitcast.55), calls=%async_computation.3 | async-start | bytes 4194304 | tf_op jit(solution)/shard_map/all_to_all | solution.py:300
  306.0 21.0 %all-to-all-done.3 = bf16[4,256,1024]{2,1,0:T(8,128)(2,1)} async-done(((bf16[4,256,1024]{2,1,0:T(8,128)(2,1)}), bf16[4,256,1024]{2,1,0:T(8,128)(2,1)}, u32[]{:S(2)}, u32[]{:S(2)}) %all-to-all-start.3) | async-done | bytes 2097184 | tf_op jit(solution)/shard_map/all_to_all | solution.py:300
  326.9 4.4 %reshape.113 = bf16[256,4,1,4,2,128]{5,4,3,0,1,2:T(2,128)(2,1)} reshape(bf16[256,4,1024]{2,0,1:T(8,128)(2,1)} %bitcast.16) | data formatting | bytes 4194304 | tf_op jit(solution)/shard_map/reshape | solution.py:352
  337.3 4.5 %reshape_squeeze.6 = bf16[256,4096]{1,0:T(8,128)(2,1)} reshape(bf16[256,4,2,4,1,128]{5,3,2,1,0,4:T(4,128)(2,1)} %get-tuple-element.28) | data formatting | bytes 4194304 | tf_op jit(solution)/shard_map/reshape;squeeze | solution.py:356
  (54 shorter events, 46.8 us)
Async XLA Ops:
  27.2 52.8 %all-to-all-start.1 = ((bf16[128,8,2048]{2,0,1:T(8,128)(2,1)}), bf16[128,8,2048]{2,0,1:T(8,128)(2,1)}, u32[]{:S(2)}, u32[]{:S(2)}) async-start(bf16[128,8,2048]{2,0,1:T(8,128)(2,1)} %all_to_all.70), calls=%async_computation.1 | async-start | bytes 8388608 | tf_op jit(solution)/shard_map/all_to_all | solution.py:173
  43.4 4.6 %copy-start.6 = (s32[4096]{0:T(1024)S(1)}, s32[4096]{0:T(1024)}, u32[]{:S(2)}) copy-start(s32[4096]{0:T(1024)} %param.9) | copy-start | bytes 49156
  80.0 52.8 %all-to-all-start = ((bf16[128,8,2048]{0,2,1:T(8,128)(2,1)}), bf16[128,8,2048]{0,2,1:T(8,128)(2,1)}, u32[]{:S(2)}, u32[]{:S(2)}) async-start(bf16[128,8,2048]{0,2,1:T(8,128)(2,1)} %bitcast.54), calls=%async_computation | async-start | bytes 8388608 | tf_op jit(solution)/shard_map/all_to_all | solution.py:173
  89.8 51.8 %collective-permute-start = (bf16[512,2048]{1,0:T(8,128)(2,1)}, bf16[512,2048]{1,0:T(8,128)(2,1)S(1)}, u32[]{:S(2)}, u32[]{:S(2)}) collective-permute-start(bf16[512,2048]{1,0:T(8,128)(2,1)} %bitcast.10), channel_id=1, source_target_pairs={{0,8},{8,16},{16,24},{1,9},{9,17},{17,25},{2,10},{10,18},{18,26},{... | collective-permute-start | bytes 6291464 | tf_op jit(solution)/shard_map/ppermute | solution.py:21
  139.3 94.3 %collective-permute-start.2 = (bf16[1024,2048]{1,0:T(8,128)(2,1)}, bf16[1024,2048]{1,0:T(8,128)(2,1)}, u32[]{:S(2)}, u32[]{:S(2)}) collective-permute-start(bf16[1024,2048]{1,0:T(8,128)(2,1)} %bitcast.33), channel_id=1, source_target_pairs={{8,0},{16,8},{24,16},{9,1},{17,9},{25,17},{10,2},{18,10},{26,18},{... | collective-permute-start | bytes 12582920 | tf_op jit(solution)/shard_map/ppermute | solution.py:21
  141.6 5.5 %copy-start = (bf16[512,2048]{1,0:T(8,128)(2,1)}, bf16[512,2048]{1,0:T(8,128)(2,1)S(1)}, u32[]{:S(2)}) copy-start(bf16[512,2048]{1,0:T(8,128)(2,1)S(1)} %collective-permute-done.refs_2_.refs_3_.refs_8_.refs_9_.refs_4_.refs_5_.refs_6_.refs_11_.refs_12_.refs_13_) | copy-start | bytes 6291460
  141.7 50.2 %collective-permute-start.1 = (bf16[512,2048]{1,0:T(8,128)(2,1)}, bf16[512,2048]{1,0:T(8,128)(2,1)}, u32[]{:S(2)}, u32[]{:S(2)}) collective-permute-start(bf16[512,2048]{1,0:T(8,128)(2,1)} %bitcast.62), channel_id=1, source_target_pairs={{0,8},{8,16},{16,24},{1,9},{9,17},{17,25},{2,10},{10,18},{18,26},{... | collective-permute-start | bytes 6291464 | tf_op jit(solution)/shard_map/ppermute | solution.py:21
  191.8 30.9 %copy-start.3 = (bf16[512,1024]{1,0:T(8,128)(2,1)S(1)}, bf16[512,1024]{1,0:T(8,128)(2,1)}, u32[]{:S(2)}) copy-start(bf16[512,1024]{1,0:T(8,128)(2,1)} %get-tuple-element.23) | copy-start | bytes 3145732
  225.4 3.8 %copy-start.5 = (f32[8,2,512]{2,1,0:T(2,128)S(1)}, f32[8,2,512]{2,1,0:T(2,128)}, u32[]{:S(2)}) copy-start(f32[8,2,512]{2,1,0:T(2,128)} %get-tuple-element.24) | copy-start | bytes 98308
  225.4 3.8 %copy-start.4 = (f32[8,2,512]{2,1,0:T(2,128)S(1)}, f32[8,2,512]{2,1,0:T(2,128)}, u32[]{:S(2)}) copy-start(f32[8,2,512]{2,1,0:T(2,128)} %get-tuple-element.25) | copy-start | bytes 98308
  225.4 38.7 %all-to-all-start.2 = ((bf16[4,256,1024]{2,1,0:T(8,128)(2,1)}), bf16[4,256,1024]{2,1,0:T(8,128)(2,1)S(1)}, u32[]{:S(2)}, u32[]{:S(2)}) async-start(bf16[4,256,1024]{2,1,0:T(8,128)(2,1)} %bitcast.58), calls=%async_computation.2 | async-start | bytes 4194304 | tf_op jit(solution)/shard_map/all_to_all | solution.py:300
  229.2 6.5 %copy-start.1 = (f32[8,2,1024]{2,1,0:T(2,128)}, f32[8,2,1024]{2,1,0:T(2,128)S(1)}, u32[]{:S(2)}) copy-start(f32[8,2,1024]{2,1,0:T(2,128)S(1)} %constant_dynamic-update-slice_fusion.refs_18_.refs_19_.refs_21_.refs_23_) | copy-start | bytes 196612
  229.3 6.5 %collective-permute-start.3 = (f32[8,2,1024]{2,1,0:T(2,128)S(1)}, f32[8,2,1024]{2,1,0:T(2,128)S(1)}, u32[]{:S(2)}, u32[]{:S(2)}) collective-permute-start(f32[8,2,1024]{2,1,0:T(2,128)S(1)} %constant_dynamic-update-slice_fusion.refs_18_.refs_19_.refs_21_.refs_23_), channel_id=1, source_target_pairs={{8,0},{16,8},{24,16},{9,1},{17,9},{25,17},{10,2},{18,10},{26,18},{... | collective-permute-start | bytes 196616 | tf_op jit(solution)/shard_map/ppermute | solution.py:21
  235.7 0.6 copy-start.2
  264.2 32.5 %all-to-all-start.4 = ((bf16[4,256,1024]{2,1,0:T(8,128)(2,1)}), bf16[4,256,1024]{2,1,0:T(8,128)(2,1)}, u32[]{:S(2)}, u32[]{:S(2)}) async-start(bf16[4,256,1024]{2,1,0:T(8,128)(2,1)} %bitcast.56), calls=%async_computation.4 | async-start | bytes 4194304 | tf_op jit(solution)/shard_map/all_to_all | solution.py:300
  296.7 30.2 %all-to-all-start.3 = ((bf16[4,256,1024]{2,1,0:T(8,128)(2,1)}), bf16[4,256,1024]{2,1,0:T(8,128)(2,1)}, u32[]{:S(2)}, u32[]{:S(2)}) async-start(bf16[4,256,1024]{2,1,0:T(8,128)(2,1)} %bitcast.55), calls=%async_computation.3 | async-start | bytes 4194304 | tf_op jit(solution)/shard_map/all_to_all | solution.py:300

commit v16 on v15

--- a/solution.py
+++ b/solution.py
@@ -196,11 +196,11 @@
         k_doc = lax.dynamic_slice_in_dim(docs_pad, k_start + pad, span)
         k_pos = k_start + cols
         mask = (k_pos[None, :] <= own_pos[:, None]) & (k_doc[None, :] == own_doc[:, None])
-        q_bias.append(jnp.where(mask, 0.0, masked_value).astype(jnp.float32))
+        q_bias.append(jnp.where(mask, 0.0, masked_value).astype(jnp.bfloat16))
         q_doc = lax.dynamic_slice_in_dim(docs_pad, t_start + pad, span)
         q_pos = t_start + cols
         mask = (own_pos[:, None] <= q_pos[None, :]) & (own_doc[:, None] == q_doc[None, :])
-        k_bias.append(jnp.where(mask, 0.0, masked_value).astype(jnp.float32))
+        k_bias.append(jnp.where(mask, 0.0, masked_value).astype(jnp.bfloat16))
     q_bias = jnp.concatenate(q_bias, axis=0)
     k_bias = jnp.concatenate(k_bias, axis=0)
     qd, (q_bias, k_bias) = to_plane(attn_q, attn_dout, (q_bias, k_bias))

time: 347 us -> 347 us (level)
  waiting for transfers between devices: 103 us -> 109 us
  other arithmetic: 18.5 us -> 14.8 us
    all_to_all x2, waiting for transfers between devices: 64.1 us -> 70.1 us  [to_plane(): lax.all_to_all(x, ('clo', 'head'), split_axis=1, concat_axis=0, tiled=True)]
  transfers between devices with their start and end apart: 9 -> 9, of which waited for: 6 -> 6; matrix products, arithmetic and copies ran while one was open for 12% -> 10% of each run, Pallas kernels for 34% -> 34%
where the time goes in v16:
time: 347 us; the launch traced here: 345 us
  Pallas kernels  117 us (34%)
  waiting for transfers between devices  109 us (31%)
  local copies, waits for them, and re-layouts  66.2 us (19%)
  starting transfers between devices  36.1 us (10%)
  other arithmetic  14.8 us (4%)
    all_to_all x2, waiting for transfers between devices, to_plane(): lax.all_to_all(x, ('clo', 'head'), split_axis=1, concat_axis=0, tiled=True)  70.1 us
    pallas_call x2, Pallas kernels, query_side_pieces(): pl.pallas_call(_query_side_kernel(nblk, scale, layout), out_shape=(jax.Sh...  61.7 us
    pallas_call x2, Pallas kernels, _per_device(): pl.pallas_call(_key_side_kernel(nblk, scale, layout), out_shape=jax.Shape...  55.7 us
    all_to_all x3, waiting for transfers between devices, from_plane(): return lax.all_to_all(x, 'clo', split_axis=0, concat_axis=1, tiled=True)  21 us
    ppermute x4, waiting for transfers between devices, shifted(): lax.ppermute(value, axis, [(source, source + steps) for source in range(l...  18.3 us
    all_to_all x2, local copies, waits for them, and re-layouts, to_plane(): lax.all_to_all(x, ('clo', 'head'), split_axis=1, concat_axis=0, tiled=True)  14.4 us
    ppermute x4, starting transfers between devices, shifted(): lax.ppermute(value, axis, [(source, source + steps) for source in range(l...  13.2 us
    all_to_all x3, starting transfers between devices, from_plane(): return lax.all_to_all(x, 'clo', split_axis=0, concat_axis=1, tiled=True)  13 us
  transfers between devices with their start and end apart: 9, of which 6 were waited for; matrix products, arithmetic and copies ran while one was open for 10% of the time, Pallas kernels for 34%

profile of v16, /device:TPU:20, one launch (start us, length us, event | category | flops | bytes accessed | tf_op | source)
XLA Modules:
  0.0 344.7 jit_solution(2730865618364041151)
XLA Ops:
  4.0 4.5 %reshape.112 = bf16[128,2,4,1,1024]{4,2,1,0,3:T(4,128)(2,1)} reshape(bf16[128,8192]{1,0:T(8,128)(2,1)} %param.7) | data formatting | bytes 4194304 | tf_op jit(solution)/shard_map/reshape | solution.py:169
  8.4 4.7 %maximum_bitcast_fusion.1 = bf16[128,4,2,2,1024]{4,1,2,0,3:T(4,128)(2,1)S(1)} fusion(bf16[128,2,4,1,1024]{4,2,1,0,3:T(4,128)(2,1)} %reshape.112, bf16[128,2,4,1,1024]{4,2,1,0,3:T(4,128)(2,1)S(1)} %reshape.111), kind=kLoop, calls=%fused_computation.1 | loop fusion | flops 2097152 | bytes 8388608 | tf_op jit(solution)/shard_map/transpose | solution.py:170
  13.2 6.3 %copy.21 = bf16[128,4,2,2,1024]{4,3,0,2,1:T(2,128)(2,1)} copy(bf16[128,4,2,2,1024]{4,1,2,0,3:T(4,128)(2,1)S(1)} %maximum_bitcast_fusion.1) | data formatting | bytes 8388608 | tf_op jit(solution)/shard_map/transpose | solution.py:170
  19.4 7.9 %all_to_all.70 = bf16[128,8,2048]{2,0,1:T(8,128)(2,1)} reshape(bf16[128,4,2,2,1024]{4,3,0,2,1:T(2,128)(2,1)} %copy.21) | data formatting | bytes 8388608 | tf_op jit(solution)/shard_map/all_to_all | solution.py:173
  27.3 4.9 %all-to-all-start.1 = ((bf16[128,8,2048]{2,0,1:T(8,128)(2,1)}), bf16[128,8,2048]{2,0,1:T(8,128)(2,1)}, u32[]{:S(2)}, u32[]{:S(2)}) async-start(bf16[128,8,2048]{2,0,1:T(8,128)(2,1)} %all_to_all.70), calls=%async_computation.1 | async-start | bytes 8388608 | tf_op jit(solution)/shard_map/all_to_all | solution.py:173
  35.5 4.1 %copy.18 = bf16[128,8192]{0,1:T(8,128)(2,1)} copy(bf16[128,8192]{1,0:T(8,128)(2,1)} %param.8) | data formatting | bytes 4194304 | tf_op args[3]
  49.5 30.5 %all-to-all-done.1 = bf16[128,8,2048]{2,0,1:T(8,128)(2,1)} async-done(((bf16[128,8,2048]{2,0,1:T(8,128)(2,1)}), bf16[128,8,2048]{2,0,1:T(8,128)(2,1)}, u32[]{:S(2)}, u32[]{:S(2)}) %all-to-all-start.1) | async-done | bytes 4194336 | tf_op jit(solution)/shard_map/all_to_all | solution.py:173
  80.1 5.0 %all-to-all-start = ((bf16[128,8,2048]{0,2,1:T(8,128)(2,1)}), bf16[128,8,2048]{0,2,1:T(8,128)(2,1)}, u32[]{:S(2)}, u32[]{:S(2)}) async-start(bf16[128,8,2048]{0,2,1:T(8,128)(2,1)} %bitcast.54), calls=%async_computation | async-start | bytes 8388608 | tf_op jit(solution)/shard_map/all_to_all | solution.py:173
  85.1 4.8 %fusion.1 = (bf16[4,128,2048]{2,1,0:T(8,128)(2,1)}, bf16[4,128,2048]{2,1,0:T(8,128)(2,1)}) fusion(bf16[8,128,2048]{2,1,0:T(8,128)(2,1)} %bitcast.8), kind=kLoop, calls=%fused_computation.31 | loop fusion | bytes 8388608 | tf_op jit(solution)/shard_map/slice | solution.py:179
  89.9 3.5 %collective-permute-start = (bf16[512,2048]{1,0:T(8,128)(2,1)}, bf16[512,2048]{1,0:T(8,128)(2,1)S(1)}, u32[]{:S(2)}, u32[]{:S(2)}) collective-permute-start(bf16[512,2048]{1,0:T(8,128)(2,1)} %bitcast.10), channel_id=1, source_target_pairs={{0,8},{8,16},{16,24},{1,9},{9,17},{17,25},{2,10},{10,18},{18,26},{... | collective-permute-start | bytes 6291464 | tf_op jit(solution)/shard_map/ppermute | solution.py:21
  93.4 39.5 %all-to-all-done = bf16[128,8,2048]{0,2,1:T(8,128)(2,1)} async-done(((bf16[128,8,2048]{0,2,1:T(8,128)(2,1)}), bf16[128,8,2048]{0,2,1:T(8,128)(2,1)}, u32[]{:S(2)}, u32[]{:S(2)}) %all-to-all-start) | async-done | bytes 4194336 | tf_op jit(solution)/shard_map/all_to_all | solution.py:173
  132.9 6.6 %copy.20 = bf16[8,128,2048]{2,1,0:T(8,128)(2,1)} copy(bf16[8,128,2048]{1,2,0:T(8,128)(2,1)} %bitcast.5) | data formatting | bytes 8388608 | tf_op jit(solution)/shard_map/all_to_all | solution.py:173
  141.9 5.4 %collective-permute-start.1 = (bf16[512,2048]{1,0:T(8,128)(2,1)}, bf16[512,2048]{1,0:T(8,128)(2,1)}, u32[]{:S(2)}, u32[]{:S(2)}) collective-permute-start(bf16[512,2048]{1,0:T(8,128)(2,1)} %bitcast.62), channel_id=1, source_target_pairs={{0,8},{8,16},{16,24},{1,9},{9,17},{17,25},{2,10},{10,18},{18,26},{... | collective-permute-start | bytes 6291464 | tf_op jit(solution)/shard_map/ppermute | solution.py:21
  147.4 31.0 %attn_query_side.2 = (bf16[512,1024]{1,0:T(8,128)(2,1)}, f32[8,2,512]{2,1,0:T(2,128)}) custom-call(bf16[1024,2048]{1,0:T(8,128)(2,1)} %bitcast.34, bf16[1024,2048]{1,0:T(8,128)(2,1)} %bitcast.35, bf16[512,2048]{1,0:T(8,128)(2,1)} %copy-done, bf16[512,2048]{1,0:T(8,128)(2,1)} %copy-done, ...), custom_call_target="tpu_custom_call" | custom-call | tf_op jit(solution)/shard_map/attn_query_side/pallas_call | solution.py:267
  178.3 13.7 %collective-permute-done.1.refs_2_.refs_3_.refs_9_.refs_10_ = bf16[512,2048]{1,0:T(8,128)(2,1)} collective-permute-done((bf16[512,2048]{1,0:T(8,128)(2,1)}, bf16[512,2048]{1,0:T(8,128)(2,1)}, u32[]{:S(2)}, u32[]{:S(2)}) %collective-permute-start.1) | collective-permute-done | bytes 2097184 | tf_op jit(solution)/shard_map/ppermute | solution.py:21
  192.1 30.7 %attn_query_side.3 = (bf16[512,1024]{1,0:T(8,128)(2,1)}, f32[8,2,512]{2,1,0:T(2,128)}) custom-call(bf16[1024,2048]{1,0:T(8,128)(2,1)} %bitcast.36, bf16[1024,2048]{1,0:T(8,128)(2,1)} %bitcast.37, bf16[512,2048]{1,0:T(8,128)(2,1)} %collective-permute-done.1.refs_2_.refs_3_.refs_9_.refs_10_, ...), custom_call_target="tpu_custom_call" | custom-call | tf_op jit(solution)/shard_map/attn_query_side/pallas_call | solution.py:267
  225.5 3.7 %all-to-all-start.2 = ((bf16[4,256,1024]{2,1,0:T(8,128)(2,1)}), bf16[4,256,1024]{2,1,0:T(8,128)(2,1)S(1)}, u32[]{:S(2)}, u32[]{:S(2)}) async-start(bf16[4,256,1024]{2,1,0:T(8,128)(2,1)} %bitcast.58), calls=%async_computation.2 | async-start | bytes 4194304 | tf_op jit(solution)/shard_map/all_to_all | solution.py:300
  236.4 27.7 %attn_key_side.3 = bf16[1024,1024]{1,0:T(8,128)(2,1)} custom-call(bf16[1024,2048]{1,0:T(8,128)(2,1)} %bitcast.11.refs_4_.refs_5_.refs_6_.refs_7_.refs_10_.refs_11_.refs_12_.refs_13_.refs_8_.refs_14_.refs_15_.refs_0_.refs_1_, ...), custom_call_target="tpu_custom_call" | custom-call | tf_op jit(solution)/shard_map/attn_key_side/pallas_call | solution.py:343
  264.1 4.7 %all-to-all-start.4 = ((bf16[4,256,1024]{2,1,0:T(8,128)(2,1)}), bf16[4,256,1024]{2,1,0:T(8,128)(2,1)}, u32[]{:S(2)}, u32[]{:S(2)}) async-start(bf16[4,256,1024]{2,1,0:T(8,128)(2,1)} %bitcast.56), calls=%async_computation.4 | async-start | bytes 4194304 | tf_op jit(solution)/shard_map/all_to_all | solution.py:300
  268.9 28.0 %attn_key_side.2 = bf16[1024,1024]{1,0:T(8,128)(2,1)} custom-call(bf16[1024,2048]{1,0:T(8,128)(2,1)} %bitcast.11.refs_4_.refs_5_.refs_6_.refs_7_.refs_10_.refs_11_.refs_12_.refs_13_.refs_8_.refs_14_.refs_15_.refs_0_.refs_1_, ...), custom_call_target="tpu_custom_call" | custom-call | tf_op jit(solution)/shard_map/attn_key_side/pallas_call | solution.py:343
  296.9 4.5 %all-to-all-start.3 = ((bf16[4,256,1024]{2,1,0:T(8,128)(2,1)}), bf16[4,256,1024]{2,1,0:T(8,128)(2,1)}, u32[]{:S(2)}, u32[]{:S(2)}) async-start(bf16[4,256,1024]{2,1,0:T(8,128)(2,1)} %bitcast.55), calls=%async_computation.3 | async-start | bytes 4194304 | tf_op jit(solution)/shard_map/all_to_all | solution.py:300
  306.2 21.0 %all-to-all-done.3 = bf16[4,256,1024]{2,1,0:T(8,128)(2,1)} async-done(((bf16[4,256,1024]{2,1,0:T(8,128)(2,1)}), bf16[4,256,1024]{2,1,0:T(8,128)(2,1)}, u32[]{:S(2)}, u32[]{:S(2)}) %all-to-all-start.3) | async-done | bytes 2097184 | tf_op jit(solution)/shard_map/all_to_all | solution.py:300
  327.1 4.4 %reshape.113 = bf16[256,4,1,4,2,128]{5,4,3,0,1,2:T(2,128)(2,1)} reshape(bf16[256,4,1024]{2,0,1:T(8,128)(2,1)} %bitcast.16) | data formatting | bytes 4194304 | tf_op jit(solution)/shard_map/reshape | solution.py:352
  337.5 4.5 %reshape_squeeze.7 = bf16[256,4096]{1,0:T(8,128)(2,1)} reshape(bf16[256,4,2,4,1,128]{5,3,2,1,0,4:T(4,128)(2,1)} %get-tuple-element.27) | data formatting | bytes 4194304 | tf_op jit(solution)/shard_map/reshape;squeeze | solution.py:357
  (54 shorter events, 42.1 us)
Async XLA Ops:
  27.3 52.8 %all-to-all-start.1 = ((bf16[128,8,2048]{2,0,1:T(8,128)(2,1)}), bf16[128,8,2048]{2,0,1:T(8,128)(2,1)}, u32[]{:S(2)}, u32[]{:S(2)}) async-start(bf16[128,8,2048]{2,0,1:T(8,128)(2,1)} %all_to_all.70), calls=%async_computation.1 | async-start | bytes 8388608 | tf_op jit(solution)/shard_map/all_to_all | solution.py:173
  41.5 2.3 copy-start.6
  80.1 52.9 %all-to-all-start = ((bf16[128,8,2048]{0,2,1:T(8,128)(2,1)}), bf16[128,8,2048]{0,2,1:T(8,128)(2,1)}, u32[]{:S(2)}, u32[]{:S(2)}) async-start(bf16[128,8,2048]{0,2,1:T(8,128)(2,1)} %bitcast.54), calls=%async_computation | async-start | bytes 8388608 | tf_op jit(solution)/shard_map/all_to_all | solution.py:173
  89.9 52.0 %collective-permute-start = (bf16[512,2048]{1,0:T(8,128)(2,1)}, bf16[512,2048]{1,0:T(8,128)(2,1)S(1)}, u32[]{:S(2)}, u32[]{:S(2)}) collective-permute-start(bf16[512,2048]{1,0:T(8,128)(2,1)} %bitcast.10), channel_id=1, source_target_pairs={{0,8},{8,16},{16,24},{1,9},{9,17},{17,25},{2,10},{10,18},{18,26},{... | collective-permute-start | bytes 6291464 | tf_op jit(solution)/shard_map/ppermute | solution.py:21
  139.5 94.3 %collective-permute-start.2 = (bf16[1024,2048]{1,0:T(8,128)(2,1)}, bf16[1024,2048]{1,0:T(8,128)(2,1)}, u32[]{:S(2)}, u32[]{:S(2)}) collective-permute-start(bf16[1024,2048]{1,0:T(8,128)(2,1)} %bitcast.33), channel_id=1, source_target_pairs={{8,0},{16,8},{24,16},{9,1},{17,9},{25,17},{10,2},{18,10},{26,18},{... | collective-permute-start | bytes 12582920 | tf_op jit(solution)/shard_map/ppermute | solution.py:21
  141.9 5.5 %copy-start = (bf16[512,2048]{1,0:T(8,128)(2,1)}, bf16[512,2048]{1,0:T(8,128)(2,1)S(1)}, u32[]{:S(2)}) copy-start(bf16[512,2048]{1,0:T(8,128)(2,1)S(1)} %collective-permute-done.refs_2_.refs_3_.refs_8_.refs_9_.refs_4_.refs_5_.refs_6_.refs_11_.refs_12_.refs_13_) | copy-start | bytes 6291460
  141.9 50.2 %collective-permute-start.1 = (bf16[512,2048]{1,0:T(8,128)(2,1)}, bf16[512,2048]{1,0:T(8,128)(2,1)}, u32[]{:S(2)}, u32[]{:S(2)}) collective-permute-start(bf16[512,2048]{1,0:T(8,128)(2,1)} %bitcast.62), channel_id=1, source_target_pairs={{0,8},{8,16},{16,24},{1,9},{9,17},{17,25},{2,10},{10,18},{18,26},{... | collective-permute-start | bytes 6291464 | tf_op jit(solution)/shard_map/ppermute | solution.py:21
  192.1 30.7 %copy-start.3 = (bf16[512,1024]{1,0:T(8,128)(2,1)S(1)}, bf16[512,1024]{1,0:T(8,128)(2,1)}, u32[]{:S(2)}) copy-start(bf16[512,1024]{1,0:T(8,128)(2,1)} %get-tuple-element.23) | copy-start | bytes 3145732
  225.5 3.8 %copy-start.5 = (f32[8,2,512]{2,1,0:T(2,128)S(1)}, f32[8,2,512]{2,1,0:T(2,128)}, u32[]{:S(2)}) copy-start(f32[8,2,512]{2,1,0:T(2,128)} %get-tuple-element.24) | copy-start | bytes 98308
  225.5 3.8 %copy-start.4 = (f32[8,2,512]{2,1,0:T(2,128)S(1)}, f32[8,2,512]{2,1,0:T(2,128)}, u32[]{:S(2)}) copy-start(f32[8,2,512]{2,1,0:T(2,128)} %get-tuple-element.25) | copy-start | bytes 98308
  225.5 38.6 %all-to-all-start.2 = ((bf16[4,256,1024]{2,1,0:T(8,128)(2,1)}), bf16[4,256,1024]{2,1,0:T(8,128)(2,1)S(1)}, u32[]{:S(2)}, u32[]{:S(2)}) async-start(bf16[4,256,1024]{2,1,0:T(8,128)(2,1)} %bitcast.58), calls=%async_computation.2 | async-start | bytes 4194304 | tf_op jit(solution)/shard_map/all_to_all | solution.py:300
  229.3 6.5 %copy-start.1 = (f32[8,2,1024]{2,1,0:T(2,128)}, f32[8,2,1024]{2,1,0:T(2,128)S(1)}, u32[]{:S(2)}) copy-start(f32[8,2,1024]{2,1,0:T(2,128)S(1)} %constant_dynamic-update-slice_fusion.refs_18_.refs_19_.refs_21_.refs_23_) | copy-start | bytes 196612
  229.3 6.5 %collective-permute-start.3 = (f32[8,2,1024]{2,1,0:T(2,128)S(1)}, f32[8,2,1024]{2,1,0:T(2,128)S(1)}, u32[]{:S(2)}, u32[]{:S(2)}) collective-permute-start(f32[8,2,1024]{2,1,0:T(2,128)S(1)} %constant_dynamic-update-slice_fusion.refs_18_.refs_19_.refs_21_.refs_23_), channel_id=1, source_target_pairs={{8,0},{16,8},{24,16},{9,1},{17,9},{25,17},{10,2},{18,10},{26,18},{... | collective-permute-start | bytes 196616 | tf_op jit(solution)/shard_map/ppermute | solution.py:21
  235.8 0.6 copy-start.2
  264.1 32.7 %all-to-all-start.4 = ((bf16[4,256,1024]{2,1,0:T(8,128)(2,1)}), bf16[4,256,1024]{2,1,0:T(8,128)(2,1)}, u32[]{:S(2)}, u32[]{:S(2)}) async-start(bf16[4,256,1024]{2,1,0:T(8,128)(2,1)} %bitcast.56), calls=%async_computation.4 | async-start | bytes 4194304 | tf_op jit(solution)/shard_map/all_to_all | solution.py:300
  296.9 30.2 %all-to-all-start.3 = ((bf16[4,256,1024]{2,1,0:T(8,128)(2,1)}), bf16[4,256,1024]{2,1,0:T(8,128)(2,1)}, u32[]{:S(2)}, u32[]{:S(2)}) async-start(bf16[4,256,1024]{2,1,0:T(8,128)(2,1)} %bitcast.55), calls=%async_computation.3 | async-start | bytes 4194304 | tf_op jit(solution)/shard_map/all_to_all | solution.py:300
